TPU v7x, 32 devices: a whole 2x2x4 slice. The times are simulated.
32 devices in a mesh: req: 8 (over z, y), tp: 4 (over x, core).
Axes of the slice: x: 2, y: 2, z: 4, core: 2. Of those that a mesh axis runs over, the one named last changes fastest.
Arguments:
- tokens_in: bfloat16 [24, 4, 2048], P('req'), may hold values from -6 to 6
- attn_norm: bfloat16 [2048], replicated, may hold values from 0.099609375 to 1.8984375
- qkv_weight: bfloat16 [2048, 3, 2048], P(None, None, 'tp'), may hold values from -0.125 to 0.125
- qkv_bias: bfloat16 [3, 2048], P(None, 'tp'), may hold values from -12 to 12
- out_weight: bfloat16 [2048, 2048], P('tp'), may hold values from -0.125 to 0.125
- cache_keys: bfloat16 [320, 128, 2048], P('req', None, 'tp'), may hold values from -12 to 12
- cache_values: bfloat16 [320, 128, 2048], P('req', None, 'tp'), may hold values from -6 to 6
- page_table: int32 [24, 37], replicated, may hold values from -1 to 319, as said below
- cache_lengths: int32 [24], replicated, may hold values from 1 to 4736, as said below
- mlp_norm: bfloat16 [2048], replicated, may hold values from 0.099609375 to 1.8984375
- routes: int32 [24, 4, 4], P('req'), may hold values from 0 to 7, all different within a row; in each aligned block of 12 rows (0 to 11, 12 to 23, ..., all dimensions but the last counted through in order) at most 6 rows name the same one
- route_gates: float32 [24, 4, 4], P('req'), may hold values from 0.05 to 0.5
- expert_w_gate: bfloat16 [8, 2048, 1408], P('req', None, 'tp'), may hold values from -0.125 to 0.125
- expert_w_up: bfloat16 [8, 2048, 1408], P('req', None, 'tp'), may hold values from -0.125 to 0.125
- expert_w_down: bfloat16 [8, 1408, 2048], P('req', 'tp'), may hold values from -0.15625 to 0.15625
- shared_w_gate: bfloat16 [2048, 5632], P('tp', 'req'), may hold values from -0.125 to 0.125
- shared_w_up: bfloat16 [2048, 5632], P('tp', 'req'), may hold values from -0.125 to 0.125
- shared_w_down: bfloat16 [5632, 2048], P('req', 'tp'), may hold values from -0.078125 to 0.078125
- shared_switch: bfloat16 [2048], replicated, may hold values from -0.125 to 0.125
Outputs:
- layer_out: bfloat16 [24, 4, 2048], P('req', None, 'tp')
Inputs may be any that keep to these rules, and one draw needn't show every extreme that they name: `page_table`: entry [r, j] is the pool page holding positions j*128 to (j+1)*128 - 1 of request r's cache, or -1. No pool page is named twice. 6 requests, drawn from the seed, have all 37 entries set, all outside the first 12 pages of every block of 40 pool pages; every other request r has exactly its first 4 entries set, all among pool pages (r // 3)*40 to (r // 3)*40 + 3*4 - 1. `cache_lengths`: A long request has 2368 to 4736 cached tokens, any other 1 to 512; both largest values occur in every draw. `routes`: the 4 experts of a token differ. Among the 12 tokens of each aligned block of rows (those of one index of req) no expert is named more than 6 times, and in some of those blocks one expert is named exactly 6 times.
All inputs are finite; a program needn't handle non-finite values.
Results may differ from a plain program's by a relative error of at most 0.006.
Values may be sent and summed in bfloat16 or wider, within the bound.
No kernel may reach another device: no remote copies, remote signals or barrier semaphores. Data moves between devices by JAX's collectives and lax.ppermute only.
A program may use at most 128 MiB of HBM per device.

v0:
```python
import math

import jax
import jax.numpy as jnp
from jax import lax
from jax.sharding import PartitionSpec as P

HD = 128
TOPK = 4


NEG = -1e30
EPS = 1e-06
THETA = 1000000.0
HIGHEST = lax.Precision.HIGHEST


def rms_norm(inputs, gain_vector):
    values = inputs.astype(jnp.float32)
    scaled = values * lax.rsqrt(jnp.mean(values * values, axis=-1, keepdims=True) + EPS)
    return (scaled * gain_vector.astype(jnp.float32)).astype(jnp.bfloat16)


def rotate(values, positions):
    half_dim = values.shape[-1] // 2
    exponents = jnp.arange(half_dim, dtype=jnp.float32) * (2.0 / values.shape[-1])
    frequency = jnp.power(THETA, -exponents)
    angles = positions.astype(jnp.float32)[..., None, None] * frequency
    cosines = jnp.cos(angles)
    sine_part = jnp.sin(angles)
    front_half = values[..., :half_dim]
    back_half = values[..., half_dim:]
    return jnp.concatenate(
        [
            front_half * cosines - back_half * sine_part,
            back_half * cosines + front_half * sine_part,
        ],
        axis=-1,
    )


def per_device(
    tokens_in,
    attn_norm,
    qkv_weight,
    qkv_bias,
    out_weight,
    cache_keys,
    cache_values,
    page_table,
    cache_lengths,
    mlp_norm,
    routes,
    route_gates,
    expert_w_gate,
    expert_w_up,
    expert_w_down,
    shared_w_gate,
    shared_w_up,
    shared_w_down,
    shared_switch,
):
    req_rows, step_count, model_width = tokens_in.shape
    head_width = qkv_weight.shape[2]
    local_heads = head_width // HD
    req_count = lax.axis_size("req")
    tp_count = lax.axis_size("tp")
    req_index = lax.axis_index("req")
    tp_index = lax.axis_index("tp")
    all_requests = page_table.shape[0]
    pool_here = cache_keys.shape[0]
    page_len = cache_keys.shape[1]
    score_scale = 1.0 / math.sqrt(HD)
    col_share = model_width // tp_count
    row_count = req_rows * step_count
    normed = rms_norm(tokens_in, attn_norm)
    projected = jnp.einsum(
        "rsd,dcf->rscf", normed, qkv_weight, preferred_element_type=jnp.float32
    ) + qkv_bias.astype(jnp.float32)
    own_lengths = lax.dynamic_slice_in_dim(cache_lengths, req_index * req_rows, req_rows)
    positions = own_lengths[:, None] + jnp.arange(step_count, dtype=jnp.int32)[None, :]
    head_shape = (req_rows, step_count, local_heads, HD)
    query_new = rotate(projected[:, :, 0].reshape(head_shape), positions).astype(jnp.bfloat16)
    key_new = rotate(projected[:, :, 1].reshape(head_shape), positions).astype(jnp.bfloat16)
    value_new = projected[:, :, 2].reshape(head_shape).astype(jnp.bfloat16)
    query_all = lax.all_gather(query_new, "req", axis=0, tiled=True)
    slot_ids = req_index * pool_here + jnp.arange(pool_here, dtype=jnp.int32)
    matches = (page_table[:, :, None] == slot_ids[None, None, :]).astype(jnp.int32)
    request_ids = jnp.arange(all_requests, dtype=jnp.int32)
    page_ids = jnp.arange(page_table.shape[1], dtype=jnp.int32)
    owner = jnp.sum(matches * request_ids[:, None, None], axis=(0, 1))
    logical = jnp.sum(matches * page_ids[None, :, None], axis=(0, 1))
    present = jnp.sum(matches, axis=(0, 1)) > 0
    token_pos = logical[:, None] * page_len + jnp.arange(page_len, dtype=jnp.int32)[None, :]
    live = present[:, None] & (token_pos < cache_lengths[owner][:, None])
    page_queries = query_all[owner]
    page_keys = cache_keys.reshape(pool_here, page_len, local_heads, HD)
    page_values = cache_values.reshape(pool_here, page_len, local_heads, HD)
    scores = (
        jnp.einsum("pshd,pkhd->pshk", page_queries, page_keys, preferred_element_type=jnp.float32)
        * score_scale
    )
    page_mask = live[:, None, None, :]
    masked = jnp.where(page_mask, scores, NEG)
    page_max = jnp.max(masked, axis=-1)
    weights = jnp.where(page_mask, jnp.exp(masked - page_max[..., None]), 0.0)
    page_sum = jnp.sum(weights, axis=-1)
    page_out = jnp.einsum(
        "pshk,pkhd->pshd",
        weights.astype(jnp.bfloat16),
        page_values,
        preferred_element_type=jnp.float32,
    )
    belongs = (owner[None, :] == request_ids[:, None]) & present[None, :]
    owned = belongs[:, :, None, None]
    local_max = jnp.max(jnp.where(owned, page_max[None], NEG), axis=1)
    factors = jnp.where(owned, jnp.exp(page_max[None] - local_max[:, None]), 0.0)
    local_out = jnp.einsum("rpsh,pshd->rshd", factors, page_out, precision=HIGHEST)
    local_sum = jnp.einsum("rpsh,psh->rsh", factors, page_sum, precision=HIGHEST)
    first_row = req_index * req_rows
    global_max = lax.pmax(local_max, "req")
    rescale = jnp.exp(local_max - global_max)
    summed_out, summed_sum = lax.psum((local_out * rescale[..., None], local_sum * rescale), "req")
    cache_max = lax.dynamic_slice_in_dim(global_max, first_row, req_rows)
    cache_out = lax.dynamic_slice_in_dim(summed_out, first_row, req_rows)
    cache_sum = lax.dynamic_slice_in_dim(summed_sum, first_row, req_rows)
    new_scores = (
        jnp.einsum("rshd,rthd->rsht", query_new, key_new, preferred_element_type=jnp.float32)
        * score_scale
    )
    causal = jnp.arange(step_count)[:, None] >= jnp.arange(step_count)[None, :]
    new_mask = causal[None, :, None, :]
    new_masked = jnp.where(new_mask, new_scores, NEG)
    new_max = jnp.max(new_masked, axis=-1)
    new_weights = jnp.where(new_mask, jnp.exp(new_masked - new_max[..., None]), 0.0)
    new_sum = jnp.sum(new_weights, axis=-1)
    new_out = jnp.einsum(
        "rsht,rthd->rshd",
        new_weights.astype(jnp.bfloat16),
        value_new,
        preferred_element_type=jnp.float32,
    )
    top_max = jnp.maximum(cache_max, new_max)
    cache_factor = jnp.exp(cache_max - top_max)
    new_factor = jnp.exp(new_max - top_max)
    attended = (cache_out * cache_factor[..., None] + new_out * new_factor[..., None]) / (
        cache_sum * cache_factor + new_sum * new_factor
    )[..., None]
    attended = attended.astype(jnp.bfloat16).reshape(row_count, head_width)
    attn_part = jnp.dot(attended, out_weight, preferred_element_type=jnp.float32)
    attn_full = lax.psum(attn_part, "tp")
    resid = tokens_in.reshape(row_count, model_width).astype(jnp.float32) + attn_full
    mixed = rms_norm(resid, mlp_norm)
    expert_count = req_count * expert_w_gate.shape[0]
    capacity = max(2, (row_count * TOPK + expert_count - 1) // expert_count)
    picks = routes.reshape(row_count * TOPK)
    gates_flat = route_gates.reshape(row_count * TOPK)
    expert_hot = (picks[:, None] == jnp.arange(expert_count, dtype=jnp.int32)[None, :]).astype(
        jnp.int32
    )
    slot_index = jnp.sum((jnp.cumsum(expert_hot, axis=0) - 1) * expert_hot, axis=1)
    destination = picks * capacity + slot_index
    dest_hot = (
        destination[:, None] == jnp.arange(expert_count * capacity, dtype=jnp.int32)[None, :]
    ).astype(jnp.float32)
    token_hot = (
        (jnp.arange(row_count * TOPK, dtype=jnp.int32) // TOPK)[:, None]
        == jnp.arange(row_count, dtype=jnp.int32)[None, :]
    ).astype(jnp.float32)
    placement = jnp.einsum("cx,ct->xt", dest_hot, token_hot, precision=HIGHEST).astype(jnp.bfloat16)
    outgoing = jnp.dot(placement, mixed, preferred_element_type=jnp.float32).astype(jnp.bfloat16)
    outgoing = outgoing.reshape(expert_count, capacity, model_width)
    combine_map = jnp.einsum(
        "ct,cx->tx", token_hot, dest_hot * gates_flat[:, None], precision=HIGHEST
    )
    w_gate_here = expert_w_gate[0]
    w_up_here = expert_w_up[0]
    w_down_here = expert_w_down[0]
    received = lax.all_to_all(outgoing, "req", split_axis=0, concat_axis=0, tiled=True)
    sources = received.shape[0]
    item_count = received.shape[1]
    flat_rows = received.reshape(sources * item_count, model_width)
    gate_pre = jnp.dot(flat_rows, w_gate_here, preferred_element_type=jnp.float32)
    up_pre = jnp.dot(flat_rows, w_up_here, preferred_element_type=jnp.float32)
    hidden = (jax.nn.silu(gate_pre) * up_pre).astype(jnp.bfloat16)
    partial_out = jnp.dot(hidden, w_down_here, preferred_element_type=jnp.float32).reshape(
        sources, item_count, model_width
    )
    summed = lax.psum(partial_out, "tp").astype(jnp.bfloat16)
    returned = lax.all_to_all(summed, "req", split_axis=0, concat_axis=0, tiled=True)
    returned_cols = returned.shape[2]
    moe_out = jnp.dot(
        combine_map,
        returned.reshape(expert_count * capacity, returned_cols).astype(jnp.float32),
        precision=HIGHEST,
    )
    moe_out = lax.dynamic_slice_in_dim(moe_out, tp_index * col_share, col_share, 1)
    mixed_cols = lax.dynamic_slice_in_dim(mixed, tp_index * col_share, col_share, 1)
    piece = lax.all_gather(mixed_cols, "req", axis=0, tiled=True)
    gate_part = jnp.dot(piece, shared_w_gate, preferred_element_type=jnp.float32)
    up_part = jnp.dot(piece, shared_w_up, preferred_element_type=jnp.float32)
    shared_pre = jnp.concatenate([gate_part, up_part], axis=1)
    shared_pre = lax.psum(shared_pre, "tp")
    unit_count = shared_w_gate.shape[1]
    shared_hidden = (jax.nn.silu(shared_pre[:, :unit_count]) * shared_pre[:, unit_count:]).astype(
        jnp.bfloat16
    )
    shared_mine = lax.psum_scatter(
        jnp.dot(shared_hidden, shared_w_down, preferred_element_type=jnp.float32),
        "req",
        scatter_dimension=0,
        tiled=True,
    )
    switch = jax.nn.sigmoid(jnp.dot(mixed, shared_switch, preferred_element_type=jnp.float32))
    resid_mine = lax.dynamic_slice_in_dim(resid, tp_index * col_share, col_share, 1)
    final = resid_mine + moe_out + switch[:, None] * shared_mine
    return final.astype(jnp.bfloat16).reshape(req_rows, step_count, col_share)


def solution(mesh):
    return jax.shard_map(
        per_device,
        mesh=mesh,
        in_specs=(
            P("req", None, None),
            P(),
            P(None, None, "tp"),
            P(None, "tp"),
            P("tp", None),
            P("req", None, "tp"),
            P("req", None, "tp"),
            P(),
            P(),
            P(),
            P("req", None, None),
            P("req", None, None),
            P("req", None, "tp"),
            P("req", None, "tp"),
            P("req", "tp", None),
            P("tp", "req"),
            P("tp", "req"),
            P("req", "tp"),
            P(),
        ),
        out_specs=P("req", None, "tp"),
        check_vma=False,
    )
```

profile of v0, /device:TPU:0, one launch (start us, length us, event | category | flops | bytes accessed | tf_op | source)
XLA Modules:
  0.0 321.9 jit_solution(12219065390824033137)
XLA Ops:
  10.9 1.4 gather_fusion
  12.4 3.8 %fusion.28 = f32[3,4,3,512]{3,1,2,0:T(4,128)S(1)} fusion(bf16[2048,3,512]{2,0,1:T(8,128)(2,1)} %param.21, bf16[3,4,2048]{2,1,0:T(4,128)(2,1)} %param.19, f32[2048]{0:T(1024)S(1)} %convert_element_type.78, f32[3,4]{1,0:T(4,128)S(1)} %add_rsqrt_fusion, f32[3,512]{1,0:T(4,128)S(1)} %convert_element_type.80), kind=kOutput, calls=%fused_computation.23 | convolution fusion | flops 75614208 | bytes 6428720 | tf_op jit(solution)/shard_map/rsd,dcf->rscf/dot_general | solution.py:77
  17.7 32.3 %all_gather.6 = bf16[24,4,4,128]{3,2,1,0:T(4,128)(2,1)S(1)} all-gather(bf16[3,4,4,128]{3,2,1,0:T(4,128)(2,1)S(1)} %copy.91), channel_id=1, replica_groups=mesh['req'=8,'tp'=4] {'req'}, dimensions={0}, use_global_device_ids=true | all-gather | bytes 110592 | tf_op jit(solution)/shard_map/all_gather | solution.py:86
  50.8 5.4 %fusion.114 = (f32[40,4,4]{1,2,0:T(4,128)S(1)}, f32[40,4,4,128]{3,1,2,0:T(4,128)S(1)}) fusion(bf16[40,4,4,128]{3,2,1,0:T(4,128)(2,1)S(1)} %gather_fusion.1, pred[40,128]{1,0:T(8,128)(4,1)S(1)} %fusion.81, bf16[40,128,512]{2,1,0:T(8,128)(2,1)} %param.24), kind=kOutput, calls=%fused_computation.150 | convolution fusion | flops 21216640 | bytes 5742080 | tf_op jit(solution)/shard_map/pshd,pkhd->pshk/dot_general | solution.py:100
  56.5 22.2 %pmax.7 = f32[24,4,4]{0,2,1:T(4,128)} all-reduce(f32[24,4,4]{0,2,1:T(4,128)S(1)} %select_reduce_fusion), channel_id=1, replica_groups=mesh['req'=8,'tp'=4] {'req'}, use_global_device_ids=true, to_apply=%region_6.7 | all-reduce | flops 384 | bytes 3072 | tf_op jit(solution)/shard_map/pmax | solution.py:121
  79.8 4.1 %fusion.15 = f32[40,4,4,128]{3,1,2,0:T(4,128)S(1)} fusion(f32[40,4,4,128]{3,1,2,0:T(4,128)S(1)} %get-tuple-element.28, f32[40,4,4]{1,2,0:T(4,128)S(1)} %get-tuple-element.27, pred[40,128]{1,0:T(8,128)(4,1)} %copy-done.7, bf16[40,128,512]{2,1,0:T(8,128)(2,1)} %param.25), kind=kOutput, calls=%fused_computation.17 | convolution fusion | flops 21217280 | bytes 5905920 | tf_op jit(solution)/shard_map/pshk,pkhd->pshd/dot_general | solution.py:108
  86.9 2.0 fusion.21
  92.2 17.4 %psum.36 = f32[24,4,4]{0,2,1:T(4,128)S(1)} all-reduce(f32[24,4,4]{0,2,1:T(4,128)S(1)} %bitcast.134), channel_id=1, replica_groups=mesh['req'=8,'tp'=4] {'req'}, use_global_device_ids=true, to_apply=%region_10.11 | all-reduce | flops 384 | bytes 3072 | tf_op jit(solution)/shard_map/psum | solution.py:123
  110.4 46.0 %all-reduce.7.cloned.1.call-done = f32[24,4,4,128]{3,0,2,1:T(8,128)} async-done(((f32[24,4,4,128]{3,0,2,1:T(8,128)}), f32[24,4,4,128]{3,0,2,1:T(8,128)}) %all-reduce.7.cloned.1.call-update) | async-done | bytes 196624 | tf_op jit(solution)/shard_map/psum | solution.py:123
  161.1 28.1 %all-reduce.9.cloned.1.call-done = f32[12,2048]{1,0:T(8,128)} async-done(((f32[12,2048]{1,0:T(8,128)}), f32[12,2048]{1,0:T(8,128)}) %all-reduce.9.cloned.1.call-update) | async-done | bytes 98320 | tf_op jit(solution)/shard_map/psum | solution.py:151
  190.4 30.6 %all-gather = bf16[8,12,512]{2,1,0:T(8,128)(2,1)S(1)} all-gather(bf16[1,12,512]{2,1,0:T(8,128)(2,1)S(1)} %dynamic-slice_bitcast_fusion), channel_id=1, replica_groups=mesh['req'=8,'tp'=4] {'req'}, dimensions={0}, use_global_device_ids=true | all-gather | bytes 110592 | tf_op jit(solution)/shard_map/all_gather | solution.py:199
  221.4 1.5 fusion.117
  224.9 5.5 %all-to-all-start = ((bf16[8,6,2048]{2,1,0:T(8,128)(2,1)}), bf16[8,6,2048]{2,1,0:T(8,128)(2,1)S(1)}, u32[]{:S(2)}, u32[]{:S(2)}) async-start(bf16[8,6,2048]{2,1,0:T(8,128)(2,1)} %reshape.235), calls=%async_computation | async-start | bytes 524288 | tf_op jit(solution)/shard_map/all_to_all | solution.py:179
  231.9 25.2 %all-reduce.11.cloned.1.call-done = f32[96,1408]{1,0:T(8,128)} async-done(((f32[96,1408]{1,0:T(8,128)}), f32[96,1408]{1,0:T(8,128)}) %all-reduce.11.cloned.1.call-update) | async-done | bytes 540688 | tf_op jit(solution)/shard_map/psum | solution.py:203
  257.1 1.6 fusion.56
  258.7 1.9 fusion.13
  260.7 1.9 fusion.25
  262.6 1.7 fusion.9
  264.3 14.5 %all-reduce.12 = bf16[8,6,2048]{2,0,1:T(8,128)(2,1)S(1)} all-reduce(f32[8,6,2048]{2,0,1:T(8,128)S(1)} %fusion.9), channel_id=1, replica_groups=mesh['req'=8,'tp'=4] {'tp'}, use_global_device_ids=true, to_apply=%region_16.17 | all-reduce | flops 98304 | bytes 589824 | tf_op jit(solution)/shard_map/psum | solution.py:189
  279.6 5.4 %all-to-all-start.1 = ((bf16[8,6,2048]{2,1,0:T(8,128)(2,1)}), bf16[8,6,2048]{2,1,0:T(8,128)(2,1)S(1)}, u32[]{:S(2)}, u32[]{:S(2)}) async-start(bf16[8,6,2048]{2,1,0:T(8,128)(2,1)} %copy.108), calls=%async_computation.1 | async-start | bytes 524288 | tf_op jit(solution)/shard_map/all_to_all | solution.py:190
  285.1 24.1 %fusion = f32[16,512]{1,0:T(8,128)S(1)} fusion(f32[96,512]{1,0:T(8,128)S(1)} %fusion.56), kind=kCustom, calls=%all-reduce-scatter | all-reduce-scatter fusion | flops 65537 | bytes 229888
  309.2 2.1 collective-permute-start
  311.2 1.3 collective-permute-start.1
  312.7 1.4 collective-permute-done.1
  (100 shorter events, 26.4 us)
Async XLA Ops:
  6.5 150.9 %copy-start = (bf16[512,2048]{1,0:T(8,128)(2,1)S(1)}, bf16[512,2048]{1,0:T(8,128)(2,1)}, u32[]{:S(2)}) copy-start(bf16[512,2048]{1,0:T(8,128)(2,1)} %param.23) | copy-start | bytes 6291460
  6.5 149.8 %all-reduce.7.cloned.1.call-start = ((), (), s32[]{:S(2)}) async-start(), calls=%async_computation.2 | async-start | bytes 393216 | tf_op jit(solution)/shard_map/psum | solution.py:123
  10.9 45.4 %copy-start.6 = (pred[24,40]{1,0:T(8,128)(4,1)}, pred[24,40]{1,0:T(8,128)(4,1)S(1)}, u32[]{:S(2)}) copy-start(pred[24,40]{1,0:T(8,128)(4,1)S(1)} %fusion.98) | copy-start | bytes 2884
  16.2 0.9 copy-start.5
  17.1 0.6 copy-start.4
  50.8 27.9 %copy-start.7 = (pred[40,128]{1,0:T(8,128)(4,1)}, pred[40,128]{1,0:T(8,128)(4,1)S(1)}, u32[]{:S(2)}) copy-start(pred[40,128]{1,0:T(8,128)(4,1)S(1)} %fusion.81) | copy-start | bytes 15364
  56.3 22.3 %copy-start.3 = (f32[40,4,4]{0,2,1:T(4,128)}, f32[40,4,4]{0,2,1:T(4,128)S(1)}, u32[]{:S(2)}) copy-start(f32[40,4,4]{0,2,1:T(4,128)S(1)} %copy.96) | copy-start | bytes 7684
  56.5 22.2 %copy-start.2 = (f32[24,4,4]{0,2,1:T(4,128)}, f32[24,4,4]{0,2,1:T(4,128)S(1)}, u32[]{:S(2)}) copy-start(f32[24,4,4]{0,2,1:T(4,128)S(1)} %select_reduce_fusion) | copy-start | bytes 4612
  79.8 141.2 %copy-start.1 = (bf16[512,704]{0,1:T(8,128)(2,1)S(1)}, bf16[512,704]{0,1:T(8,128)(2,1)}, u32[]{:S(2)}) copy-start(bf16[512,704]{0,1:T(8,128)(2,1)} %param.35) | copy-start | bytes 2162692
  86.8 143.8 %copy-start.8 = (bf16[2048]{0:T(1024)(128)(2,1)S(1)}, bf16[2048]{0:T(1024)(128)(2,1)}, u32[]{:S(2)}) copy-start(bf16[2048]{0:T(1024)(128)(2,1)} %param.37) | copy-start | bytes 12292
  86.8 143.8 %copy-start.9 = (u32[32]{0:T(128)S(1)}, u32[32]{0:T(128)}, u32[]{:S(2)}) copy-start(u32[32]{0:T(128)} %constant.87) | copy-start | bytes 388
  88.9 100.4 %all-reduce.9.cloned.1.call-start = ((), (), s32[]{:S(2)}) async-start(), calls=%async_computation.3 | async-start | bytes 262144 | tf_op jit(solution)/shard_map/psum | solution.py:151
  158.5 98.5 %all-reduce.11.cloned.1.call-start = ((), (), s32[]{:S(2)}) async-start(), calls=%async_computation.4 | async-start | bytes 1081344 | tf_op jit(solution)/shard_map/psum | solution.py:203
  224.9 33.8 %all-to-all-start = ((bf16[8,6,2048]{2,1,0:T(8,128)(2,1)}), bf16[8,6,2048]{2,1,0:T(8,128)(2,1)S(1)}, u32[]{:S(2)}, u32[]{:S(2)}) async-start(bf16[8,6,2048]{2,1,0:T(8,128)(2,1)} %reshape.235), calls=%async_computation | async-start | bytes 524288 | tf_op jit(solution)/shard_map/all_to_all | solution.py:179
  279.6 34.7 %all-to-all-start.1 = ((bf16[8,6,2048]{2,1,0:T(8,128)(2,1)}), bf16[8,6,2048]{2,1,0:T(8,128)(2,1)S(1)}, u32[]{:S(2)}, u32[]{:S(2)}) async-start(bf16[8,6,2048]{2,1,0:T(8,128)(2,1)} %copy.108), calls=%async_computation.1 | async-start | bytes 524288 | tf_op jit(solution)/shard_map/all_to_all | solution.py:190
  309.2 4.9 %collective-permute-start = (f32[16,512]{1,0:T(8,128)S(1)}, f32[16,512]{1,0:T(8,128)S(1)}, u32[]{:S(2)}, u32[]{:S(2)}) collective-permute-start(f32[16,512]{1,0:T(8,128)S(1)} %fusion), channel_id=1, source_target_pairs={{0,4},{4,8},{8,12},{12,16},{16,20},{20,24},{24,28},{1,5},{5,9},{9,... | collective-permute-start | bytes 98312
  311.2 2.9 collective-permute-start.1
Sparse Core Ops, SparseCore 0:
  89.0 67.3 all-reduce.6
  158.8 30.4 all-reduce.8
  224.0 33.0 all-reduce.10
where the time goes:
time: 323 us; the launch traced here: 322 us
  blocking collectives  141 us (44%)
  waiting for transfers between devices  101 us (31%)
  matrix products  29.5 us (9%)
  starting transfers between devices  14.3 us (4%)
  between operations  14.2 us (4%)
  local copies, waits for them, and re-layouts  11.4 us (4%)
  other arithmetic  10.7 us (3%)
    psum x1, waiting for transfers between devices, per_device(): lax.psum((local_out * rescale[..., None], local_sum * rescale), 'req')  46 us
    all_gather x1, blocking collectives, per_device(): query_all = lax.all_gather(query_new, 'req', axis=0, tiled=True)  32.3 us
    all_gather x1, blocking collectives, per_device(): piece = lax.all_gather(mixed_cols, 'req', axis=0, tiled=True)  30.6 us
    psum x1, waiting for transfers between devices, per_device(): attn_full = lax.psum(attn_part, 'tp')  28.1 us
    psum x1, waiting for transfers between devices, per_device(): shared_pre = lax.psum(shared_pre, 'tp')  25.2 us
    unnamed x1, blocking collectives  24.1 us
    pmax x1, blocking collectives, per_device(): global_max = lax.pmax(local_max, 'req')  22.2 us
    psum x1, blocking collectives, per_device(): lax.psum((local_out * rescale[..., None], local_sum * rescale), 'req')  17.4 us
  transfers between devices with their start and end apart: 7, of which 4 were waited for; matrix products, arithmetic and copies ran while one was open for 11% of the time, Pallas kernels for 0%

commit v1 on v0

--- a/solution.py
+++ b/solution.py
@@ -36,6 +36,13 @@
             back_half * cosines + front_half * sine_part,
         ],
         axis=-1,
+    )
+
+
+def bcast_a2a(values, axis, count):
+    spread = jnp.broadcast_to(values[None], (count,) + values.shape)
+    return lax.all_to_all(spread, axis, 0, 0, tiled=True).reshape(
+        (count * values.shape[0],) + values.shape[1:]
     )
 
 
@@ -83,7 +90,7 @@
     query_new = rotate(projected[:, :, 0].reshape(head_shape), positions).astype(jnp.bfloat16)
     key_new = rotate(projected[:, :, 1].reshape(head_shape), positions).astype(jnp.bfloat16)
     value_new = projected[:, :, 2].reshape(head_shape).astype(jnp.bfloat16)
-    query_all = lax.all_gather(query_new, "req", axis=0, tiled=True)
+    query_all = bcast_a2a(query_new, "req", req_count)
     slot_ids = req_index * pool_here + jnp.arange(pool_here, dtype=jnp.int32)
     matches = (page_table[:, :, None] == slot_ids[None, None, :]).astype(jnp.int32)
     request_ids = jnp.arange(all_requests, dtype=jnp.int32)
@@ -117,13 +124,28 @@
     factors = jnp.where(owned, jnp.exp(page_max[None] - local_max[:, None]), 0.0)
     local_out = jnp.einsum("rpsh,pshd->rshd", factors, page_out, precision=HIGHEST)
     local_sum = jnp.einsum("rpsh,psh->rsh", factors, page_sum, precision=HIGHEST)
-    first_row = req_index * req_rows
-    global_max = lax.pmax(local_max, "req")
-    rescale = jnp.exp(local_max - global_max)
-    summed_out, summed_sum = lax.psum((local_out * rescale[..., None], local_sum * rescale), "req")
-    cache_max = lax.dynamic_slice_in_dim(global_max, first_row, req_rows)
-    cache_out = lax.dynamic_slice_in_dim(summed_out, first_row, req_rows)
-    cache_sum = lax.dynamic_slice_in_dim(summed_sum, first_row, req_rows)
+    stat_width = step_count * local_heads
+    out_width = stat_width * HD
+    packed = jnp.concatenate(
+        [
+            local_out.reshape(req_count, req_rows * out_width),
+            local_max.reshape(req_count, req_rows * stat_width),
+            local_sum.reshape(req_count, req_rows * stat_width),
+        ],
+        axis=1,
+    )
+    gathered = lax.all_to_all(packed, "req", 0, 0, tiled=True)
+    part_out = gathered[:, : req_rows * out_width].reshape(req_count, req_rows, step_count, local_heads, HD)
+    part_max = gathered[:, req_rows * out_width : req_rows * (out_width + stat_width)].reshape(
+        req_count, req_rows, step_count, local_heads
+    )
+    part_sum = gathered[:, req_rows * (out_width + stat_width) :].reshape(
+        req_count, req_rows, step_count, local_heads
+    )
+    cache_max = jnp.max(part_max, axis=0)
+    rescale = jnp.exp(part_max - cache_max[None])
+    cache_out = jnp.sum(part_out * rescale[..., None], axis=0)
+    cache_sum = jnp.sum(part_sum * rescale, axis=0)
     new_scores = (
         jnp.einsum("rshd,rthd->rsht", query_new, key_new, preferred_element_type=jnp.float32)
         * score_scale
@@ -148,7 +170,7 @@
     )[..., None]
     attended = attended.astype(jnp.bfloat16).reshape(row_count, head_width)
     attn_part = jnp.dot(attended, out_weight, preferred_element_type=jnp.float32)
-    attn_full = lax.psum(attn_part, "tp")
+    attn_full = jnp.sum(bcast_a2a(attn_part, "tp", tp_count).reshape(tp_count, row_count, model_width), axis=0)
     resid = tokens_in.reshape(row_count, model_width).astype(jnp.float32) + attn_full
     mixed = rms_norm(resid, mlp_norm)
     expert_count = req_count * expert_w_gate.shape[0]
@@ -169,48 +191,64 @@
     ).astype(jnp.float32)
     placement = jnp.einsum("cx,ct->xt", dest_hot, token_hot, precision=HIGHEST).astype(jnp.bfloat16)
     outgoing = jnp.dot(placement, mixed, preferred_element_type=jnp.float32).astype(jnp.bfloat16)
-    outgoing = outgoing.reshape(expert_count, capacity, model_width)
     combine_map = jnp.einsum(
         "ct,cx->tx", token_hot, dest_hot * gates_flat[:, None], precision=HIGHEST
     )
     w_gate_here = expert_w_gate[0]
     w_up_here = expert_w_up[0]
     w_down_here = expert_w_down[0]
-    received = lax.all_to_all(outgoing, "req", split_axis=0, concat_axis=0, tiled=True)
-    sources = received.shape[0]
-    item_count = received.shape[1]
-    flat_rows = received.reshape(sources * item_count, model_width)
+    mixed_cols = lax.dynamic_slice_in_dim(mixed, tp_index * col_share, col_share, 1)
+    shared_send = jnp.broadcast_to(mixed_cols[None], (req_count, row_count, col_share))
+    dispatch = jnp.concatenate(
+        [
+            outgoing.reshape(req_count, capacity * model_width),
+            shared_send.reshape(req_count, row_count * col_share),
+        ],
+        axis=1,
+    )
+    received = lax.all_to_all(dispatch, "req", 0, 0, tiled=True)
+    item_count = capacity
+    flat_rows = received[:, : capacity * model_width].reshape(req_count * capacity, model_width)
+    piece = received[:, capacity * model_width :].reshape(req_count * row_count, col_share)
     gate_pre = jnp.dot(flat_rows, w_gate_here, preferred_element_type=jnp.float32)
     up_pre = jnp.dot(flat_rows, w_up_here, preferred_element_type=jnp.float32)
     hidden = (jax.nn.silu(gate_pre) * up_pre).astype(jnp.bfloat16)
-    partial_out = jnp.dot(hidden, w_down_here, preferred_element_type=jnp.float32).reshape(
-        sources, item_count, model_width
-    )
-    summed = lax.psum(partial_out, "tp").astype(jnp.bfloat16)
-    returned = lax.all_to_all(summed, "req", split_axis=0, concat_axis=0, tiled=True)
-    returned_cols = returned.shape[2]
-    moe_out = jnp.dot(
-        combine_map,
-        returned.reshape(expert_count * capacity, returned_cols).astype(jnp.float32),
-        precision=HIGHEST,
-    )
-    moe_out = lax.dynamic_slice_in_dim(moe_out, tp_index * col_share, col_share, 1)
-    mixed_cols = lax.dynamic_slice_in_dim(mixed, tp_index * col_share, col_share, 1)
-    piece = lax.all_gather(mixed_cols, "req", axis=0, tiled=True)
+    partial_out = jnp.dot(hidden, w_down_here, preferred_element_type=jnp.float32)
+    expert_rows = req_count * capacity
+    partial_split = partial_out.reshape(expert_rows, tp_count, col_share).transpose(1, 0, 2)
     gate_part = jnp.dot(piece, shared_w_gate, preferred_element_type=jnp.float32)
     up_part = jnp.dot(piece, shared_w_up, preferred_element_type=jnp.float32)
-    shared_pre = jnp.concatenate([gate_part, up_part], axis=1)
-    shared_pre = lax.psum(shared_pre, "tp")
     unit_count = shared_w_gate.shape[1]
-    shared_hidden = (jax.nn.silu(shared_pre[:, :unit_count]) * shared_pre[:, unit_count:]).astype(
+    all_rows = req_count * row_count
+    share_rows = all_rows // tp_count
+    shared_pre = jnp.concatenate([gate_part, up_part], axis=1).reshape(
+        tp_count, share_rows * 2 * unit_count
+    )
+    reduce_in = jnp.concatenate(
+        [partial_split.reshape(tp_count, expert_rows * col_share), shared_pre], axis=1
+    )
+    reduce_out = jnp.sum(lax.all_to_all(reduce_in, "tp", 0, 0, tiled=True), axis=0)
+    expert_sum = reduce_out[: expert_rows * col_share].reshape(expert_rows, col_share)
+    shared_sum = reduce_out[expert_rows * col_share :].reshape(share_rows, 2 * unit_count)
+    shared_hidden = (jax.nn.silu(shared_sum[:, :unit_count]) * shared_sum[:, unit_count:]).astype(
         jnp.bfloat16
     )
-    shared_mine = lax.psum_scatter(
-        jnp.dot(shared_hidden, shared_w_down, preferred_element_type=jnp.float32),
-        "req",
-        scatter_dimension=0,
-        tiled=True,
-    )
+    hidden_all = bcast_a2a(shared_hidden, "tp", tp_count).reshape(all_rows, unit_count)
+    shared_down = jnp.dot(hidden_all, shared_w_down, preferred_element_type=jnp.float32)
+    ey = expert_sum.astype(jnp.bfloat16).astype(jnp.float32)
+    back_in = jnp.concatenate(
+        [
+            ey.reshape(req_count, capacity * col_share),
+            shared_down.reshape(req_count, row_count * col_share),
+        ],
+        axis=1,
+    )
+    back = lax.all_to_all(back_in, "req", 0, 0, tiled=True)
+    returned = back[:, : capacity * col_share].reshape(expert_count * capacity, col_share)
+    shared_mine = jnp.sum(
+        back[:, capacity * col_share :].reshape(req_count, row_count, col_share), axis=0
+    )
+    moe_out = jnp.dot(combine_map, returned, precision=HIGHEST)
     switch = jax.nn.sigmoid(jnp.dot(mixed, shared_switch, preferred_element_type=jnp.float32))
     resid_mine = lax.dynamic_slice_in_dim(resid, tp_index * col_share, col_share, 1)
     final = resid_mine + moe_out + switch[:, None] * shared_mine

time: 323 us -> 139 us (0.43)
  blocking collectives: 141 us -> 28.4 us
  waiting for transfers between devices: 101 us -> 35 us
  between operations: 14.2 us -> 0.61 us
  starting transfers between devices: 14.3 us -> 20.9 us
  matrix products: 29.5 us -> 25.2 us
  local copies, waits for them, and re-layouts: 11.4 us -> 14.9 us
    psum x3 -> x0, waiting for transfers between devices: 99.3 us -> none  [the longest x1 46 us: per_device(): lax.psum((local_out * rescale[..., None], local_sum * rescale), 'req')]
    all_gather x2 -> x0, blocking collectives: 62.9 us -> none  [the longest x1 32.3 us: per_device(): query_all = lax.all_gather(query_new, 'req', axis=0, tiled=True)]
    all_to_all x2 -> x5, waiting for transfers between devices: 0.01 us -> 35 us  [the longest x3 18.6 us: bcast_a2a(): lax.all_to_all(spread, axis, 0, 0, tiled=True)]
    psum x2 -> x0, blocking collectives: 31.8 us -> none  [the longest x1 17.4 us: per_device(): lax.psum((local_out * rescale[..., None], local_sum * rescale), 'req')]
    all_to_all x0 -> x2, blocking collectives: none -> 28.4 us  [the longest x1 15.6 us: per_device(): lax.all_to_all(reduce_in, 'tp', 0, 0, tiled=True)]
    unnamed x1 -> x0, blocking collectives: 24.1 us -> none
    pmax x1 -> x0, blocking collectives: 22.2 us -> none  [per_device(): global_max = lax.pmax(local_max, 'req')]
    all_to_all x2 -> x5, starting transfers between devices: 10.9 us -> 20.9 us  [the longest x3 14.1 us: bcast_a2a(): lax.all_to_all(spread, axis, 0, 0, tiled=True)]
  transfers between devices with their start and end apart: 7 -> 5, of which waited for: 4 -> 5; matrix products, arithmetic and copies ran while one was open for 11% -> 2% of each run, Pallas kernels for 0% -> 0%
where the time goes in v1:
time: 139 us; the launch traced here: 138 us
  waiting for transfers between devices  35 us (25%)
  blocking collectives  28.4 us (20%)
  matrix products  25.2 us (18%)
  starting transfers between devices  20.9 us (15%)
  local copies, waits for them, and re-layouts  14.9 us (11%)
  other arithmetic  13.2 us (9%)
    all_to_all x3, waiting for transfers between devices, bcast_a2a(): lax.all_to_all(spread, axis, 0, 0, tiled=True)  18.6 us
    all_to_all x1, blocking collectives, per_device(): lax.all_to_all(reduce_in, 'tp', 0, 0, tiled=True)  15.6 us
    all_to_all x3, starting transfers between devices, bcast_a2a(): lax.all_to_all(spread, axis, 0, 0, tiled=True)  14.1 us
    all_to_all x1, blocking collectives, per_device(): received = lax.all_to_all(dispatch, 'req', 0, 0, tiled=True)  12.8 us
    all_to_all x1, waiting for transfers between devices, per_device(): back = lax.all_to_all(back_in, 'req', 0, 0, tiled=True)  8.88 us
    all_to_all x1, waiting for transfers between devices, per_device(): gathered = lax.all_to_all(packed, 'req', 0, 0, tiled=True)  7.47 us
    dot_general x1, matrix products, per_device(): jnp.einsum('pshd,pkhd->pshk', page_queries, page_keys, preferred_element_...  5.41 us
    dot_general x1, matrix products, per_device(): jnp.einsum('pshk,pkhd->pshd', weights.astype(jnp.bfloat16), page_values,...  4 us
  transfers between devices with their start and end apart: 5, of which 5 were waited for; matrix products, arithmetic and copies ran while one was open for 2% of the time, Pallas kernels for 0%

profile of v1, /device:TPU:0, one launch (start us, length us, event | category | flops | bytes accessed | tf_op | source)
XLA Modules:
  0.0 138.2 jit_solution(13858909295819936853)
XLA Ops:
  3.3 3.8 %fusion.31 = f32[3,4,3,512]{3,1,2,0:T(4,128)S(1)} fusion(bf16[2048,3,512]{2,0,1:T(8,128)(2,1)} %param.21, bf16[3,4,2048]{2,1,0:T(4,128)(2,1)} %param.19, f32[2048]{0:T(1024)S(1)} %convert_element_type.83, f32[3,4]{1,0:T(4,128)S(1)} %add_rsqrt_fusion.1, f32[3,512]{1,0:T(4,128)S(1)} %convert_element_type.85), kind=kOutput, calls=%fused_computation.26 | convolution fusion | flops 75614208 | bytes 6428720 | tf_op jit(solution)/shard_map/rsd,dcf->rscf/dot_general | solution.py:84
  8.1 7.3 %all-to-all-start = ((bf16[8,3,4,4,128]{4,3,2,1,0:T(4,128)(2,1)}), bf16[8,3,4,4,128]{4,3,2,1,0:T(4,128)(2,1)S(1)}, u32[]{:S(2)}, u32[]{:S(2)}) async-start(bf16[8,3,4,4,128]{4,3,2,1,0:T(4,128)(2,1)} %broadcast_in_dim.77), calls=%async_computation | async-start | bytes 196608 | tf_op jit(solution)/shard_map/all_to_all | solution.py:44
  17.1 5.4 %all-to-all-done = bf16[8,3,4,4,128]{4,3,2,1,0:T(4,128)(2,1)S(1)} async-done(((bf16[8,3,4,4,128]{4,3,2,1,0:T(4,128)(2,1)}), bf16[8,3,4,4,128]{4,3,2,1,0:T(4,128)(2,1)S(1)}, u32[]{:S(2)}, u32[]{:S(2)}) %all-to-all-start) | async-done | bytes 98336 | tf_op jit(solution)/shard_map/all_to_all | solution.py:44
  23.2 5.4 %fusion.118 = (f32[40,4,4]{1,2,0:T(4,128)S(1)}, f32[40,4,4,128]{3,1,2,0:T(4,128)S(1)}) fusion(bf16[40,4,4,128]{3,2,1,0:T(4,128)(2,1)S(1)} %gather_fusion.1, pred[40,128]{1,0:T(8,128)(4,1)S(1)} %fusion.88, bf16[40,128,512]{2,1,0:T(8,128)(2,1)} %param.24), kind=kOutput, calls=%fused_computation.162 | convolution fusion | flops 21216640 | bytes 5742080 | tf_op jit(solution)/shard_map/pshd,pkhd->pshk/dot_general | solution.py:107
  30.1 4.0 %fusion.19 = f32[40,4,4,128]{3,1,2,0:T(4,128)S(1)} fusion(f32[40,4,4,128]{3,1,2,0:T(4,128)S(1)} %get-tuple-element.26, f32[40,4,4]{1,2,0:T(4,128)S(1)} %get-tuple-element.25, pred[40,128]{1,0:T(8,128)(4,1)S(1)} %fusion.88, bf16[40,128,512]{2,1,0:T(8,128)(2,1)} %param.25), kind=kOutput, calls=%fused_computation.21 | convolution fusion | flops 21217280 | bytes 5905920 | tf_op jit(solution)/shard_map/pshk,pkhd->pshd/dot_general | solution.py:115
  35.9 3.4 %all-to-all-start.1 = ((f32[8,1,6240]{2,1,0:T(1,128)}), f32[8,1,6240]{2,1,0:T(1,128)S(1)}, u32[]{:S(2)}, u32[]{:S(2)}) async-start(f32[8,1,6240]{2,1,0:T(1,128)} %copy.141), calls=%async_computation.1 | async-start | bytes 401408 | tf_op jit(solution)/shard_map/all_to_all | solution.py:137
  39.6 7.5 %all-to-all-done.1 = f32[8,1,6240]{2,1,0:T(1,128)S(1)} async-done(((f32[8,1,6240]{2,1,0:T(1,128)}), f32[8,1,6240]{2,1,0:T(1,128)S(1)}, u32[]{:S(2)}, u32[]{:S(2)}) %all-to-all-start.1) | async-done | bytes 199712 | tf_op jit(solution)/shard_map/all_to_all | solution.py:137
  47.1 2.3 %copy.142 = f32[8,1,6240]{0,2,1:T(8,128)} copy(f32[8,1,6240]{2,1,0:T(1,128)S(1)} %all-to-all-done.1) | data formatting | bytes 399360 | tf_op jit(solution)/shard_map/all_to_all | solution.py:137
  50.2 0.9 fusion.84
  51.6 2.8 %fusion.8 = f32[6144]{0:T(1024)S(1)} fusion(f32[8,6240]{0,1:T(8,128)} %bitcast.151, f32[8,3,4,4]{0,3,2,1:T(4,128)S(1)} %subtract_exponential_fusion), kind=kLoop, calls=%fused_computation.11 | loop fusion | flops 92160 | bytes 222720 | tf_op jit(solution)/shard_map/reduce_sum | solution.py:147
  55.9 3.5 %all-to-all-start.2 = ((f32[4,12,2048]{2,1,0:T(8,128)}), f32[4,12,2048]{2,1,0:T(8,128)S(1)}, u32[]{:S(2)}, u32[]{:S(2)}) async-start(f32[4,12,2048]{2,1,0:T(8,128)} %broadcast_in_dim.86), calls=%async_computation.2 | async-start | bytes 1048576 | tf_op jit(solution)/shard_map/all_to_all | solution.py:44
  59.7 8.5 %all-to-all-done.2 = f32[4,12,2048]{2,1,0:T(8,128)S(1)} async-done(((f32[4,12,2048]{2,1,0:T(8,128)}), f32[4,12,2048]{2,1,0:T(8,128)S(1)}, u32[]{:S(2)}, u32[]{:S(2)}) %all-to-all-start.2) | async-done | bytes 393248 | tf_op jit(solution)/shard_map/all_to_all | solution.py:44
  71.5 12.8 %all_to_all.60 = bf16[8,2,9216]{2,1,0:T(2,128)(2,1)S(1)} all-to-all(bf16[8,2,9216]{2,1,0:T(2,128)(2,1)S(1)} %reshape.423), channel_id=1, replica_groups=mesh['req'=8,'tp'=4] {'req'}, dimensions={0} | all-to-all | bytes 589824 | tf_op jit(solution)/shard_map/all_to_all | solution.py:209
  85.0 2.6 %fusion.14 = f32[48,352]{1,0:T(8,128)} fusion(bf16[48,2048]{1,0:T(8,128)(2,1)S(1)} %reshape.384, bf16[1,2048,352]{1,2,0:T(8,128)(2,1)} %param.31), kind=kOutput, calls=%fused_computation.18 | convolution fusion | flops 69206016 | bytes 1705984 | tf_op jit(solution)/shard_map/dot_general | solution.py:213
  87.6 3.0 %fusion.16 = f32[1,4,48,512]{3,2,1,0:T(8,128)S(1)} fusion(bf16[44,4,8,512]{3,2,1,0:T(8,128)(2,1)} %bitcast.153, bf16[48,2048]{1,0:T(8,128)(2,1)S(1)} %reshape.384, bf16[1,2048,352]{1,2,0:T(8,128)(2,1)} %param.32, f32[48,352]{1,0:T(8,128)} %fusion.14), kind=kOutput, calls=%fused_computation.20 | convolution fusion | flops 138513408 | bytes 3540992 | tf_op jit(solution)/shard_map/dot_general | solution.py:216
  90.6 1.0 copy.172
  92.1 1.5 %fusion.122 = f32[96,704]{1,0:T(8,128)S(1)} fusion(bf16[96,512]{1,0:T(8,128)(2,1)S(1)} %reshape.386, bf16[512,704]{0,1:T(8,128)(2,1)} %param.35), kind=kOutput, calls=%fused_computation.166 | convolution fusion | flops 69206016 | bytes 1089536 | tf_op jit(solution)/shard_map/dot_general | solution.py:220
  94.0 1.2 pad_maximum_fusion
  95.8 15.6 %all_to_all.61 = f32[4,1,58368]{2,1,0:T(1,128)S(1)} all-to-all(f32[4,1,58368]{2,1,0:T(1,128)S(1)} %all_to_all.47), channel_id=1, replica_groups=mesh['req'=8,'tp'=4] {'tp'}, dimensions={0} | all-to-all | bytes 1867776 | tf_op jit(solution)/shard_map/all_to_all | solution.py:230
  113.1 3.3 %all-to-all-start.5 = ((bf16[4,24,704]{2,1,0:T(8,128)(2,1)}), bf16[4,24,704]{2,1,0:T(8,128)(2,1)S(1)}, u32[]{:S(2)}, u32[]{:S(2)}) async-start(bf16[4,24,704]{2,1,0:T(8,128)(2,1)} %broadcast_in_dim.89), calls=%async_computation.5 | async-start | bytes 294912 | tf_op jit(solution)/shard_map/all_to_all | solution.py:44
  116.5 4.7 %all-to-all-done.5 = bf16[4,24,704]{2,1,0:T(8,128)(2,1)S(1)} async-done(((bf16[4,24,704]{2,1,0:T(8,128)(2,1)}), bf16[4,24,704]{2,1,0:T(8,128)(2,1)S(1)}, u32[]{:S(2)}, u32[]{:S(2)}) %all-to-all-start.5) | async-done | bytes 135200 | tf_op jit(solution)/shard_map/all_to_all | solution.py:44
  121.2 1.4 fusion.123
  123.6 3.4 %all-to-all-start.6 = ((f32[8,1,9216]{2,1,0:T(1,128)}), f32[8,1,9216]{2,1,0:T(1,128)S(1)}, u32[]{:S(2)}, u32[]{:S(2)}) async-start(f32[8,1,9216]{2,1,0:T(1,128)} %all_to_all.50), calls=%async_computation.6 | async-start | bytes 589824 | tf_op jit(solution)/shard_map/all_to_all | solution.py:246
  127.6 8.9 %all-to-all-done.6 = f32[8,1,9216]{2,1,0:T(1,128)S(1)} async-done(((f32[8,1,9216]{2,1,0:T(1,128)}), f32[8,1,9216]{2,1,0:T(1,128)S(1)}, u32[]{:S(2)}, u32[]{:S(2)}) %all-to-all-start.6) | async-done | bytes 294944 | tf_op jit(solution)/shard_map/all_to_all | solution.py:246
  (130 shorter events, 23.5 us)
Async XLA Ops:
  0.0 54.7 %copy-start = (bf16[512,2048]{1,0:T(8,128)(2,1)S(1)}, bf16[512,2048]{1,0:T(8,128)(2,1)}, u32[]{:S(2)}) copy-start(bf16[512,2048]{1,0:T(8,128)(2,1)} %param.23) | copy-start | bytes 6291460
  3.3 12.1 %copy-start.6 = (s32[24,37]{1,0:T(8,128)S(1)}, s32[24,37]{1,0:T(8,128)}, u32[]{:S(2)}) copy-start(s32[24,37]{1,0:T(8,128)} %param.26) | copy-start | bytes 10660
  3.3 12.5 %copy-start.1 = (s32[24]{0:T(128)S(1)}, s32[24]{0:T(128)}, u32[]{:S(2)}) copy-start(s32[24]{0:T(128)} %param.27) | copy-start | bytes 292
  3.3 13.3 %copy-start.7 = (s32[3,4,4]{2,1,0:T(4,128)S(1)}, s32[3,4,4]{2,1,0:T(4,128)}, u32[]{:S(2)}) copy-start(s32[3,4,4]{2,1,0:T(4,128)} %param.29) | copy-start | bytes 580
  8.1 14.4 %all-to-all-start = ((bf16[8,3,4,4,128]{4,3,2,1,0:T(4,128)(2,1)}), bf16[8,3,4,4,128]{4,3,2,1,0:T(4,128)(2,1)S(1)}, u32[]{:S(2)}, u32[]{:S(2)}) async-start(bf16[8,3,4,4,128]{4,3,2,1,0:T(4,128)(2,1)} %broadcast_in_dim.77), calls=%async_computation | async-start | bytes 196608 | tf_op jit(solution)/shard_map/all_to_all | solution.py:44
  35.9 11.1 %all-to-all-start.1 = ((f32[8,1,6240]{2,1,0:T(1,128)}), f32[8,1,6240]{2,1,0:T(1,128)S(1)}, u32[]{:S(2)}, u32[]{:S(2)}) async-start(f32[8,1,6240]{2,1,0:T(1,128)} %copy.141), calls=%async_computation.1 | async-start | bytes 401408 | tf_op jit(solution)/shard_map/all_to_all | solution.py:137
  51.6 7.8 %copy-start.3 = (bf16[3,4,2048]{2,1,0:T(4,128)(2,1)S(1)}, bf16[3,4,2048]{2,1,0:T(4,128)(2,1)}, u32[]{:S(2)}) copy-start(bf16[3,4,2048]{2,1,0:T(4,128)(2,1)} %param.19) | copy-start | bytes 147460
  54.4 5.0 %copy-start.9 = (bf16[2048]{0:T(1024)(128)(2,1)S(1)}, bf16[2048]{0:T(1024)(128)(2,1)}, u32[]{:S(2)}) copy-start(bf16[2048]{0:T(1024)(128)(2,1)} %param.28) | copy-start | bytes 12292
  55.9 12.3 %all-to-all-start.2 = ((f32[4,12,2048]{2,1,0:T(8,128)}), f32[4,12,2048]{2,1,0:T(8,128)S(1)}, u32[]{:S(2)}, u32[]{:S(2)}) async-start(f32[4,12,2048]{2,1,0:T(8,128)} %broadcast_in_dim.86), calls=%async_computation.2 | async-start | bytes 1048576 | tf_op jit(solution)/shard_map/all_to_all | solution.py:44
  69.2 0.6 copy-start.4
  85.0 6.8 %copy-start.2 = (bf16[512,704]{0,1:T(8,128)(2,1)S(1)}, bf16[512,704]{0,1:T(8,128)(2,1)}, u32[]{:S(2)}) copy-start(bf16[512,704]{0,1:T(8,128)(2,1)} %param.34) | copy-start | bytes 2162692
  111.5 15.6 %copy-start.10 = (bf16[2048]{0:T(1024)(128)(2,1)S(1)}, bf16[2048]{0:T(1024)(128)(2,1)}, u32[]{:S(2)}) copy-start(bf16[2048]{0:T(1024)(128)(2,1)} %param.37) | copy-start | bytes 12292
  111.5 15.6 %copy-start.8 = (f32[3,4,4]{2,1,0:T(4,128)S(1)}, f32[3,4,4]{2,1,0:T(4,128)}, u32[]{:S(2)}) copy-start(f32[3,4,4]{2,1,0:T(4,128)} %param.30) | copy-start | bytes 580
  111.5 16.0 %copy-start.5 = (bf16[12,2048]{1,0:T(8,128)(2,1)S(1)}, bf16[12,2048]{1,0:T(8,128)(2,1)}, u32[]{:S(2)}) copy-start(bf16[12,2048]{1,0:T(8,128)(2,1)} %copy-done.4) | copy-start | bytes 147460
  113.1 8.1 %all-to-all-start.5 = ((bf16[4,24,704]{2,1,0:T(8,128)(2,1)}), bf16[4,24,704]{2,1,0:T(8,128)(2,1)S(1)}, u32[]{:S(2)}, u32[]{:S(2)}) async-start(bf16[4,24,704]{2,1,0:T(8,128)(2,1)} %broadcast_in_dim.89), calls=%async_computation.5 | async-start | bytes 294912 | tf_op jit(solution)/shard_map/all_to_all | solution.py:44
  123.6 12.8 %all-to-all-start.6 = ((f32[8,1,9216]{2,1,0:T(1,128)}), f32[8,1,9216]{2,1,0:T(1,128)S(1)}, u32[]{:S(2)}, u32[]{:S(2)}) async-start(f32[8,1,9216]{2,1,0:T(1,128)} %all_to_all.50), calls=%async_computation.6 | async-start | bytes 589824 | tf_op jit(solution)/shard_map/all_to_all | solution.py:246

commit v2 on v1

--- a/solution.py
+++ b/solution.py
@@ -101,23 +101,26 @@
     token_pos = logical[:, None] * page_len + jnp.arange(page_len, dtype=jnp.int32)[None, :]
     live = present[:, None] & (token_pos < cache_lengths[owner][:, None])
     page_queries = query_all[owner]
-    page_keys = cache_keys.reshape(pool_here, page_len, local_heads, HD)
-    page_values = cache_values.reshape(pool_here, page_len, local_heads, HD)
+    head_eye = jnp.arange(local_heads)[:, None] == jnp.arange(local_heads)[None, :]
+    block_queries = jnp.where(
+        head_eye[None, None, :, :, None], page_queries[:, :, :, None, :], jnp.zeros((), jnp.bfloat16)
+    ).reshape(pool_here, step_count * local_heads, head_width)
     scores = (
-        jnp.einsum("pshd,pkhd->pshk", page_queries, page_keys, preferred_element_type=jnp.float32)
+        jnp.einsum("pxd,pkd->pxk", block_queries, cache_keys, preferred_element_type=jnp.float32)
         * score_scale
-    )
+    ).reshape(pool_here, step_count, local_heads, page_len)
     page_mask = live[:, None, None, :]
     masked = jnp.where(page_mask, scores, NEG)
     page_max = jnp.max(masked, axis=-1)
     weights = jnp.where(page_mask, jnp.exp(masked - page_max[..., None]), 0.0)
     page_sum = jnp.sum(weights, axis=-1)
-    page_out = jnp.einsum(
-        "pshk,pkhd->pshd",
-        weights.astype(jnp.bfloat16),
-        page_values,
+    wide_out = jnp.einsum(
+        "pxk,pkd->pxd",
+        weights.astype(jnp.bfloat16).reshape(pool_here, step_count * local_heads, page_len),
+        cache_values,
         preferred_element_type=jnp.float32,
-    )
+    ).reshape(pool_here, step_count, local_heads, local_heads, HD)
+    page_out = jnp.sum(jnp.where(head_eye[None, None, :, :, None], wide_out, 0.0), axis=3)
     belongs = (owner[None, :] == request_ids[:, None]) & present[None, :]
     owned = belongs[:, :, None, None]
     local_max = jnp.max(jnp.where(owned, page_max[None], NEG), axis=1)
@@ -125,27 +128,30 @@
     local_out = jnp.einsum("rpsh,pshd->rshd", factors, page_out, precision=HIGHEST)
     local_sum = jnp.einsum("rpsh,psh->rsh", factors, page_sum, precision=HIGHEST)
     stat_width = step_count * local_heads
-    out_width = stat_width * HD
+    stat_row = jnp.concatenate(
+        [
+            local_max.reshape(all_requests, stat_width),
+            local_sum.reshape(all_requests, stat_width),
+            jnp.zeros((all_requests, HD - 2 * stat_width), jnp.float32),
+        ],
+        axis=1,
+    )
     packed = jnp.concatenate(
-        [
-            local_out.reshape(req_count, req_rows * out_width),
-            local_max.reshape(req_count, req_rows * stat_width),
-            local_sum.reshape(req_count, req_rows * stat_width),
-        ],
-        axis=1,
-    )
-    gathered = lax.all_to_all(packed, "req", 0, 0, tiled=True)
-    part_out = gathered[:, : req_rows * out_width].reshape(req_count, req_rows, step_count, local_heads, HD)
-    part_max = gathered[:, req_rows * out_width : req_rows * (out_width + stat_width)].reshape(
-        req_count, req_rows, step_count, local_heads
-    )
-    part_sum = gathered[:, req_rows * (out_width + stat_width) :].reshape(
-        req_count, req_rows, step_count, local_heads
-    )
+        [local_out.reshape(all_requests, stat_width, HD), stat_row[:, None, :]], axis=1
+    )
+    gathered = lax.all_to_all(packed, "req", 0, 0, tiled=True).reshape(
+        req_count, req_rows, stat_width + 1, HD
+    )
+    part_out = gathered[:, :, :stat_width, :]
+    part_max = gathered[:, :, stat_width, :stat_width]
+    part_sum = gathered[:, :, stat_width, stat_width : 2 * stat_width]
     cache_max = jnp.max(part_max, axis=0)
     rescale = jnp.exp(part_max - cache_max[None])
-    cache_out = jnp.sum(part_out * rescale[..., None], axis=0)
-    cache_sum = jnp.sum(part_sum * rescale, axis=0)
+    cache_out = jnp.sum(part_out * rescale[..., None], axis=0).reshape(
+        req_rows, step_count, local_heads, HD
+    )
+    cache_sum = jnp.sum(part_sum * rescale, axis=0).reshape(req_rows, step_count, local_heads)
+    cache_max = cache_max.reshape(req_rows, step_count, local_heads)
     new_scores = (
         jnp.einsum("rshd,rthd->rsht", query_new, key_new, preferred_element_type=jnp.float32)
         * score_scale
@@ -213,9 +219,13 @@
     gate_pre = jnp.dot(flat_rows, w_gate_here, preferred_element_type=jnp.float32)
     up_pre = jnp.dot(flat_rows, w_up_here, preferred_element_type=jnp.float32)
     hidden = (jax.nn.silu(gate_pre) * up_pre).astype(jnp.bfloat16)
-    partial_out = jnp.dot(hidden, w_down_here, preferred_element_type=jnp.float32)
     expert_rows = req_count * capacity
-    partial_split = partial_out.reshape(expert_rows, tp_count, col_share).transpose(1, 0, 2)
+    partial_split = jnp.einsum(
+        "rk,kjc->jrc",
+        hidden,
+        w_down_here.reshape(w_down_here.shape[0], tp_count, col_share),
+        preferred_element_type=jnp.float32,
+    )
     gate_part = jnp.dot(piece, shared_w_gate, preferred_element_type=jnp.float32)
     up_part = jnp.dot(piece, shared_w_up, preferred_element_type=jnp.float32)
     unit_count = shared_w_gate.shape[1]

time: 139 us -> 148 us (1.065)
  blocking collectives: 28.4 us -> 15.6 us
  local copies, waits for them, and re-layouts: 14.9 us -> 27 us
  waiting for transfers between devices: 35 us -> 40.3 us
  starting transfers between devices: 20.9 us -> 25.3 us
    all_to_all x1 -> x0, blocking collectives: 12.8 us -> none  [per_device(): received = lax.all_to_all(dispatch, 'req', 0, 0, tiled=True)]
    all_to_all x1 -> x2, waiting for transfers between devices: 7.47 us -> 14.3 us  [the longest x1 8.27 us: per_device(): lax.all_to_all(packed, 'req', 0, 0, tiled=True)]
    all_to_all x1 -> x2, starting transfers between devices: 3.39 us -> 7.65 us  [the longest x1 4.23 us: per_device(): received = lax.all_to_all(dispatch, 'req', 0, 0, tiled=True)]
    unnamed x32 -> x42, local copies, waits for them, and re-layouts: 2.03 us -> 5.59 us
    another operation x0 -> x1, local copies, waits for them, and re-layouts: none -> 3.47 us  [per_device(): w_down_here.reshape(w_down_here.shape[0], tp_count, col_share)]
    all_to_all x2 -> x0, local copies, waits for them, and re-layouts: 3.14 us -> none  [per_device(): gathered = lax.all_to_all(packed, 'req', 0, 0, tiled=True)]
    reduce_sum x2 -> x3, other arithmetic: 3.73 us -> 1.24 us  [the longest x1 1 us: per_device(): jnp.sum(jnp.where(head_eye[None, None, :, :, None], wide_out, 0.0), axis=3)]
    reshape x3 -> x8, local copies, waits for them, and re-layouts: 0.27 us -> 2.26 us  [the longest x1 1.7 us: per_device(): wide_out = jnp.einsum('pxk,pkd->pxd', weights.astype(jnp.bfloat16).reshap...]
  transfers between devices with their start and end apart: 5 -> 6, of which waited for: 5 -> 6; matrix products, arithmetic and copies ran while one was open for 2% -> 5% of each run, Pallas kernels for 0% -> 0%
where the time goes in v2:
time: 148 us; the launch traced here: 146 us
  waiting for transfers between devices  40.3 us (27%)
  local copies, waits for them, and re-layouts  27 us (18%)
  starting transfers between devices  25.3 us (17%)
  matrix products  25 us (17%)
  blocking collectives  15.6 us (11%)
  other arithmetic  12.3 us (8%)
    all_to_all x3, waiting for transfers between devices, bcast_a2a(): lax.all_to_all(spread, axis, 0, 0, tiled=True)  17.3 us
    all_to_all x1, blocking collectives, per_device(): lax.all_to_all(reduce_in, 'tp', 0, 0, tiled=True)  15.6 us
    all_to_all x3, starting transfers between devices, bcast_a2a(): lax.all_to_all(spread, axis, 0, 0, tiled=True)  14.1 us
    all_to_all x1, waiting for transfers between devices, per_device(): back = lax.all_to_all(back_in, 'req', 0, 0, tiled=True)  8.67 us
    all_to_all x1, waiting for transfers between devices, per_device(): lax.all_to_all(packed, 'req', 0, 0, tiled=True)  8.27 us
    all_to_all x1, waiting for transfers between devices, per_device(): received = lax.all_to_all(dispatch, 'req', 0, 0, tiled=True)  6.01 us
    unnamed x42, local copies, waits for them, and re-layouts  5.59 us
    dot_general x1, matrix products, per_device(): jnp.einsum('pxk,pkd->pxd', weights.astype(jnp.bfloat16).reshape(pool_here...  4.42 us
  transfers between devices with their start and end apart: 6, of which 6 were waited for; matrix products, arithmetic and copies ran while one was open for 5% of the time, Pallas kernels for 0%

profile of v2, /device:TPU:0, one launch (start us, length us, event | category | flops | bytes accessed | tf_op | source)
XLA Modules:
  0.0 146.3 jit_solution(197500691069901196)
XLA Ops:
  2.5 3.8 %fusion.18 = f32[3,4,3,512]{3,1,2,0:T(4,128)S(1)} fusion(bf16[2048,3,512]{2,0,1:T(8,128)(2,1)} %param.21, bf16[3,4,2048]{2,1,0:T(4,128)(2,1)} %param.19, f32[2048]{0:T(1024)S(1)} %convert_element_type.84, f32[3,4]{1,0:T(4,128)S(1)} %add_rsqrt_fusion.1, f32[3,512]{1,0:T(4,128)S(1)} %convert_element_type.86), kind=kOutput, calls=%fused_computation.17 | convolution fusion | flops 75614208 | bytes 6428720 | tf_op jit(solution)/shard_map/rsd,dcf->rscf/dot_general | solution.py:84
  8.1 7.3 %all-to-all-start = ((bf16[8,3,4,4,128]{4,3,2,1,0:T(4,128)(2,1)}), bf16[8,3,4,4,128]{4,3,2,1,0:T(4,128)(2,1)S(1)}, u32[]{:S(2)}, u32[]{:S(2)}) async-start(bf16[8,3,4,4,128]{4,3,2,1,0:T(4,128)(2,1)} %broadcast_in_dim.123), calls=%async_computation | async-start | bytes 196608 | tf_op jit(solution)/shard_map/all_to_all | solution.py:44
  18.4 4.1 %all-to-all-done = bf16[8,3,4,4,128]{4,3,2,1,0:T(4,128)(2,1)S(1)} async-done(((bf16[8,3,4,4,128]{4,3,2,1,0:T(4,128)(2,1)}), bf16[8,3,4,4,128]{4,3,2,1,0:T(4,128)(2,1)S(1)}, u32[]{:S(2)}, u32[]{:S(2)}) %all-to-all-start) | async-done | bytes 98336 | tf_op jit(solution)/shard_map/all_to_all | solution.py:44
  23.8 4.0 %fusion.115 = (f32[40,16]{1,0:T(8,128)S(1)}, f32[40,16,128]{2,1,0:T(8,128)S(1)}) fusion(bf16[40,128,512]{2,1,0:T(8,128)(2,1)} %param.24, bf16[40,16,512]{2,1,0:T(8,128)(2,1)S(1)} %broadcast_in_dim.125, pred[16,512]{1,0:T(8,128)(4,1)S(1)} %bitcast.159, pred[40,128]{1,0:T(8,128)(4,1)S(1)} %fusion.78), kind=kOutput, calls=%fused_computation.171 | convolution fusion | flops 84458880 | bytes 6241792 | tf_op jit(solution)/shard_map/pxd,pkd->pxk/dot_general | solution.py:109
  29.1 4.4 %fusion.50 = f32[40,16,512]{2,1,0:T(8,128)} fusion(bf16[40,128,512]{2,1,0:T(8,128)(2,1)} %param.25, f32[40,16,128]{2,1,0:T(8,128)S(1)} %get-tuple-element.29, f32[40,16]{1,0:T(8,128)S(1)} %get-tuple-element.28, pred[40,128]{1,0:T(8,128)(4,1)S(1)} %fusion.78), kind=kOutput, calls=%fused_computation.63 | convolution fusion | flops 84131840 | bytes 6888960 | tf_op jit(solution)/shard_map/pxk,pkd->pxd/dot_general | solution.py:117
  33.5 1.7 %reshape.391 = f32[40,4,4,4,128]{4,3,2,1,0:T(4,128)S(1)} reshape(f32[40,16,512]{2,1,0:T(8,128)} %fusion.50) | data formatting | bytes 2621440 | tf_op jit(solution)/shard_map/reshape | solution.py:122
  37.7 3.4 %all-to-all-start.1 = ((f32[24,17,128]{2,1,0:T(8,128)}), f32[24,17,128]{2,1,0:T(8,128)S(1)}, u32[]{:S(2)}, u32[]{:S(2)}) async-start(f32[24,17,128]{2,1,0:T(8,128)} %pad_maximum_fusion.2), calls=%async_computation.1 | async-start | bytes 589824 | tf_op jit(solution)/shard_map/all_to_all | solution.py:142
  41.4 8.3 %all-to-all-done.1 = f32[24,17,128]{2,1,0:T(8,128)S(1)} async-done(((f32[24,17,128]{2,1,0:T(8,128)}), f32[24,17,128]{2,1,0:T(8,128)S(1)}, u32[]{:S(2)}, u32[]{:S(2)}) %all-to-all-start.1) | async-done | bytes 208928 | tf_op jit(solution)/shard_map/all_to_all | solution.py:142
  52.1 3.5 %all-to-all-start.2 = ((f32[4,12,2048]{2,1,0:T(8,128)}), f32[4,12,2048]{2,1,0:T(8,128)S(1)}, u32[]{:S(2)}, u32[]{:S(2)}) async-start(f32[4,12,2048]{2,1,0:T(8,128)} %broadcast_in_dim.206), calls=%async_computation.2 | async-start | bytes 1048576 | tf_op jit(solution)/shard_map/all_to_all | solution.py:44
  55.9 8.5 %all-to-all-done.2 = f32[4,12,2048]{2,1,0:T(8,128)S(1)} async-done(((f32[4,12,2048]{2,1,0:T(8,128)}), f32[4,12,2048]{2,1,0:T(8,128)S(1)}, u32[]{:S(2)}, u32[]{:S(2)}) %all-to-all-start.2) | async-done | bytes 393248 | tf_op jit(solution)/shard_map/all_to_all | solution.py:44
  68.3 4.2 %all-to-all-start.3 = ((bf16[8,2,9216]{2,1,0:T(2,128)(2,1)}), bf16[8,2,9216]{2,1,0:T(2,128)(2,1)}, u32[]{:S(2)}, u32[]{:S(2)}) async-start(bf16[8,2,9216]{2,1,0:T(2,128)(2,1)} %reshape.441), calls=%async_computation.3 | async-start | bytes 589824 | tf_op jit(solution)/shard_map/all_to_all | solution.py:215
  72.5 3.5 %reshape_squeeze.12 = bf16[352,4,512]{2,1,0:T(4,128)(2,1)S(1)} reshape(bf16[1,352,2048]{2,1,0:T(8,128)(2,1)} %param.33) | data formatting | bytes 2883584 | tf_op jit(solution)/shard_map/reshape;squeeze | solution.py:226
  76.0 6.0 %all-to-all-done.3 = bf16[8,2,9216]{2,1,0:T(2,128)(2,1)} async-done(((bf16[8,2,9216]{2,1,0:T(2,128)(2,1)}), bf16[8,2,9216]{2,1,0:T(2,128)(2,1)}, u32[]{:S(2)}, u32[]{:S(2)}) %all-to-all-start.3) | async-done | bytes 294944 | tf_op jit(solution)/shard_map/all_to_all | solution.py:215
  82.0 1.9 %reshape.442 = bf16[8,1,18432]{2,1,0:T(2,128)(2,1)} reshape(bf16[8,2,9216]{2,1,0:T(2,128)(2,1)} %all-to-all-done.3) | data formatting | bytes 589824
  86.4 1.7 %reshape.404 = bf16[96,512]{1,0:T(8,128)(2,1)} reshape(bf16[8,6144]{1,0:T(8,128)(2,1)} %slice.97) | data formatting | bytes 196608 | tf_op jit(solution)/shard_map/reshape | solution.py:218
  91.9 2.1 %reshape.405 = f32[4,33792]{1,0:T(4,128)} reshape(f32[96,1408]{1,0:T(8,128)} %pad_maximum_fusion.1) | data formatting | bytes 1081344 | tf_op jit(solution)/shard_map/reshape | solution.py:234
  94.0 1.9 %reshape.402 = bf16[48,2048]{1,0:T(8,128)(2,1)} reshape(bf16[8,12288]{1,0:T(8,128)(2,1)} %slice.96) | data formatting | bytes 393216 | tf_op jit(solution)/shard_map/reshape | solution.py:217
  95.9 2.7 %fusion.4 = f32[48,352]{1,0:T(8,128)} fusion(bf16[48,2048]{1,0:T(8,128)(2,1)} %reshape.402, bf16[1,2048,352]{1,2,0:T(8,128)(2,1)} %param.31), kind=kOutput, calls=%fused_computation.7 | convolution fusion | flops 69206016 | bytes 1705984 | tf_op jit(solution)/shard_map/dot_general | solution.py:219
  98.5 3.3 %fusion.8 = f32[1,4,48,512]{3,2,1,0:T(8,128)} fusion(bf16[352,4,512]{2,1,0:T(4,128)(2,1)S(1)} %reshape_squeeze.12, bf16[48,2048]{1,0:T(8,128)(2,1)} %reshape.402, bf16[1,2048,352]{1,2,0:T(8,128)(2,1)} %param.32, f32[48,352]{1,0:T(8,128)} %fusion.4), kind=kOutput, calls=%fused_computation.12 | convolution fusion | flops 138513408 | bytes 3540992 | tf_op jit(solution)/shard_map/rk,kjc->jrc/dot_general | solution.py:223
  105.0 15.6 %all_to_all.53 = f32[4,1,58368]{2,1,0:T(1,128)S(1)} all-to-all(f32[4,1,58368]{2,1,0:T(1,128)S(1)} %all_to_all.40), channel_id=1, replica_groups=mesh['req'=8,'tp'=4] {'tp'}, dimensions={0} | all-to-all | bytes 1867776 | tf_op jit(solution)/shard_map/all_to_all | solution.py:240
  122.3 3.3 %all-to-all-start.5 = ((bf16[4,24,704]{2,1,0:T(8,128)(2,1)}), bf16[4,24,704]{2,1,0:T(8,128)(2,1)S(1)}, u32[]{:S(2)}, u32[]{:S(2)}) async-start(bf16[4,24,704]{2,1,0:T(8,128)(2,1)} %broadcast_in_dim.209), calls=%async_computation.5 | async-start | bytes 294912 | tf_op jit(solution)/shard_map/all_to_all | solution.py:44
  125.7 4.7 %all-to-all-done.5 = bf16[4,24,704]{2,1,0:T(8,128)(2,1)S(1)} async-done(((bf16[4,24,704]{2,1,0:T(8,128)(2,1)}), bf16[4,24,704]{2,1,0:T(8,128)(2,1)S(1)}, u32[]{:S(2)}, u32[]{:S(2)}) %all-to-all-start.5) | async-done | bytes 135200 | tf_op jit(solution)/shard_map/all_to_all | solution.py:44
  131.7 3.6 %all-to-all-start.6 = ((f32[8,1,9216]{2,1,0:T(1,128)}), f32[8,1,9216]{2,1,0:T(1,128)S(1)}, u32[]{:S(2)}, u32[]{:S(2)}) async-start(f32[8,1,9216]{2,1,0:T(1,128)} %all_to_all.43), calls=%async_computation.6 | async-start | bytes 589824 | tf_op jit(solution)/shard_map/all_to_all | solution.py:256
  135.8 8.7 %all-to-all-done.6 = f32[8,1,9216]{2,1,0:T(1,128)S(1)} async-done(((f32[8,1,9216]{2,1,0:T(1,128)}), f32[8,1,9216]{2,1,0:T(1,128)S(1)}, u32[]{:S(2)}, u32[]{:S(2)}) %all-to-all-start.6) | async-done | bytes 294944 | tf_op jit(solution)/shard_map/all_to_all | solution.py:256
  (148 shorter events, 33.5 us)
Async XLA Ops:
  0.0 50.8 %copy-start = (bf16[512,2048]{1,0:T(8,128)(2,1)S(1)}, bf16[512,2048]{1,0:T(8,128)(2,1)}, u32[]{:S(2)}) copy-start(bf16[512,2048]{1,0:T(8,128)(2,1)} %param.23) | copy-start | bytes 6291460
  2.5 3.9 %copy-start.1 = (s32[24]{0:T(128)S(1)}, s32[24]{0:T(128)}, u32[]{:S(2)}) copy-start(s32[24]{0:T(128)} %param.27) | copy-start | bytes 292
  2.5 12.9 %copy-start.10 = (s32[3,4,4]{2,1,0:T(4,128)S(1)}, s32[3,4,4]{2,1,0:T(4,128)}, u32[]{:S(2)}) copy-start(s32[3,4,4]{2,1,0:T(4,128)} %param.29) | copy-start | bytes 580
  2.5 13.9 %copy-start.9 = (s32[24,37]{1,0:T(8,128)S(1)}, s32[24,37]{1,0:T(8,128)}, u32[]{:S(2)}) copy-start(s32[24,37]{1,0:T(8,128)} %param.26) | copy-start | bytes 10660
  8.1 14.4 %all-to-all-start = ((bf16[8,3,4,4,128]{4,3,2,1,0:T(4,128)(2,1)}), bf16[8,3,4,4,128]{4,3,2,1,0:T(4,128)(2,1)S(1)}, u32[]{:S(2)}, u32[]{:S(2)}) async-start(bf16[8,3,4,4,128]{4,3,2,1,0:T(4,128)(2,1)} %broadcast_in_dim.123), calls=%async_computation | async-start | bytes 196608 | tf_op jit(solution)/shard_map/all_to_all | solution.py:44
  35.2 1.7 %copy-start.15 = (f32[128]{0:T(128)S(1)}, f32[128]{0:T(128)}, u32[]{:S(2)}) copy-start(f32[128]{0:T(128)} %pad.14.clone) | copy-start | bytes 1540
  36.2 4.9 %copy-start.7 = (bf16[3,4,4,64]{3,1,2,0:T(4,128)(2,1)S(1)}, bf16[3,4,4,64]{3,1,2,0:T(4,128)(2,1)}, u32[]{:S(2)}) copy-start(bf16[3,4,4,64]{3,1,2,0:T(4,128)(2,1)} %get-tuple-element.18) | copy-start | bytes 18436
  36.2 4.9 %copy-start.8 = (bf16[3,4,4,64]{3,1,2,0:T(4,128)(2,1)S(1)}, bf16[3,4,4,64]{3,1,2,0:T(4,128)(2,1)}, u32[]{:S(2)}) copy-start(bf16[3,4,4,64]{3,1,2,0:T(4,128)(2,1)} %get-tuple-element.19) | copy-start | bytes 18436
  37.7 12.0 %all-to-all-start.1 = ((f32[24,17,128]{2,1,0:T(8,128)}), f32[24,17,128]{2,1,0:T(8,128)S(1)}, u32[]{:S(2)}, u32[]{:S(2)}) async-start(f32[24,17,128]{2,1,0:T(8,128)} %pad_maximum_fusion.2), calls=%async_computation.1 | async-start | bytes 589824 | tf_op jit(solution)/shard_map/all_to_all | solution.py:142
  50.8 4.7 %copy-start.14 = (s32[48]{0:T(128)S(1)}, s32[48]{0:T(128)}, u32[]{:S(2)}) copy-start(s32[48]{0:T(128)} %select_reduce_fusion.2) | copy-start | bytes 580
  50.8 4.7 %copy-start.4 = (bf16[3,4,2048]{2,1,0:T(4,128)(2,1)S(1)}, bf16[3,4,2048]{2,1,0:T(4,128)(2,1)}, u32[]{:S(2)}) copy-start(bf16[3,4,2048]{2,1,0:T(4,128)(2,1)} %param.19) | copy-start | bytes 147460
  51.2 4.4 %copy-start.12 = (bf16[2048]{0:T(1024)(128)(2,1)S(1)}, bf16[2048]{0:T(1024)(128)(2,1)}, u32[]{:S(2)}) copy-start(bf16[2048]{0:T(1024)(128)(2,1)} %param.28) | copy-start | bytes 12292
  52.1 12.3 %all-to-all-start.2 = ((f32[4,12,2048]{2,1,0:T(8,128)}), f32[4,12,2048]{2,1,0:T(8,128)S(1)}, u32[]{:S(2)}, u32[]{:S(2)}) async-start(f32[4,12,2048]{2,1,0:T(8,128)} %broadcast_in_dim.206), calls=%async_computation.2 | async-start | bytes 1048576 | tf_op jit(solution)/shard_map/all_to_all | solution.py:44
  65.3 0.6 copy-start.5
  68.3 13.7 %all-to-all-start.3 = ((bf16[8,2,9216]{2,1,0:T(2,128)(2,1)}), bf16[8,2,9216]{2,1,0:T(2,128)(2,1)}, u32[]{:S(2)}, u32[]{:S(2)}) async-start(bf16[8,2,9216]{2,1,0:T(2,128)(2,1)} %reshape.441), calls=%async_computation.3 | async-start | bytes 589824 | tf_op jit(solution)/shard_map/all_to_all | solution.py:215
  88.1 1.6 %copy-start.2 = (bf16[512,704]{0,1:T(8,128)(2,1)S(1)}, bf16[512,704]{0,1:T(8,128)(2,1)}, u32[]{:S(2)}) copy-start(bf16[512,704]{0,1:T(8,128)(2,1)} %param.34) | copy-start | bytes 2162692
  121.5 8.9 %copy-start.3 = (bf16[704,512]{1,0:T(8,128)(2,1)S(1)}, bf16[704,512]{1,0:T(8,128)(2,1)}, u32[]{:S(2)}) copy-start(bf16[704,512]{1,0:T(8,128)(2,1)} %param.36) | copy-start | bytes 2162692
  122.3 8.1 %all-to-all-start.5 = ((bf16[4,24,704]{2,1,0:T(8,128)(2,1)}), bf16[4,24,704]{2,1,0:T(8,128)(2,1)S(1)}, u32[]{:S(2)}, u32[]{:S(2)}) async-start(bf16[4,24,704]{2,1,0:T(8,128)(2,1)} %broadcast_in_dim.209), calls=%async_computation.5 | async-start | bytes 294912 | tf_op jit(solution)/shard_map/all_to_all | solution.py:44
  130.4 4.9 %copy-start.11 = (f32[3,4,4]{2,1,0:T(4,128)S(1)}, f32[3,4,4]{2,1,0:T(4,128)}, u32[]{:S(2)}) copy-start(f32[3,4,4]{2,1,0:T(4,128)} %param.30) | copy-start | bytes 580
  130.4 5.0 %copy-start.13 = (bf16[2048]{0:T(1024)(128)(2,1)S(1)}, bf16[2048]{0:T(1024)(128)(2,1)}, u32[]{:S(2)}) copy-start(bf16[2048]{0:T(1024)(128)(2,1)} %param.37) | copy-start | bytes 12292
  130.7 5.0 %copy-start.6 = (bf16[12,2048]{1,0:T(8,128)(2,1)S(1)}, bf16[12,2048]{1,0:T(8,128)(2,1)}, u32[]{:S(2)}) copy-start(bf16[12,2048]{1,0:T(8,128)(2,1)} %copy-done.5) | copy-start | bytes 147460
  131.7 12.8 %all-to-all-start.6 = ((f32[8,1,9216]{2,1,0:T(1,128)}), f32[8,1,9216]{2,1,0:T(1,128)S(1)}, u32[]{:S(2)}, u32[]{:S(2)}) async-start(f32[8,1,9216]{2,1,0:T(1,128)} %all_to_all.43), calls=%async_computation.6 | async-start | bytes 589824 | tf_op jit(solution)/shard_map/all_to_all | solution.py:256

commit v3 on v2

--- a/solution.py
+++ b/solution.py
@@ -101,26 +101,23 @@
     token_pos = logical[:, None] * page_len + jnp.arange(page_len, dtype=jnp.int32)[None, :]
     live = present[:, None] & (token_pos < cache_lengths[owner][:, None])
     page_queries = query_all[owner]
-    head_eye = jnp.arange(local_heads)[:, None] == jnp.arange(local_heads)[None, :]
-    block_queries = jnp.where(
-        head_eye[None, None, :, :, None], page_queries[:, :, :, None, :], jnp.zeros((), jnp.bfloat16)
-    ).reshape(pool_here, step_count * local_heads, head_width)
+    page_keys = cache_keys.reshape(pool_here, page_len, local_heads, HD)
+    page_values = cache_values.reshape(pool_here, page_len, local_heads, HD)
     scores = (
-        jnp.einsum("pxd,pkd->pxk", block_queries, cache_keys, preferred_element_type=jnp.float32)
+        jnp.einsum("pshd,pkhd->pshk", page_queries, page_keys, preferred_element_type=jnp.float32)
         * score_scale
-    ).reshape(pool_here, step_count, local_heads, page_len)
+    )
     page_mask = live[:, None, None, :]
     masked = jnp.where(page_mask, scores, NEG)
     page_max = jnp.max(masked, axis=-1)
     weights = jnp.where(page_mask, jnp.exp(masked - page_max[..., None]), 0.0)
     page_sum = jnp.sum(weights, axis=-1)
-    wide_out = jnp.einsum(
-        "pxk,pkd->pxd",
-        weights.astype(jnp.bfloat16).reshape(pool_here, step_count * local_heads, page_len),
-        cache_values,
+    page_out = jnp.einsum(
+        "pshk,pkhd->pshd",
+        weights.astype(jnp.bfloat16),
+        page_values,
         preferred_element_type=jnp.float32,
-    ).reshape(pool_here, step_count, local_heads, local_heads, HD)
-    page_out = jnp.sum(jnp.where(head_eye[None, None, :, :, None], wide_out, 0.0), axis=3)
+    )
     belongs = (owner[None, :] == request_ids[:, None]) & present[None, :]
     owned = belongs[:, :, None, None]
     local_max = jnp.max(jnp.where(owned, page_max[None], NEG), axis=1)
@@ -219,13 +216,9 @@
     gate_pre = jnp.dot(flat_rows, w_gate_here, preferred_element_type=jnp.float32)
     up_pre = jnp.dot(flat_rows, w_up_here, preferred_element_type=jnp.float32)
     hidden = (jax.nn.silu(gate_pre) * up_pre).astype(jnp.bfloat16)
+    partial_out = jnp.dot(hidden, w_down_here, preferred_element_type=jnp.float32)
     expert_rows = req_count * capacity
-    partial_split = jnp.einsum(
-        "rk,kjc->jrc",
-        hidden,
-        w_down_here.reshape(w_down_here.shape[0], tp_count, col_share),
-        preferred_element_type=jnp.float32,
-    )
+    partial_split = partial_out.reshape(expert_rows, tp_count, col_share).transpose(1, 0, 2)
     gate_part = jnp.dot(piece, shared_w_gate, preferred_element_type=jnp.float32)
     up_part = jnp.dot(piece, shared_w_up, preferred_element_type=jnp.float32)
     unit_count = shared_w_gate.shape[1]

time: 148 us -> 134 us (0.905)
  local copies, waits for them, and re-layouts: 27 us -> 11.6 us
  blocking collectives: 15.6 us -> 29.1 us
  waiting for transfers between devices: 40.3 us -> 35.7 us
  starting transfers between devices: 25.3 us -> 20.9 us
  other arithmetic: 12.3 us -> 9.39 us
    all_to_all x0 -> x1, blocking collectives: none -> 13.5 us  [per_device(): received = lax.all_to_all(dispatch, 'req', 0, 0, tiled=True)]
    all_to_all x1 -> x0, waiting for transfers between devices: 6.01 us -> none  [per_device(): received = lax.all_to_all(dispatch, 'req', 0, 0, tiled=True)]
    all_to_all x1 -> x0, starting transfers between devices: 4.23 us -> none  [per_device(): received = lax.all_to_all(dispatch, 'req', 0, 0, tiled=True)]
    unnamed x42 -> x31, local copies, waits for them, and re-layouts: 5.59 us -> 1.95 us
    another operation x1 -> x0, local copies, waits for them, and re-layouts: 3.47 us -> none  [per_device(): w_down_here.reshape(w_down_here.shape[0], tp_count, col_share)]
    reshape x1, local copies, waits for them, and re-layouts: 2.1 us -> 0.23 us  [per_device(): jnp.concatenate([gate_part, up_part], axis=1)]
    reshape x1 -> x0, local copies, waits for them, and re-layouts: 1.7 us -> none  [per_device(): wide_out = jnp.einsum('pxk,pkd->pxd', weights.astype(jnp.bfloat16).reshap...]
    reshape x1, local copies, waits for them, and re-layouts: 1.86 us -> 0.25 us  [per_device(): received[:, :capacity * model_width]]
  transfers between devices with their start and end apart: 6 -> 5, of which waited for: 6 -> 5; matrix products, arithmetic and copies ran while one was open for 5% -> 2% of each run, Pallas kernels for 0% -> 0%
where the time goes in v3:
time: 134 us; the launch traced here: 133 us
  waiting for transfers between devices  35.7 us (27%)
  blocking collectives  29.1 us (22%)
  matrix products  25.6 us (19%)
  starting transfers between devices  20.9 us (16%)
  local copies, waits for them, and re-layouts  11.6 us (9%)
  other arithmetic  9.39 us (7%)
    all_to_all x3, waiting for transfers between devices, bcast_a2a(): lax.all_to_all(spread, axis, 0, 0, tiled=True)  18.6 us
    all_to_all x1, blocking collectives, per_device(): lax.all_to_all(reduce_in, 'tp', 0, 0, tiled=True)  15.6 us
    all_to_all x3, starting transfers between devices, bcast_a2a(): lax.all_to_all(spread, axis, 0, 0, tiled=True)  14.1 us
    all_to_all x1, blocking collectives, per_device(): received = lax.all_to_all(dispatch, 'req', 0, 0, tiled=True)  13.5 us
    all_to_all x1, waiting for transfers between devices, per_device(): back = lax.all_to_all(back_in, 'req', 0, 0, tiled=True)  8.87 us
    all_to_all x1, waiting for transfers between devices, per_device(): lax.all_to_all(packed, 'req', 0, 0, tiled=True)  8.29 us
    dot_general x1, matrix products, per_device(): jnp.einsum('pshd,pkhd->pshk', page_queries, page_keys, preferred_element_...  5.41 us
    dot_general x1, matrix products, per_device(): jnp.einsum('pshk,pkhd->pshd', weights.astype(jnp.bfloat16), page_values,...  4 us
  transfers between devices with their start and end apart: 5, of which 5 were waited for; matrix products, arithmetic and copies ran while one was open for 2% of the time, Pallas kernels for 0%

profile of v3, /device:TPU:0, one launch (start us, length us, event | category | flops | bytes accessed | tf_op | source)
XLA Modules:
  0.0 132.9 jit_solution(14686708544687235092)
XLA Ops:
  1.0 0.9 multiply_reduce_fusion.1
  3.3 3.8 %fusion.30 = f32[3,4,3,512]{3,1,2,0:T(4,128)S(1)} fusion(bf16[2048,3,512]{2,0,1:T(8,128)(2,1)} %param.21, bf16[3,4,2048]{2,1,0:T(4,128)(2,1)} %param.19, f32[2048]{0:T(1024)S(1)} %convert_element_type.83, f32[3,4]{1,0:T(4,128)S(1)} %add_rsqrt_fusion.1, f32[3,512]{1,0:T(4,128)S(1)} %convert_element_type.85), kind=kOutput, calls=%fused_computation.23 | convolution fusion | flops 75614208 | bytes 6428720 | tf_op jit(solution)/shard_map/rsd,dcf->rscf/dot_general | solution.py:84
  8.1 7.3 %all-to-all-start = ((bf16[8,3,4,4,128]{4,3,2,1,0:T(4,128)(2,1)}), bf16[8,3,4,4,128]{4,3,2,1,0:T(4,128)(2,1)S(1)}, u32[]{:S(2)}, u32[]{:S(2)}) async-start(bf16[8,3,4,4,128]{4,3,2,1,0:T(4,128)(2,1)} %broadcast_in_dim.81), calls=%async_computation | async-start | bytes 196608 | tf_op jit(solution)/shard_map/all_to_all | solution.py:44
  17.2 5.3 %all-to-all-done = bf16[8,3,4,4,128]{4,3,2,1,0:T(4,128)(2,1)S(1)} async-done(((bf16[8,3,4,4,128]{4,3,2,1,0:T(4,128)(2,1)}), bf16[8,3,4,4,128]{4,3,2,1,0:T(4,128)(2,1)S(1)}, u32[]{:S(2)}, u32[]{:S(2)}) %all-to-all-start) | async-done | bytes 98336 | tf_op jit(solution)/shard_map/all_to_all | solution.py:44
  23.2 5.4 %fusion.129 = (f32[40,4,4]{1,2,0:T(4,128)S(1)}, f32[40,4,4,128]{3,1,2,0:T(4,128)S(1)}) fusion(bf16[40,4,4,128]{3,2,1,0:T(4,128)(2,1)S(1)} %gather_fusion.1, pred[40,128]{1,0:T(8,128)(4,1)S(1)} %fusion.93, bf16[40,128,512]{2,1,0:T(8,128)(2,1)} %param.24), kind=kOutput, calls=%fused_computation.173 | convolution fusion | flops 21216640 | bytes 5742080 | tf_op jit(solution)/shard_map/pshd,pkhd->pshk/dot_general | solution.py:107
  29.5 4.0 %fusion.18 = f32[40,4,4,128]{3,1,2,0:T(4,128)S(1)} fusion(f32[40,4,4,128]{3,1,2,0:T(4,128)S(1)} %get-tuple-element.29, f32[40,4,4]{1,2,0:T(4,128)S(1)} %get-tuple-element.28, pred[40,128]{1,0:T(8,128)(4,1)S(1)} %fusion.93, bf16[40,128,512]{2,1,0:T(8,128)(2,1)} %param.25), kind=kOutput, calls=%fused_computation.19 | convolution fusion | flops 21217280 | bytes 5905920 | tf_op jit(solution)/shard_map/pshk,pkhd->pshd/dot_general | solution.py:115
  35.6 3.4 %all-to-all-start.1 = ((f32[24,17,128]{2,1,0:T(8,128)}), f32[24,17,128]{2,1,0:T(8,128)S(1)}, u32[]{:S(2)}, u32[]{:S(2)}) async-start(f32[24,17,128]{2,1,0:T(8,128)} %pad_maximum_fusion.2), calls=%async_computation.1 | async-start | bytes 589824 | tf_op jit(solution)/shard_map/all_to_all | solution.py:139
  39.3 8.3 %all-to-all-done.1 = f32[24,17,128]{2,1,0:T(8,128)S(1)} async-done(((f32[24,17,128]{2,1,0:T(8,128)}), f32[24,17,128]{2,1,0:T(8,128)S(1)}, u32[]{:S(2)}, u32[]{:S(2)}) %all-to-all-start.1) | async-done | bytes 208928 | tf_op jit(solution)/shard_map/all_to_all | solution.py:139
  50.0 3.5 %all-to-all-start.2 = ((f32[4,12,2048]{2,1,0:T(8,128)}), f32[4,12,2048]{2,1,0:T(8,128)S(1)}, u32[]{:S(2)}, u32[]{:S(2)}) async-start(f32[4,12,2048]{2,1,0:T(8,128)} %broadcast_in_dim.92), calls=%async_computation.2 | async-start | bytes 1048576 | tf_op jit(solution)/shard_map/all_to_all | solution.py:44
  53.8 8.5 %all-to-all-done.2 = f32[4,12,2048]{2,1,0:T(8,128)S(1)} async-done(((f32[4,12,2048]{2,1,0:T(8,128)}), f32[4,12,2048]{2,1,0:T(8,128)S(1)}, u32[]{:S(2)}, u32[]{:S(2)}) %all-to-all-start.2) | async-done | bytes 393248 | tf_op jit(solution)/shard_map/all_to_all | solution.py:44
  65.5 13.5 %all_to_all.53 = bf16[8,2,9216]{2,1,0:T(2,128)(2,1)S(1)} all-to-all(bf16[8,2,9216]{2,1,0:T(2,128)(2,1)S(1)} %reshape.420), channel_id=1, replica_groups=mesh['req'=8,'tp'=4] {'req'}, dimensions={0} | all-to-all | bytes 589824 | tf_op jit(solution)/shard_map/all_to_all | solution.py:212
  79.9 2.5 %fusion.13 = f32[48,352]{1,0:T(8,128)} fusion(bf16[48,2048]{1,0:T(8,128)(2,1)S(1)} %reshape.381, bf16[1,2048,352]{1,2,0:T(8,128)(2,1)} %param.31), kind=kOutput, calls=%fused_computation.16 | convolution fusion | flops 69206016 | bytes 1705984 | tf_op jit(solution)/shard_map/dot_general | solution.py:216
  82.4 3.0 %fusion.15 = f32[1,4,48,512]{3,2,1,0:T(8,128)S(1)} fusion(bf16[44,4,8,512]{3,2,1,0:T(8,128)(2,1)} %bitcast.167, bf16[48,2048]{1,0:T(8,128)(2,1)S(1)} %reshape.381, bf16[1,2048,352]{1,2,0:T(8,128)(2,1)} %param.32, f32[48,352]{1,0:T(8,128)} %fusion.13), kind=kOutput, calls=%fused_computation.18 | convolution fusion | flops 138513408 | bytes 3540992 | tf_op jit(solution)/shard_map/dot_general | solution.py:219
  85.4 1.0 copy.183
  86.8 1.5 %fusion.132 = f32[96,704]{1,0:T(8,128)S(1)} fusion(bf16[96,512]{1,0:T(8,128)(2,1)S(1)} %reshape.383, bf16[512,704]{0,1:T(8,128)(2,1)} %param.34), kind=kOutput, calls=%fused_computation.176 | convolution fusion | flops 69206016 | bytes 1089536 | tf_op jit(solution)/shard_map/dot_general | solution.py:222
  88.6 1.2 pad_maximum_fusion
  90.5 15.6 %all_to_all.54 = f32[4,1,58368]{2,1,0:T(1,128)S(1)} all-to-all(f32[4,1,58368]{2,1,0:T(1,128)S(1)} %all_to_all.40), channel_id=1, replica_groups=mesh['req'=8,'tp'=4] {'tp'}, dimensions={0} | all-to-all | bytes 1867776 | tf_op jit(solution)/shard_map/all_to_all | solution.py:233
  107.8 3.3 %all-to-all-start.5 = ((bf16[4,24,704]{2,1,0:T(8,128)(2,1)}), bf16[4,24,704]{2,1,0:T(8,128)(2,1)S(1)}, u32[]{:S(2)}, u32[]{:S(2)}) async-start(bf16[4,24,704]{2,1,0:T(8,128)(2,1)} %broadcast_in_dim.95), calls=%async_computation.5 | async-start | bytes 294912 | tf_op jit(solution)/shard_map/all_to_all | solution.py:44
  111.2 4.7 %all-to-all-done.5 = bf16[4,24,704]{2,1,0:T(8,128)(2,1)S(1)} async-done(((bf16[4,24,704]{2,1,0:T(8,128)(2,1)}), bf16[4,24,704]{2,1,0:T(8,128)(2,1)S(1)}, u32[]{:S(2)}, u32[]{:S(2)}) %all-to-all-start.5) | async-done | bytes 135200 | tf_op jit(solution)/shard_map/all_to_all | solution.py:44
  115.9 1.4 %fusion.134 = f32[96,512]{1,0:T(8,128)S(1)} fusion(bf16[96,704]{1,0:T(8,128)(2,1)S(1)} %bitcast.176, bf16[704,512]{1,0:T(8,128)(2,1)} %param.36), kind=kOutput, calls=%fused_computation.178 | convolution fusion | flops 69206016 | bytes 1052672 | tf_op jit(solution)/shard_map/dot_general | solution.py:240
  117.4 0.9 all_to_all.43
  118.3 3.4 %all-to-all-start.6 = ((f32[8,1,9216]{2,1,0:T(1,128)}), f32[8,1,9216]{2,1,0:T(1,128)S(1)}, u32[]{:S(2)}, u32[]{:S(2)}) async-start(f32[8,1,9216]{2,1,0:T(1,128)} %all_to_all.43), calls=%async_computation.6 | async-start | bytes 589824 | tf_op jit(solution)/shard_map/all_to_all | solution.py:249
  122.3 8.9 %all-to-all-done.6 = f32[8,1,9216]{2,1,0:T(1,128)S(1)} async-done(((f32[8,1,9216]{2,1,0:T(1,128)}), f32[8,1,9216]{2,1,0:T(1,128)S(1)}, u32[]{:S(2)}, u32[]{:S(2)}) %all-to-all-start.6) | async-done | bytes 294944 | tf_op jit(solution)/shard_map/all_to_all | solution.py:249
  131.4 0.9 fusion.37
  (129 shorter events, 20.1 us)
Async XLA Ops:
  0.0 48.8 %copy-start = (bf16[512,2048]{1,0:T(8,128)(2,1)S(1)}, bf16[512,2048]{1,0:T(8,128)(2,1)}, u32[]{:S(2)}) copy-start(bf16[512,2048]{1,0:T(8,128)(2,1)} %param.23) | copy-start | bytes 6291460
  0.0 15.9 %copy-start.1 = (s32[24]{0:T(128)S(1)}, s32[24]{0:T(128)}, u32[]{:S(2)}) copy-start(s32[24]{0:T(128)} %param.27) | copy-start | bytes 292
  0.0 15.4 %copy-start.7 = (s32[3,4,4]{2,1,0:T(4,128)S(1)}, s32[3,4,4]{2,1,0:T(4,128)}, u32[]{:S(2)}) copy-start(s32[3,4,4]{2,1,0:T(4,128)} %param.29) | copy-start | bytes 580
  0.0 15.5 %copy-start.6 = (s32[24,37]{1,0:T(8,128)S(1)}, s32[24,37]{1,0:T(8,128)}, u32[]{:S(2)}) copy-start(s32[24,37]{1,0:T(8,128)} %param.26) | copy-start | bytes 10660
  8.1 14.4 %all-to-all-start = ((bf16[8,3,4,4,128]{4,3,2,1,0:T(4,128)(2,1)}), bf16[8,3,4,4,128]{4,3,2,1,0:T(4,128)(2,1)S(1)}, u32[]{:S(2)}, u32[]{:S(2)}) async-start(bf16[8,3,4,4,128]{4,3,2,1,0:T(4,128)(2,1)} %broadcast_in_dim.81), calls=%async_computation | async-start | bytes 196608 | tf_op jit(solution)/shard_map/all_to_all | solution.py:44
  33.5 20.0 %copy-start.3 = (bf16[3,4,2048]{2,1,0:T(4,128)(2,1)S(1)}, bf16[3,4,2048]{2,1,0:T(4,128)(2,1)}, u32[]{:S(2)}) copy-start(bf16[3,4,2048]{2,1,0:T(4,128)(2,1)} %param.19) | copy-start | bytes 147460
  33.5 20.1 %copy-start.9 = (bf16[2048]{0:T(1024)(128)(2,1)S(1)}, bf16[2048]{0:T(1024)(128)(2,1)}, u32[]{:S(2)}) copy-start(bf16[2048]{0:T(1024)(128)(2,1)} %param.28) | copy-start | bytes 12292
  35.6 12.0 %all-to-all-start.1 = ((f32[24,17,128]{2,1,0:T(8,128)}), f32[24,17,128]{2,1,0:T(8,128)S(1)}, u32[]{:S(2)}, u32[]{:S(2)}) async-start(f32[24,17,128]{2,1,0:T(8,128)} %pad_maximum_fusion.2), calls=%async_computation.1 | async-start | bytes 589824 | tf_op jit(solution)/shard_map/all_to_all | solution.py:139
  50.0 12.3 %all-to-all-start.2 = ((f32[4,12,2048]{2,1,0:T(8,128)}), f32[4,12,2048]{2,1,0:T(8,128)S(1)}, u32[]{:S(2)}, u32[]{:S(2)}) async-start(f32[4,12,2048]{2,1,0:T(8,128)} %broadcast_in_dim.92), calls=%async_computation.2 | async-start | bytes 1048576 | tf_op jit(solution)/shard_map/all_to_all | solution.py:44
  63.3 0.6 copy-start.4
  79.2 7.2 %copy-start.2 = (bf16[512,704]{0,1:T(8,128)(2,1)S(1)}, bf16[512,704]{0,1:T(8,128)(2,1)}, u32[]{:S(2)}) copy-start(bf16[512,704]{0,1:T(8,128)(2,1)} %param.35) | copy-start | bytes 2162692
  89.8 31.9 %copy-start.8 = (f32[3,4,4]{2,1,0:T(4,128)S(1)}, f32[3,4,4]{2,1,0:T(4,128)}, u32[]{:S(2)}) copy-start(f32[3,4,4]{2,1,0:T(4,128)} %param.30) | copy-start | bytes 580
  89.9 32.0 %copy-start.10 = (bf16[2048]{0:T(1024)(128)(2,1)S(1)}, bf16[2048]{0:T(1024)(128)(2,1)}, u32[]{:S(2)}) copy-start(bf16[2048]{0:T(1024)(128)(2,1)} %param.37) | copy-start | bytes 12292
  89.9 32.3 %copy-start.5 = (bf16[12,2048]{1,0:T(8,128)(2,1)S(1)}, bf16[12,2048]{1,0:T(8,128)(2,1)}, u32[]{:S(2)}) copy-start(bf16[12,2048]{1,0:T(8,128)(2,1)} %copy-done.4) | copy-start | bytes 147460
  107.8 8.1 %all-to-all-start.5 = ((bf16[4,24,704]{2,1,0:T(8,128)(2,1)}), bf16[4,24,704]{2,1,0:T(8,128)(2,1)S(1)}, u32[]{:S(2)}, u32[]{:S(2)}) async-start(bf16[4,24,704]{2,1,0:T(8,128)(2,1)} %broadcast_in_dim.95), calls=%async_computation.5 | async-start | bytes 294912 | tf_op jit(solution)/shard_map/all_to_all | solution.py:44
  118.3 12.8 %all-to-all-start.6 = ((f32[8,1,9216]{2,1,0:T(1,128)}), f32[8,1,9216]{2,1,0:T(1,128)S(1)}, u32[]{:S(2)}, u32[]{:S(2)}) async-start(f32[8,1,9216]{2,1,0:T(1,128)} %all_to_all.43), calls=%async_computation.6 | async-start | bytes 589824 | tf_op jit(solution)/shard_map/all_to_all | solution.py:249

commit v4 on v3

--- a/solution.py
+++ b/solution.py
@@ -223,20 +223,29 @@
     up_part = jnp.dot(piece, shared_w_up, preferred_element_type=jnp.float32)
     unit_count = shared_w_gate.shape[1]
     all_rows = req_count * row_count
-    share_rows = all_rows // tp_count
-    shared_pre = jnp.concatenate([gate_part, up_part], axis=1).reshape(
-        tp_count, share_rows * 2 * unit_count
-    )
+    expert_high = partial_split.astype(jnp.bfloat16)
+    expert_low = (partial_split - expert_high.astype(jnp.float32)).astype(jnp.bfloat16)
+    shared_pre = jnp.concatenate([gate_part, up_part], axis=1).astype(jnp.bfloat16)
     reduce_in = jnp.concatenate(
-        [partial_split.reshape(tp_count, expert_rows * col_share), shared_pre], axis=1
-    )
-    reduce_out = jnp.sum(lax.all_to_all(reduce_in, "tp", 0, 0, tiled=True), axis=0)
-    expert_sum = reduce_out[: expert_rows * col_share].reshape(expert_rows, col_share)
-    shared_sum = reduce_out[expert_rows * col_share :].reshape(share_rows, 2 * unit_count)
-    shared_hidden = (jax.nn.silu(shared_sum[:, :unit_count]) * shared_sum[:, unit_count:]).astype(
+        [
+            expert_high.reshape(tp_count, expert_rows * col_share),
+            expert_low.reshape(tp_count, expert_rows * col_share),
+            jnp.broadcast_to(
+                shared_pre.reshape(1, all_rows * 2 * unit_count),
+                (tp_count, all_rows * 2 * unit_count),
+            ),
+        ],
+        axis=1,
+    )
+    reduce_out = lax.all_to_all(reduce_in, "tp", 0, 0, tiled=True).astype(jnp.float32)
+    expert_part = expert_rows * col_share
+    expert_sum = jnp.sum(
+        reduce_out[:, :expert_part] + reduce_out[:, expert_part : 2 * expert_part], axis=0
+    ).reshape(expert_rows, col_share)
+    shared_sum = jnp.sum(reduce_out[:, 2 * expert_part :], axis=0).reshape(all_rows, 2 * unit_count)
+    hidden_all = (jax.nn.silu(shared_sum[:, :unit_count]) * shared_sum[:, unit_count:]).astype(
         jnp.bfloat16
     )
-    hidden_all = bcast_a2a(shared_hidden, "tp", tp_count).reshape(all_rows, unit_count)
     shared_down = jnp.dot(hidden_all, shared_w_down, preferred_element_type=jnp.float32)
     ey = expert_sum.astype(jnp.bfloat16).astype(jnp.float32)
     back_in = jnp.concatenate(

time: 134 us -> 157 us (1.17)
  other arithmetic: 9.39 us -> 22.2 us
  local copies, waits for them, and re-layouts: 11.6 us -> 21.7 us
  blocking collectives: 29.1 us -> 36.9 us
  waiting for transfers between devices: 35.7 us -> 31.4 us
  starting transfers between devices: 20.9 us -> 17.6 us
    unnamed x31 -> x29, local copies, waits for them, and re-layouts: 1.95 us -> 13.2 us
    all_to_all x0 -> x2, other arithmetic: none -> 9.7 us  [per_device(): lax.all_to_all(reduce_in, 'tp', 0, 0, tiled=True).astype(jnp.float32)]
    all_to_all x1, blocking collectives: 15.6 us -> 23.4 us  [per_device(): lax.all_to_all(reduce_in, 'tp', 0, 0, tiled=True).astype(jnp.float32)]
    reduce_sum x1 -> x2, other arithmetic: 0.85 us -> 5.86 us  [the longest x1 5.57 us: per_device(): jnp.sum(reduce_out[:, 2 * expert_part:], axis=0)]
    all_to_all x3 -> x2, waiting for transfers between devices: 18.6 us -> 13.8 us  [bcast_a2a(): lax.all_to_all(spread, axis, 0, 0, tiled=True)]
    all_to_all x3 -> x2, starting transfers between devices: 14.1 us -> 10.8 us  [bcast_a2a(): lax.all_to_all(spread, axis, 0, 0, tiled=True)]
  transfers between devices with their start and end apart: 5 -> 4, of which waited for: 5 -> 4; matrix products, arithmetic and copies ran while one was open for 2% -> 2% of each run, Pallas kernels for 0% -> 0%
where the time goes in v4:
time: 157 us; the launch traced here: 156 us
  blocking collectives  36.9 us (24%)
  waiting for transfers between devices  31.4 us (20%)
  matrix products  25.4 us (16%)
  other arithmetic  22.2 us (14%)
  local copies, waits for them, and re-layouts  21.7 us (14%)
  starting transfers between devices  17.6 us (11%)
    all_to_all x1, blocking collectives, per_device(): lax.all_to_all(reduce_in, 'tp', 0, 0, tiled=True).astype(jnp.float32)  23.4 us
    all_to_all x2, waiting for transfers between devices, bcast_a2a(): lax.all_to_all(spread, axis, 0, 0, tiled=True)  13.8 us
    all_to_all x1, blocking collectives, per_device(): received = lax.all_to_all(dispatch, 'req', 0, 0, tiled=True)  13.5 us
    unnamed x29, local copies, waits for them, and re-layouts  13.2 us
    all_to_all x2, starting transfers between devices, bcast_a2a(): lax.all_to_all(spread, axis, 0, 0, tiled=True)  10.8 us
    all_to_all x2, other arithmetic, per_device(): lax.all_to_all(reduce_in, 'tp', 0, 0, tiled=True).astype(jnp.float32)  9.7 us
    all_to_all x1, waiting for transfers between devices, per_device(): back = lax.all_to_all(back_in, 'req', 0, 0, tiled=True)  9.34 us
    all_to_all x1, waiting for transfers between devices, per_device(): lax.all_to_all(packed, 'req', 0, 0, tiled=True)  8.27 us
  transfers between devices with their start and end apart: 4, of which 4 were waited for; matrix products, arithmetic and copies ran while one was open for 2% of the time, Pallas kernels for 0%

profile of v4, /device:TPU:0, one launch (start us, length us, event | category | flops | bytes accessed | tf_op | source)
XLA Modules:
  0.0 155.8 jit_solution(10692810095028306036)
XLA Ops:
  3.3 3.8 %fusion.30 = f32[3,4,3,512]{3,1,2,0:T(4,128)S(1)} fusion(bf16[2048,3,512]{2,0,1:T(8,128)(2,1)} %param.21, bf16[3,4,2048]{2,1,0:T(4,128)(2,1)} %param.19, f32[2048]{0:T(1024)S(1)} %convert_element_type.114, f32[3,4]{1,0:T(4,128)S(1)} %add_rsqrt_fusion.1, f32[3,512]{1,0:T(4,128)S(1)} %convert_element_type.116), kind=kOutput, calls=%fused_computation.28 | convolution fusion | flops 75614208 | bytes 6428720 | tf_op jit(solution)/shard_map/rsd,dcf->rscf/dot_general | solution.py:84
  8.1 7.3 %all-to-all-start = ((bf16[8,3,4,4,128]{4,3,2,1,0:T(4,128)(2,1)}), bf16[8,3,4,4,128]{4,3,2,1,0:T(4,128)(2,1)S(1)}, u32[]{:S(2)}, u32[]{:S(2)}) async-start(bf16[8,3,4,4,128]{4,3,2,1,0:T(4,128)(2,1)} %broadcast_in_dim.81), calls=%async_computation | async-start | bytes 196608 | tf_op jit(solution)/shard_map/all_to_all | solution.py:44
  17.2 5.3 %all-to-all-done = bf16[8,3,4,4,128]{4,3,2,1,0:T(4,128)(2,1)S(1)} async-done(((bf16[8,3,4,4,128]{4,3,2,1,0:T(4,128)(2,1)}), bf16[8,3,4,4,128]{4,3,2,1,0:T(4,128)(2,1)S(1)}, u32[]{:S(2)}, u32[]{:S(2)}) %all-to-all-start) | async-done | bytes 98336 | tf_op jit(solution)/shard_map/all_to_all | solution.py:44
  23.2 5.4 %fusion.134 = (f32[40,4,4]{1,2,0:T(4,128)S(1)}, f32[40,4,4,128]{3,1,2,0:T(4,128)S(1)}) fusion(bf16[40,4,4,128]{3,2,1,0:T(4,128)(2,1)S(1)} %gather_fusion.1, pred[40,128]{1,0:T(8,128)(4,1)S(1)} %fusion.97, bf16[40,128,512]{2,1,0:T(8,128)(2,1)} %param.24), kind=kOutput, calls=%fused_computation.184 | convolution fusion | flops 21216640 | bytes 5742080 | tf_op jit(solution)/shard_map/pshd,pkhd->pshk/dot_general | solution.py:107
  29.5 4.0 %fusion.18 = f32[40,4,4,128]{3,1,2,0:T(4,128)S(1)} fusion(f32[40,4,4,128]{3,1,2,0:T(4,128)S(1)} %get-tuple-element.31, f32[40,4,4]{1,2,0:T(4,128)S(1)} %get-tuple-element.30, pred[40,128]{1,0:T(8,128)(4,1)S(1)} %fusion.97, bf16[40,128,512]{2,1,0:T(8,128)(2,1)} %param.25), kind=kOutput, calls=%fused_computation.22 | convolution fusion | flops 21217280 | bytes 5905920 | tf_op jit(solution)/shard_map/pshk,pkhd->pshd/dot_general | solution.py:115
  35.7 3.4 %all-to-all-start.1 = ((f32[24,17,128]{2,1,0:T(8,128)}), f32[24,17,128]{2,1,0:T(8,128)S(1)}, u32[]{:S(2)}, u32[]{:S(2)}) async-start(f32[24,17,128]{2,1,0:T(8,128)} %pad_maximum_fusion), calls=%async_computation.1 | async-start | bytes 589824 | tf_op jit(solution)/shard_map/all_to_all | solution.py:139
  39.4 8.3 %all-to-all-done.1 = f32[24,17,128]{2,1,0:T(8,128)S(1)} async-done(((f32[24,17,128]{2,1,0:T(8,128)}), f32[24,17,128]{2,1,0:T(8,128)S(1)}, u32[]{:S(2)}, u32[]{:S(2)}) %all-to-all-start.1) | async-done | bytes 208928 | tf_op jit(solution)/shard_map/all_to_all | solution.py:139
  50.0 3.5 %all-to-all-start.2 = ((f32[4,12,2048]{2,1,0:T(8,128)}), f32[4,12,2048]{2,1,0:T(8,128)S(1)}, u32[]{:S(2)}, u32[]{:S(2)}) async-start(f32[4,12,2048]{2,1,0:T(8,128)} %broadcast_in_dim.92), calls=%async_computation.2 | async-start | bytes 1048576 | tf_op jit(solution)/shard_map/all_to_all | solution.py:44
  53.8 8.5 %all-to-all-done.2 = f32[4,12,2048]{2,1,0:T(8,128)S(1)} async-done(((f32[4,12,2048]{2,1,0:T(8,128)}), f32[4,12,2048]{2,1,0:T(8,128)S(1)}, u32[]{:S(2)}, u32[]{:S(2)}) %all-to-all-start.2) | async-done | bytes 393248 | tf_op jit(solution)/shard_map/all_to_all | solution.py:44
  64.9 13.5 %all_to_all.48 = bf16[8,2,9216]{2,1,0:T(2,128)(2,1)S(1)} all-to-all(bf16[8,2,9216]{2,1,0:T(2,128)(2,1)S(1)} %reshape.410), channel_id=1, replica_groups=mesh['req'=8,'tp'=4] {'req'}, dimensions={0} | all-to-all | bytes 589824 | tf_op jit(solution)/shard_map/all_to_all | solution.py:212
  79.2 1.9 %fusion.13 = f32[48,352]{1,0:T(8,128)S(1)} fusion(bf16[48,2048]{1,0:T(8,128)(2,1)S(1)} %reshape.374, bf16[1,2048,352]{1,2,0:T(8,128)(2,1)} %param.31), kind=kOutput, calls=%fused_computation.19 | convolution fusion | flops 69206016 | bytes 1705984 | tf_op jit(solution)/shard_map/dot_general | solution.py:216
  81.2 2.9 %convert_bitcast_fusion = (bf16[1,4,48,512]{3,2,1,0:T(8,128)(2,1)S(1)}, bf16[1,4,48,512]{3,2,1,0:T(8,128)(2,1)S(1)}) fusion(bf16[44,4,8,512]{3,2,1,0:T(8,128)(2,1)} %bitcast.183, bf16[48,2048]{1,0:T(8,128)(2,1)S(1)} %reshape.374, bf16[1,2048,352]{1,2,0:T(8,128)(2,1)} %param.32, f32[48,352]{1,0:T(8,128)S(1)} %fusion.13), kind=kOutput, calls=%fused_computation.85 | convolution fusion | flops 138906624 | bytes 3540992 | tf_op jit(solution)/shard_map/dot_general | solution.py:219
  84.3 1.5 convolution_convert_fusion.1
  85.7 1.5 convolution_convert_fusion.2
  87.9 5.0 %maximum_bitcast_fusion = bf16[4,1,184320]{2,0,1:T(4,128)(2,1)} fusion(bf16[4,24576]{1,0:T(4,128)(2,1)S(1)} %bitcast.191, bf16[4,24576]{1,0:T(4,128)(2,1)S(1)} %bitcast.190, bf16[184320]{0:T(1024)(128)(2,1)S(1)} %pad.4.clone), kind=kLoop, calls=%fused_computation.13 | loop fusion | flops 4423680 | bytes 2236416 | tf_op jit(solution)/shard_map/all_to_all | solution.py:240
  92.8 4.7 %reduce.4 = bf16[4,184320]{1,0:T(4,128)(2,1)} reduce(bf16[4,1,184320]{2,0,1:T(4,128)(2,1)} %maximum_bitcast_fusion, bf16[]{:T(256)} %broadcast.288), dimensions={1}, to_apply=%copy.166.reduce_sub_computation | reduce | bytes 2949122 | tf_op jit(solution)/shard_map/all_to_all | solution.py:240
  97.6 4.0 %reshape.412 = bf16[4,2,92160]{2,1,0:T(2,128)(2,1)} reshape(bf16[4,184320]{1,0:T(4,128)(2,1)} %reduce.4) | data formatting | bytes 2949120
  101.6 23.4 %all_to_all.49 = bf16[4,2,92160]{2,1,0:T(2,128)(2,1)} all-to-all(bf16[4,2,92160]{2,1,0:T(2,128)(2,1)} %reshape.412), channel_id=1, replica_groups=mesh['req'=8,'tp'=4] {'tp'}, dimensions={0} | all-to-all | bytes 2949120 | tf_op jit(solution)/shard_map/all_to_all | solution.py:240
  125.0 4.4 %reshape.413 = bf16[4,1,184320]{2,1,0:T(2,128)(2,1)} reshape(bf16[4,2,92160]{2,1,0:T(2,128)(2,1)} %all_to_all.49) | data formatting | bytes 2949120
  129.4 3.7 %copy.242 = f32[4,1,184320]{2,0,1:T(4,128)S(1)} copy(bf16[4,1,184320]{2,1,0:T(2,128)(2,1)} %reshape.413) | data formatting | bytes 4423680
  133.3 5.6 %slice_reduce_fusion = f32[135168]{0:T(1024)S(1)} fusion(f32[4,184320]{1,0:T(4,128)S(1)} %bitcast.182), kind=kLoop, calls=%fused_computation.12 | loop fusion | flops 405504 | bytes 2703360 | tf_op jit(solution)/shard_map/reduce_sum | solution.py:245
  139.1 1.4 fusion.73
  141.5 3.4 %all-to-all-start.5 = ((f32[8,1,9216]{2,1,0:T(1,128)}), f32[8,1,9216]{2,1,0:T(1,128)S(1)}, u32[]{:S(2)}, u32[]{:S(2)}) async-start(f32[8,1,9216]{2,1,0:T(1,128)} %all_to_all.39), calls=%async_computation.5 | async-start | bytes 589824 | tf_op jit(solution)/shard_map/all_to_all | solution.py:258
  145.5 9.3 %all-to-all-done.5 = f32[8,1,9216]{2,1,0:T(1,128)S(1)} async-done(((f32[8,1,9216]{2,1,0:T(1,128)}), f32[8,1,9216]{2,1,0:T(1,128)S(1)}, u32[]{:S(2)}, u32[]{:S(2)}) %all-to-all-start.5) | async-done | bytes 294944 | tf_op jit(solution)/shard_map/all_to_all | solution.py:258
  (123 shorter events, 19.5 us)
Async XLA Ops:
  0.0 48.8 %copy-start = (bf16[512,2048]{1,0:T(8,128)(2,1)S(1)}, bf16[512,2048]{1,0:T(8,128)(2,1)}, u32[]{:S(2)}) copy-start(bf16[512,2048]{1,0:T(8,128)(2,1)} %param.23) | copy-start | bytes 6291460
  3.3 12.1 %copy-start.4 = (s32[3,4,4]{2,1,0:T(4,128)S(1)}, s32[3,4,4]{2,1,0:T(4,128)}, u32[]{:S(2)}) copy-start(s32[3,4,4]{2,1,0:T(4,128)} %param.29) | copy-start | bytes 580
  3.3 12.2 %copy-start.3 = (s32[24,37]{1,0:T(8,128)S(1)}, s32[24,37]{1,0:T(8,128)}, u32[]{:S(2)}) copy-start(s32[24,37]{1,0:T(8,128)} %param.26) | copy-start | bytes 10660
  3.3 12.6 %copy-start.1 = (s32[24]{0:T(128)S(1)}, s32[24]{0:T(128)}, u32[]{:S(2)}) copy-start(s32[24]{0:T(128)} %param.27) | copy-start | bytes 292
  8.1 14.4 %all-to-all-start = ((bf16[8,3,4,4,128]{4,3,2,1,0:T(4,128)(2,1)}), bf16[8,3,4,4,128]{4,3,2,1,0:T(4,128)(2,1)S(1)}, u32[]{:S(2)}, u32[]{:S(2)}) async-start(bf16[8,3,4,4,128]{4,3,2,1,0:T(4,128)(2,1)} %broadcast_in_dim.81), calls=%async_computation | async-start | bytes 196608 | tf_op jit(solution)/shard_map/all_to_all | solution.py:44
  35.7 12.0 %all-to-all-start.1 = ((f32[24,17,128]{2,1,0:T(8,128)}), f32[24,17,128]{2,1,0:T(8,128)S(1)}, u32[]{:S(2)}, u32[]{:S(2)}) async-start(f32[24,17,128]{2,1,0:T(8,128)} %pad_maximum_fusion), calls=%async_computation.1 | async-start | bytes 589824 | tf_op jit(solution)/shard_map/all_to_all | solution.py:139
  39.1 14.4 %copy-start.2 = (bf16[3,4,2048]{2,1,0:T(4,128)(2,1)S(1)}, bf16[3,4,2048]{2,1,0:T(4,128)(2,1)}, u32[]{:S(2)}) copy-start(bf16[3,4,2048]{2,1,0:T(4,128)(2,1)} %param.19) | copy-start | bytes 147460
  39.3 14.2 %copy-start.6 = (bf16[2048]{0:T(1024)(128)(2,1)S(1)}, bf16[2048]{0:T(1024)(128)(2,1)}, u32[]{:S(2)}) copy-start(bf16[2048]{0:T(1024)(128)(2,1)} %param.28) | copy-start | bytes 12292
  50.0 12.3 %all-to-all-start.2 = ((f32[4,12,2048]{2,1,0:T(8,128)}), f32[4,12,2048]{2,1,0:T(8,128)S(1)}, u32[]{:S(2)}, u32[]{:S(2)}) async-start(f32[4,12,2048]{2,1,0:T(8,128)} %broadcast_in_dim.92), calls=%async_computation.2 | async-start | bytes 1048576 | tf_op jit(solution)/shard_map/all_to_all | solution.py:44
  138.9 6.1 %copy-start.5 = (f32[3,4,4]{2,1,0:T(4,128)S(1)}, f32[3,4,4]{2,1,0:T(4,128)}, u32[]{:S(2)}) copy-start(f32[3,4,4]{2,1,0:T(4,128)} %param.30) | copy-start | bytes 580
  138.9 6.1 %copy-start.7 = (bf16[2048]{0:T(1024)(128)(2,1)S(1)}, bf16[2048]{0:T(1024)(128)(2,1)}, u32[]{:S(2)}) copy-start(bf16[2048]{0:T(1024)(128)(2,1)} %param.37) | copy-start | bytes 12292
  141.5 13.3 %all-to-all-start.5 = ((f32[8,1,9216]{2,1,0:T(1,128)}), f32[8,1,9216]{2,1,0:T(1,128)S(1)}, u32[]{:S(2)}, u32[]{:S(2)}) async-start(f32[8,1,9216]{2,1,0:T(1,128)} %all_to_all.39), calls=%async_computation.5 | async-start | bytes 589824 | tf_op jit(solution)/shard_map/all_to_all | solution.py:258

commit v5 on v3

--- a/solution.py
+++ b/solution.py
@@ -81,16 +81,23 @@
     col_share = model_width // tp_count
     row_count = req_rows * step_count
     normed = rms_norm(tokens_in, attn_norm)
-    projected = jnp.einsum(
-        "rsd,dcf->rscf", normed, qkv_weight, preferred_element_type=jnp.float32
-    ) + qkv_bias.astype(jnp.float32)
     own_lengths = lax.dynamic_slice_in_dim(cache_lengths, req_index * req_rows, req_rows)
     positions = own_lengths[:, None] + jnp.arange(step_count, dtype=jnp.int32)[None, :]
     head_shape = (req_rows, step_count, local_heads, HD)
-    query_new = rotate(projected[:, :, 0].reshape(head_shape), positions).astype(jnp.bfloat16)
-    key_new = rotate(projected[:, :, 1].reshape(head_shape), positions).astype(jnp.bfloat16)
-    value_new = projected[:, :, 2].reshape(head_shape).astype(jnp.bfloat16)
-    query_all = bcast_a2a(query_new, "req", req_count)
+
+    def project(part, rows):
+        return jnp.einsum(
+            "rsd,df->rsf", rows, qkv_weight[:, part], preferred_element_type=jnp.float32
+        ) + qkv_bias[part].astype(jnp.float32)
+
+    query_new = rotate(project(0, normed).reshape(head_shape), positions).astype(jnp.bfloat16)
+    query_spread = jnp.broadcast_to(query_new[None], (req_count,) + query_new.shape)
+    normed_late, query_spread = lax.optimization_barrier((normed, query_spread))
+    query_all = lax.all_to_all(query_spread, "req", 0, 0, tiled=True).reshape(
+        (req_count * req_rows,) + query_new.shape[1:]
+    )
+    key_new = rotate(project(1, normed_late).reshape(head_shape), positions).astype(jnp.bfloat16)
+    value_new = project(2, normed_late).reshape(head_shape).astype(jnp.bfloat16)
     slot_ids = req_index * pool_here + jnp.arange(pool_here, dtype=jnp.int32)
     matches = (page_table[:, :, None] == slot_ids[None, None, :]).astype(jnp.int32)
     request_ids = jnp.arange(all_requests, dtype=jnp.int32)

time: 134 us -> 134 us (level)
  waiting for transfers between devices: 35.7 us -> 33.6 us
    all_to_all x3 -> x2, starting transfers between devices: 14.1 us -> 6.8 us  [bcast_a2a(): lax.all_to_all(spread, axis, 0, 0, tiled=True)]
    all_to_all x0 -> x1, starting transfers between devices: none -> 7.29 us  [per_device(): lax.all_to_all(query_spread, 'req', 0, 0, tiled=True)]
    all_to_all x3 -> x2, waiting for transfers between devices: 18.6 us -> 13.2 us  [bcast_a2a(): lax.all_to_all(spread, axis, 0, 0, tiled=True)]
    all_to_all x0 -> x1, waiting for transfers between devices: none -> 3.25 us  [per_device(): lax.all_to_all(query_spread, 'req', 0, 0, tiled=True)]
    dot_general x1, matrix products: 0.21 us -> 2.16 us  [per_device(): jnp.einsum('rsht,rthd->rshd', new_weights.astype(jnp.bfloat16), value_new...]
    dot_general x1 -> x2, matrix products: 3.81 us -> 3.97 us  [project(): jnp.einsum('rsd,df->rsf', rows, qkv_weight[:, part], preferred_element_ty...]
  transfers between devices with their start and end apart: 5 -> 5, of which waited for: 5 -> 5; matrix products, arithmetic and copies ran while one was open for 2% -> 4% of each run, Pallas kernels for 0% -> 0%
where the time goes in v5:
time: 134 us; the launch traced here: 133 us
  waiting for transfers between devices  33.6 us (25%)
  blocking collectives  29.1 us (22%)
  matrix products  26.7 us (20%)
  starting transfers between devices  20.9 us (16%)
  local copies, waits for them, and re-layouts  11.5 us (9%)
  other arithmetic  10.5 us (8%)
    all_to_all x1, blocking collectives, per_device(): lax.all_to_all(reduce_in, 'tp', 0, 0, tiled=True)  15.6 us
    all_to_all x1, blocking collectives, per_device(): received = lax.all_to_all(dispatch, 'req', 0, 0, tiled=True)  13.5 us
    all_to_all x2, waiting for transfers between devices, bcast_a2a(): lax.all_to_all(spread, axis, 0, 0, tiled=True)  13.2 us
    all_to_all x1, waiting for transfers between devices, per_device(): back = lax.all_to_all(back_in, 'req', 0, 0, tiled=True)  8.87 us
    all_to_all x1, waiting for transfers between devices, per_device(): lax.all_to_all(packed, 'req', 0, 0, tiled=True)  8.28 us
    all_to_all x1, starting transfers between devices, per_device(): lax.all_to_all(query_spread, 'req', 0, 0, tiled=True)  7.29 us
    all_to_all x2, starting transfers between devices, bcast_a2a(): lax.all_to_all(spread, axis, 0, 0, tiled=True)  6.8 us
    dot_general x1, matrix products, per_device(): jnp.einsum('pshd,pkhd->pshk', page_queries, page_keys, preferred_element_...  5.41 us
  transfers between devices with their start and end apart: 5, of which 5 were waited for; matrix products, arithmetic and copies ran while one was open for 4% of the time, Pallas kernels for 0%

profile of v5, /device:TPU:0, one launch (start us, length us, event | category | flops | bytes accessed | tf_op | source)
XLA Modules:
  0.0 133.0 jit_solution(11326077718467471588)
XLA Ops:
  1.0 0.9 multiply_reduce_fusion.1
  4.4 2.0 %fusion.45 = f32[3,4,4,128]{3,1,2,0:T(4,128)S(1)} fusion(bf16[3,4,2048]{2,1,0:T(4,128)(2,1)S(1)} %multiply_convert_fusion.1, bf16[2048,3,512]{2,0,1:T(8,128)(2,1)} %param.21, f32[512]{0:T(512)S(1)} %bitcast.210), kind=kOutput, calls=%fused_computation.35 | convolution fusion | flops 25171968 | bytes 2172928 | tf_op jit(solution)/shard_map/rsd,df->rsf/dot_general | solution.py:89
  7.3 7.3 %all-to-all-start = ((bf16[8,3,4,4,128]{4,3,2,1,0:T(4,128)(2,1)}), bf16[8,3,4,4,128]{4,3,2,1,0:T(4,128)(2,1)S(1)}, u32[]{:S(2)}, u32[]{:S(2)}) async-start(bf16[8,3,4,4,128]{4,3,2,1,0:T(4,128)(2,1)} %broadcast_in_dim.81), calls=%async_computation | async-start | bytes 196608 | tf_op jit(solution)/shard_map/all_to_all | solution.py:96
  16.1 2.0 %fusion.51 = f32[3,4,4,128]{3,1,2,0:T(4,128)S(1)} fusion(bf16[3,4,2048]{2,1,0:T(4,128)(2,1)S(1)} %multiply_convert_fusion.1, bf16[2048,3,512]{2,0,1:T(8,128)(2,1)} %param.21, f32[512]{0:T(512)S(1)} %bitcast.209), kind=kOutput, calls=%fused_computation.37 | convolution fusion | flops 25171968 | bytes 2172928 | tf_op jit(solution)/shard_map/rsd,df->rsf/dot_general | solution.py:89
  18.4 3.3 %all-to-all-done = bf16[8,3,4,4,128]{4,3,2,1,0:T(4,128)(2,1)S(1)} async-done(((bf16[8,3,4,4,128]{4,3,2,1,0:T(4,128)(2,1)}), bf16[8,3,4,4,128]{4,3,2,1,0:T(4,128)(2,1)S(1)}, u32[]{:S(2)}, u32[]{:S(2)}) %all-to-all-start) | async-done | bytes 98336 | tf_op jit(solution)/shard_map/all_to_all | solution.py:96
  22.4 5.4 %fusion.151 = (f32[40,4,4]{1,2,0:T(4,128)S(1)}, f32[40,4,4,128]{3,1,2,0:T(4,128)S(1)}) fusion(bf16[40,4,4,128]{3,2,1,0:T(4,128)(2,1)S(1)} %gather_fusion.1, pred[40,128]{1,0:T(8,128)(4,1)S(1)} %fusion.116, bf16[40,128,512]{2,1,0:T(8,128)(2,1)} %param.24), kind=kOutput, calls=%fused_computation.183 | convolution fusion | flops 21216640 | bytes 5742080 | tf_op jit(solution)/shard_map/pshd,pkhd->pshk/dot_general | solution.py:114
  28.6 4.0 %fusion.25 = f32[40,4,4,128]{3,1,2,0:T(4,128)S(1)} fusion(f32[40,4,4,128]{3,1,2,0:T(4,128)S(1)} %get-tuple-element.32, f32[40,4,4]{1,2,0:T(4,128)S(1)} %get-tuple-element.31, pred[40,128]{1,0:T(8,128)(4,1)S(1)} %fusion.116, bf16[40,128,512]{2,1,0:T(8,128)(2,1)} %param.25), kind=kOutput, calls=%fused_computation.26 | convolution fusion | flops 21217280 | bytes 5905920 | tf_op jit(solution)/shard_map/pshk,pkhd->pshd/dot_general | solution.py:122
  34.8 3.4 %all-to-all-start.1 = ((f32[24,17,128]{2,1,0:T(8,128)}), f32[24,17,128]{2,1,0:T(8,128)S(1)}, u32[]{:S(2)}, u32[]{:S(2)}) async-start(f32[24,17,128]{2,1,0:T(8,128)} %pad_maximum_fusion.2), calls=%async_computation.1 | async-start | bytes 589824 | tf_op jit(solution)/shard_map/all_to_all | solution.py:146
  38.5 8.3 %all-to-all-done.1 = f32[24,17,128]{2,1,0:T(8,128)S(1)} async-done(((f32[24,17,128]{2,1,0:T(8,128)}), f32[24,17,128]{2,1,0:T(8,128)S(1)}, u32[]{:S(2)}, u32[]{:S(2)}) %all-to-all-start.1) | async-done | bytes 208928 | tf_op jit(solution)/shard_map/all_to_all | solution.py:146
  47.7 2.2 %fusion.62 = bf16[3,4,4,128]{3,1,2,0:T(4,128)(2,1)S(1)} fusion(bf16[3,4,2048]{2,1,0:T(4,128)(2,1)S(1)} %multiply_convert_fusion.1, bf16[2048,3,512]{2,0,1:T(8,128)(2,1)} %param.21, f32[3,4,4,128]{3,0,2,1:T(4,128)S(1)} %bitcast.208, f32[3,4,4,4]{1,3,2,0:T(4,128)S(1)} %get-tuple-element.34, f32[3,4,4]{1,2,0:T(4,128)S(1)} %get-tuple-element.14, ...), kind=kOutput, calls=%fused_computation.46 | convolution fusion | flops 25258560 | bytes 2186768 | tf_op jit(solution)/shard_map/rsht,rthd->rshd/dot_general | solution.py:169
  51.1 3.5 %all-to-all-start.2 = ((f32[4,12,2048]{2,1,0:T(8,128)}), f32[4,12,2048]{2,1,0:T(8,128)S(1)}, u32[]{:S(2)}, u32[]{:S(2)}) async-start(f32[4,12,2048]{2,1,0:T(8,128)} %broadcast_in_dim.92), calls=%async_computation.2 | async-start | bytes 1048576 | tf_op jit(solution)/shard_map/all_to_all | solution.py:44
  54.9 8.5 %all-to-all-done.2 = f32[4,12,2048]{2,1,0:T(8,128)S(1)} async-done(((f32[4,12,2048]{2,1,0:T(8,128)}), f32[4,12,2048]{2,1,0:T(8,128)S(1)}, u32[]{:S(2)}, u32[]{:S(2)}) %all-to-all-start.2) | async-done | bytes 393248 | tf_op jit(solution)/shard_map/all_to_all | solution.py:44
  66.7 13.5 %all_to_all.53 = bf16[8,2,9216]{2,1,0:T(2,128)(2,1)S(1)} all-to-all(bf16[8,2,9216]{2,1,0:T(2,128)(2,1)S(1)} %reshape.453), channel_id=1, replica_groups=mesh['req'=8,'tp'=4] {'req'}, dimensions={0} | all-to-all | bytes 589824 | tf_op jit(solution)/shard_map/all_to_all | solution.py:219
  81.0 2.5 %fusion.20 = f32[48,352]{1,0:T(8,128)} fusion(bf16[48,2048]{1,0:T(8,128)(2,1)S(1)} %reshape.410, bf16[1,2048,352]{1,2,0:T(8,128)(2,1)} %param.31), kind=kOutput, calls=%fused_computation.23 | convolution fusion | flops 69206016 | bytes 1705984 | tf_op jit(solution)/shard_map/dot_general | solution.py:223
  83.6 3.0 %fusion.22 = f32[1,4,48,512]{3,2,1,0:T(8,128)S(1)} fusion(bf16[44,4,8,512]{3,2,1,0:T(8,128)(2,1)} %bitcast.192, bf16[48,2048]{1,0:T(8,128)(2,1)S(1)} %reshape.410, bf16[1,2048,352]{1,2,0:T(8,128)(2,1)} %param.32, f32[48,352]{1,0:T(8,128)} %fusion.20), kind=kOutput, calls=%fused_computation.25 | convolution fusion | flops 138513408 | bytes 3540992 | tf_op jit(solution)/shard_map/dot_general | solution.py:226
  86.6 1.0 copy.182
  88.7 1.2 pad_maximum_fusion
  90.6 15.6 %all_to_all.54 = f32[4,1,58368]{2,1,0:T(1,128)S(1)} all-to-all(f32[4,1,58368]{2,1,0:T(1,128)S(1)} %all_to_all.40), channel_id=1, replica_groups=mesh['req'=8,'tp'=4] {'tp'}, dimensions={0} | all-to-all | bytes 1867776 | tf_op jit(solution)/shard_map/all_to_all | solution.py:240
  107.9 3.3 %all-to-all-start.5 = ((bf16[4,24,704]{2,1,0:T(8,128)(2,1)}), bf16[4,24,704]{2,1,0:T(8,128)(2,1)S(1)}, u32[]{:S(2)}, u32[]{:S(2)}) async-start(bf16[4,24,704]{2,1,0:T(8,128)(2,1)} %broadcast_in_dim.95), calls=%async_computation.5 | async-start | bytes 294912 | tf_op jit(solution)/shard_map/all_to_all | solution.py:44
  111.3 4.7 %all-to-all-done.5 = bf16[4,24,704]{2,1,0:T(8,128)(2,1)S(1)} async-done(((bf16[4,24,704]{2,1,0:T(8,128)(2,1)}), bf16[4,24,704]{2,1,0:T(8,128)(2,1)S(1)}, u32[]{:S(2)}, u32[]{:S(2)}) %all-to-all-start.5) | async-done | bytes 135200 | tf_op jit(solution)/shard_map/all_to_all | solution.py:44
  116.0 1.4 %fusion.156 = f32[96,512]{1,0:T(8,128)S(1)} fusion(bf16[96,704]{1,0:T(8,128)(2,1)S(1)} %bitcast.201, bf16[704,512]{1,0:T(8,128)(2,1)} %param.36), kind=kOutput, calls=%fused_computation.188 | convolution fusion | flops 69206016 | bytes 1052672 | tf_op jit(solution)/shard_map/dot_general | solution.py:247
  118.4 3.4 %all-to-all-start.6 = ((f32[8,1,9216]{2,1,0:T(1,128)}), f32[8,1,9216]{2,1,0:T(1,128)S(1)}, u32[]{:S(2)}, u32[]{:S(2)}) async-start(f32[8,1,9216]{2,1,0:T(1,128)} %all_to_all.43), calls=%async_computation.6 | async-start | bytes 589824 | tf_op jit(solution)/shard_map/all_to_all | solution.py:256
  122.4 8.9 %all-to-all-done.6 = f32[8,1,9216]{2,1,0:T(1,128)S(1)} async-done(((f32[8,1,9216]{2,1,0:T(1,128)}), f32[8,1,9216]{2,1,0:T(1,128)S(1)}, u32[]{:S(2)}, u32[]{:S(2)}) %all-to-all-start.6) | async-done | bytes 294944 | tf_op jit(solution)/shard_map/all_to_all | solution.py:256
  131.4 0.9 fusion.41
  (133 shorter events, 22.2 us)
Async XLA Ops:
  0.0 49.9 %copy-start = (bf16[512,2048]{1,0:T(8,128)(2,1)S(1)}, bf16[512,2048]{1,0:T(8,128)(2,1)}, u32[]{:S(2)}) copy-start(bf16[512,2048]{1,0:T(8,128)(2,1)} %param.23) | copy-start | bytes 6291460
  0.0 15.0 %copy-start.1 = (s32[24]{0:T(128)S(1)}, s32[24]{0:T(128)}, u32[]{:S(2)}) copy-start(s32[24]{0:T(128)} %param.27) | copy-start | bytes 292
  0.0 14.5 %copy-start.8 = (s32[3,4,4]{2,1,0:T(4,128)S(1)}, s32[3,4,4]{2,1,0:T(4,128)}, u32[]{:S(2)}) copy-start(s32[3,4,4]{2,1,0:T(4,128)} %param.29) | copy-start | bytes 580
  0.0 14.6 %copy-start.7 = (s32[24,37]{1,0:T(8,128)S(1)}, s32[24,37]{1,0:T(8,128)}, u32[]{:S(2)}) copy-start(s32[24,37]{1,0:T(8,128)} %param.26) | copy-start | bytes 10660
  7.3 14.4 %all-to-all-start = ((bf16[8,3,4,4,128]{4,3,2,1,0:T(4,128)(2,1)}), bf16[8,3,4,4,128]{4,3,2,1,0:T(4,128)(2,1)S(1)}, u32[]{:S(2)}, u32[]{:S(2)}) async-start(bf16[8,3,4,4,128]{4,3,2,1,0:T(4,128)(2,1)} %broadcast_in_dim.81), calls=%async_computation | async-start | bytes 196608 | tf_op jit(solution)/shard_map/all_to_all | solution.py:96
  34.8 12.0 %all-to-all-start.1 = ((f32[24,17,128]{2,1,0:T(8,128)}), f32[24,17,128]{2,1,0:T(8,128)S(1)}, u32[]{:S(2)}, u32[]{:S(2)}) async-start(f32[24,17,128]{2,1,0:T(8,128)} %pad_maximum_fusion.2), calls=%async_computation.1 | async-start | bytes 589824 | tf_op jit(solution)/shard_map/all_to_all | solution.py:146
  49.9 4.8 %copy-start.2 = (bf16[3,4,2048]{2,1,0:T(4,128)(2,1)S(1)}, bf16[3,4,2048]{2,1,0:T(4,128)(2,1)}, u32[]{:S(2)}) copy-start(bf16[3,4,2048]{2,1,0:T(4,128)(2,1)} %param.19) | copy-start | bytes 147460
  49.9 4.8 %copy-start.10 = (bf16[2048]{0:T(1024)(128)(2,1)S(1)}, bf16[2048]{0:T(1024)(128)(2,1)}, u32[]{:S(2)}) copy-start(bf16[2048]{0:T(1024)(128)(2,1)} %param.28) | copy-start | bytes 12292
  51.1 12.3 %all-to-all-start.2 = ((f32[4,12,2048]{2,1,0:T(8,128)}), f32[4,12,2048]{2,1,0:T(8,128)S(1)}, u32[]{:S(2)}, u32[]{:S(2)}) async-start(f32[4,12,2048]{2,1,0:T(8,128)} %broadcast_in_dim.92), calls=%async_computation.2 | async-start | bytes 1048576 | tf_op jit(solution)/shard_map/all_to_all | solution.py:44
  64.4 0.6 copy-start.5
  83.6 4.0 %copy-start.3 = (bf16[512,704]{0,1:T(8,128)(2,1)S(1)}, bf16[512,704]{0,1:T(8,128)(2,1)}, u32[]{:S(2)}) copy-start(bf16[512,704]{0,1:T(8,128)(2,1)} %param.35) | copy-start | bytes 2162692
  86.6 1.4 %copy-start.4 = (bf16[512,704]{0,1:T(8,128)(2,1)S(1)}, bf16[512,704]{0,1:T(8,128)(2,1)}, u32[]{:S(2)}) copy-start(bf16[512,704]{0,1:T(8,128)(2,1)} %param.34) | copy-start | bytes 2162692
  107.1 14.7 %copy-start.9 = (f32[3,4,4]{2,1,0:T(4,128)S(1)}, f32[3,4,4]{2,1,0:T(4,128)}, u32[]{:S(2)}) copy-start(f32[3,4,4]{2,1,0:T(4,128)} %param.30) | copy-start | bytes 580
  107.1 14.8 %copy-start.11 = (bf16[2048]{0:T(1024)(128)(2,1)S(1)}, bf16[2048]{0:T(1024)(128)(2,1)}, u32[]{:S(2)}) copy-start(bf16[2048]{0:T(1024)(128)(2,1)} %param.37) | copy-start | bytes 12292
  107.2 15.0 %copy-start.6 = (bf16[12,2048]{1,0:T(8,128)(2,1)S(1)}, bf16[12,2048]{1,0:T(8,128)(2,1)}, u32[]{:S(2)}) copy-start(bf16[12,2048]{1,0:T(8,128)(2,1)} %copy-done.5) | copy-start | bytes 147460
  107.9 8.1 %all-to-all-start.5 = ((bf16[4,24,704]{2,1,0:T(8,128)(2,1)}), bf16[4,24,704]{2,1,0:T(8,128)(2,1)S(1)}, u32[]{:S(2)}, u32[]{:S(2)}) async-start(bf16[4,24,704]{2,1,0:T(8,128)(2,1)} %broadcast_in_dim.95), calls=%async_computation.5 | async-start | bytes 294912 | tf_op jit(solution)/shard_map/all_to_all | solution.py:44
  118.4 12.8 %all-to-all-start.6 = ((f32[8,1,9216]{2,1,0:T(1,128)}), f32[8,1,9216]{2,1,0:T(1,128)S(1)}, u32[]{:S(2)}, u32[]{:S(2)}) async-start(f32[8,1,9216]{2,1,0:T(1,128)} %all_to_all.43), calls=%async_computation.6 | async-start | bytes 589824 | tf_op jit(solution)/shard_map/all_to_all | solution.py:256

commit v6 on v5

--- a/solution.py
+++ b/solution.py
@@ -37,6 +37,25 @@
         ],
         axis=-1,
     )
+
+
+def shift_exchange(chunks, axis, count, spread=False):
+    me = lax.axis_index(axis)
+    pieces = [chunks if spread else lax.dynamic_index_in_dim(chunks, me, 0, keepdims=False)]
+    for shift in range(1, count):
+        send = chunks if spread else lax.dynamic_index_in_dim(
+            chunks, (me + shift) % count, 0, keepdims=False
+        )
+        pairs = [(source, (source + shift) % count) for source in range(count)]
+        pieces.append(lax.ppermute(send, axis, pairs))
+    return pieces
+
+
+def by_source(pieces, axis, count):
+    me = lax.axis_index(axis)
+    stacked = jnp.stack(pieces)
+    order = (me - jnp.arange(count, dtype=jnp.int32)) % count
+    return jnp.take(stacked, order, axis=0)
 
 
 def bcast_a2a(values, axis, count):
@@ -180,7 +199,9 @@
     )[..., None]
     attended = attended.astype(jnp.bfloat16).reshape(row_count, head_width)
     attn_part = jnp.dot(attended, out_weight, preferred_element_type=jnp.float32)
-    attn_full = jnp.sum(bcast_a2a(attn_part, "tp", tp_count).reshape(tp_count, row_count, model_width), axis=0)
+    attn_full = jnp.sum(
+        by_source(shift_exchange(attn_part, "tp", tp_count, spread=True), "tp", tp_count), axis=0
+    )
     resid = tokens_in.reshape(row_count, model_width).astype(jnp.float32) + attn_full
     mixed = rms_norm(resid, mlp_norm)
     expert_count = req_count * expert_w_gate.shape[0]
@@ -237,13 +258,15 @@
     reduce_in = jnp.concatenate(
         [partial_split.reshape(tp_count, expert_rows * col_share), shared_pre], axis=1
     )
-    reduce_out = jnp.sum(lax.all_to_all(reduce_in, "tp", 0, 0, tiled=True), axis=0)
+    reduce_out = sum(shift_exchange(reduce_in, "tp", tp_count))
     expert_sum = reduce_out[: expert_rows * col_share].reshape(expert_rows, col_share)
     shared_sum = reduce_out[expert_rows * col_share :].reshape(share_rows, 2 * unit_count)
     shared_hidden = (jax.nn.silu(shared_sum[:, :unit_count]) * shared_sum[:, unit_count:]).astype(
         jnp.bfloat16
     )
-    hidden_all = bcast_a2a(shared_hidden, "tp", tp_count).reshape(all_rows, unit_count)
+    hidden_all = by_source(
+        shift_exchange(shared_hidden, "tp", tp_count, spread=True), "tp", tp_count
+    ).reshape(all_rows, unit_count)
     shared_down = jnp.dot(hidden_all, shared_w_down, preferred_element_type=jnp.float32)
     ey = expert_sum.astype(jnp.bfloat16).astype(jnp.float32)
     back_in = jnp.concatenate(

time: 134 us -> 125 us (0.933)
  blocking collectives: 29.1 us -> 0 us
  waiting for transfers between devices: 33.6 us -> 49.9 us
  local copies, waits for them, and re-layouts: 11.5 us -> 14.5 us
  starting transfers between devices: 20.9 us -> 23.6 us
    all_to_all x2 -> x0, blocking collectives: 29.1 us -> none  [the longest x1 15.6 us: per_device(): lax.all_to_all(reduce_in, 'tp', 0, 0, tiled=True)]
    ppermute x0 -> x9, waiting for transfers between devices: none -> 20 us  [shift_exchange(): pieces.append(lax.ppermute(send, axis, pairs))]
    ppermute x0 -> x9, starting transfers between devices: none -> 5.72 us  [shift_exchange(): pieces.append(lax.ppermute(send, axis, pairs))]
    all_to_all x2 -> x1, waiting for transfers between devices: 13.2 us -> 8.32 us  [per_device(): received = lax.all_to_all(dispatch, 'req', 0, 0, tiled=True)]
    all_to_all x2 -> x1, starting transfers between devices: 6.8 us -> 3.6 us  [per_device(): received = lax.all_to_all(dispatch, 'req', 0, 0, tiled=True)]
    unnamed x33 -> x36, local copies, waits for them, and re-layouts: 1.95 us -> 4.17 us
    dynamic_slice x0 -> x1, local copies, waits for them, and re-layouts: none -> 1.5 us  [shift_exchange(): lax.dynamic_index_in_dim(chunks, (me + shift) % count, 0, keepdims=False)]
    all_to_all x1, waiting for transfers between devices: 8.87 us -> 10.3 us  [per_device(): back = lax.all_to_all(back_in, 'req', 0, 0, tiled=True)]
  transfers between devices with their start and end apart: 5 -> 13, of which waited for: 5 -> 11; matrix products, arithmetic and copies ran while one was open for 4% -> 4% of each run, Pallas kernels for 0% -> 0%
where the time goes in v6:
time: 125 us; the launch traced here: 124 us
  waiting for transfers between devices  49.9 us (40%)
  matrix products  25.6 us (20%)
  starting transfers between devices  23.6 us (19%)
  local copies, waits for them, and re-layouts  14.5 us (12%)
  other arithmetic  9.96 us (8%)
    ppermute x9, waiting for transfers between devices, shift_exchange(): pieces.append(lax.ppermute(send, axis, pairs))  20 us
    all_to_all x1, waiting for transfers between devices, per_device(): back = lax.all_to_all(back_in, 'req', 0, 0, tiled=True)  10.3 us
    all_to_all x1, waiting for transfers between devices, per_device(): lax.all_to_all(packed, 'req', 0, 0, tiled=True)  8.34 us
    all_to_all x1, waiting for transfers between devices, per_device(): received = lax.all_to_all(dispatch, 'req', 0, 0, tiled=True)  8.32 us
    all_to_all x1, starting transfers between devices, per_device(): lax.all_to_all(query_spread, 'req', 0, 0, tiled=True)  7.29 us
    ppermute x9, starting transfers between devices, shift_exchange(): pieces.append(lax.ppermute(send, axis, pairs))  5.72 us
    dot_general x1, matrix products, per_device(): jnp.einsum('pshd,pkhd->pshk', page_queries, page_keys, preferred_element_...  5.41 us
    unnamed x36, local copies, waits for them, and re-layouts  4.17 us
  transfers between devices with their start and end apart: 13, of which 11 were waited for; matrix products, arithmetic and copies ran while one was open for 4% of the time, Pallas kernels for 0%

profile of v6, /device:TPU:0, one launch (start us, length us, event | category | flops | bytes accessed | tf_op | source)
XLA Modules:
  0.0 124.3 jit_solution(4392781081797846003)
XLA Ops:
  4.4 2.0 %fusion.45 = f32[3,4,4,128]{3,1,2,0:T(4,128)S(1)} fusion(bf16[3,4,2048]{2,1,0:T(4,128)(2,1)S(1)} %multiply_convert_fusion.1, bf16[2048,3,512]{2,0,1:T(8,128)(2,1)} %param.21, f32[512]{0:T(512)S(1)} %bitcast.235), kind=kOutput, calls=%fused_computation.37 | convolution fusion | flops 25171968 | bytes 2172928 | tf_op jit(solution)/shard_map/rsd,df->rsf/dot_general | solution.py:108
  7.3 7.3 %all-to-all-start = ((bf16[8,3,4,4,128]{4,3,2,1,0:T(4,128)(2,1)}), bf16[8,3,4,4,128]{4,3,2,1,0:T(4,128)(2,1)S(1)}, u32[]{:S(2)}, u32[]{:S(2)}) async-start(bf16[8,3,4,4,128]{4,3,2,1,0:T(4,128)(2,1)} %broadcast_in_dim.99), calls=%async_computation | async-start | bytes 196608 | tf_op jit(solution)/shard_map/all_to_all | solution.py:115
  16.2 2.0 %fusion.51 = f32[3,4,4,128]{3,1,2,0:T(4,128)S(1)} fusion(bf16[3,4,2048]{2,1,0:T(4,128)(2,1)S(1)} %multiply_convert_fusion.1, bf16[2048,3,512]{2,0,1:T(8,128)(2,1)} %param.21, f32[512]{0:T(512)S(1)} %bitcast.234), kind=kOutput, calls=%fused_computation.39 | convolution fusion | flops 25171968 | bytes 2172928 | tf_op jit(solution)/shard_map/rsd,df->rsf/dot_general | solution.py:108
  18.7 3.0 %all-to-all-done = bf16[8,3,4,4,128]{4,3,2,1,0:T(4,128)(2,1)S(1)} async-done(((bf16[8,3,4,4,128]{4,3,2,1,0:T(4,128)(2,1)}), bf16[8,3,4,4,128]{4,3,2,1,0:T(4,128)(2,1)S(1)}, u32[]{:S(2)}, u32[]{:S(2)}) %all-to-all-start) | async-done | bytes 98336 | tf_op jit(solution)/shard_map/all_to_all | solution.py:115
  22.4 5.4 %fusion.154 = (f32[40,4,4]{1,2,0:T(4,128)S(1)}, f32[40,4,4,128]{3,1,2,0:T(4,128)S(1)}) fusion(bf16[40,4,4,128]{3,2,1,0:T(4,128)(2,1)S(1)} %gather_fusion.1, pred[40,128]{1,0:T(8,128)(4,1)S(1)} %fusion.116, bf16[40,128,512]{2,1,0:T(8,128)(2,1)} %param.24), kind=kOutput, calls=%fused_computation.208 | convolution fusion | flops 21216640 | bytes 5742080 | tf_op jit(solution)/shard_map/pshd,pkhd->pshk/dot_general | solution.py:133
  28.6 4.0 %fusion.25 = f32[40,4,4,128]{3,1,2,0:T(4,128)S(1)} fusion(f32[40,4,4,128]{3,1,2,0:T(4,128)S(1)} %get-tuple-element.36, f32[40,4,4]{1,2,0:T(4,128)S(1)} %get-tuple-element.35, pred[40,128]{1,0:T(8,128)(4,1)S(1)} %fusion.116, bf16[40,128,512]{2,1,0:T(8,128)(2,1)} %param.25), kind=kOutput, calls=%fused_computation.28 | convolution fusion | flops 21217280 | bytes 5905920 | tf_op jit(solution)/shard_map/pshk,pkhd->pshd/dot_general | solution.py:141
  34.8 3.4 %all-to-all-start.1 = ((f32[24,17,128]{2,1,0:T(8,128)}), f32[24,17,128]{2,1,0:T(8,128)S(1)}, u32[]{:S(2)}, u32[]{:S(2)}) async-start(f32[24,17,128]{2,1,0:T(8,128)} %pad_maximum_fusion.2), calls=%async_computation.1 | async-start | bytes 589824 | tf_op jit(solution)/shard_map/all_to_all | solution.py:165
  38.6 8.3 %all-to-all-done.1 = f32[24,17,128]{2,1,0:T(8,128)S(1)} async-done(((f32[24,17,128]{2,1,0:T(8,128)}), f32[24,17,128]{2,1,0:T(8,128)S(1)}, u32[]{:S(2)}, u32[]{:S(2)}) %all-to-all-start.1) | async-done | bytes 208928 | tf_op jit(solution)/shard_map/all_to_all | solution.py:165
  47.8 2.2 %fusion.62 = bf16[3,4,4,128]{3,1,2,0:T(4,128)(2,1)S(1)} fusion(bf16[3,4,2048]{2,1,0:T(4,128)(2,1)S(1)} %multiply_convert_fusion.1, bf16[2048,3,512]{2,0,1:T(8,128)(2,1)} %param.21, f32[3,4,4,128]{3,0,2,1:T(4,128)S(1)} %bitcast.233, f32[3,4,4,4]{1,3,2,0:T(4,128)S(1)} %get-tuple-element.38, f32[3,4,4]{1,2,0:T(4,128)S(1)} %get-tuple-element.14, ...), kind=kOutput, calls=%fused_computation.48 | convolution fusion | flops 25258560 | bytes 2186768 | tf_op jit(solution)/shard_map/rsht,rthd->rshd/dot_general | solution.py:188
  50.4 1.5 %collective-permute-start.1 = (f32[12,2048]{1,0:T(8,128)S(1)}, f32[12,2048]{1,0:T(8,128)S(1)}, u32[]{:S(2)}, u32[]{:S(2)}) collective-permute-start(f32[12,2048]{1,0:T(8,128)S(1)} %fusion.156), channel_id=1, source_target_pairs={{0,2},{1,3},{2,0},{3,1},{4,6},{5,7},{6,4},{7,5},{8,10},{9,11},{10,... | collective-permute-start | bytes 294920 | tf_op jit(solution)/shard_map/ppermute | solution.py:50
  53.3 5.7 %collective-permute-done.1 = f32[12,2048]{1,0:T(8,128)S(1)} collective-permute-done((f32[12,2048]{1,0:T(8,128)S(1)}, f32[12,2048]{1,0:T(8,128)S(1)}, u32[]{:S(2)}, u32[]{:S(2)}) %collective-permute-start.1) | collective-permute-done | bytes 98336 | tf_op jit(solution)/shard_map/ppermute | solution.py:50
  64.2 3.6 %all-to-all-start.2 = ((bf16[8,2,9216]{2,1,0:T(2,128)(2,1)}), bf16[8,2,9216]{2,1,0:T(2,128)(2,1)S(1)}, u32[]{:S(2)}, u32[]{:S(2)}) async-start(bf16[8,2,9216]{2,1,0:T(2,128)(2,1)} %reshape.518), calls=%async_computation.2 | async-start | bytes 589824 | tf_op jit(solution)/shard_map/all_to_all | solution.py:240
  67.9 8.3 %all-to-all-done.2 = bf16[8,2,9216]{2,1,0:T(2,128)(2,1)S(1)} async-done(((bf16[8,2,9216]{2,1,0:T(2,128)(2,1)}), bf16[8,2,9216]{2,1,0:T(2,128)(2,1)S(1)}, u32[]{:S(2)}, u32[]{:S(2)}) %all-to-all-start.2) | async-done | bytes 294944 | tf_op jit(solution)/shard_map/all_to_all | solution.py:240
  77.1 2.6 %fusion.20 = f32[48,352]{1,0:T(8,128)} fusion(bf16[48,2048]{1,0:T(8,128)(2,1)S(1)} %reshape.460, bf16[1,2048,352]{1,2,0:T(8,128)(2,1)} %param.31), kind=kOutput, calls=%fused_computation.25 | convolution fusion | flops 69206016 | bytes 1705984 | tf_op jit(solution)/shard_map/dot_general | solution.py:244
  79.6 3.0 %fusion.22 = f32[1,4,48,512]{3,2,1,0:T(8,128)S(1)} fusion(bf16[44,4,8,512]{3,2,1,0:T(8,128)(2,1)} %bitcast.208, bf16[48,2048]{1,0:T(8,128)(2,1)S(1)} %reshape.460, bf16[1,2048,352]{1,2,0:T(8,128)(2,1)} %param.32, f32[48,352]{1,0:T(8,128)} %fusion.20), kind=kOutput, calls=%fused_computation.27 | convolution fusion | flops 138513408 | bytes 3540992 | tf_op jit(solution)/shard_map/dot_general | solution.py:247
  85.9 1.5 %constant_dynamic-slice_fusion.1 = (f32[1,58368]{1,0:T(1,128)S(1)}, f32[1,58368]{1,0:T(1,128)}, f32[1,58368]{1,0:T(1,128)S(1)}, f32[1,58368]{1,0:T(1,128)S(1)}) fusion(f32[4,58368]{1,0:T(4,128)S(1)} %constant_dynamic-update-slice_fusion, s32[]{:T(128)S(6)} %select_n.146, s32[]{:T(128)S(6)} %select_n.150, s32[]{:T(128)S(6)} %select_n.148, s32[]{:T(128)S(6)} %select_n.144), kind=kLoop, calls=%fused_computation.183 | loop fusion | bytes 1867792 | tf_op jit(solution)/shard_map/jit(dynamic_index_in_dim)/dynamic_slice | solution.py:46
  87.9 1.3 %collective-permute-start.4 = (f32[58368]{0:T(1024)S(1)}, f32[58368]{0:T(1024)}, u32[]{:S(2)}, u32[]{:S(2)}) collective-permute-start(f32[58368]{0:T(1024)S(1)} %bitcast.220), channel_id=1, source_target_pairs={{0,2},{1,3},{2,0},{3,1},{4,6},{5,7},{6,4},{7,5},{8,10},{9,11},{10,... | collective-permute-start | bytes 700424 | tf_op jit(solution)/shard_map/ppermute | solution.py:50
  89.4 4.1 %collective-permute-done.5 = f32[58368]{0:T(1024)} collective-permute-done((f32[58368]{0:T(1024)}, f32[58368]{0:T(1024)}, u32[]{:S(2)}, u32[]{:S(2)}) %collective-permute-start.5) | collective-permute-done | bytes 233504 | tf_op jit(solution)/shard_map/ppermute | solution.py:50
  93.4 2.1 %collective-permute-done.3 = f32[58368]{0:T(1024)} collective-permute-done((f32[58368]{0:T(1024)S(1)}, f32[58368]{0:T(1024)}, u32[]{:S(2)}, u32[]{:S(2)}) %collective-permute-start.3) | collective-permute-done | bytes 233504 | tf_op jit(solution)/shard_map/ppermute | solution.py:50
  95.5 5.0 %collective-permute-done.4 = f32[58368]{0:T(1024)} collective-permute-done((f32[58368]{0:T(1024)S(1)}, f32[58368]{0:T(1024)}, u32[]{:S(2)}, u32[]{:S(2)}) %collective-permute-start.4) | collective-permute-done | bytes 233504 | tf_op jit(solution)/shard_map/ppermute | solution.py:50
  102.4 1.7 %collective-permute-start.8 = (bf16[24,704]{1,0:T(8,128)(2,1)S(1)}, bf16[24,704]{1,0:T(8,128)(2,1)S(1)}, u32[]{:S(2)}, u32[]{:S(2)}) collective-permute-start(bf16[24,704]{1,0:T(8,128)(2,1)S(1)} %fusion.105), channel_id=1, source_target_pairs={{0,3},{1,0},{2,1},{3,2},{4,7},{5,4},{6,5},{7,6},{8,11},{9,8},{10,9... | collective-permute-start | bytes 101384 | tf_op jit(solution)/shard_map/ppermute | solution.py:50
  104.2 1.9 %collective-permute-done.7 = bf16[24,704]{1,0:T(8,128)(2,1)S(1)} collective-permute-done((bf16[24,704]{1,0:T(8,128)(2,1)S(1)}, bf16[24,704]{1,0:T(8,128)(2,1)S(1)}, u32[]{:S(2)}, u32[]{:S(2)}) %collective-permute-start.7) | collective-permute-done | bytes 33824 | tf_op jit(solution)/shard_map/ppermute | solution.py:50
  108.1 3.6 %all-to-all-start.3 = ((f32[8,1,9216]{2,1,0:T(1,128)}), f32[8,1,9216]{2,1,0:T(1,128)S(1)}, u32[]{:S(2)}, u32[]{:S(2)}) async-start(f32[8,1,9216]{2,1,0:T(1,128)} %all_to_all.27), calls=%async_computation.3 | async-start | bytes 589824 | tf_op jit(solution)/shard_map/all_to_all | solution.py:279
  112.2 10.3 %all-to-all-done.3 = f32[8,1,9216]{2,1,0:T(1,128)S(1)} async-done(((f32[8,1,9216]{2,1,0:T(1,128)}), f32[8,1,9216]{2,1,0:T(1,128)S(1)}, u32[]{:S(2)}, u32[]{:S(2)}) %all-to-all-start.3) | async-done | bytes 294944 | tf_op jit(solution)/shard_map/all_to_all | solution.py:279
  (159 shorter events, 29.8 us)
Async XLA Ops:
  0.0 50.0 %copy-start = (bf16[512,2048]{1,0:T(8,128)(2,1)S(1)}, bf16[512,2048]{1,0:T(8,128)(2,1)}, u32[]{:S(2)}) copy-start(bf16[512,2048]{1,0:T(8,128)(2,1)} %param.23) | copy-start | bytes 6291460
  0.0 15.1 %copy-start.1 = (s32[24]{0:T(128)S(1)}, s32[24]{0:T(128)}, u32[]{:S(2)}) copy-start(s32[24]{0:T(128)} %param.27) | copy-start | bytes 292
  0.0 14.6 %copy-start.9 = (s32[3,4,4]{2,1,0:T(4,128)S(1)}, s32[3,4,4]{2,1,0:T(4,128)}, u32[]{:S(2)}) copy-start(s32[3,4,4]{2,1,0:T(4,128)} %param.29) | copy-start | bytes 580
  0.0 14.7 %copy-start.8 = (s32[24,37]{1,0:T(8,128)S(1)}, s32[24,37]{1,0:T(8,128)}, u32[]{:S(2)}) copy-start(s32[24,37]{1,0:T(8,128)} %param.26) | copy-start | bytes 10660
  7.3 14.4 %all-to-all-start = ((bf16[8,3,4,4,128]{4,3,2,1,0:T(4,128)(2,1)}), bf16[8,3,4,4,128]{4,3,2,1,0:T(4,128)(2,1)S(1)}, u32[]{:S(2)}, u32[]{:S(2)}) async-start(bf16[8,3,4,4,128]{4,3,2,1,0:T(4,128)(2,1)} %broadcast_in_dim.99), calls=%async_computation | async-start | bytes 196608 | tf_op jit(solution)/shard_map/all_to_all | solution.py:115
  32.6 5.6 %copy-start.2 = (bf16[3,4,2048]{2,1,0:T(4,128)(2,1)S(1)}, bf16[3,4,2048]{2,1,0:T(4,128)(2,1)}, u32[]{:S(2)}) copy-start(bf16[3,4,2048]{2,1,0:T(4,128)(2,1)} %param.19) | copy-start | bytes 147460
  32.6 5.6 %copy-start.11 = (bf16[2048]{0:T(1024)(128)(2,1)S(1)}, bf16[2048]{0:T(1024)(128)(2,1)}, u32[]{:S(2)}) copy-start(bf16[2048]{0:T(1024)(128)(2,1)} %param.28) | copy-start | bytes 12292
  34.8 12.1 %all-to-all-start.1 = ((f32[24,17,128]{2,1,0:T(8,128)}), f32[24,17,128]{2,1,0:T(8,128)S(1)}, u32[]{:S(2)}, u32[]{:S(2)}) async-start(f32[24,17,128]{2,1,0:T(8,128)} %pad_maximum_fusion.2), calls=%async_computation.1 | async-start | bytes 589824 | tf_op jit(solution)/shard_map/all_to_all | solution.py:165
  50.4 2.9 %collective-permute-start.2 = (f32[12,2048]{1,0:T(8,128)S(1)}, f32[12,2048]{1,0:T(8,128)S(1)}, u32[]{:S(2)}, u32[]{:S(2)}) collective-permute-start(f32[12,2048]{1,0:T(8,128)S(1)} %fusion.156), channel_id=1, source_target_pairs={{0,3},{1,0},{2,1},{3,2},{4,7},{5,4},{6,5},{7,6},{8,11},{9,8},{10,9... | collective-permute-start | bytes 294920 | tf_op jit(solution)/shard_map/ppermute | solution.py:50
  50.4 8.6 %collective-permute-start.1 = (f32[12,2048]{1,0:T(8,128)S(1)}, f32[12,2048]{1,0:T(8,128)S(1)}, u32[]{:S(2)}, u32[]{:S(2)}) collective-permute-start(f32[12,2048]{1,0:T(8,128)S(1)} %fusion.156), channel_id=1, source_target_pairs={{0,2},{1,3},{2,0},{3,1},{4,6},{5,7},{6,4},{7,5},{8,10},{9,11},{10,... | collective-permute-start | bytes 294920 | tf_op jit(solution)/shard_map/ppermute | solution.py:50
  51.9 7.1 %collective-permute-start = (f32[12,2048]{1,0:T(8,128)S(1)}, f32[12,2048]{1,0:T(8,128)S(1)}, u32[]{:S(2)}, u32[]{:S(2)}) collective-permute-start(f32[12,2048]{1,0:T(8,128)S(1)} %fusion.156), channel_id=1, source_target_pairs={{0,1},{1,2},{2,3},{3,0},{4,5},{5,6},{6,7},{7,4},{8,9},{9,10},{10,1... | collective-permute-start | bytes 294920 | tf_op jit(solution)/shard_map/ppermute | solution.py:50
  64.2 12.0 %all-to-all-start.2 = ((bf16[8,2,9216]{2,1,0:T(2,128)(2,1)}), bf16[8,2,9216]{2,1,0:T(2,128)(2,1)S(1)}, u32[]{:S(2)}, u32[]{:S(2)}) async-start(bf16[8,2,9216]{2,1,0:T(2,128)(2,1)} %reshape.518), calls=%async_computation.2 | async-start | bytes 589824 | tf_op jit(solution)/shard_map/all_to_all | solution.py:240
  79.6 4.1 %copy-start.3 = (bf16[512,704]{0,1:T(8,128)(2,1)S(1)}, bf16[512,704]{0,1:T(8,128)(2,1)}, u32[]{:S(2)}) copy-start(bf16[512,704]{0,1:T(8,128)(2,1)} %param.35) | copy-start | bytes 2162692
  87.4 19.4 %copy-start.5 = (bf16[704,512]{1,0:T(8,128)(2,1)S(1)}, bf16[704,512]{1,0:T(8,128)(2,1)}, u32[]{:S(2)}) copy-start(bf16[704,512]{1,0:T(8,128)(2,1)} %param.36) | copy-start | bytes 2162692
  87.4 6.0 %collective-permute-start.5 = (f32[58368]{0:T(1024)}, f32[58368]{0:T(1024)}, u32[]{:S(2)}, u32[]{:S(2)}) collective-permute-start(f32[58368]{0:T(1024)} %bitcast.49), channel_id=1, source_target_pairs={{0,3},{1,0},{2,1},{3,2},{4,7},{5,4},{6,5},{7,6},{8,11},{9,8},{10,9... | collective-permute-start | bytes 700424 | tf_op jit(solution)/shard_map/ppermute | solution.py:50
  87.4 8.1 %collective-permute-start.3 = (f32[58368]{0:T(1024)S(1)}, f32[58368]{0:T(1024)}, u32[]{:S(2)}, u32[]{:S(2)}) collective-permute-start(f32[58368]{0:T(1024)S(1)} %bitcast.221), channel_id=1, source_target_pairs={{0,1},{1,2},{2,3},{3,0},{4,5},{5,6},{6,7},{7,4},{8,9},{9,10},{10,1... | collective-permute-start | bytes 700424 | tf_op jit(solution)/shard_map/ppermute | solution.py:50
  87.9 12.6 %collective-permute-start.4 = (f32[58368]{0:T(1024)S(1)}, f32[58368]{0:T(1024)}, u32[]{:S(2)}, u32[]{:S(2)}) collective-permute-start(f32[58368]{0:T(1024)S(1)} %bitcast.220), channel_id=1, source_target_pairs={{0,2},{1,3},{2,0},{3,1},{4,6},{5,7},{6,4},{7,5},{8,10},{9,11},{10,... | collective-permute-start | bytes 700424 | tf_op jit(solution)/shard_map/ppermute | solution.py:50
  101.9 4.2 %collective-permute-start.7 = (bf16[24,704]{1,0:T(8,128)(2,1)S(1)}, bf16[24,704]{1,0:T(8,128)(2,1)S(1)}, u32[]{:S(2)}, u32[]{:S(2)}) collective-permute-start(bf16[24,704]{1,0:T(8,128)(2,1)S(1)} %fusion.105), channel_id=1, source_target_pairs={{0,2},{1,3},{2,0},{3,1},{4,6},{5,7},{6,4},{7,5},{8,10},{9,11},{10,... | collective-permute-start | bytes 101384 | tf_op jit(solution)/shard_map/ppermute | solution.py:50
  102.4 3.8 %collective-permute-start.6 = (bf16[24,704]{1,0:T(8,128)(2,1)S(1)}, bf16[24,704]{1,0:T(8,128)(2,1)S(1)}, u32[]{:S(2)}, u32[]{:S(2)}) collective-permute-start(bf16[24,704]{1,0:T(8,128)(2,1)S(1)} %fusion.105), channel_id=1, source_target_pairs={{0,1},{1,2},{2,3},{3,0},{4,5},{5,6},{6,7},{7,4},{8,9},{9,10},{10,1... | collective-permute-start | bytes 101384 | tf_op jit(solution)/shard_map/ppermute | solution.py:50
  102.4 3.8 %collective-permute-start.8 = (bf16[24,704]{1,0:T(8,128)(2,1)S(1)}, bf16[24,704]{1,0:T(8,128)(2,1)S(1)}, u32[]{:S(2)}, u32[]{:S(2)}) collective-permute-start(bf16[24,704]{1,0:T(8,128)(2,1)S(1)} %fusion.105), channel_id=1, source_target_pairs={{0,3},{1,0},{2,1},{3,2},{4,7},{5,4},{6,5},{7,6},{8,11},{9,8},{10,9... | collective-permute-start | bytes 101384 | tf_op jit(solution)/shard_map/ppermute | solution.py:50
  104.2 7.5 %copy-start.10 = (f32[3,4,4]{2,1,0:T(4,128)S(1)}, f32[3,4,4]{2,1,0:T(4,128)}, u32[]{:S(2)}) copy-start(f32[3,4,4]{2,1,0:T(4,128)} %param.30) | copy-start | bytes 580
  104.2 7.6 %copy-start.12 = (bf16[2048]{0:T(1024)(128)(2,1)S(1)}, bf16[2048]{0:T(1024)(128)(2,1)}, u32[]{:S(2)}) copy-start(bf16[2048]{0:T(1024)(128)(2,1)} %param.37) | copy-start | bytes 12292
  106.1 5.9 %copy-start.7 = (bf16[12,2048]{1,0:T(8,128)(2,1)S(1)}, bf16[12,2048]{1,0:T(8,128)(2,1)}, u32[]{:S(2)}) copy-start(bf16[12,2048]{1,0:T(8,128)(2,1)} %copy-done.6) | copy-start | bytes 147460
  108.1 14.4 %all-to-all-start.3 = ((f32[8,1,9216]{2,1,0:T(1,128)}), f32[8,1,9216]{2,1,0:T(1,128)S(1)}, u32[]{:S(2)}, u32[]{:S(2)}) async-start(f32[8,1,9216]{2,1,0:T(1,128)} %all_to_all.27), calls=%async_computation.3 | async-start | bytes 589824 | tf_op jit(solution)/shard_map/all_to_all | solution.py:279
  (2 other events, 2.0 us)

commit v7 on v6

--- a/solution.py
+++ b/solution.py
@@ -7,6 +7,7 @@
 
 HD = 128
 TOPK = 4
+LANES = 128
 
 
 NEG = -1e30
@@ -115,8 +116,11 @@
     query_all = lax.all_to_all(query_spread, "req", 0, 0, tiled=True).reshape(
         (req_count * req_rows,) + query_new.shape[1:]
     )
-    key_new = rotate(project(1, normed_late).reshape(head_shape), positions).astype(jnp.bfloat16)
-    value_new = project(2, normed_late).reshape(head_shape).astype(jnp.bfloat16)
+    key_value = jnp.einsum(
+        "rsd,dcf->rscf", normed_late, qkv_weight[:, 1:], preferred_element_type=jnp.float32
+    ) + qkv_bias[1:].astype(jnp.float32)
+    key_new = rotate(key_value[:, :, 0].reshape(head_shape), positions).astype(jnp.bfloat16)
+    value_new = key_value[:, :, 1].reshape(head_shape).astype(jnp.bfloat16)
     slot_ids = req_index * pool_here + jnp.arange(pool_here, dtype=jnp.int32)
     matches = (page_table[:, :, None] == slot_ids[None, None, :]).astype(jnp.int32)
     request_ids = jnp.arange(all_requests, dtype=jnp.int32)
@@ -230,37 +234,52 @@
     w_down_here = expert_w_down[0]
     mixed_cols = lax.dynamic_slice_in_dim(mixed, tp_index * col_share, col_share, 1)
     shared_send = jnp.broadcast_to(mixed_cols[None], (req_count, row_count, col_share))
+    moe_lines = capacity * model_width // LANES
     dispatch = jnp.concatenate(
         [
-            outgoing.reshape(req_count, capacity * model_width),
-            shared_send.reshape(req_count, row_count * col_share),
+            outgoing.reshape(req_count, moe_lines, LANES),
+            shared_send.reshape(req_count, row_count * col_share // LANES, LANES),
         ],
         axis=1,
     )
     received = lax.all_to_all(dispatch, "req", 0, 0, tiled=True)
-    item_count = capacity
-    flat_rows = received[:, : capacity * model_width].reshape(req_count * capacity, model_width)
-    piece = received[:, capacity * model_width :].reshape(req_count * row_count, col_share)
+    flat_rows = received[:, :moe_lines].reshape(req_count * capacity, model_width)
+    piece = received[:, moe_lines:].reshape(req_count * row_count, col_share)
     gate_pre = jnp.dot(flat_rows, w_gate_here, preferred_element_type=jnp.float32)
     up_pre = jnp.dot(flat_rows, w_up_here, preferred_element_type=jnp.float32)
     hidden = (jax.nn.silu(gate_pre) * up_pre).astype(jnp.bfloat16)
     partial_out = jnp.dot(hidden, w_down_here, preferred_element_type=jnp.float32)
     expert_rows = req_count * capacity
-    partial_split = partial_out.reshape(expert_rows, tp_count, col_share).transpose(1, 0, 2)
     gate_part = jnp.dot(piece, shared_w_gate, preferred_element_type=jnp.float32)
     up_part = jnp.dot(piece, shared_w_up, preferred_element_type=jnp.float32)
     unit_count = shared_w_gate.shape[1]
     all_rows = req_count * row_count
     share_rows = all_rows // tp_count
-    shared_pre = jnp.concatenate([gate_part, up_part], axis=1).reshape(
-        tp_count, share_rows * 2 * unit_count
-    )
-    reduce_in = jnp.concatenate(
-        [partial_split.reshape(tp_count, expert_rows * col_share), shared_pre], axis=1
-    )
-    reduce_out = sum(shift_exchange(reduce_in, "tp", tp_count))
-    expert_sum = reduce_out[: expert_rows * col_share].reshape(expert_rows, col_share)
-    shared_sum = reduce_out[expert_rows * col_share :].reshape(share_rows, 2 * unit_count)
+    shared_pre = jnp.concatenate([gate_part, up_part], axis=1)
+    expert_lines = expert_rows * col_share // LANES
+
+    def reduce_send(target):
+        return jnp.concatenate(
+            [
+                lax.dynamic_slice_in_dim(partial_out, target * col_share, col_share, 1).reshape(
+                    expert_lines, LANES
+                ),
+                lax.dynamic_slice_in_dim(shared_pre, target * share_rows, share_rows, 0).reshape(
+                    share_rows * 2 * unit_count // LANES, LANES
+                ),
+            ],
+            axis=0,
+        )
+
+    reduce_pieces = [reduce_send(tp_index)]
+    for shift in range(1, tp_count):
+        pairs = [(source, (source + shift) % tp_count) for source in range(tp_count)]
+        reduce_pieces.append(
+            lax.ppermute(reduce_send((tp_index + shift) % tp_count), "tp", pairs)
+        )
+    reduce_out = sum(reduce_pieces)
+    expert_sum = reduce_out[:expert_lines].reshape(expert_rows, col_share)
+    shared_sum = reduce_out[expert_lines:].reshape(share_rows, 2 * unit_count)
     shared_hidden = (jax.nn.silu(shared_sum[:, :unit_count]) * shared_sum[:, unit_count:]).astype(
         jnp.bfloat16
     )
@@ -269,18 +288,17 @@
     ).reshape(all_rows, unit_count)
     shared_down = jnp.dot(hidden_all, shared_w_down, preferred_element_type=jnp.float32)
     ey = expert_sum.astype(jnp.bfloat16).astype(jnp.float32)
+    ey_lines = capacity * col_share // LANES
     back_in = jnp.concatenate(
         [
-            ey.reshape(req_count, capacity * col_share),
-            shared_down.reshape(req_count, row_count * col_share),
+            ey.reshape(req_count, ey_lines, LANES),
+            shared_down.reshape(req_count, row_count * col_share // LANES, LANES),
         ],
         axis=1,
     )
     back = lax.all_to_all(back_in, "req", 0, 0, tiled=True)
-    returned = back[:, : capacity * col_share].reshape(expert_count * capacity, col_share)
-    shared_mine = jnp.sum(
-        back[:, capacity * col_share :].reshape(req_count, row_count, col_share), axis=0
-    )
+    returned = back[:, :ey_lines].reshape(expert_count * capacity, col_share)
+    shared_mine = jnp.sum(back[:, ey_lines:].reshape(req_count, row_count, col_share), axis=0)
     moe_out = jnp.dot(combine_map, returned, precision=HIGHEST)
     switch = jax.nn.sigmoid(jnp.dot(mixed, shared_switch, preferred_element_type=jnp.float32))
     resid_mine = lax.dynamic_slice_in_dim(resid, tp_index * col_share, col_share, 1)

time: 125 us -> 123 us (0.984)
  waiting for transfers between devices: 49.9 us -> 37.8 us
  other arithmetic: 9.96 us -> 15.6 us
  local copies, waits for them, and re-layouts: 14.5 us -> 16.5 us
  starting transfers between devices: 23.6 us -> 24.9 us
    ppermute x9 -> x6, waiting for transfers between devices: 20 us -> 10 us  [shift_exchange(): pieces.append(lax.ppermute(send, axis, pairs))]
    concatenate x2 -> x6, other arithmetic: 0.17 us -> 5.35 us  [the longest x3 3.04 us: reduce_send(): jnp.concatenate([lax.dynamic_slice_in_dim(partial_out, target * col_share...]
    ppermute x0 -> x3, waiting for transfers between devices: none -> 4.76 us  [per_device(): lax.ppermute(reduce_send((tp_index + shift) % tp_count), 'tp', pairs)]
    reshape x8 -> x14, local copies, waits for them, and re-layouts: 1.05 us -> 5.52 us  [the longest x4 2.71 us: reduce_send(): lax.dynamic_slice_in_dim(partial_out, target * col_share, col_share, 1)]
    all_to_all x1, waiting for transfers between devices: 10.3 us -> 6 us  [per_device(): back = lax.all_to_all(back_in, 'req', 0, 0, tiled=True)]
    all_to_all x1, waiting for transfers between devices: 2.98 us -> 0.01 us  [per_device(): lax.all_to_all(query_spread, 'req', 0, 0, tiled=True)]
    dot_general x0 -> x1, matrix products: none -> 2.85 us  [per_device(): jnp.einsum('rsd,dcf->rscf', normed_late, qkv_weight[:, 1:], preferred_ele...]
    unnamed x36 -> x24, local copies, waits for them, and re-layouts: 4.17 us -> 1.55 us
  transfers between devices with their start and end apart: 13 -> 13, of which waited for: 11 -> 11; matrix products, arithmetic and copies ran while one was open for 4% -> 15% of each run, Pallas kernels for 0% -> 0%
where the time goes in v7:
time: 123 us; the launch traced here: 122 us
  waiting for transfers between devices  37.8 us (31%)
  matrix products  26.4 us (21%)
  starting transfers between devices  24.9 us (20%)
  local copies, waits for them, and re-layouts  16.5 us (13%)
  other arithmetic  15.6 us (13%)
    ppermute x6, waiting for transfers between devices, shift_exchange(): pieces.append(lax.ppermute(send, axis, pairs))  10 us
    all_to_all x1, waiting for transfers between devices, per_device(): lax.all_to_all(packed, 'req', 0, 0, tiled=True)  8.63 us
    all_to_all x1, waiting for transfers between devices, per_device(): received = lax.all_to_all(dispatch, 'req', 0, 0, tiled=True)  8.44 us
    all_to_all x1, starting transfers between devices, per_device(): lax.all_to_all(query_spread, 'req', 0, 0, tiled=True)  7.28 us
    all_to_all x1, waiting for transfers between devices, per_device(): back = lax.all_to_all(back_in, 'req', 0, 0, tiled=True)  6 us
    all_to_all x1, starting transfers between devices, per_device(): lax.all_to_all(packed, 'req', 0, 0, tiled=True)  6 us
    dot_general x1, matrix products, per_device(): jnp.einsum('pshd,pkhd->pshk', page_queries, page_keys, preferred_element_...  5.41 us
    ppermute x3, waiting for transfers between devices, per_device(): lax.ppermute(reduce_send((tp_index + shift) % tp_count), 'tp', pairs)  4.76 us
  transfers between devices with their start and end apart: 13, of which 11 were waited for; matrix products, arithmetic and copies ran while one was open for 15% of the time, Pallas kernels for 0%

profile of v7, /device:TPU:0, one launch (start us, length us, event | category | flops | bytes accessed | tf_op | source)
XLA Modules:
  0.0 121.9 jit_solution(16720506605028643573)
XLA Ops:
  4.3 2.0 %fusion.40 = f32[3,4,4,128]{3,1,2,0:T(4,128)S(1)} fusion(bf16[3,4,2048]{2,1,0:T(4,128)(2,1)S(1)} %multiply_convert_fusion.1, bf16[2048,3,512]{2,0,1:T(8,128)(2,1)} %param.21, f32[512]{0:T(512)S(1)} %bitcast.185), kind=kOutput, calls=%fused_computation.32 | convolution fusion | flops 25171968 | bytes 2172928 | tf_op jit(solution)/shard_map/rsd,df->rsf/dot_general | solution.py:109
  7.1 7.3 %all-to-all-start = ((bf16[8,3,4,4,128]{4,3,2,1,0:T(4,128)(2,1)}), bf16[8,3,4,4,128]{4,3,2,1,0:T(4,128)(2,1)S(1)}, u32[]{:S(2)}, u32[]{:S(2)}) async-start(bf16[8,3,4,4,128]{4,3,2,1,0:T(4,128)(2,1)} %broadcast_in_dim.99), calls=%async_computation | async-start | bytes 196608 | tf_op jit(solution)/shard_map/all_to_all | solution.py:116
  17.3 1.4 %gather_fusion = s32[40]{0:T(128)S(1)} fusion(s32[24]{0:T(128)} %param.27, s32[1024]{0:T(1024)S(1)} %pad_clamp_fusion.1), kind=kCustom, calls=%fused_computation | custom fusion | bytes 480 | tf_op jit(solution)/shard_map/gather | solution.py:132
  18.7 2.9 %fusion.30 = f32[3,4,2,512]{3,1,2,0:T(4,128)S(1)} fusion(bf16[2048,3,512]{2,0,1:T(8,128)(2,1)} %param.21, bf16[3,4,2048]{2,1,0:T(4,128)(2,1)S(1)} %multiply_convert_fusion.1, f32[2,512]{1,0:T(2,128)S(1)} %slice_convert_fusion.2), kind=kOutput, calls=%fused_computation.27 | convolution fusion | flops 50343936 | bytes 4296704 | tf_op jit(solution)/shard_map/rsd,dcf->rscf/dot_general | solution.py:119
  22.9 5.4 %fusion.137 = (f32[40,4,4]{1,2,0:T(4,128)S(1)}, f32[40,4,4,128]{3,1,2,0:T(4,128)S(1)}) fusion(bf16[40,4,4,128]{3,2,1,0:T(4,128)(2,1)S(1)} %gather_fusion.1, pred[40,128]{1,0:T(8,128)(4,1)S(1)} %fusion.98, bf16[40,128,512]{2,1,0:T(8,128)(2,1)} %param.24), kind=kOutput, calls=%fused_computation.211 | convolution fusion | flops 21216640 | bytes 5742080 | tf_op jit(solution)/shard_map/pshd,pkhd->pshk/dot_general | solution.py:137
  29.8 4.0 %fusion.18 = f32[40,4,4,128]{3,1,2,0:T(4,128)S(1)} fusion(f32[40,4,4,128]{3,1,2,0:T(4,128)S(1)} %get-tuple-element.37, f32[40,4,4]{1,2,0:T(4,128)S(1)} %get-tuple-element.36, pred[40,128]{1,0:T(8,128)(4,1)S(1)} %fusion.98, bf16[40,128,512]{2,1,0:T(8,128)(2,1)} %param.25), kind=kOutput, calls=%fused_computation.23 | convolution fusion | flops 21217280 | bytes 5905920 | tf_op jit(solution)/shard_map/pshk,pkhd->pshd/dot_general | solution.py:145
  35.3 6.0 %all-to-all-start.1 = ((f32[24,17,128]{2,1,0:T(8,128)}), f32[24,17,128]{2,1,0:T(8,128)S(1)}, u32[]{:S(2)}, u32[]{:S(2)}) async-start(f32[24,17,128]{2,1,0:T(8,128)} %pad_maximum_fusion.1), calls=%async_computation.1 | async-start | bytes 589824 | tf_op jit(solution)/shard_map/all_to_all | solution.py:169
  41.7 8.6 %all-to-all-done.1 = f32[24,17,128]{2,1,0:T(8,128)S(1)} async-done(((f32[24,17,128]{2,1,0:T(8,128)}), f32[24,17,128]{2,1,0:T(8,128)S(1)}, u32[]{:S(2)}, u32[]{:S(2)}) %all-to-all-start.1) | async-done | bytes 208928 | tf_op jit(solution)/shard_map/all_to_all | solution.py:169
  51.8 1.5 %collective-permute-start.1 = (f32[12,2048]{1,0:T(8,128)S(1)}, f32[12,2048]{1,0:T(8,128)S(1)}, u32[]{:S(2)}, u32[]{:S(2)}) collective-permute-start(f32[12,2048]{1,0:T(8,128)S(1)} %fusion.139), channel_id=1, source_target_pairs={{0,2},{1,3},{2,0},{3,1},{4,6},{5,7},{6,4},{7,5},{8,10},{9,11},{10,... | collective-permute-start | bytes 294920 | tf_op jit(solution)/shard_map/ppermute | solution.py:51
  54.7 5.7 %collective-permute-done.1 = f32[12,2048]{1,0:T(8,128)S(1)} collective-permute-done((f32[12,2048]{1,0:T(8,128)S(1)}, f32[12,2048]{1,0:T(8,128)S(1)}, u32[]{:S(2)}, u32[]{:S(2)}) %collective-permute-start.1) | collective-permute-done | bytes 98336 | tf_op jit(solution)/shard_map/ppermute | solution.py:51
  63.3 3.6 %all-to-all-start.2 = ((bf16[8,144,128]{2,1,0:T(8,128)(2,1)}), bf16[8,144,128]{2,1,0:T(8,128)(2,1)S(1)}, u32[]{:S(2)}, u32[]{:S(2)}) async-start(bf16[8,144,128]{2,1,0:T(8,128)(2,1)} %pad_maximum_fusion.2), calls=%async_computation.2 | async-start | bytes 589824 | tf_op jit(solution)/shard_map/all_to_all | solution.py:245
  67.0 8.4 %all-to-all-done.2 = bf16[8,144,128]{2,1,0:T(8,128)(2,1)S(1)} async-done(((bf16[8,144,128]{2,1,0:T(8,128)(2,1)}), bf16[8,144,128]{2,1,0:T(8,128)(2,1)S(1)}, u32[]{:S(2)}, u32[]{:S(2)}) %all-to-all-start.2) | async-done | bytes 294944 | tf_op jit(solution)/shard_map/all_to_all | solution.py:245
  75.5 1.5 %fusion.140 = f32[96,704]{1,0:T(8,128)S(1)} fusion(bf16[96,512]{1,0:T(8,128)(2,1)S(1)} %reshape.444, bf16[512,704]{0,1:T(8,128)(2,1)} %param.34), kind=kOutput, calls=%fused_computation.214 | convolution fusion | flops 69206016 | bytes 1089536 | tf_op jit(solution)/shard_map/dot_general | solution.py:253
  79.0 1.9 %fusion.16 = f32[48,352]{1,0:T(8,128)S(1)} fusion(bf16[48,2048]{1,0:T(8,128)(2,1)S(1)} %reshape.442, bf16[1,2048,352]{1,2,0:T(8,128)(2,1)} %param.31), kind=kOutput, calls=%fused_computation.21 | convolution fusion | flops 69206016 | bytes 1705984 | tf_op jit(solution)/shard_map/dot_general | solution.py:248
  80.9 2.9 %fusion.12 = f32[48,2048]{1,0:T(8,128)S(1)} fusion(bf16[1,352,2048]{2,1,0:T(8,128)(2,1)} %param.33, bf16[48,2048]{1,0:T(8,128)(2,1)S(1)} %reshape.442, bf16[1,2048,352]{1,2,0:T(8,128)(2,1)} %param.32, f32[48,352]{1,0:T(8,128)S(1)} %fusion.16), kind=kOutput, calls=%fused_computation.17 | convolution fusion | flops 138513408 | bytes 3540992 | tf_op jit(solution)/shard_map/dot_general | solution.py:251
  84.6 1.6 %pad_maximum_fusion.6 = f32[456,128]{1,0:T(8,128)} fusion(f32[264,128]{1,0:T(8,128)} %reshape.451, f32[192,128]{1,0:T(8,128)S(1)} %reshape.450), kind=kLoop, calls=%fused_computation.78 | loop fusion | flops 58368 | bytes 466944 | tf_op jit(solution)/shard_map/concatenate | solution.py:262
  88.7 1.1 collective-permute-start.4
  94.9 2.6 %collective-permute-done.4 = f32[456,128]{1,0:T(8,128)} collective-permute-done((f32[456,128]{1,0:T(8,128)}, f32[456,128]{1,0:T(8,128)}, u32[]{:S(2)}, u32[]{:S(2)}) %collective-permute-start.4) | collective-permute-done | bytes 233504 | tf_op jit(solution)/shard_map/ppermute | solution.py:278
  97.5 2.1 %collective-permute-done.3 = f32[456,128]{1,0:T(8,128)} collective-permute-done((f32[456,128]{1,0:T(8,128)}, f32[456,128]{1,0:T(8,128)}, u32[]{:S(2)}, u32[]{:S(2)}) %collective-permute-start.3) | collective-permute-done | bytes 233504 | tf_op jit(solution)/shard_map/ppermute | solution.py:278
  99.6 1.2 %fusion.66 = f32[456,128]{1,0:T(8,128)S(1)} fusion(f32[456,128]{1,0:T(8,128)} %collective-permute-done.5, f32[456,128]{1,0:T(8,128)} %collective-permute-done.4, f32[456,128]{1,0:T(8,128)} %collective-permute-done.3, f32[264,128]{1,0:T(8,128)S(1)} %reshape.445, f32[192,128]{1,0:T(8,128)S(1)} %reshape.443), kind=kLoop, calls=%fused_computation.75 | loop fusion | flops 233472 | bytes 1167360 | tf_op jit(solution)/shard_map/add | solution.py:280
  101.1 1.2 collective-permute-start.7
  102.7 2.4 %collective-permute-done.7 = bf16[24,704]{1,0:T(8,128)(2,1)S(1)} collective-permute-done((bf16[24,704]{1,0:T(8,128)(2,1)S(1)}, bf16[24,704]{1,0:T(8,128)(2,1)S(1)}, u32[]{:S(2)}, u32[]{:S(2)}) %collective-permute-start.7) | collective-permute-done | bytes 33824 | tf_op jit(solution)/shard_map/ppermute | solution.py:51
  108.0 3.5 %all-to-all-start.3 = ((f32[8,72,128]{2,1,0:T(8,128)}), f32[8,72,128]{2,1,0:T(8,128)S(1)}, u32[]{:S(2)}, u32[]{:S(2)}) async-start(f32[8,72,128]{2,1,0:T(8,128)} %pad_maximum_fusion.3), calls=%async_computation.3 | async-start | bytes 589824 | tf_op jit(solution)/shard_map/all_to_all | solution.py:299
  114.2 6.0 %all-to-all-done.3 = f32[8,72,128]{2,1,0:T(8,128)S(1)} async-done(((f32[8,72,128]{2,1,0:T(8,128)}), f32[8,72,128]{2,1,0:T(8,128)S(1)}, u32[]{:S(2)}, u32[]{:S(2)}) %all-to-all-start.3) | async-done | bytes 294944 | tf_op jit(solution)/shard_map/all_to_all | solution.py:299
  (155 shorter events, 36.2 us)
Async XLA Ops:
  0.0 51.5 %copy-start = (bf16[512,2048]{1,0:T(8,128)(2,1)S(1)}, bf16[512,2048]{1,0:T(8,128)(2,1)}, u32[]{:S(2)}) copy-start(bf16[512,2048]{1,0:T(8,128)(2,1)} %param.23) | copy-start | bytes 6291460
  7.1 15.0 %all-to-all-start = ((bf16[8,3,4,4,128]{4,3,2,1,0:T(4,128)(2,1)}), bf16[8,3,4,4,128]{4,3,2,1,0:T(4,128)(2,1)S(1)}, u32[]{:S(2)}, u32[]{:S(2)}) async-start(bf16[8,3,4,4,128]{4,3,2,1,0:T(4,128)(2,1)} %broadcast_in_dim.99), calls=%async_computation | async-start | bytes 196608 | tf_op jit(solution)/shard_map/all_to_all | solution.py:116
  22.1 19.3 %copy-start.7 = (s32[48]{0:T(128)}, s32[48]{0:T(128)S(1)}, u32[]{:S(2)}) copy-start(s32[48]{0:T(128)S(1)} %get-tuple-element.40) | copy-start | bytes 580
  22.1 19.3 %copy-start.8 = (s32[48]{0:T(128)}, s32[48]{0:T(128)S(1)}, u32[]{:S(2)}) copy-start(s32[48]{0:T(128)S(1)} %get-tuple-element.41) | copy-start | bytes 580
  29.8 11.5 %copy-start.1 = (bf16[3,4,2048]{2,1,0:T(4,128)(2,1)S(1)}, bf16[3,4,2048]{2,1,0:T(4,128)(2,1)}, u32[]{:S(2)}) copy-start(bf16[3,4,2048]{2,1,0:T(4,128)(2,1)} %param.19) | copy-start | bytes 147460
  29.8 11.5 %copy-start.6 = (bf16[2048]{0:T(1024)(128)(2,1)S(1)}, bf16[2048]{0:T(1024)(128)(2,1)}, u32[]{:S(2)}) copy-start(bf16[2048]{0:T(1024)(128)(2,1)} %param.28) | copy-start | bytes 12292
  35.3 15.0 %all-to-all-start.1 = ((f32[24,17,128]{2,1,0:T(8,128)}), f32[24,17,128]{2,1,0:T(8,128)S(1)}, u32[]{:S(2)}, u32[]{:S(2)}) async-start(f32[24,17,128]{2,1,0:T(8,128)} %pad_maximum_fusion.1), calls=%async_computation.1 | async-start | bytes 589824 | tf_op jit(solution)/shard_map/all_to_all | solution.py:169
  51.8 2.9 %collective-permute-start.2 = (f32[12,2048]{1,0:T(8,128)S(1)}, f32[12,2048]{1,0:T(8,128)S(1)}, u32[]{:S(2)}, u32[]{:S(2)}) collective-permute-start(f32[12,2048]{1,0:T(8,128)S(1)} %fusion.139), channel_id=1, source_target_pairs={{0,3},{1,0},{2,1},{3,2},{4,7},{5,4},{6,5},{7,6},{8,11},{9,8},{10,9... | collective-permute-start | bytes 294920 | tf_op jit(solution)/shard_map/ppermute | solution.py:51
  51.8 8.6 %collective-permute-start.1 = (f32[12,2048]{1,0:T(8,128)S(1)}, f32[12,2048]{1,0:T(8,128)S(1)}, u32[]{:S(2)}, u32[]{:S(2)}) collective-permute-start(f32[12,2048]{1,0:T(8,128)S(1)} %fusion.139), channel_id=1, source_target_pairs={{0,2},{1,3},{2,0},{3,1},{4,6},{5,7},{6,4},{7,5},{8,10},{9,11},{10,... | collective-permute-start | bytes 294920 | tf_op jit(solution)/shard_map/ppermute | solution.py:51
  53.4 7.1 %collective-permute-start = (f32[12,2048]{1,0:T(8,128)S(1)}, f32[12,2048]{1,0:T(8,128)S(1)}, u32[]{:S(2)}, u32[]{:S(2)}) collective-permute-start(f32[12,2048]{1,0:T(8,128)S(1)} %fusion.139), channel_id=1, source_target_pairs={{0,1},{1,2},{2,3},{3,0},{4,5},{5,6},{6,7},{7,4},{8,9},{9,10},{10,1... | collective-permute-start | bytes 294920 | tf_op jit(solution)/shard_map/ppermute | solution.py:51
  53.6 7.5 %copy-start.9 = (pred[4]{0:T(512)(128)(4,1)}, pred[4]{0:T(512)(128)(4,1)S(1)}, u32[]{:S(2)}) copy-start(pred[4]{0:T(512)(128)(4,1)S(1)} %compare_and_fusion) | copy-start | bytes 16
  61.3 15.7 %copy-start.2 = (bf16[512,704]{0,1:T(8,128)(2,1)S(1)}, bf16[512,704]{0,1:T(8,128)(2,1)}, u32[]{:S(2)}) copy-start(bf16[512,704]{0,1:T(8,128)(2,1)} %param.35) | copy-start | bytes 2162692
  62.2 18.7 %copy-start.4 = (bf16[12,2048]{1,0:T(8,128)(2,1)}, bf16[12,2048]{1,0:T(8,128)(2,1)S(1)}, u32[]{:S(2)}) copy-start(bf16[12,2048]{1,0:T(8,128)(2,1)S(1)} %get-tuple-element.12) | copy-start | bytes 147460
  63.3 12.1 %all-to-all-start.2 = ((bf16[8,144,128]{2,1,0:T(8,128)(2,1)}), bf16[8,144,128]{2,1,0:T(8,128)(2,1)S(1)}, u32[]{:S(2)}, u32[]{:S(2)}) async-start(bf16[8,144,128]{2,1,0:T(8,128)(2,1)} %pad_maximum_fusion.2), calls=%async_computation.2 | async-start | bytes 589824 | tf_op jit(solution)/shard_map/all_to_all | solution.py:245
  83.8 23.2 %copy-start.3 = (bf16[704,512]{1,0:T(8,128)(2,1)S(1)}, bf16[704,512]{1,0:T(8,128)(2,1)}, u32[]{:S(2)}) copy-start(bf16[704,512]{1,0:T(8,128)(2,1)} %param.36) | copy-start | bytes 2162692
  86.2 25.3 %copy-start.5 = (f32[3,4,4]{2,1,0:T(4,128)S(1)}, f32[3,4,4]{2,1,0:T(4,128)}, u32[]{:S(2)}) copy-start(f32[3,4,4]{2,1,0:T(4,128)} %param.30) | copy-start | bytes 580
  86.2 8.7 %collective-permute-start.5 = (f32[456,128]{1,0:T(8,128)}, f32[456,128]{1,0:T(8,128)}, u32[]{:S(2)}, u32[]{:S(2)}) collective-permute-start(f32[456,128]{1,0:T(8,128)} %pad_maximum_fusion.6), channel_id=1, source_target_pairs={{0,3},{1,0},{2,1},{3,2},{4,7},{5,4},{6,5},{7,6},{8,11},{9,8},{10,9... | collective-permute-start | bytes 700424 | tf_op jit(solution)/shard_map/ppermute | solution.py:278
  88.7 8.8 %collective-permute-start.4 = (f32[456,128]{1,0:T(8,128)}, f32[456,128]{1,0:T(8,128)}, u32[]{:S(2)}, u32[]{:S(2)}) collective-permute-start(f32[456,128]{1,0:T(8,128)} %pad_maximum_fusion.5), channel_id=1, source_target_pairs={{0,2},{1,3},{2,0},{3,1},{4,6},{5,7},{6,4},{7,5},{8,10},{9,11},{10,... | collective-permute-start | bytes 700424 | tf_op jit(solution)/shard_map/ppermute | solution.py:278
  92.4 7.2 %collective-permute-start.3 = (f32[456,128]{1,0:T(8,128)}, f32[456,128]{1,0:T(8,128)}, u32[]{:S(2)}, u32[]{:S(2)}) collective-permute-start(f32[456,128]{1,0:T(8,128)} %pad_maximum_fusion.4), channel_id=1, source_target_pairs={{0,1},{1,2},{2,3},{3,0},{4,5},{5,6},{6,7},{7,4},{8,9},{9,10},{10,1... | collective-permute-start | bytes 700424 | tf_op jit(solution)/shard_map/ppermute | solution.py:278
  101.0 1.7 %collective-permute-start.8 = (bf16[24,704]{1,0:T(8,128)(2,1)S(1)}, bf16[24,704]{1,0:T(8,128)(2,1)S(1)}, u32[]{:S(2)}, u32[]{:S(2)}) collective-permute-start(bf16[24,704]{1,0:T(8,128)(2,1)S(1)} %fusion.87), channel_id=1, source_target_pairs={{0,3},{1,0},{2,1},{3,2},{4,7},{5,4},{6,5},{7,6},{8,11},{9,8},{10,9... | collective-permute-start | bytes 101384 | tf_op jit(solution)/shard_map/ppermute | solution.py:51
  101.1 4.0 %collective-permute-start.7 = (bf16[24,704]{1,0:T(8,128)(2,1)S(1)}, bf16[24,704]{1,0:T(8,128)(2,1)S(1)}, u32[]{:S(2)}, u32[]{:S(2)}) collective-permute-start(bf16[24,704]{1,0:T(8,128)(2,1)S(1)} %fusion.87), channel_id=1, source_target_pairs={{0,2},{1,3},{2,0},{3,1},{4,6},{5,7},{6,4},{7,5},{8,10},{9,11},{10,... | collective-permute-start | bytes 101384 | tf_op jit(solution)/shard_map/ppermute | solution.py:51
  102.3 3.4 %collective-permute-start.6 = (bf16[24,704]{1,0:T(8,128)(2,1)S(1)}, bf16[24,704]{1,0:T(8,128)(2,1)S(1)}, u32[]{:S(2)}, u32[]{:S(2)}) collective-permute-start(bf16[24,704]{1,0:T(8,128)(2,1)S(1)} %fusion.87), channel_id=1, source_target_pairs={{0,1},{1,2},{2,3},{3,0},{4,5},{5,6},{6,7},{7,4},{8,9},{9,10},{10,1... | collective-permute-start | bytes 101384 | tf_op jit(solution)/shard_map/ppermute | solution.py:51
  108.0 12.2 %all-to-all-start.3 = ((f32[8,72,128]{2,1,0:T(8,128)}), f32[8,72,128]{2,1,0:T(8,128)S(1)}, u32[]{:S(2)}, u32[]{:S(2)}) async-start(f32[8,72,128]{2,1,0:T(8,128)} %pad_maximum_fusion.3), calls=%async_computation.3 | async-start | bytes 589824 | tf_op jit(solution)/shard_map/all_to_all | solution.py:299

commit v8 on v6

--- a/solution.py
+++ b/solution.py
@@ -7,6 +7,7 @@
 
 HD = 128
 TOPK = 4
+LANES = 128
 
 
 NEG = -1e30
@@ -115,8 +116,11 @@
     query_all = lax.all_to_all(query_spread, "req", 0, 0, tiled=True).reshape(
         (req_count * req_rows,) + query_new.shape[1:]
     )
-    key_new = rotate(project(1, normed_late).reshape(head_shape), positions).astype(jnp.bfloat16)
-    value_new = project(2, normed_late).reshape(head_shape).astype(jnp.bfloat16)
+    key_value = jnp.einsum(
+        "rsd,dcf->rscf", normed_late, qkv_weight[:, 1:], preferred_element_type=jnp.float32
+    ) + qkv_bias[1:].astype(jnp.float32)
+    key_new = rotate(key_value[:, :, 0].reshape(head_shape), positions).astype(jnp.bfloat16)
+    value_new = key_value[:, :, 1].reshape(head_shape).astype(jnp.bfloat16)
     slot_ids = req_index * pool_here + jnp.arange(pool_here, dtype=jnp.int32)
     matches = (page_table[:, :, None] == slot_ids[None, None, :]).astype(jnp.int32)
     request_ids = jnp.arange(all_requests, dtype=jnp.int32)
@@ -230,17 +234,17 @@
     w_down_here = expert_w_down[0]
     mixed_cols = lax.dynamic_slice_in_dim(mixed, tp_index * col_share, col_share, 1)
     shared_send = jnp.broadcast_to(mixed_cols[None], (req_count, row_count, col_share))
+    moe_lines = capacity * model_width // LANES
     dispatch = jnp.concatenate(
         [
-            outgoing.reshape(req_count, capacity * model_width),
-            shared_send.reshape(req_count, row_count * col_share),
+            outgoing.reshape(req_count, moe_lines, LANES),
+            shared_send.reshape(req_count, row_count * col_share // LANES, LANES),
         ],
         axis=1,
     )
     received = lax.all_to_all(dispatch, "req", 0, 0, tiled=True)
-    item_count = capacity
-    flat_rows = received[:, : capacity * model_width].reshape(req_count * capacity, model_width)
-    piece = received[:, capacity * model_width :].reshape(req_count * row_count, col_share)
+    flat_rows = received[:, :moe_lines].reshape(req_count * capacity, model_width)
+    piece = received[:, moe_lines:].reshape(req_count * row_count, col_share)
     gate_pre = jnp.dot(flat_rows, w_gate_here, preferred_element_type=jnp.float32)
     up_pre = jnp.dot(flat_rows, w_up_here, preferred_element_type=jnp.float32)
     hidden = (jax.nn.silu(gate_pre) * up_pre).astype(jnp.bfloat16)
@@ -269,18 +273,17 @@
     ).reshape(all_rows, unit_count)
     shared_down = jnp.dot(hidden_all, shared_w_down, preferred_element_type=jnp.float32)
     ey = expert_sum.astype(jnp.bfloat16).astype(jnp.float32)
+    ey_lines = capacity * col_share // LANES
     back_in = jnp.concatenate(
         [
-            ey.reshape(req_count, capacity * col_share),
-            shared_down.reshape(req_count, row_count * col_share),
+            ey.reshape(req_count, ey_lines, LANES),
+            shared_down.reshape(req_count, row_count * col_share // LANES, LANES),
         ],
         axis=1,
     )
     back = lax.all_to_all(back_in, "req", 0, 0, tiled=True)
-    returned = back[:, : capacity * col_share].reshape(expert_count * capacity, col_share)
-    shared_mine = jnp.sum(
-        back[:, capacity * col_share :].reshape(req_count, row_count, col_share), axis=0
-    )
+    returned = back[:, :ey_lines].reshape(expert_count * capacity, col_share)
+    shared_mine = jnp.sum(back[:, ey_lines:].reshape(req_count, row_count, col_share), axis=0)
     moe_out = jnp.dot(combine_map, returned, precision=HIGHEST)
     switch = jax.nn.sigmoid(jnp.dot(mixed, shared_switch, preferred_element_type=jnp.float32))
     resid_mine = lax.dynamic_slice_in_dim(resid, tp_index * col_share, col_share, 1)

time: 125 us -> 125 us (level)
  waiting for transfers between devices: 49.9 us -> 46.3 us
  starting transfers between devices: 23.6 us -> 26.3 us
    all_to_all x1, waiting for transfers between devices: 2.98 us -> 0.01 us  [per_device(): lax.all_to_all(query_spread, 'req', 0, 0, tiled=True)]
    dot_general x0 -> x1, matrix products: none -> 2.86 us  [per_device(): jnp.einsum('rsd,dcf->rscf', normed_late, qkv_weight[:, 1:], preferred_ele...]
    all_to_all x1, starting transfers between devices: 3.42 us -> 5.99 us  [per_device(): lax.all_to_all(packed, 'req', 0, 0, tiled=True)]
    dot_general x2 -> x1, matrix products: 3.97 us -> 1.98 us  [project(): jnp.einsum('rsd,df->rsf', rows, qkv_weight[:, part], preferred_element_ty...]
    dot_general x1, matrix products: 2.16 us -> 0.21 us  [per_device(): jnp.einsum('rsht,rthd->rshd', new_weights.astype(jnp.bfloat16), value_new...]
    concatenate x1 -> x2, other arithmetic: 0.02 us -> 1.45 us  [the longest x1 0.73 us: per_device(): jnp.concatenate([outgoing.reshape(req_count, moe_lines, LANES), shared_se...]
    all_to_all x2 -> x0, local copies, waits for them, and re-layouts: 1.42 us -> none  [the longest x1 0.91 us: per_device(): back = lax.all_to_all(back_in, 'req', 0, 0, tiled=True)]
    unnamed x36 -> x22, local copies, waits for them, and re-layouts: 4.17 us -> 3.55 us
  transfers between devices with their start and end apart: 13 -> 13, of which waited for: 11 -> 11; matrix products, arithmetic and copies ran while one was open for 4% -> 8% of each run, Pallas kernels for 0% -> 0%
where the time goes in v8:
time: 125 us; the launch traced here: 124 us
  waiting for transfers between devices  46.3 us (37%)
  matrix products  26.4 us (21%)
  starting transfers between devices  26.3 us (21%)
  local copies, waits for them, and re-layouts  13.4 us (11%)
  other arithmetic  11 us (9%)
    ppermute x9, waiting for transfers between devices, shift_exchange(): pieces.append(lax.ppermute(send, axis, pairs))  19.6 us
    all_to_all x1, waiting for transfers between devices, per_device(): back = lax.all_to_all(back_in, 'req', 0, 0, tiled=True)  9.61 us
    all_to_all x1, waiting for transfers between devices, per_device(): lax.all_to_all(packed, 'req', 0, 0, tiled=True)  8.66 us
    all_to_all x1, waiting for transfers between devices, per_device(): received = lax.all_to_all(dispatch, 'req', 0, 0, tiled=True)  8.44 us
    all_to_all x1, starting transfers between devices, per_device(): lax.all_to_all(query_spread, 'req', 0, 0, tiled=True)  7.28 us
    all_to_all x1, starting transfers between devices, per_device(): lax.all_to_all(packed, 'req', 0, 0, tiled=True)  5.99 us
    ppermute x9, starting transfers between devices, shift_exchange(): pieces.append(lax.ppermute(send, axis, pairs))  5.87 us
    dot_general x1, matrix products, per_device(): jnp.einsum('pshd,pkhd->pshk', page_queries, page_keys, preferred_element_...  5.41 us
  transfers between devices with their start and end apart: 13, of which 11 were waited for; matrix products, arithmetic and copies ran while one was open for 8% of the time, Pallas kernels for 0%

profile of v8, /device:TPU:0, one launch (start us, length us, event | category | flops | bytes accessed | tf_op | source)
XLA Modules:
  0.0 124.1 jit_solution(7964635326891014698)
XLA Ops:
  4.3 2.0 %fusion.45 = f32[3,4,4,128]{3,1,2,0:T(4,128)S(1)} fusion(bf16[3,4,2048]{2,1,0:T(4,128)(2,1)S(1)} %multiply_convert_fusion.1, bf16[2048,3,512]{2,0,1:T(8,128)(2,1)} %param.21, f32[512]{0:T(512)S(1)} %bitcast.209), kind=kOutput, calls=%fused_computation.35 | convolution fusion | flops 25171968 | bytes 2172928 | tf_op jit(solution)/shard_map/rsd,df->rsf/dot_general | solution.py:109
  7.1 7.3 %all-to-all-start = ((bf16[8,3,4,4,128]{4,3,2,1,0:T(4,128)(2,1)}), bf16[8,3,4,4,128]{4,3,2,1,0:T(4,128)(2,1)S(1)}, u32[]{:S(2)}, u32[]{:S(2)}) async-start(bf16[8,3,4,4,128]{4,3,2,1,0:T(4,128)(2,1)} %broadcast_in_dim.99), calls=%async_computation | async-start | bytes 196608 | tf_op jit(solution)/shard_map/all_to_all | solution.py:116
  17.0 1.4 %gather_fusion = s32[40]{0:T(128)S(1)} fusion(s32[24]{0:T(128)} %param.27, s32[1024]{0:T(1024)S(1)} %pad_clamp_fusion.1), kind=kCustom, calls=%fused_computation | custom fusion | bytes 480 | tf_op jit(solution)/shard_map/gather | solution.py:132
  18.8 2.9 %fusion.34 = f32[3,4,2,512]{3,1,2,0:T(4,128)S(1)} fusion(bf16[2048,3,512]{2,0,1:T(8,128)(2,1)} %param.21, bf16[3,4,2048]{2,1,0:T(4,128)(2,1)S(1)} %multiply_convert_fusion.1, f32[2,512]{1,0:T(2,128)S(1)} %slice_convert_fusion.2), kind=kOutput, calls=%fused_computation.29 | convolution fusion | flops 50343936 | bytes 4296704 | tf_op jit(solution)/shard_map/rsd,dcf->rscf/dot_general | solution.py:119
  22.9 5.4 %fusion.138 = (f32[40,4,4]{1,2,0:T(4,128)S(1)}, f32[40,4,4,128]{3,1,2,0:T(4,128)S(1)}) fusion(bf16[40,4,4,128]{3,2,1,0:T(4,128)(2,1)S(1)} %gather_fusion.1, pred[40,128]{1,0:T(8,128)(4,1)S(1)} %fusion.99, bf16[40,128,512]{2,1,0:T(8,128)(2,1)} %param.24), kind=kOutput, calls=%fused_computation.200 | convolution fusion | flops 21216640 | bytes 5742080 | tf_op jit(solution)/shard_map/pshd,pkhd->pshk/dot_general | solution.py:137
  29.1 4.0 %fusion.22 = f32[40,4,4,128]{3,1,2,0:T(4,128)S(1)} fusion(f32[40,4,4,128]{3,1,2,0:T(4,128)S(1)} %get-tuple-element.33, f32[40,4,4]{1,2,0:T(4,128)S(1)} %get-tuple-element.32, pred[40,128]{1,0:T(8,128)(4,1)S(1)} %fusion.99, bf16[40,128,512]{2,1,0:T(8,128)(2,1)} %param.25), kind=kOutput, calls=%fused_computation.25 | convolution fusion | flops 21217280 | bytes 5905920 | tf_op jit(solution)/shard_map/pshk,pkhd->pshd/dot_general | solution.py:145
  35.3 6.0 %all-to-all-start.1 = ((f32[24,17,128]{2,1,0:T(8,128)}), f32[24,17,128]{2,1,0:T(8,128)S(1)}, u32[]{:S(2)}, u32[]{:S(2)}) async-start(f32[24,17,128]{2,1,0:T(8,128)} %pad_maximum_fusion.2), calls=%async_computation.1 | async-start | bytes 589824 | tf_op jit(solution)/shard_map/all_to_all | solution.py:169
  41.7 8.7 %all-to-all-done.1 = f32[24,17,128]{2,1,0:T(8,128)S(1)} async-done(((f32[24,17,128]{2,1,0:T(8,128)}), f32[24,17,128]{2,1,0:T(8,128)S(1)}, u32[]{:S(2)}, u32[]{:S(2)}) %all-to-all-start.1) | async-done | bytes 208928 | tf_op jit(solution)/shard_map/all_to_all | solution.py:169
  51.9 1.5 %collective-permute-start.1 = (f32[12,2048]{1,0:T(8,128)S(1)}, f32[12,2048]{1,0:T(8,128)S(1)}, u32[]{:S(2)}, u32[]{:S(2)}) collective-permute-start(f32[12,2048]{1,0:T(8,128)S(1)} %fusion.140), channel_id=1, source_target_pairs={{0,2},{1,3},{2,0},{3,1},{4,6},{5,7},{6,4},{7,5},{8,10},{9,11},{10,... | collective-permute-start | bytes 294920 | tf_op jit(solution)/shard_map/ppermute | solution.py:51
  54.7 5.7 %collective-permute-done.1 = f32[12,2048]{1,0:T(8,128)S(1)} collective-permute-done((f32[12,2048]{1,0:T(8,128)S(1)}, f32[12,2048]{1,0:T(8,128)S(1)}, u32[]{:S(2)}, u32[]{:S(2)}) %collective-permute-start.1) | collective-permute-done | bytes 98336 | tf_op jit(solution)/shard_map/ppermute | solution.py:51
  63.9 3.6 %all-to-all-start.2 = ((bf16[8,144,128]{2,1,0:T(8,128)(2,1)}), bf16[8,144,128]{2,1,0:T(8,128)(2,1)S(1)}, u32[]{:S(2)}, u32[]{:S(2)}) async-start(bf16[8,144,128]{2,1,0:T(8,128)(2,1)} %pad_maximum_fusion.3), calls=%async_computation.2 | async-start | bytes 589824 | tf_op jit(solution)/shard_map/all_to_all | solution.py:245
  67.5 8.4 %all-to-all-done.2 = bf16[8,144,128]{2,1,0:T(8,128)(2,1)S(1)} async-done(((bf16[8,144,128]{2,1,0:T(8,128)(2,1)}), bf16[8,144,128]{2,1,0:T(8,128)(2,1)S(1)}, u32[]{:S(2)}, u32[]{:S(2)}) %all-to-all-start.2) | async-done | bytes 294944 | tf_op jit(solution)/shard_map/all_to_all | solution.py:245
  76.2 2.6 %fusion.17 = f32[48,352]{1,0:T(8,128)} fusion(bf16[48,2048]{1,0:T(8,128)(2,1)S(1)} %reshape.438, bf16[1,2048,352]{1,2,0:T(8,128)(2,1)} %param.31), kind=kOutput, calls=%fused_computation.22 | convolution fusion | flops 69206016 | bytes 1705984 | tf_op jit(solution)/shard_map/dot_general | solution.py:248
  78.7 3.0 %fusion.19 = f32[1,4,48,512]{3,2,1,0:T(8,128)S(1)} fusion(bf16[44,4,8,512]{3,2,1,0:T(8,128)(2,1)} %bitcast.187, bf16[48,2048]{1,0:T(8,128)(2,1)S(1)} %reshape.438, bf16[1,2048,352]{1,2,0:T(8,128)(2,1)} %param.32, f32[48,352]{1,0:T(8,128)} %fusion.17), kind=kOutput, calls=%fused_computation.24 | convolution fusion | flops 138513408 | bytes 3540992 | tf_op jit(solution)/shard_map/dot_general | solution.py:251
  83.1 1.5 %fusion.141 = f32[96,704]{1,0:T(8,128)S(1)} fusion(bf16[96,512]{1,0:T(8,128)(2,1)S(1)} %reshape.440, bf16[512,704]{0,1:T(8,128)(2,1)} %param.34), kind=kOutput, calls=%fused_computation.203 | convolution fusion | flops 69206016 | bytes 1089536 | tf_op jit(solution)/shard_map/dot_general | solution.py:254
  86.2 1.6 %constant_dynamic-slice_fusion.1 = (f32[1,58368]{1,0:T(1,128)}, f32[1,58368]{1,0:T(1,128)}, f32[1,58368]{1,0:T(1,128)S(1)}, f32[1,58368]{1,0:T(1,128)S(1)}) fusion(f32[4,58368]{1,0:T(4,128)S(1)} %constant_dynamic-update-slice_fusion, s32[]{:T(128)S(6)} %select_n.146, s32[]{:T(128)S(6)} %select_n.150, s32[]{:T(128)S(6)} %select_n.148, s32[]{:T(128)S(6)} %select_n.144), kind=kLoop, calls=%fused_computation.175 | loop fusion | bytes 1867792 | tf_op jit(solution)/shard_map/jit(dynamic_index_in_dim)/dynamic_slice | solution.py:47
  89.6 4.1 %collective-permute-done.5 = f32[58368]{0:T(1024)} collective-permute-done((f32[58368]{0:T(1024)}, f32[58368]{0:T(1024)}, u32[]{:S(2)}, u32[]{:S(2)}) %collective-permute-start.5) | collective-permute-done | bytes 233504 | tf_op jit(solution)/shard_map/ppermute | solution.py:51
  93.7 2.4 %collective-permute-done.3 = f32[58368]{0:T(1024)} collective-permute-done((f32[58368]{0:T(1024)}, f32[58368]{0:T(1024)}, u32[]{:S(2)}, u32[]{:S(2)}) %collective-permute-start.3) | collective-permute-done | bytes 233504 | tf_op jit(solution)/shard_map/ppermute | solution.py:51
  96.1 4.4 %collective-permute-done.4 = f32[58368]{0:T(1024)} collective-permute-done((f32[58368]{0:T(1024)S(1)}, f32[58368]{0:T(1024)}, u32[]{:S(2)}, u32[]{:S(2)}) %collective-permute-start.4) | collective-permute-done | bytes 233504 | tf_op jit(solution)/shard_map/ppermute | solution.py:51
  100.5 1.2 add_add_fusion
  102.6 1.7 %collective-permute-start.8 = (bf16[24,704]{1,0:T(8,128)(2,1)S(1)}, bf16[24,704]{1,0:T(8,128)(2,1)S(1)}, u32[]{:S(2)}, u32[]{:S(2)}) collective-permute-start(bf16[24,704]{1,0:T(8,128)(2,1)S(1)} %fusion.88), channel_id=1, source_target_pairs={{0,3},{1,0},{2,1},{3,2},{4,7},{5,4},{6,5},{7,6},{8,11},{9,8},{10,9... | collective-permute-start | bytes 101384 | tf_op jit(solution)/shard_map/ppermute | solution.py:51
  104.4 1.7 %collective-permute-done.7 = bf16[24,704]{1,0:T(8,128)(2,1)S(1)} collective-permute-done((bf16[24,704]{1,0:T(8,128)(2,1)S(1)}, bf16[24,704]{1,0:T(8,128)(2,1)S(1)}, u32[]{:S(2)}, u32[]{:S(2)}) %collective-permute-start.7) | collective-permute-done | bytes 33824 | tf_op jit(solution)/shard_map/ppermute | solution.py:51
  107.9 3.6 %all-to-all-start.3 = ((f32[8,72,128]{2,1,0:T(8,128)}), f32[8,72,128]{2,1,0:T(8,128)S(1)}, u32[]{:S(2)}, u32[]{:S(2)}) async-start(f32[8,72,128]{2,1,0:T(8,128)} %pad_maximum_fusion.4), calls=%async_computation.3 | async-start | bytes 589824 | tf_op jit(solution)/shard_map/all_to_all | solution.py:284
  112.9 9.6 %all-to-all-done.3 = f32[8,72,128]{2,1,0:T(8,128)S(1)} async-done(((f32[8,72,128]{2,1,0:T(8,128)}), f32[8,72,128]{2,1,0:T(8,128)S(1)}, u32[]{:S(2)}, u32[]{:S(2)}) %all-to-all-start.3) | async-done | bytes 294944 | tf_op jit(solution)/shard_map/all_to_all | solution.py:284
  (144 shorter events, 29.4 us)
Async XLA Ops:
  0.0 51.5 %copy-start = (bf16[512,2048]{1,0:T(8,128)(2,1)S(1)}, bf16[512,2048]{1,0:T(8,128)(2,1)}, u32[]{:S(2)}) copy-start(bf16[512,2048]{1,0:T(8,128)(2,1)} %param.23) | copy-start | bytes 6291460
  7.1 15.0 %all-to-all-start = ((bf16[8,3,4,4,128]{4,3,2,1,0:T(4,128)(2,1)}), bf16[8,3,4,4,128]{4,3,2,1,0:T(4,128)(2,1)S(1)}, u32[]{:S(2)}, u32[]{:S(2)}) async-start(bf16[8,3,4,4,128]{4,3,2,1,0:T(4,128)(2,1)} %broadcast_in_dim.99), calls=%async_computation | async-start | bytes 196608 | tf_op jit(solution)/shard_map/all_to_all | solution.py:116
  29.1 12.2 %copy-start.1 = (bf16[3,4,2048]{2,1,0:T(4,128)(2,1)S(1)}, bf16[3,4,2048]{2,1,0:T(4,128)(2,1)}, u32[]{:S(2)}) copy-start(bf16[3,4,2048]{2,1,0:T(4,128)(2,1)} %param.19) | copy-start | bytes 147460
  29.1 12.2 %copy-start.6 = (bf16[2048]{0:T(1024)(128)(2,1)S(1)}, bf16[2048]{0:T(1024)(128)(2,1)}, u32[]{:S(2)}) copy-start(bf16[2048]{0:T(1024)(128)(2,1)} %param.28) | copy-start | bytes 12292
  35.3 15.0 %all-to-all-start.1 = ((f32[24,17,128]{2,1,0:T(8,128)}), f32[24,17,128]{2,1,0:T(8,128)S(1)}, u32[]{:S(2)}, u32[]{:S(2)}) async-start(f32[24,17,128]{2,1,0:T(8,128)} %pad_maximum_fusion.2), calls=%async_computation.1 | async-start | bytes 589824 | tf_op jit(solution)/shard_map/all_to_all | solution.py:169
  51.9 2.9 %collective-permute-start.2 = (f32[12,2048]{1,0:T(8,128)S(1)}, f32[12,2048]{1,0:T(8,128)S(1)}, u32[]{:S(2)}, u32[]{:S(2)}) collective-permute-start(f32[12,2048]{1,0:T(8,128)S(1)} %fusion.140), channel_id=1, source_target_pairs={{0,3},{1,0},{2,1},{3,2},{4,7},{5,4},{6,5},{7,6},{8,11},{9,8},{10,9... | collective-permute-start | bytes 294920 | tf_op jit(solution)/shard_map/ppermute | solution.py:51
  51.9 8.6 %collective-permute-start.1 = (f32[12,2048]{1,0:T(8,128)S(1)}, f32[12,2048]{1,0:T(8,128)S(1)}, u32[]{:S(2)}, u32[]{:S(2)}) collective-permute-start(f32[12,2048]{1,0:T(8,128)S(1)} %fusion.140), channel_id=1, source_target_pairs={{0,2},{1,3},{2,0},{3,1},{4,6},{5,7},{6,4},{7,5},{8,10},{9,11},{10,... | collective-permute-start | bytes 294920 | tf_op jit(solution)/shard_map/ppermute | solution.py:51
  53.4 7.1 %collective-permute-start = (f32[12,2048]{1,0:T(8,128)S(1)}, f32[12,2048]{1,0:T(8,128)S(1)}, u32[]{:S(2)}, u32[]{:S(2)}) collective-permute-start(f32[12,2048]{1,0:T(8,128)S(1)} %fusion.140), channel_id=1, source_target_pairs={{0,1},{1,2},{2,3},{3,0},{4,5},{5,6},{6,7},{7,4},{8,9},{9,10},{10,1... | collective-permute-start | bytes 294920 | tf_op jit(solution)/shard_map/ppermute | solution.py:51
  62.2 0.6 copy-start.4
  63.2 19.6 %copy-start.2 = (bf16[512,704]{0,1:T(8,128)(2,1)S(1)}, bf16[512,704]{0,1:T(8,128)(2,1)}, u32[]{:S(2)}) copy-start(bf16[512,704]{0,1:T(8,128)(2,1)} %param.35) | copy-start | bytes 2162692
  63.9 12.1 %all-to-all-start.2 = ((bf16[8,144,128]{2,1,0:T(8,128)(2,1)}), bf16[8,144,128]{2,1,0:T(8,128)(2,1)S(1)}, u32[]{:S(2)}, u32[]{:S(2)}) async-start(bf16[8,144,128]{2,1,0:T(8,128)(2,1)} %pad_maximum_fusion.3), calls=%async_computation.2 | async-start | bytes 589824 | tf_op jit(solution)/shard_map/all_to_all | solution.py:245
  85.0 22.0 %copy-start.3 = (bf16[704,512]{1,0:T(8,128)(2,1)S(1)}, bf16[704,512]{1,0:T(8,128)(2,1)}, u32[]{:S(2)}) copy-start(bf16[704,512]{1,0:T(8,128)(2,1)} %param.36) | copy-start | bytes 2162692
  86.1 25.4 %copy-start.5 = (f32[3,4,4]{2,1,0:T(4,128)S(1)}, f32[3,4,4]{2,1,0:T(4,128)}, u32[]{:S(2)}) copy-start(f32[3,4,4]{2,1,0:T(4,128)} %param.30) | copy-start | bytes 580
  86.1 25.5 %copy-start.7 = (bf16[2048]{0:T(1024)(128)(2,1)S(1)}, bf16[2048]{0:T(1024)(128)(2,1)}, u32[]{:S(2)}) copy-start(bf16[2048]{0:T(1024)(128)(2,1)} %param.37) | copy-start | bytes 12292
  87.8 5.9 %collective-permute-start.5 = (f32[58368]{0:T(1024)}, f32[58368]{0:T(1024)}, u32[]{:S(2)}, u32[]{:S(2)}) collective-permute-start(f32[58368]{0:T(1024)} %bitcast.45), channel_id=1, source_target_pairs={{0,3},{1,0},{2,1},{3,2},{4,7},{5,4},{6,5},{7,6},{8,11},{9,8},{10,9... | collective-permute-start | bytes 700424 | tf_op jit(solution)/shard_map/ppermute | solution.py:51
  87.8 8.3 %collective-permute-start.3 = (f32[58368]{0:T(1024)}, f32[58368]{0:T(1024)}, u32[]{:S(2)}, u32[]{:S(2)}) collective-permute-start(f32[58368]{0:T(1024)} %bitcast.43), channel_id=1, source_target_pairs={{0,1},{1,2},{2,3},{3,0},{4,5},{5,6},{6,7},{7,4},{8,9},{9,10},{10,1... | collective-permute-start | bytes 700424 | tf_op jit(solution)/shard_map/ppermute | solution.py:51
  88.3 12.2 %collective-permute-start.4 = (f32[58368]{0:T(1024)S(1)}, f32[58368]{0:T(1024)}, u32[]{:S(2)}, u32[]{:S(2)}) collective-permute-start(f32[58368]{0:T(1024)S(1)} %bitcast.195), channel_id=1, source_target_pairs={{0,2},{1,3},{2,0},{3,1},{4,6},{5,7},{6,4},{7,5},{8,10},{9,11},{10,... | collective-permute-start | bytes 700424 | tf_op jit(solution)/shard_map/ppermute | solution.py:51
  101.8 4.3 %collective-permute-start.7 = (bf16[24,704]{1,0:T(8,128)(2,1)S(1)}, bf16[24,704]{1,0:T(8,128)(2,1)S(1)}, u32[]{:S(2)}, u32[]{:S(2)}) collective-permute-start(bf16[24,704]{1,0:T(8,128)(2,1)S(1)} %fusion.88), channel_id=1, source_target_pairs={{0,2},{1,3},{2,0},{3,1},{4,6},{5,7},{6,4},{7,5},{8,10},{9,11},{10,... | collective-permute-start | bytes 101384 | tf_op jit(solution)/shard_map/ppermute | solution.py:51
  102.6 3.7 %collective-permute-start.6 = (bf16[24,704]{1,0:T(8,128)(2,1)S(1)}, bf16[24,704]{1,0:T(8,128)(2,1)S(1)}, u32[]{:S(2)}, u32[]{:S(2)}) collective-permute-start(bf16[24,704]{1,0:T(8,128)(2,1)S(1)} %fusion.88), channel_id=1, source_target_pairs={{0,1},{1,2},{2,3},{3,0},{4,5},{5,6},{6,7},{7,4},{8,9},{9,10},{10,1... | collective-permute-start | bytes 101384 | tf_op jit(solution)/shard_map/ppermute | solution.py:51
  102.6 3.6 %collective-permute-start.8 = (bf16[24,704]{1,0:T(8,128)(2,1)S(1)}, bf16[24,704]{1,0:T(8,128)(2,1)S(1)}, u32[]{:S(2)}, u32[]{:S(2)}) collective-permute-start(bf16[24,704]{1,0:T(8,128)(2,1)S(1)} %fusion.88), channel_id=1, source_target_pairs={{0,3},{1,0},{2,1},{3,2},{4,7},{5,4},{6,5},{7,6},{8,11},{9,8},{10,9... | collective-permute-start | bytes 101384 | tf_op jit(solution)/shard_map/ppermute | solution.py:51
  107.9 14.5 %all-to-all-start.3 = ((f32[8,72,128]{2,1,0:T(8,128)}), f32[8,72,128]{2,1,0:T(8,128)S(1)}, u32[]{:S(2)}, u32[]{:S(2)}) async-start(f32[8,72,128]{2,1,0:T(8,128)} %pad_maximum_fusion.4), calls=%async_computation.3 | async-start | bytes 589824 | tf_op jit(solution)/shard_map/all_to_all | solution.py:284

commit v9 on v8

--- a/solution.py
+++ b/solution.py
@@ -245,12 +245,7 @@
     received = lax.all_to_all(dispatch, "req", 0, 0, tiled=True)
     flat_rows = received[:, :moe_lines].reshape(req_count * capacity, model_width)
     piece = received[:, moe_lines:].reshape(req_count * row_count, col_share)
-    gate_pre = jnp.dot(flat_rows, w_gate_here, preferred_element_type=jnp.float32)
-    up_pre = jnp.dot(flat_rows, w_up_here, preferred_element_type=jnp.float32)
-    hidden = (jax.nn.silu(gate_pre) * up_pre).astype(jnp.bfloat16)
-    partial_out = jnp.dot(hidden, w_down_here, preferred_element_type=jnp.float32)
     expert_rows = req_count * capacity
-    partial_split = partial_out.reshape(expert_rows, tp_count, col_share).transpose(1, 0, 2)
     gate_part = jnp.dot(piece, shared_w_gate, preferred_element_type=jnp.float32)
     up_part = jnp.dot(piece, shared_w_up, preferred_element_type=jnp.float32)
     unit_count = shared_w_gate.shape[1]
@@ -259,12 +254,19 @@
     shared_pre = jnp.concatenate([gate_part, up_part], axis=1).reshape(
         tp_count, share_rows * 2 * unit_count
     )
-    reduce_in = jnp.concatenate(
-        [partial_split.reshape(tp_count, expert_rows * col_share), shared_pre], axis=1
-    )
-    reduce_out = sum(shift_exchange(reduce_in, "tp", tp_count))
-    expert_sum = reduce_out[: expert_rows * col_share].reshape(expert_rows, col_share)
-    shared_sum = reduce_out[expert_rows * col_share :].reshape(share_rows, 2 * unit_count)
+    flat_rows, shared_pre = lax.optimization_barrier((flat_rows, shared_pre))
+    gate_pre = jnp.dot(flat_rows, w_gate_here, preferred_element_type=jnp.float32)
+    up_pre = jnp.dot(flat_rows, w_up_here, preferred_element_type=jnp.float32)
+    hidden = (jax.nn.silu(gate_pre) * up_pre).astype(jnp.bfloat16)
+    shared_sum = sum(shift_exchange(shared_pre, "tp", tp_count)).reshape(
+        share_rows, 2 * unit_count
+    )
+    hidden, shared_sum = lax.optimization_barrier((hidden, shared_sum))
+    partial_out = jnp.dot(hidden, w_down_here, preferred_element_type=jnp.float32)
+    partial_split = partial_out.reshape(expert_rows, tp_count, col_share).transpose(1, 0, 2)
+    expert_sum = sum(
+        shift_exchange(partial_split.reshape(tp_count, expert_rows * col_share), "tp", tp_count)
+    ).reshape(expert_rows, col_share)
     shared_hidden = (jax.nn.silu(shared_sum[:, :unit_count]) * shared_sum[:, unit_count:]).astype(
         jnp.bfloat16
     )

time: 125 us -> 118 us (0.944)
  waiting for transfers between devices: 46.3 us -> 39.6 us
  starting transfers between devices: 26.3 us -> 28.3 us
  local copies, waits for them, and re-layouts: 13.4 us -> 11.5 us
    ppermute x9 -> x12, waiting for transfers between devices: 19.6 us -> 14 us  [shift_exchange(): pieces.append(lax.ppermute(send, axis, pairs))]
    unnamed x22 -> x33, local copies, waits for them, and re-layouts: 3.55 us -> 1.14 us
    ppermute x9 -> x12, starting transfers between devices: 5.87 us -> 7.81 us  [shift_exchange(): pieces.append(lax.ppermute(send, axis, pairs))]
    dot_general x0 -> x1, matrix products: none -> 1.92 us  [per_device(): up_pre = jnp.dot(flat_rows, w_up_here, preferred_element_type=jnp.float32)]
    dot_general x1, matrix products: 2.97 us -> 1.71 us  [per_device(): jnp.dot(hidden, w_down_here, preferred_element_type=jnp.float32)]
  transfers between devices with their start and end apart: 13 -> 16, of which waited for: 11 -> 10; matrix products, arithmetic and copies ran while one was open for 8% -> 15% of each run, Pallas kernels for 0% -> 0%
where the time goes in v9:
time: 118 us; the launch traced here: 117 us
  waiting for transfers between devices  39.6 us (34%)
  starting transfers between devices  28.3 us (24%)
  matrix products  25.6 us (22%)
  local copies, waits for them, and re-layouts  11.5 us (10%)
  other arithmetic  10.9 us (9%)
    ppermute x12, waiting for transfers between devices, shift_exchange(): pieces.append(lax.ppermute(send, axis, pairs))  14 us
    all_to_all x1, waiting for transfers between devices, per_device(): back = lax.all_to_all(back_in, 'req', 0, 0, tiled=True)  9.32 us
    all_to_all x1, waiting for transfers between devices, per_device(): lax.all_to_all(packed, 'req', 0, 0, tiled=True)  8.64 us
    ppermute x12, starting transfers between devices, shift_exchange(): pieces.append(lax.ppermute(send, axis, pairs))  7.81 us
    all_to_all x1, waiting for transfers between devices, per_device(): received = lax.all_to_all(dispatch, 'req', 0, 0, tiled=True)  7.6 us
    all_to_all x1, starting transfers between devices, per_device(): lax.all_to_all(query_spread, 'req', 0, 0, tiled=True)  7.28 us
    all_to_all x1, starting transfers between devices, per_device(): lax.all_to_all(packed, 'req', 0, 0, tiled=True)  5.99 us
    dot_general x1, matrix products, per_device(): jnp.einsum('pshd,pkhd->pshk', page_queries, page_keys, preferred_element_...  5.41 us
  transfers between devices with their start and end apart: 16, of which 10 were waited for; matrix products, arithmetic and copies ran while one was open for 15% of the time, Pallas kernels for 0%

profile of v9, /device:TPU:0, one launch (start us, length us, event | category | flops | bytes accessed | tf_op | source)
XLA Modules:
  0.0 116.6 jit_solution(4281601701743318173)
XLA Ops:
  4.3 2.0 %fusion.42 = f32[3,4,4,128]{3,1,2,0:T(4,128)S(1)} fusion(bf16[3,4,2048]{2,1,0:T(4,128)(2,1)S(1)} %multiply_convert_fusion.1, bf16[2048,3,512]{2,0,1:T(8,128)(2,1)} %param.21, f32[512]{0:T(512)S(1)} %bitcast.212), kind=kOutput, calls=%fused_computation.34 | convolution fusion | flops 25171968 | bytes 2172928 | tf_op jit(solution)/shard_map/rsd,df->rsf/dot_general | solution.py:109
  7.1 7.3 %all-to-all-start = ((bf16[8,3,4,4,128]{4,3,2,1,0:T(4,128)(2,1)}), bf16[8,3,4,4,128]{4,3,2,1,0:T(4,128)(2,1)S(1)}, u32[]{:S(2)}, u32[]{:S(2)}) async-start(bf16[8,3,4,4,128]{4,3,2,1,0:T(4,128)(2,1)} %broadcast_in_dim.99), calls=%async_computation | async-start | bytes 196608 | tf_op jit(solution)/shard_map/all_to_all | solution.py:116
  17.0 1.4 %gather_fusion = s32[40]{0:T(128)S(1)} fusion(s32[24]{0:T(128)} %param.27, s32[1024]{0:T(1024)S(1)} %pad_clamp_fusion.1), kind=kCustom, calls=%fused_computation | custom fusion | bytes 480 | tf_op jit(solution)/shard_map/gather | solution.py:132
  18.8 2.9 %fusion.34 = f32[3,4,2,512]{3,1,2,0:T(4,128)S(1)} fusion(bf16[2048,3,512]{2,0,1:T(8,128)(2,1)} %param.21, bf16[3,4,2048]{2,1,0:T(4,128)(2,1)S(1)} %multiply_convert_fusion.1, f32[2,512]{1,0:T(2,128)S(1)} %slice_convert_fusion.1), kind=kOutput, calls=%fused_computation.29 | convolution fusion | flops 50343936 | bytes 4296704 | tf_op jit(solution)/shard_map/rsd,dcf->rscf/dot_general | solution.py:119
  22.9 5.4 %fusion.126 = (f32[40,4,4]{1,2,0:T(4,128)S(1)}, f32[40,4,4,128]{3,1,2,0:T(4,128)S(1)}) fusion(bf16[40,4,4,128]{3,2,1,0:T(4,128)(2,1)S(1)} %gather_fusion.1, pred[40,128]{1,0:T(8,128)(4,1)S(1)} %fusion.88, bf16[40,128,512]{2,1,0:T(8,128)(2,1)} %param.24), kind=kOutput, calls=%fused_computation.194 | convolution fusion | flops 21216640 | bytes 5742080 | tf_op jit(solution)/shard_map/pshd,pkhd->pshk/dot_general | solution.py:137
  29.2 4.0 %fusion.22 = f32[40,4,4,128]{3,1,2,0:T(4,128)S(1)} fusion(f32[40,4,4,128]{3,1,2,0:T(4,128)S(1)} %get-tuple-element.45, f32[40,4,4]{1,2,0:T(4,128)S(1)} %get-tuple-element.44, pred[40,128]{1,0:T(8,128)(4,1)S(1)} %fusion.88, bf16[40,128,512]{2,1,0:T(8,128)(2,1)} %param.25), kind=kOutput, calls=%fused_computation.25 | convolution fusion | flops 21217280 | bytes 5905920 | tf_op jit(solution)/shard_map/pshk,pkhd->pshd/dot_general | solution.py:145
  35.3 6.0 %all-to-all-start.1 = ((f32[24,17,128]{2,1,0:T(8,128)}), f32[24,17,128]{2,1,0:T(8,128)S(1)}, u32[]{:S(2)}, u32[]{:S(2)}) async-start(f32[24,17,128]{2,1,0:T(8,128)} %pad_maximum_fusion.2), calls=%async_computation.1 | async-start | bytes 589824 | tf_op jit(solution)/shard_map/all_to_all | solution.py:169
  41.7 8.6 %all-to-all-done.1 = f32[24,17,128]{2,1,0:T(8,128)S(1)} async-done(((f32[24,17,128]{2,1,0:T(8,128)}), f32[24,17,128]{2,1,0:T(8,128)S(1)}, u32[]{:S(2)}, u32[]{:S(2)}) %all-to-all-start.1) | async-done | bytes 208928 | tf_op jit(solution)/shard_map/all_to_all | solution.py:169
  51.9 1.5 %collective-permute-start.1 = (f32[12,2048]{1,0:T(8,128)S(1)}, f32[12,2048]{1,0:T(8,128)S(1)}, u32[]{:S(2)}, u32[]{:S(2)}) collective-permute-start(f32[12,2048]{1,0:T(8,128)S(1)} %fusion.128), channel_id=1, source_target_pairs={{0,2},{1,3},{2,0},{3,1},{4,6},{5,7},{6,4},{7,5},{8,10},{9,11},{10,... | collective-permute-start | bytes 294920 | tf_op jit(solution)/shard_map/ppermute | solution.py:51
  54.7 5.7 %collective-permute-done.1 = f32[12,2048]{1,0:T(8,128)S(1)} collective-permute-done((f32[12,2048]{1,0:T(8,128)S(1)}, f32[12,2048]{1,0:T(8,128)S(1)}, u32[]{:S(2)}, u32[]{:S(2)}) %collective-permute-start.1) | collective-permute-done | bytes 98336 | tf_op jit(solution)/shard_map/ppermute | solution.py:51
  63.4 3.6 %all-to-all-start.2 = ((bf16[8,144,128]{2,1,0:T(8,128)(2,1)}), bf16[8,144,128]{2,1,0:T(8,128)(2,1)S(1)}, u32[]{:S(2)}, u32[]{:S(2)}) async-start(bf16[8,144,128]{2,1,0:T(8,128)(2,1)} %pad_maximum_fusion.3), calls=%async_computation.2 | async-start | bytes 589824 | tf_op jit(solution)/shard_map/all_to_all | solution.py:245
  67.8 7.6 %all-to-all-done.2 = bf16[8,144,128]{2,1,0:T(8,128)(2,1)S(1)} async-done(((bf16[8,144,128]{2,1,0:T(8,128)(2,1)}), bf16[8,144,128]{2,1,0:T(8,128)(2,1)S(1)}, u32[]{:S(2)}, u32[]{:S(2)}) %all-to-all-start.2) | async-done | bytes 294944 | tf_op jit(solution)/shard_map/all_to_all | solution.py:245
  76.0 1.5 %fusion.129 = f32[96,704]{1,0:T(8,128)S(1)} fusion(bf16[96,512]{1,0:T(8,128)(2,1)S(1)} %reshape.427, bf16[512,704]{0,1:T(8,128)(2,1)} %param.34), kind=kOutput, calls=%fused_computation.197 | convolution fusion | flops 69206016 | bytes 1089536 | tf_op jit(solution)/shard_map/dot_general | solution.py:249
  78.9 1.1 collective-permute-start.4
  80.1 1.9 %fusion.17 = f32[48,352]{1,0:T(8,128)S(1)} fusion(bf16[48,2048]{1,0:T(8,128)(2,1)S(1)} %reshape.426, bf16[1,2048,352]{1,2,0:T(8,128)(2,1)} %param.31), kind=kOutput, calls=%fused_computation.22 | convolution fusion | flops 69206016 | bytes 1705984 | tf_op jit(solution)/shard_map/dot_general | solution.py:258
  82.0 1.9 %fusion.31 = bf16[48,352]{1,0:T(8,128)(2,1)S(1)} fusion(bf16[48,2048]{1,0:T(8,128)(2,1)S(1)} %reshape.426, bf16[1,2048,352]{1,2,0:T(8,128)(2,1)} %param.32, f32[48,352]{1,0:T(8,128)S(1)} %fusion.17), kind=kOutput, calls=%fused_computation.28 | convolution fusion | flops 69307392 | bytes 1739776 | tf_op jit(solution)/shard_map/dot_general | solution.py:259
  84.3 2.3 %collective-permute-done.4 = f32[33792]{0:T(1024)S(1)} collective-permute-done((f32[33792]{0:T(1024)S(1)}, f32[33792]{0:T(1024)S(1)}, u32[]{:S(2)}, u32[]{:S(2)}) %collective-permute-start.4) | collective-permute-done | bytes 135200 | tf_op jit(solution)/shard_map/ppermute | solution.py:51
  87.6 1.7 %collective-permute-start.11 = (bf16[24,704]{1,0:T(8,128)(2,1)S(1)}, bf16[24,704]{1,0:T(8,128)(2,1)S(1)}, u32[]{:S(2)}, u32[]{:S(2)}) collective-permute-start(bf16[24,704]{1,0:T(8,128)(2,1)S(1)} %multiply_convert_fusion.2), channel_id=1, source_target_pairs={{0,3},{1,0},{2,1},{3,2},{4,7},{5,4},{6,5},{7,6},{8,11},{9,8},{10,9... | collective-permute-start | bytes 101384 | tf_op jit(solution)/shard_map/ppermute | solution.py:51
  89.3 1.7 %fusion.19 = f32[1,4,48,512]{3,2,1,0:T(8,128)S(1)} fusion(bf16[44,4,8,512]{3,2,1,0:T(8,128)(2,1)} %bitcast.186, bf16[48,352]{1,0:T(8,128)(2,1)S(1)} %fusion.31), kind=kOutput, calls=%fused_computation.24 | convolution fusion | flops 69206016 | bytes 1868800 | tf_op jit(solution)/shard_map/dot_general | solution.py:265
  92.9 1.4 %collective-permute-start.7 = (f32[24576]{0:T(1024)S(1)}, f32[24576]{0:T(1024)}, u32[]{:S(2)}, u32[]{:S(2)}) collective-permute-start(f32[24576]{0:T(1024)S(1)} %bitcast.202), channel_id=1, source_target_pairs={{0,2},{1,3},{2,0},{3,1},{4,6},{5,7},{6,4},{7,5},{8,10},{9,11},{10,... | collective-permute-start | bytes 294920 | tf_op jit(solution)/shard_map/ppermute | solution.py:51
  95.3 2.6 %collective-permute-done.6 = f32[24576]{0:T(1024)} collective-permute-done((f32[24576]{0:T(1024)}, f32[24576]{0:T(1024)}, u32[]{:S(2)}, u32[]{:S(2)}) %collective-permute-start.6) | collective-permute-done | bytes 98336 | tf_op jit(solution)/shard_map/ppermute | solution.py:51
  97.9 1.9 %collective-permute-done.7 = f32[24576]{0:T(1024)} collective-permute-done((f32[24576]{0:T(1024)S(1)}, f32[24576]{0:T(1024)}, u32[]{:S(2)}, u32[]{:S(2)}) %collective-permute-start.7) | collective-permute-done | bytes 98336 | tf_op jit(solution)/shard_map/ppermute | solution.py:51
  101.5 3.6 %all-to-all-start.3 = ((f32[8,72,128]{2,1,0:T(8,128)}), f32[8,72,128]{2,1,0:T(8,128)S(1)}, u32[]{:S(2)}, u32[]{:S(2)}) async-start(f32[8,72,128]{2,1,0:T(8,128)} %pad_maximum_fusion.4), calls=%async_computation.3 | async-start | bytes 589824 | tf_op jit(solution)/shard_map/all_to_all | solution.py:286
  105.7 9.3 %all-to-all-done.3 = f32[8,72,128]{2,1,0:T(8,128)S(1)} async-done(((f32[8,72,128]{2,1,0:T(8,128)}), f32[8,72,128]{2,1,0:T(8,128)S(1)}, u32[]{:S(2)}, u32[]{:S(2)}) %all-to-all-start.3) | async-done | bytes 294944 | tf_op jit(solution)/shard_map/all_to_all | solution.py:286
  (161 shorter events, 28.9 us)
Async XLA Ops:
  0.0 51.5 %copy-start = (bf16[512,2048]{1,0:T(8,128)(2,1)S(1)}, bf16[512,2048]{1,0:T(8,128)(2,1)}, u32[]{:S(2)}) copy-start(bf16[512,2048]{1,0:T(8,128)(2,1)} %param.23) | copy-start | bytes 6291460
  7.1 15.0 %all-to-all-start = ((bf16[8,3,4,4,128]{4,3,2,1,0:T(4,128)(2,1)}), bf16[8,3,4,4,128]{4,3,2,1,0:T(4,128)(2,1)S(1)}, u32[]{:S(2)}, u32[]{:S(2)}) async-start(bf16[8,3,4,4,128]{4,3,2,1,0:T(4,128)(2,1)} %broadcast_in_dim.99), calls=%async_computation | async-start | bytes 196608 | tf_op jit(solution)/shard_map/all_to_all | solution.py:116
  22.1 19.3 %copy-start.9 = (s32[48]{0:T(128)}, s32[48]{0:T(128)S(1)}, u32[]{:S(2)}) copy-start(s32[48]{0:T(128)S(1)} %get-tuple-element.48) | copy-start | bytes 580
  22.1 19.3 %copy-start.11 = (s32[48]{0:T(128)}, s32[48]{0:T(128)S(1)}, u32[]{:S(2)}) copy-start(s32[48]{0:T(128)S(1)} %get-tuple-element.49) | copy-start | bytes 580
  35.3 15.0 %all-to-all-start.1 = ((f32[24,17,128]{2,1,0:T(8,128)}), f32[24,17,128]{2,1,0:T(8,128)S(1)}, u32[]{:S(2)}, u32[]{:S(2)}) async-start(f32[24,17,128]{2,1,0:T(8,128)} %pad_maximum_fusion.2), calls=%async_computation.1 | async-start | bytes 589824 | tf_op jit(solution)/shard_map/all_to_all | solution.py:169
  51.9 2.9 %collective-permute-start.2 = (f32[12,2048]{1,0:T(8,128)S(1)}, f32[12,2048]{1,0:T(8,128)S(1)}, u32[]{:S(2)}, u32[]{:S(2)}) collective-permute-start(f32[12,2048]{1,0:T(8,128)S(1)} %fusion.128), channel_id=1, source_target_pairs={{0,3},{1,0},{2,1},{3,2},{4,7},{5,4},{6,5},{7,6},{8,11},{9,8},{10,9... | collective-permute-start | bytes 294920 | tf_op jit(solution)/shard_map/ppermute | solution.py:51
  51.9 8.6 %collective-permute-start.1 = (f32[12,2048]{1,0:T(8,128)S(1)}, f32[12,2048]{1,0:T(8,128)S(1)}, u32[]{:S(2)}, u32[]{:S(2)}) collective-permute-start(f32[12,2048]{1,0:T(8,128)S(1)} %fusion.128), channel_id=1, source_target_pairs={{0,2},{1,3},{2,0},{3,1},{4,6},{5,7},{6,4},{7,5},{8,10},{9,11},{10,... | collective-permute-start | bytes 294920 | tf_op jit(solution)/shard_map/ppermute | solution.py:51
  53.4 7.1 %collective-permute-start = (f32[12,2048]{1,0:T(8,128)S(1)}, f32[12,2048]{1,0:T(8,128)S(1)}, u32[]{:S(2)}, u32[]{:S(2)}) collective-permute-start(f32[12,2048]{1,0:T(8,128)S(1)} %fusion.128), channel_id=1, source_target_pairs={{0,1},{1,2},{2,3},{3,0},{4,5},{5,6},{6,7},{7,4},{8,9},{9,10},{10,1... | collective-permute-start | bytes 294920 | tf_op jit(solution)/shard_map/ppermute | solution.py:51
  63.4 12.1 %all-to-all-start.2 = ((bf16[8,144,128]{2,1,0:T(8,128)(2,1)}), bf16[8,144,128]{2,1,0:T(8,128)(2,1)S(1)}, u32[]{:S(2)}, u32[]{:S(2)}) async-start(bf16[8,144,128]{2,1,0:T(8,128)(2,1)} %pad_maximum_fusion.3), calls=%async_computation.2 | async-start | bytes 589824 | tf_op jit(solution)/shard_map/all_to_all | solution.py:245
  78.4 5.6 %collective-permute-start.5 = (f32[33792]{0:T(1024)S(1)}, f32[33792]{0:T(1024)S(1)}, u32[]{:S(2)}, u32[]{:S(2)}) collective-permute-start(f32[33792]{0:T(1024)S(1)} %bitcast.198), channel_id=1, source_target_pairs={{0,3},{1,0},{2,1},{3,2},{4,7},{5,4},{6,5},{7,6},{8,11},{9,8},{10,9... | collective-permute-start | bytes 405512 | tf_op jit(solution)/shard_map/ppermute | solution.py:51
  78.4 5.8 %collective-permute-start.3 = (f32[33792]{0:T(1024)S(1)}, f32[33792]{0:T(1024)S(1)}, u32[]{:S(2)}, u32[]{:S(2)}) collective-permute-start(f32[33792]{0:T(1024)S(1)} %bitcast.197), channel_id=1, source_target_pairs={{0,1},{1,2},{2,3},{3,0},{4,5},{5,6},{6,7},{7,4},{8,9},{9,10},{10,1... | collective-permute-start | bytes 405512 | tf_op jit(solution)/shard_map/ppermute | solution.py:51
  78.9 7.7 %collective-permute-start.4 = (f32[33792]{0:T(1024)S(1)}, f32[33792]{0:T(1024)S(1)}, u32[]{:S(2)}, u32[]{:S(2)}) collective-permute-start(f32[33792]{0:T(1024)S(1)} %bitcast.196), channel_id=1, source_target_pairs={{0,2},{1,3},{2,0},{3,1},{4,6},{5,7},{6,4},{7,5},{8,10},{9,11},{10,... | collective-permute-start | bytes 405512 | tf_op jit(solution)/shard_map/ppermute | solution.py:51
  86.6 18.5 %copy-start.6 = (f32[3,4,4]{2,1,0:T(4,128)S(1)}, f32[3,4,4]{2,1,0:T(4,128)}, u32[]{:S(2)}) copy-start(f32[3,4,4]{2,1,0:T(4,128)} %param.30) | copy-start | bytes 580
  86.6 18.6 %copy-start.8 = (bf16[2048]{0:T(1024)(128)(2,1)S(1)}, bf16[2048]{0:T(1024)(128)(2,1)}, u32[]{:S(2)}) copy-start(bf16[2048]{0:T(1024)(128)(2,1)} %param.37) | copy-start | bytes 12292
  86.7 18.6 %copy-start.10 = (s32[48]{0:T(128)S(1)}, s32[48]{0:T(128)}, u32[]{:S(2)}) copy-start(s32[48]{0:T(128)} %copy-done.9) | copy-start | bytes 580
  86.7 18.6 %copy-start.12 = (s32[48]{0:T(128)S(1)}, s32[48]{0:T(128)}, u32[]{:S(2)}) copy-start(s32[48]{0:T(128)} %copy-done.11) | copy-start | bytes 580
  86.7 18.8 %copy-start.5 = (bf16[12,2048]{1,0:T(8,128)(2,1)S(1)}, bf16[12,2048]{1,0:T(8,128)(2,1)}, u32[]{:S(2)}) copy-start(bf16[12,2048]{1,0:T(8,128)(2,1)} %copy-done.4) | copy-start | bytes 147460
  86.8 6.1 %collective-permute-start.10 = (bf16[24,704]{1,0:T(8,128)(2,1)S(1)}, bf16[24,704]{1,0:T(8,128)(2,1)S(1)}, u32[]{:S(2)}, u32[]{:S(2)}) collective-permute-start(bf16[24,704]{1,0:T(8,128)(2,1)S(1)} %multiply_convert_fusion.2), channel_id=1, source_target_pairs={{0,2},{1,3},{2,0},{3,1},{4,6},{5,7},{6,4},{7,5},{8,10},{9,11},{10,... | collective-permute-start | bytes 101384 | tf_op jit(solution)/shard_map/ppermute | solution.py:51
  87.5 6.8 %collective-permute-start.9 = (bf16[24,704]{1,0:T(8,128)(2,1)S(1)}, bf16[24,704]{1,0:T(8,128)(2,1)S(1)}, u32[]{:S(2)}, u32[]{:S(2)}) collective-permute-start(bf16[24,704]{1,0:T(8,128)(2,1)S(1)} %multiply_convert_fusion.2), channel_id=1, source_target_pairs={{0,1},{1,2},{2,3},{3,0},{4,5},{5,6},{6,7},{7,4},{8,9},{9,10},{10,1... | collective-permute-start | bytes 101384 | tf_op jit(solution)/shard_map/ppermute | solution.py:51
  87.6 6.7 %collective-permute-start.11 = (bf16[24,704]{1,0:T(8,128)(2,1)S(1)}, bf16[24,704]{1,0:T(8,128)(2,1)S(1)}, u32[]{:S(2)}, u32[]{:S(2)}) collective-permute-start(bf16[24,704]{1,0:T(8,128)(2,1)S(1)} %multiply_convert_fusion.2), channel_id=1, source_target_pairs={{0,3},{1,0},{2,1},{3,2},{4,7},{5,4},{6,5},{7,6},{8,11},{9,8},{10,9... | collective-permute-start | bytes 101384 | tf_op jit(solution)/shard_map/ppermute | solution.py:51
  92.4 2.9 %collective-permute-start.8 = (f32[24576]{0:T(1024)}, f32[24576]{0:T(1024)}, u32[]{:S(2)}, u32[]{:S(2)}) collective-permute-start(f32[24576]{0:T(1024)} %bitcast.49), channel_id=1, source_target_pairs={{0,3},{1,0},{2,1},{3,2},{4,7},{5,4},{6,5},{7,6},{8,11},{9,8},{10,9... | collective-permute-start | bytes 294920 | tf_op jit(solution)/shard_map/ppermute | solution.py:51
  92.4 5.5 %collective-permute-start.6 = (f32[24576]{0:T(1024)}, f32[24576]{0:T(1024)}, u32[]{:S(2)}, u32[]{:S(2)}) collective-permute-start(f32[24576]{0:T(1024)} %bitcast.47), channel_id=1, source_target_pairs={{0,1},{1,2},{2,3},{3,0},{4,5},{5,6},{6,7},{7,4},{8,9},{9,10},{10,1... | collective-permute-start | bytes 294920 | tf_op jit(solution)/shard_map/ppermute | solution.py:51
  92.9 6.8 %collective-permute-start.7 = (f32[24576]{0:T(1024)S(1)}, f32[24576]{0:T(1024)}, u32[]{:S(2)}, u32[]{:S(2)}) collective-permute-start(f32[24576]{0:T(1024)S(1)} %bitcast.202), channel_id=1, source_target_pairs={{0,2},{1,3},{2,0},{3,1},{4,6},{5,7},{6,4},{7,5},{8,10},{9,11},{10,... | collective-permute-start | bytes 294920 | tf_op jit(solution)/shard_map/ppermute | solution.py:51
  101.5 13.5 %all-to-all-start.3 = ((f32[8,72,128]{2,1,0:T(8,128)}), f32[8,72,128]{2,1,0:T(8,128)S(1)}, u32[]{:S(2)}, u32[]{:S(2)}) async-start(f32[8,72,128]{2,1,0:T(8,128)} %pad_maximum_fusion.4), calls=%async_computation.3 | async-start | bytes 589824 | tf_op jit(solution)/shard_map/all_to_all | solution.py:286
  (6 other events, 68.0 us)

commit v10 on v9

--- a/solution.py
+++ b/solution.py
@@ -131,12 +131,15 @@
     token_pos = logical[:, None] * page_len + jnp.arange(page_len, dtype=jnp.int32)[None, :]
     live = present[:, None] & (token_pos < cache_lengths[owner][:, None])
     page_queries = query_all[owner]
-    page_keys = cache_keys.reshape(pool_here, page_len, local_heads, HD)
     page_values = cache_values.reshape(pool_here, page_len, local_heads, HD)
+    head_eye = jnp.arange(local_heads)[:, None] == jnp.arange(local_heads)[None, :]
+    block_queries = jnp.where(
+        head_eye[None, None, :, :, None], page_queries[:, :, :, None, :], jnp.zeros((), jnp.bfloat16)
+    ).reshape(pool_here, step_count * local_heads, head_width)
     scores = (
-        jnp.einsum("pshd,pkhd->pshk", page_queries, page_keys, preferred_element_type=jnp.float32)
+        jnp.einsum("pxd,pkd->pxk", block_queries, cache_keys, preferred_element_type=jnp.float32)
         * score_scale
-    )
+    ).reshape(pool_here, step_count, local_heads, page_len)
     page_mask = live[:, None, None, :]
     masked = jnp.where(page_mask, scores, NEG)
     page_max = jnp.max(masked, axis=-1)

time: 118 us -> 113 us (0.958)
  waiting for transfers between devices: 39.6 us -> 42.7 us
  matrix products: 25.6 us -> 22.9 us
  starting transfers between devices: 28.3 us -> 25.6 us
  local copies, waits for them, and re-layouts: 11.5 us -> 9.86 us
    all_to_all x1, waiting for transfers between devices: 0.01 us -> 1.99 us  [per_device(): lax.all_to_all(query_spread, 'req', 0, 0, tiled=True)]
    all_to_all x1, starting transfers between devices: 5.99 us -> 4.02 us  [per_device(): lax.all_to_all(packed, 'req', 0, 0, tiled=True)]
    ppermute x12, waiting for transfers between devices: 14 us -> 15.9 us  [shift_exchange(): pieces.append(lax.ppermute(send, axis, pairs))]
    all_to_all x1, waiting for transfers between devices: 9.32 us -> 7.92 us  [per_device(): back = lax.all_to_all(back_in, 'req', 0, 0, tiled=True)]
    dot_general x1, matrix products: 5.41 us -> 4.03 us  [per_device(): jnp.einsum('pxd,pkd->pxk', block_queries, cache_keys, preferred_element_t...]
    dot_general x1, matrix products: 1.92 us -> 0.56 us  [per_device(): up_pre = jnp.dot(flat_rows, w_up_here, preferred_element_type=jnp.float32)]
  transfers between devices with their start and end apart: 16 -> 16, of which waited for: 10 -> 11; matrix products, arithmetic and copies ran while one was open for 15% -> 11% of each run, Pallas kernels for 0% -> 0%
where the time goes in v10:
time: 113 us; the launch traced here: 112 us
  waiting for transfers between devices  42.7 us (38%)
  starting transfers between devices  25.6 us (23%)
  matrix products  22.9 us (20%)
  other arithmetic  10.1 us (9%)
  local copies, waits for them, and re-layouts  9.86 us (9%)
    ppermute x12, waiting for transfers between devices, shift_exchange(): pieces.append(lax.ppermute(send, axis, pairs))  15.9 us
    all_to_all x1, waiting for transfers between devices, per_device(): lax.all_to_all(packed, 'req', 0, 0, tiled=True)  8.66 us
    all_to_all x1, waiting for transfers between devices, per_device(): received = lax.all_to_all(dispatch, 'req', 0, 0, tiled=True)  8.28 us
    all_to_all x1, waiting for transfers between devices, per_device(): back = lax.all_to_all(back_in, 'req', 0, 0, tiled=True)  7.92 us
    all_to_all x1, starting transfers between devices, per_device(): lax.all_to_all(query_spread, 'req', 0, 0, tiled=True)  7.29 us
    ppermute x12, starting transfers between devices, shift_exchange(): pieces.append(lax.ppermute(send, axis, pairs))  7.1 us
    dot_general x1, matrix products, per_device(): jnp.einsum('pxd,pkd->pxk', block_queries, cache_keys, preferred_element_t...  4.03 us
    all_to_all x1, starting transfers between devices, per_device(): lax.all_to_all(packed, 'req', 0, 0, tiled=True)  4.02 us
  transfers between devices with their start and end apart: 16, of which 11 were waited for; matrix products, arithmetic and copies ran while one was open for 11% of the time, Pallas kernels for 0%

profile of v10, /device:TPU:0, one launch (start us, length us, event | category | flops | bytes accessed | tf_op | source)
XLA Modules:
  0.0 111.9 jit_solution(12021296010068635650)
XLA Ops:
  4.3 2.0 %fusion.36 = f32[3,4,4,128]{3,1,2,0:T(4,128)S(1)} fusion(bf16[3,4,2048]{2,1,0:T(4,128)(2,1)S(1)} %multiply_convert_fusion.1, bf16[2048,3,512]{2,0,1:T(8,128)(2,1)} %param.21, f32[512]{0:T(512)S(1)} %bitcast.214), kind=kOutput, calls=%fused_computation.31 | convolution fusion | flops 25171968 | bytes 2172928 | tf_op jit(solution)/shard_map/rsd,df->rsf/dot_general | solution.py:109
  7.1 7.3 %all-to-all-start = ((bf16[8,3,4,4,128]{4,3,2,1,0:T(4,128)(2,1)}), bf16[8,3,4,4,128]{4,3,2,1,0:T(4,128)(2,1)S(1)}, u32[]{:S(2)}, u32[]{:S(2)}) async-start(bf16[8,3,4,4,128]{4,3,2,1,0:T(4,128)(2,1)} %broadcast_in_dim.197), calls=%async_computation | async-start | bytes 196608 | tf_op jit(solution)/shard_map/all_to_all | solution.py:116
  16.2 2.9 %fusion.28 = f32[3,4,2,512]{3,1,2,0:T(4,128)S(1)} fusion(bf16[2048,3,512]{2,0,1:T(8,128)(2,1)} %param.21, bf16[3,4,2048]{2,1,0:T(4,128)(2,1)S(1)} %multiply_convert_fusion.1, f32[2,512]{1,0:T(2,128)S(1)} %slice_convert_fusion.1), kind=kOutput, calls=%fused_computation.26 | convolution fusion | flops 50343936 | bytes 4296704 | tf_op jit(solution)/shard_map/rsd,dcf->rscf/dot_general | solution.py:119
  19.6 2.0 %all-to-all-done = bf16[8,3,4,4,128]{4,3,2,1,0:T(4,128)(2,1)S(1)} async-done(((bf16[8,3,4,4,128]{4,3,2,1,0:T(4,128)(2,1)}), bf16[8,3,4,4,128]{4,3,2,1,0:T(4,128)(2,1)S(1)}, u32[]{:S(2)}, u32[]{:S(2)}) %all-to-all-start) | async-done | bytes 98336 | tf_op jit(solution)/shard_map/all_to_all | solution.py:116
  22.9 4.0 %select_reduce_fusion.2 = (f32[40,16]{1,0:T(8,128)S(1)}, f32[40,16,128]{2,1,0:T(8,128)S(1)}) fusion(pred[40,128]{1,0:T(8,128)(4,1)S(1)} %fusion.81, bf16[40,128,512]{2,1,0:T(8,128)(2,1)} %param.24, bf16[40,16,512]{2,1,0:T(8,128)(2,1)S(1)} %broadcast_in_dim.199, pred[16,512]{1,0:T(8,128)(4,1)S(1)} %bitcast.211), kind=kOutput, calls=%fused_computation.66 | convolution fusion | flops 84458880 | bytes 6241792 | tf_op jit(solution)/shard_map/pxd,pkd->pxk/dot_general | solution.py:140
  28.3 4.0 %fusion.19 = f32[40,4,4,128]{3,1,2,0:T(4,128)S(1)} fusion(f32[40,4,4,128]{3,2,1,0:T(4,128)S(1)} %bitcast.182, f32[40,4,4]{1,2,0:T(4,128)S(1)} %copy.85, pred[40,128]{1,0:T(8,128)(4,1)S(1)} %fusion.81, bf16[40,128,512]{2,1,0:T(8,128)(2,1)} %param.25), kind=kOutput, calls=%fused_computation.23 | convolution fusion | flops 21299200 | bytes 5905920 | tf_op jit(solution)/shard_map/pshk,pkhd->pshd/dot_general | solution.py:148
  33.7 4.0 %all-to-all-start.1 = ((f32[24,17,128]{2,1,0:T(8,128)}), f32[24,17,128]{2,1,0:T(8,128)S(1)}, u32[]{:S(2)}, u32[]{:S(2)}) async-start(f32[24,17,128]{2,1,0:T(8,128)} %pad_maximum_fusion.2), calls=%async_computation.1 | async-start | bytes 589824 | tf_op jit(solution)/shard_map/all_to_all | solution.py:172
  38.1 8.7 %all-to-all-done.1 = f32[24,17,128]{2,1,0:T(8,128)S(1)} async-done(((f32[24,17,128]{2,1,0:T(8,128)}), f32[24,17,128]{2,1,0:T(8,128)S(1)}, u32[]{:S(2)}, u32[]{:S(2)}) %all-to-all-start.1) | async-done | bytes 208928 | tf_op jit(solution)/shard_map/all_to_all | solution.py:172
  48.3 1.5 %collective-permute-start.1 = (f32[12,2048]{1,0:T(8,128)S(1)}, f32[12,2048]{1,0:T(8,128)S(1)}, u32[]{:S(2)}, u32[]{:S(2)}) collective-permute-start(f32[12,2048]{1,0:T(8,128)S(1)} %fusion.122), channel_id=1, source_target_pairs={{0,2},{1,3},{2,0},{3,1},{4,6},{5,7},{6,4},{7,5},{8,10},{9,11},{10,... | collective-permute-start | bytes 294920 | tf_op jit(solution)/shard_map/ppermute | solution.py:51
  50.1 1.1 %collective-permute-done.2 = f32[12,2048]{1,0:T(8,128)S(1)} collective-permute-done((f32[12,2048]{1,0:T(8,128)S(1)}, f32[12,2048]{1,0:T(8,128)S(1)}, u32[]{:S(2)}, u32[]{:S(2)}) %collective-permute-start.2) | collective-permute-done | bytes 98336 | tf_op jit(solution)/shard_map/ppermute | solution.py:51
  51.2 5.7 %collective-permute-done.1 = f32[12,2048]{1,0:T(8,128)S(1)} collective-permute-done((f32[12,2048]{1,0:T(8,128)S(1)}, f32[12,2048]{1,0:T(8,128)S(1)}, u32[]{:S(2)}, u32[]{:S(2)}) %collective-permute-start.1) | collective-permute-done | bytes 98336 | tf_op jit(solution)/shard_map/ppermute | solution.py:51
  60.4 3.6 %all-to-all-start.2 = ((bf16[8,144,128]{2,1,0:T(8,128)(2,1)}), bf16[8,144,128]{2,1,0:T(8,128)(2,1)S(1)}, u32[]{:S(2)}, u32[]{:S(2)}) async-start(bf16[8,144,128]{2,1,0:T(8,128)(2,1)} %pad_maximum_fusion.3), calls=%async_computation.2 | async-start | bytes 589824 | tf_op jit(solution)/shard_map/all_to_all | solution.py:248
  64.2 8.3 %all-to-all-done.2 = bf16[8,144,128]{2,1,0:T(8,128)(2,1)S(1)} async-done(((bf16[8,144,128]{2,1,0:T(8,128)(2,1)}), bf16[8,144,128]{2,1,0:T(8,128)(2,1)S(1)}, u32[]{:S(2)}, u32[]{:S(2)}) %all-to-all-start.2) | async-done | bytes 294944 | tf_op jit(solution)/shard_map/all_to_all | solution.py:248
  72.7 1.5 %fusion.124 = f32[96,704]{1,0:T(8,128)S(1)} fusion(bf16[96,512]{1,0:T(8,128)(2,1)S(1)} %reshape.450, bf16[512,704]{0,1:T(8,128)(2,1)} %param.35), kind=kOutput, calls=%fused_computation.203 | convolution fusion | flops 69206016 | bytes 1089536 | tf_op jit(solution)/shard_map/dot_general | solution.py:253
  75.4 1.2 %collective-permute-start.4 = (f32[33792]{0:T(1024)S(1)}, f32[33792]{0:T(1024)S(1)}, u32[]{:S(2)}, u32[]{:S(2)}) collective-permute-start(f32[33792]{0:T(1024)S(1)} %bitcast.192), channel_id=1, source_target_pairs={{0,2},{1,3},{2,0},{3,1},{4,6},{5,7},{6,4},{7,5},{8,10},{9,11},{10,... | collective-permute-start | bytes 405512 | tf_op jit(solution)/shard_map/ppermute | solution.py:51
  76.8 1.9 %fusion.14 = f32[48,352]{1,0:T(8,128)S(1)} fusion(bf16[48,2048]{1,0:T(8,128)(2,1)S(1)} %reshape.449, bf16[1,2048,352]{1,2,0:T(8,128)(2,1)} %param.31), kind=kOutput, calls=%fused_computation.19 | convolution fusion | flops 69206016 | bytes 1705984 | tf_op jit(solution)/shard_map/dot_general | solution.py:261
  79.3 4.2 %collective-permute-done.4 = f32[33792]{0:T(1024)S(1)} collective-permute-done((f32[33792]{0:T(1024)S(1)}, f32[33792]{0:T(1024)S(1)}, u32[]{:S(2)}, u32[]{:S(2)}) %collective-permute-start.4) | collective-permute-done | bytes 135200 | tf_op jit(solution)/shard_map/ppermute | solution.py:51
  85.3 1.8 %fusion.16 = f32[1,4,48,512]{3,2,1,0:T(8,128)S(1)} fusion(bf16[44,4,8,512]{3,2,1,0:T(8,128)(2,1)} %bitcast.181, bf16[48,352]{1,0:T(8,128)(2,1)S(1)} %fusion.25), kind=kOutput, calls=%fused_computation.21 | convolution fusion | flops 69206016 | bytes 1868800 | tf_op jit(solution)/shard_map/dot_general | solution.py:268
  88.4 1.6 %collective-permute-start.8 = (f32[24576]{0:T(1024)}, f32[24576]{0:T(1024)}, u32[]{:S(2)}, u32[]{:S(2)}) collective-permute-start(f32[24576]{0:T(1024)} %bitcast.52), channel_id=1, source_target_pairs={{0,3},{1,0},{2,1},{3,2},{4,7},{5,4},{6,5},{7,6},{8,11},{9,8},{10,9... | collective-permute-start | bytes 294920 | tf_op jit(solution)/shard_map/ppermute | solution.py:51
  90.0 1.1 %collective-permute-start.7 = (f32[24576]{0:T(1024)S(1)}, f32[24576]{0:T(1024)}, u32[]{:S(2)}, u32[]{:S(2)}) collective-permute-start(f32[24576]{0:T(1024)S(1)} %bitcast.202), channel_id=1, source_target_pairs={{0,2},{1,3},{2,0},{3,1},{4,6},{5,7},{6,4},{7,5},{8,10},{9,11},{10,... | collective-permute-start | bytes 294920 | tf_op jit(solution)/shard_map/ppermute | solution.py:51
  92.9 3.6 %collective-permute-done.7 = f32[24576]{0:T(1024)} collective-permute-done((f32[24576]{0:T(1024)S(1)}, f32[24576]{0:T(1024)}, u32[]{:S(2)}, u32[]{:S(2)}) %collective-permute-start.7) | collective-permute-done | bytes 98336 | tf_op jit(solution)/shard_map/ppermute | solution.py:51
  96.5 1.0 add_convert_fusion
  98.3 3.5 %all-to-all-start.3 = ((f32[8,72,128]{2,1,0:T(8,128)}), f32[8,72,128]{2,1,0:T(8,128)S(1)}, u32[]{:S(2)}, u32[]{:S(2)}) async-start(f32[8,72,128]{2,1,0:T(8,128)} %pad_maximum_fusion.4), calls=%async_computation.3 | async-start | bytes 589824 | tf_op jit(solution)/shard_map/all_to_all | solution.py:289
  102.3 7.9 %all-to-all-done.3 = f32[8,72,128]{2,1,0:T(8,128)S(1)} async-done(((f32[8,72,128]{2,1,0:T(8,128)}), f32[8,72,128]{2,1,0:T(8,128)S(1)}, u32[]{:S(2)}, u32[]{:S(2)}) %all-to-all-start.3) | async-done | bytes 294944 | tf_op jit(solution)/shard_map/all_to_all | solution.py:289
  (167 shorter events, 26.7 us)
Async XLA Ops:
  0.0 47.9 %copy-start = (bf16[512,2048]{1,0:T(8,128)(2,1)S(1)}, bf16[512,2048]{1,0:T(8,128)(2,1)}, u32[]{:S(2)}) copy-start(bf16[512,2048]{1,0:T(8,128)(2,1)} %param.23) | copy-start | bytes 6291460
  0.0 14.4 %copy-start.13 = (bf16[3,512]{1,0:T(4,128)(2,1)S(1)}, bf16[3,512]{1,0:T(4,128)(2,1)}, u32[]{:S(2)}) copy-start(bf16[3,512]{1,0:T(4,128)(2,1)} %param.22) | copy-start | bytes 9220
  0.0 15.3 %copy-start.1 = (s32[24]{0:T(128)S(1)}, s32[24]{0:T(128)}, u32[]{:S(2)}) copy-start(s32[24]{0:T(128)} %param.27) | copy-start | bytes 292
  0.0 14.5 %copy-start.9 = (s32[3,4,4]{2,1,0:T(4,128)S(1)}, s32[3,4,4]{2,1,0:T(4,128)}, u32[]{:S(2)}) copy-start(s32[3,4,4]{2,1,0:T(4,128)} %param.29) | copy-start | bytes 580
  0.0 14.9 %copy-start.8 = (s32[24,37]{1,0:T(8,128)S(1)}, s32[24,37]{1,0:T(8,128)}, u32[]{:S(2)}) copy-start(s32[24,37]{1,0:T(8,128)} %param.26) | copy-start | bytes 10660
  7.1 14.4 %all-to-all-start = ((bf16[8,3,4,4,128]{4,3,2,1,0:T(4,128)(2,1)}), bf16[8,3,4,4,128]{4,3,2,1,0:T(4,128)(2,1)S(1)}, u32[]{:S(2)}, u32[]{:S(2)}) async-start(bf16[8,3,4,4,128]{4,3,2,1,0:T(4,128)(2,1)} %broadcast_in_dim.197), calls=%async_computation | async-start | bytes 196608 | tf_op jit(solution)/shard_map/all_to_all | solution.py:116
  33.7 13.0 %all-to-all-start.1 = ((f32[24,17,128]{2,1,0:T(8,128)}), f32[24,17,128]{2,1,0:T(8,128)S(1)}, u32[]{:S(2)}, u32[]{:S(2)}) async-start(f32[24,17,128]{2,1,0:T(8,128)} %pad_maximum_fusion.2), calls=%async_computation.1 | async-start | bytes 589824 | tf_op jit(solution)/shard_map/all_to_all | solution.py:172
  48.3 2.9 %collective-permute-start.2 = (f32[12,2048]{1,0:T(8,128)S(1)}, f32[12,2048]{1,0:T(8,128)S(1)}, u32[]{:S(2)}, u32[]{:S(2)}) collective-permute-start(f32[12,2048]{1,0:T(8,128)S(1)} %fusion.122), channel_id=1, source_target_pairs={{0,3},{1,0},{2,1},{3,2},{4,7},{5,4},{6,5},{7,6},{8,11},{9,8},{10,9... | collective-permute-start | bytes 294920 | tf_op jit(solution)/shard_map/ppermute | solution.py:51
  48.3 8.6 %collective-permute-start.1 = (f32[12,2048]{1,0:T(8,128)S(1)}, f32[12,2048]{1,0:T(8,128)S(1)}, u32[]{:S(2)}, u32[]{:S(2)}) collective-permute-start(f32[12,2048]{1,0:T(8,128)S(1)} %fusion.122), channel_id=1, source_target_pairs={{0,2},{1,3},{2,0},{3,1},{4,6},{5,7},{6,4},{7,5},{8,10},{9,11},{10,... | collective-permute-start | bytes 294920 | tf_op jit(solution)/shard_map/ppermute | solution.py:51
  49.8 7.1 %collective-permute-start = (f32[12,2048]{1,0:T(8,128)S(1)}, f32[12,2048]{1,0:T(8,128)S(1)}, u32[]{:S(2)}, u32[]{:S(2)}) collective-permute-start(f32[12,2048]{1,0:T(8,128)S(1)} %fusion.122), channel_id=1, source_target_pairs={{0,1},{1,2},{2,3},{3,0},{4,5},{5,6},{6,7},{7,4},{8,9},{9,10},{10,1... | collective-permute-start | bytes 294920 | tf_op jit(solution)/shard_map/ppermute | solution.py:51
  59.5 14.6 %copy-start.4 = (bf16[512,704]{0,1:T(8,128)(2,1)S(1)}, bf16[512,704]{0,1:T(8,128)(2,1)}, u32[]{:S(2)}) copy-start(bf16[512,704]{0,1:T(8,128)(2,1)} %param.34) | copy-start | bytes 2162692
  60.4 12.1 %all-to-all-start.2 = ((bf16[8,144,128]{2,1,0:T(8,128)(2,1)}), bf16[8,144,128]{2,1,0:T(8,128)(2,1)S(1)}, u32[]{:S(2)}, u32[]{:S(2)}) async-start(bf16[8,144,128]{2,1,0:T(8,128)(2,1)} %pad_maximum_fusion.3), calls=%async_computation.2 | async-start | bytes 589824 | tf_op jit(solution)/shard_map/all_to_all | solution.py:248
  75.4 3.9 %collective-permute-start.5 = (f32[33792]{0:T(1024)S(1)}, f32[33792]{0:T(1024)S(1)}, u32[]{:S(2)}, u32[]{:S(2)}) collective-permute-start(f32[33792]{0:T(1024)S(1)} %bitcast.193), channel_id=1, source_target_pairs={{0,3},{1,0},{2,1},{3,2},{4,7},{5,4},{6,5},{7,6},{8,11},{9,8},{10,9... | collective-permute-start | bytes 405512 | tf_op jit(solution)/shard_map/ppermute | solution.py:51
  75.4 8.1 %collective-permute-start.4 = (f32[33792]{0:T(1024)S(1)}, f32[33792]{0:T(1024)S(1)}, u32[]{:S(2)}, u32[]{:S(2)}) collective-permute-start(f32[33792]{0:T(1024)S(1)} %bitcast.192), channel_id=1, source_target_pairs={{0,2},{1,3},{2,0},{3,1},{4,6},{5,7},{6,4},{7,5},{8,10},{9,11},{10,... | collective-permute-start | bytes 405512 | tf_op jit(solution)/shard_map/ppermute | solution.py:51
  76.7 7.3 %collective-permute-start.3 = (f32[33792]{0:T(1024)S(1)}, f32[33792]{0:T(1024)S(1)}, u32[]{:S(2)}, u32[]{:S(2)}) collective-permute-start(f32[33792]{0:T(1024)S(1)} %bitcast.191), channel_id=1, source_target_pairs={{0,1},{1,2},{2,3},{3,0},{4,5},{5,6},{6,7},{7,4},{8,9},{9,10},{10,1... | collective-permute-start | bytes 405512 | tf_op jit(solution)/shard_map/ppermute | solution.py:51
  84.1 7.1 %collective-permute-start.11 = (bf16[24,704]{1,0:T(8,128)(2,1)S(1)}, bf16[24,704]{1,0:T(8,128)(2,1)S(1)}, u32[]{:S(2)}, u32[]{:S(2)}) collective-permute-start(bf16[24,704]{1,0:T(8,128)(2,1)S(1)} %multiply_convert_fusion.2), channel_id=1, source_target_pairs={{0,3},{1,0},{2,1},{3,2},{4,7},{5,4},{6,5},{7,6},{8,11},{9,8},{10,9... | collective-permute-start | bytes 101384 | tf_op jit(solution)/shard_map/ppermute | solution.py:51
  84.1 7.0 %collective-permute-start.10 = (bf16[24,704]{1,0:T(8,128)(2,1)S(1)}, bf16[24,704]{1,0:T(8,128)(2,1)S(1)}, u32[]{:S(2)}, u32[]{:S(2)}) collective-permute-start(bf16[24,704]{1,0:T(8,128)(2,1)S(1)} %multiply_convert_fusion.2), channel_id=1, source_target_pairs={{0,2},{1,3},{2,0},{3,1},{4,6},{5,7},{6,4},{7,5},{8,10},{9,11},{10,... | collective-permute-start | bytes 101384 | tf_op jit(solution)/shard_map/ppermute | solution.py:51
  85.1 6.1 %collective-permute-start.9 = (bf16[24,704]{1,0:T(8,128)(2,1)S(1)}, bf16[24,704]{1,0:T(8,128)(2,1)S(1)}, u32[]{:S(2)}, u32[]{:S(2)}) collective-permute-start(bf16[24,704]{1,0:T(8,128)(2,1)S(1)} %multiply_convert_fusion.2), channel_id=1, source_target_pairs={{0,1},{1,2},{2,3},{3,0},{4,5},{5,6},{6,7},{7,4},{8,9},{9,10},{10,1... | collective-permute-start | bytes 101384 | tf_op jit(solution)/shard_map/ppermute | solution.py:51
  88.4 13.4 %copy-start.10 = (f32[3,4,4]{2,1,0:T(4,128)S(1)}, f32[3,4,4]{2,1,0:T(4,128)}, u32[]{:S(2)}) copy-start(f32[3,4,4]{2,1,0:T(4,128)} %param.30) | copy-start | bytes 580
  88.4 13.5 %copy-start.12 = (bf16[2048]{0:T(1024)(128)(2,1)S(1)}, bf16[2048]{0:T(1024)(128)(2,1)}, u32[]{:S(2)}) copy-start(bf16[2048]{0:T(1024)(128)(2,1)} %param.37) | copy-start | bytes 12292
  88.4 4.6 %collective-permute-start.8 = (f32[24576]{0:T(1024)}, f32[24576]{0:T(1024)}, u32[]{:S(2)}, u32[]{:S(2)}) collective-permute-start(f32[24576]{0:T(1024)} %bitcast.52), channel_id=1, source_target_pairs={{0,3},{1,0},{2,1},{3,2},{4,7},{5,4},{6,5},{7,6},{8,11},{9,8},{10,9... | collective-permute-start | bytes 294920 | tf_op jit(solution)/shard_map/ppermute | solution.py:51
  90.0 6.5 %collective-permute-start.7 = (f32[24576]{0:T(1024)S(1)}, f32[24576]{0:T(1024)}, u32[]{:S(2)}, u32[]{:S(2)}) collective-permute-start(f32[24576]{0:T(1024)S(1)} %bitcast.202), channel_id=1, source_target_pairs={{0,2},{1,3},{2,0},{3,1},{4,6},{5,7},{6,4},{7,5},{8,10},{9,11},{10,... | collective-permute-start | bytes 294920 | tf_op jit(solution)/shard_map/ppermute | solution.py:51
  91.2 5.4 %collective-permute-start.6 = (f32[24576]{0:T(1024)S(1)}, f32[24576]{0:T(1024)}, u32[]{:S(2)}, u32[]{:S(2)}) collective-permute-start(f32[24576]{0:T(1024)S(1)} %bitcast.201), channel_id=1, source_target_pairs={{0,1},{1,2},{2,3},{3,0},{4,5},{5,6},{6,7},{7,4},{8,9},{9,10},{10,1... | collective-permute-start | bytes 294920 | tf_op jit(solution)/shard_map/ppermute | solution.py:51
  98.3 12.0 %all-to-all-start.3 = ((f32[8,72,128]{2,1,0:T(8,128)}), f32[8,72,128]{2,1,0:T(8,128)S(1)}, u32[]{:S(2)}, u32[]{:S(2)}) async-start(f32[8,72,128]{2,1,0:T(8,128)} %pad_maximum_fusion.4), calls=%async_computation.3 | async-start | bytes 589824 | tf_op jit(solution)/shard_map/all_to_all | solution.py:289
  (6 other events, 33.1 us)

commit v11 on v10

--- a/solution.py
+++ b/solution.py
@@ -264,8 +264,8 @@
     shared_sum = sum(shift_exchange(shared_pre, "tp", tp_count)).reshape(
         share_rows, 2 * unit_count
     )
-    hidden, shared_sum = lax.optimization_barrier((hidden, shared_sum))
     partial_out = jnp.dot(hidden, w_down_here, preferred_element_type=jnp.float32)
+    partial_out, shared_sum = lax.optimization_barrier((partial_out, shared_sum))
     partial_split = partial_out.reshape(expert_rows, tp_count, col_share).transpose(1, 0, 2)
     expert_sum = sum(
         shift_exchange(partial_split.reshape(tp_count, expert_rows * col_share), "tp", tp_count)

time: 113 us -> 112 us (level)
  waiting for transfers between devices: 42.7 us -> 40 us
  matrix products: 22.9 us -> 24.6 us
  other arithmetic: 10.1 us -> 11.4 us
    ppermute x12, waiting for transfers between devices: 15.9 us -> 11.7 us  [shift_exchange(): pieces.append(lax.ppermute(send, axis, pairs))]
    all_to_all x1, waiting for transfers between devices: 7.92 us -> 9.34 us  [per_device(): back = lax.all_to_all(back_in, 'req', 0, 0, tiled=True)]
    dot_general x1, matrix products: 1.78 us -> 2.93 us  [per_device(): jnp.dot(hidden, w_down_here, preferred_element_type=jnp.float32)]
  transfers between devices with their start and end apart: 16 -> 16, of which waited for: 11 -> 11; matrix products, arithmetic and copies ran while one was open for 11% -> 13% of each run, Pallas kernels for 0% -> 0%
where the time goes in v11:
time: 112 us; the launch traced here: 111 us
  waiting for transfers between devices  40 us (36%)
  starting transfers between devices  25.5 us (23%)
  matrix products  24.6 us (22%)
  other arithmetic  11.4 us (10%)
  local copies, waits for them, and re-layouts  8.81 us (8%)
    ppermute x12, waiting for transfers between devices, shift_exchange(): pieces.append(lax.ppermute(send, axis, pairs))  11.7 us
    all_to_all x1, waiting for transfers between devices, per_device(): back = lax.all_to_all(back_in, 'req', 0, 0, tiled=True)  9.34 us
    all_to_all x1, waiting for transfers between devices, per_device(): lax.all_to_all(packed, 'req', 0, 0, tiled=True)  8.64 us
    all_to_all x1, waiting for transfers between devices, per_device(): received = lax.all_to_all(dispatch, 'req', 0, 0, tiled=True)  8.28 us
    all_to_all x1, starting transfers between devices, per_device(): lax.all_to_all(query_spread, 'req', 0, 0, tiled=True)  7.29 us
    ppermute x12, starting transfers between devices, shift_exchange(): pieces.append(lax.ppermute(send, axis, pairs))  6.95 us
    all_to_all x1, starting transfers between devices, per_device(): lax.all_to_all(packed, 'req', 0, 0, tiled=True)  4.05 us
    dot_general x1, matrix products, per_device(): jnp.einsum('pxd,pkd->pxk', block_queries, cache_keys, preferred_element_t...  4.03 us
  transfers between devices with their start and end apart: 16, of which 11 were waited for; matrix products, arithmetic and copies ran while one was open for 13% of the time, Pallas kernels for 0%

profile of v11, /device:TPU:0, one launch (start us, length us, event | category | flops | bytes accessed | tf_op | source)
XLA Modules:
  0.0 111.0 jit_solution(7837707608594642366)
XLA Ops:
  4.3 2.0 %fusion.34 = f32[3,4,4,128]{3,1,2,0:T(4,128)S(1)} fusion(bf16[3,4,2048]{2,1,0:T(4,128)(2,1)S(1)} %multiply_convert_fusion.1, bf16[2048,3,512]{2,0,1:T(8,128)(2,1)} %param.21, f32[512]{0:T(512)S(1)} %bitcast.205), kind=kOutput, calls=%fused_computation.29 | convolution fusion | flops 25171968 | bytes 2172928 | tf_op jit(solution)/shard_map/rsd,df->rsf/dot_general | solution.py:109
  7.2 7.3 %all-to-all-start = ((bf16[8,3,4,4,128]{4,3,2,1,0:T(4,128)(2,1)}), bf16[8,3,4,4,128]{4,3,2,1,0:T(4,128)(2,1)S(1)}, u32[]{:S(2)}, u32[]{:S(2)}) async-start(bf16[8,3,4,4,128]{4,3,2,1,0:T(4,128)(2,1)} %broadcast_in_dim.197), calls=%async_computation | async-start | bytes 196608 | tf_op jit(solution)/shard_map/all_to_all | solution.py:116
  16.2 2.9 %fusion.24 = f32[3,4,2,512]{3,1,2,0:T(4,128)S(1)} fusion(bf16[2048,3,512]{2,0,1:T(8,128)(2,1)} %param.21, bf16[3,4,2048]{2,1,0:T(4,128)(2,1)S(1)} %multiply_convert_fusion.1, f32[2,512]{1,0:T(2,128)S(1)} %slice_convert_fusion.1), kind=kOutput, calls=%fused_computation.24 | convolution fusion | flops 50343936 | bytes 4296704 | tf_op jit(solution)/shard_map/rsd,dcf->rscf/dot_general | solution.py:119
  19.6 2.0 %all-to-all-done = bf16[8,3,4,4,128]{4,3,2,1,0:T(4,128)(2,1)S(1)} async-done(((bf16[8,3,4,4,128]{4,3,2,1,0:T(4,128)(2,1)}), bf16[8,3,4,4,128]{4,3,2,1,0:T(4,128)(2,1)S(1)}, u32[]{:S(2)}, u32[]{:S(2)}) %all-to-all-start) | async-done | bytes 98336 | tf_op jit(solution)/shard_map/all_to_all | solution.py:116
  22.9 4.0 %select_reduce_fusion.2 = (f32[40,16]{1,0:T(8,128)S(1)}, f32[40,16,128]{2,1,0:T(8,128)S(1)}) fusion(pred[40,128]{1,0:T(8,128)(4,1)S(1)} %fusion.84, bf16[40,128,512]{2,1,0:T(8,128)(2,1)} %param.24, bf16[40,16,512]{2,1,0:T(8,128)(2,1)S(1)} %broadcast_in_dim.199, pred[16,512]{1,0:T(8,128)(4,1)S(1)} %bitcast.202), kind=kOutput, calls=%fused_computation.64 | convolution fusion | flops 84458880 | bytes 6241792 | tf_op jit(solution)/shard_map/pxd,pkd->pxk/dot_general | solution.py:140
  28.3 4.0 %fusion.15 = f32[40,4,4,128]{3,1,2,0:T(4,128)S(1)} fusion(f32[40,4,4,128]{3,2,1,0:T(4,128)S(1)} %bitcast.173, f32[40,4,4]{1,2,0:T(4,128)S(1)} %copy.82, pred[40,128]{1,0:T(8,128)(4,1)S(1)} %fusion.84, bf16[40,128,512]{2,1,0:T(8,128)(2,1)} %param.25), kind=kOutput, calls=%fused_computation.21 | convolution fusion | flops 21299200 | bytes 5905920 | tf_op jit(solution)/shard_map/pshk,pkhd->pshd/dot_general | solution.py:148
  33.7 4.0 %all-to-all-start.1 = ((f32[24,17,128]{2,1,0:T(8,128)}), f32[24,17,128]{2,1,0:T(8,128)S(1)}, u32[]{:S(2)}, u32[]{:S(2)}) async-start(f32[24,17,128]{2,1,0:T(8,128)} %pad_maximum_fusion.2), calls=%async_computation.1 | async-start | bytes 589824 | tf_op jit(solution)/shard_map/all_to_all | solution.py:172
  38.2 8.6 %all-to-all-done.1 = f32[24,17,128]{2,1,0:T(8,128)S(1)} async-done(((f32[24,17,128]{2,1,0:T(8,128)}), f32[24,17,128]{2,1,0:T(8,128)S(1)}, u32[]{:S(2)}, u32[]{:S(2)}) %all-to-all-start.1) | async-done | bytes 208928 | tf_op jit(solution)/shard_map/all_to_all | solution.py:172
  48.4 1.5 %collective-permute-start.1 = (f32[12,2048]{1,0:T(8,128)S(1)}, f32[12,2048]{1,0:T(8,128)S(1)}, u32[]{:S(2)}, u32[]{:S(2)}) collective-permute-start(f32[12,2048]{1,0:T(8,128)S(1)} %fusion.126), channel_id=1, source_target_pairs={{0,2},{1,3},{2,0},{3,1},{4,6},{5,7},{6,4},{7,5},{8,10},{9,11},{10,... | collective-permute-start | bytes 294920 | tf_op jit(solution)/shard_map/ppermute | solution.py:51
  50.1 1.1 %collective-permute-done.2 = f32[12,2048]{1,0:T(8,128)S(1)} collective-permute-done((f32[12,2048]{1,0:T(8,128)S(1)}, f32[12,2048]{1,0:T(8,128)S(1)}, u32[]{:S(2)}, u32[]{:S(2)}) %collective-permute-start.2) | collective-permute-done | bytes 98336 | tf_op jit(solution)/shard_map/ppermute | solution.py:51
  51.2 5.7 %collective-permute-done.1 = f32[12,2048]{1,0:T(8,128)S(1)} collective-permute-done((f32[12,2048]{1,0:T(8,128)S(1)}, f32[12,2048]{1,0:T(8,128)S(1)}, u32[]{:S(2)}, u32[]{:S(2)}) %collective-permute-start.1) | collective-permute-done | bytes 98336 | tf_op jit(solution)/shard_map/ppermute | solution.py:51
  59.8 3.6 %all-to-all-start.2 = ((bf16[8,144,128]{2,1,0:T(8,128)(2,1)}), bf16[8,144,128]{2,1,0:T(8,128)(2,1)S(1)}, u32[]{:S(2)}, u32[]{:S(2)}) async-start(bf16[8,144,128]{2,1,0:T(8,128)(2,1)} %pad_maximum_fusion.3), calls=%async_computation.2 | async-start | bytes 589824 | tf_op jit(solution)/shard_map/all_to_all | solution.py:248
  63.6 8.3 %all-to-all-done.2 = bf16[8,144,128]{2,1,0:T(8,128)(2,1)S(1)} async-done(((bf16[8,144,128]{2,1,0:T(8,128)(2,1)}), bf16[8,144,128]{2,1,0:T(8,128)(2,1)S(1)}, u32[]{:S(2)}, u32[]{:S(2)}) %all-to-all-start.2) | async-done | bytes 294944 | tf_op jit(solution)/shard_map/all_to_all | solution.py:248
  72.1 1.5 %fusion.128 = f32[96,704]{1,0:T(8,128)S(1)} fusion(bf16[96,512]{1,0:T(8,128)(2,1)S(1)} %reshape.451, bf16[512,704]{0,1:T(8,128)(2,1)} %param.35), kind=kOutput, calls=%fused_computation.207 | convolution fusion | flops 69206016 | bytes 1089536 | tf_op jit(solution)/shard_map/dot_general | solution.py:253
  75.4 1.1 %collective-permute-start.4 = (f32[33792]{0:T(1024)S(1)}, f32[33792]{0:T(1024)}, u32[]{:S(2)}, u32[]{:S(2)}) collective-permute-start(f32[33792]{0:T(1024)S(1)} %bitcast.182), channel_id=1, source_target_pairs={{0,2},{1,3},{2,0},{3,1},{4,6},{5,7},{6,4},{7,5},{8,10},{9,11},{10,... | collective-permute-start | bytes 405512 | tf_op jit(solution)/shard_map/ppermute | solution.py:51
  76.5 1.9 %fusion.13 = f32[48,352]{1,0:T(8,128)S(1)} fusion(bf16[48,2048]{1,0:T(8,128)(2,1)S(1)} %reshape.450, bf16[1,2048,352]{1,2,0:T(8,128)(2,1)} %param.31), kind=kOutput, calls=%fused_computation.18 | convolution fusion | flops 69206016 | bytes 1705984 | tf_op jit(solution)/shard_map/dot_general | solution.py:261
  78.4 2.9 %fusion.9 = f32[48,2048]{1,0:T(8,128)S(1)} fusion(bf16[1,352,2048]{2,1,0:T(8,128)(2,1)} %param.33, bf16[48,2048]{1,0:T(8,128)(2,1)S(1)} %reshape.450, bf16[1,2048,352]{1,2,0:T(8,128)(2,1)} %param.32, f32[48,352]{1,0:T(8,128)S(1)} %fusion.13), kind=kOutput, calls=%fused_computation.14 | convolution fusion | flops 138513408 | bytes 3540992 | tf_op jit(solution)/shard_map/dot_general | solution.py:267
  81.4 1.8 %collective-permute-done.4 = f32[33792]{0:T(1024)} collective-permute-done((f32[33792]{0:T(1024)S(1)}, f32[33792]{0:T(1024)}, u32[]{:S(2)}, u32[]{:S(2)}) %collective-permute-start.4) | collective-permute-done | bytes 135200 | tf_op jit(solution)/shard_map/ppermute | solution.py:51
  83.2 1.1 add_add_fusion
  85.7 1.7 %collective-permute-start.11 = (bf16[24,704]{1,0:T(8,128)(2,1)}, bf16[24,704]{1,0:T(8,128)(2,1)}, u32[]{:S(2)}, u32[]{:S(2)}) collective-permute-start(bf16[24,704]{1,0:T(8,128)(2,1)} %multiply_convert_fusion.2), channel_id=1, source_target_pairs={{0,3},{1,0},{2,1},{3,2},{4,7},{5,4},{6,5},{7,6},{8,11},{9,8},{10,9... | collective-permute-start | bytes 101384 | tf_op jit(solution)/shard_map/ppermute | solution.py:51
  91.5 1.4 %fusion.129 = f32[96,512]{1,0:T(8,128)S(1)} fusion(bf16[96,704]{1,0:T(8,128)(2,1)S(1)} %bitcast_select_fusion, bf16[704,512]{1,0:T(8,128)(2,1)} %param.36), kind=kOutput, calls=%fused_computation.208 | convolution fusion | flops 69206016 | bytes 1052672 | tf_op jit(solution)/shard_map/dot_general | solution.py:279
  93.3 1.9 %collective-permute-done.7 = f32[24576]{0:T(1024)S(1)} collective-permute-done((f32[24576]{0:T(1024)S(1)}, f32[24576]{0:T(1024)S(1)}, u32[]{:S(2)}, u32[]{:S(2)}) %collective-permute-start.7) | collective-permute-done | bytes 98336 | tf_op jit(solution)/shard_map/ppermute | solution.py:51
  95.9 3.6 %all-to-all-start.3 = ((f32[8,72,128]{2,1,0:T(8,128)}), f32[8,72,128]{2,1,0:T(8,128)S(1)}, u32[]{:S(2)}, u32[]{:S(2)}) async-start(f32[8,72,128]{2,1,0:T(8,128)} %pad_maximum_fusion.4), calls=%async_computation.3 | async-start | bytes 589824 | tf_op jit(solution)/shard_map/all_to_all | solution.py:289
  100.1 9.3 %all-to-all-done.3 = f32[8,72,128]{2,1,0:T(8,128)S(1)} async-done(((f32[8,72,128]{2,1,0:T(8,128)}), f32[8,72,128]{2,1,0:T(8,128)S(1)}, u32[]{:S(2)}, u32[]{:S(2)}) %all-to-all-start.3) | async-done | bytes 294944 | tf_op jit(solution)/shard_map/all_to_all | solution.py:289
  (166 shorter events, 27.1 us)
Async XLA Ops:
  0.0 48.0 %copy-start = (bf16[512,2048]{1,0:T(8,128)(2,1)S(1)}, bf16[512,2048]{1,0:T(8,128)(2,1)}, u32[]{:S(2)}) copy-start(bf16[512,2048]{1,0:T(8,128)(2,1)} %param.23) | copy-start | bytes 6291460
  0.0 15.1 %copy-start.1 = (s32[24]{0:T(128)S(1)}, s32[24]{0:T(128)}, u32[]{:S(2)}) copy-start(s32[24]{0:T(128)} %param.27) | copy-start | bytes 292
  0.0 14.5 %copy-start.9 = (bf16[3,512]{1,0:T(4,128)(2,1)S(1)}, bf16[3,512]{1,0:T(4,128)(2,1)}, u32[]{:S(2)}) copy-start(bf16[3,512]{1,0:T(4,128)(2,1)} %param.22) | copy-start | bytes 9220
  0.0 14.5 %copy-start.5 = (s32[3,4,4]{2,1,0:T(4,128)S(1)}, s32[3,4,4]{2,1,0:T(4,128)}, u32[]{:S(2)}) copy-start(s32[3,4,4]{2,1,0:T(4,128)} %param.29) | copy-start | bytes 580
  0.0 14.7 %copy-start.4 = (s32[24,37]{1,0:T(8,128)S(1)}, s32[24,37]{1,0:T(8,128)}, u32[]{:S(2)}) copy-start(s32[24,37]{1,0:T(8,128)} %param.26) | copy-start | bytes 10660
  7.2 14.4 %all-to-all-start = ((bf16[8,3,4,4,128]{4,3,2,1,0:T(4,128)(2,1)}), bf16[8,3,4,4,128]{4,3,2,1,0:T(4,128)(2,1)S(1)}, u32[]{:S(2)}, u32[]{:S(2)}) async-start(bf16[8,3,4,4,128]{4,3,2,1,0:T(4,128)(2,1)} %broadcast_in_dim.197), calls=%async_computation | async-start | bytes 196608 | tf_op jit(solution)/shard_map/all_to_all | solution.py:116
  19.6 18.3 %copy-start.10 = (s32[48]{0:T(128)}, s32[48]{0:T(128)S(1)}, u32[]{:S(2)}) copy-start(s32[48]{0:T(128)S(1)} %get-tuple-element.48) | copy-start | bytes 580
  19.6 18.3 %copy-start.12 = (s32[48]{0:T(128)}, s32[48]{0:T(128)S(1)}, u32[]{:S(2)}) copy-start(s32[48]{0:T(128)S(1)} %get-tuple-element.49) | copy-start | bytes 580
  33.7 13.1 %all-to-all-start.1 = ((f32[24,17,128]{2,1,0:T(8,128)}), f32[24,17,128]{2,1,0:T(8,128)S(1)}, u32[]{:S(2)}, u32[]{:S(2)}) async-start(f32[24,17,128]{2,1,0:T(8,128)} %pad_maximum_fusion.2), calls=%async_computation.1 | async-start | bytes 589824 | tf_op jit(solution)/shard_map/all_to_all | solution.py:172
  48.3 2.9 %collective-permute-start.2 = (f32[12,2048]{1,0:T(8,128)S(1)}, f32[12,2048]{1,0:T(8,128)S(1)}, u32[]{:S(2)}, u32[]{:S(2)}) collective-permute-start(f32[12,2048]{1,0:T(8,128)S(1)} %fusion.126), channel_id=1, source_target_pairs={{0,3},{1,0},{2,1},{3,2},{4,7},{5,4},{6,5},{7,6},{8,11},{9,8},{10,9... | collective-permute-start | bytes 294920 | tf_op jit(solution)/shard_map/ppermute | solution.py:51
  48.4 8.6 %collective-permute-start.1 = (f32[12,2048]{1,0:T(8,128)S(1)}, f32[12,2048]{1,0:T(8,128)S(1)}, u32[]{:S(2)}, u32[]{:S(2)}) collective-permute-start(f32[12,2048]{1,0:T(8,128)S(1)} %fusion.126), channel_id=1, source_target_pairs={{0,2},{1,3},{2,0},{3,1},{4,6},{5,7},{6,4},{7,5},{8,10},{9,11},{10,... | collective-permute-start | bytes 294920 | tf_op jit(solution)/shard_map/ppermute | solution.py:51
  49.9 7.1 %collective-permute-start = (f32[12,2048]{1,0:T(8,128)S(1)}, f32[12,2048]{1,0:T(8,128)S(1)}, u32[]{:S(2)}, u32[]{:S(2)}) collective-permute-start(f32[12,2048]{1,0:T(8,128)S(1)} %fusion.126), channel_id=1, source_target_pairs={{0,1},{1,2},{2,3},{3,0},{4,5},{5,6},{6,7},{7,4},{8,9},{9,10},{10,1... | collective-permute-start | bytes 294920 | tf_op jit(solution)/shard_map/ppermute | solution.py:51
  59.0 14.6 %copy-start.3 = (bf16[512,704]{0,1:T(8,128)(2,1)S(1)}, bf16[512,704]{0,1:T(8,128)(2,1)}, u32[]{:S(2)}) copy-start(bf16[512,704]{0,1:T(8,128)(2,1)} %param.34) | copy-start | bytes 2162692
  59.8 12.1 %all-to-all-start.2 = ((bf16[8,144,128]{2,1,0:T(8,128)(2,1)}), bf16[8,144,128]{2,1,0:T(8,128)(2,1)S(1)}, u32[]{:S(2)}, u32[]{:S(2)}) async-start(bf16[8,144,128]{2,1,0:T(8,128)(2,1)} %pad_maximum_fusion.3), calls=%async_computation.2 | async-start | bytes 589824 | tf_op jit(solution)/shard_map/all_to_all | solution.py:248
  74.8 6.6 %collective-permute-start.5 = (f32[33792]{0:T(1024)S(1)}, f32[33792]{0:T(1024)}, u32[]{:S(2)}, u32[]{:S(2)}) collective-permute-start(f32[33792]{0:T(1024)S(1)} %bitcast.184), channel_id=1, source_target_pairs={{0,3},{1,0},{2,1},{3,2},{4,7},{5,4},{6,5},{7,6},{8,11},{9,8},{10,9... | collective-permute-start | bytes 405512 | tf_op jit(solution)/shard_map/ppermute | solution.py:51
  74.9 6.5 %collective-permute-start.3 = (f32[33792]{0:T(1024)S(1)}, f32[33792]{0:T(1024)}, u32[]{:S(2)}, u32[]{:S(2)}) collective-permute-start(f32[33792]{0:T(1024)S(1)} %bitcast.183), channel_id=1, source_target_pairs={{0,1},{1,2},{2,3},{3,0},{4,5},{5,6},{6,7},{7,4},{8,9},{9,10},{10,1... | collective-permute-start | bytes 405512 | tf_op jit(solution)/shard_map/ppermute | solution.py:51
  75.4 7.8 %collective-permute-start.4 = (f32[33792]{0:T(1024)S(1)}, f32[33792]{0:T(1024)}, u32[]{:S(2)}, u32[]{:S(2)}) collective-permute-start(f32[33792]{0:T(1024)S(1)} %bitcast.182), channel_id=1, source_target_pairs={{0,2},{1,3},{2,0},{3,1},{4,6},{5,7},{6,4},{7,5},{8,10},{9,11},{10,... | collective-permute-start | bytes 405512 | tf_op jit(solution)/shard_map/ppermute | solution.py:51
  85.0 4.5 %collective-permute-start.10 = (bf16[24,704]{1,0:T(8,128)(2,1)}, bf16[24,704]{1,0:T(8,128)(2,1)S(1)}, u32[]{:S(2)}, u32[]{:S(2)}) collective-permute-start(bf16[24,704]{1,0:T(8,128)(2,1)} %multiply_convert_fusion.2), channel_id=1, source_target_pairs={{0,2},{1,3},{2,0},{3,1},{4,6},{5,7},{6,4},{7,5},{8,10},{9,11},{10,... | collective-permute-start | bytes 101384 | tf_op jit(solution)/shard_map/ppermute | solution.py:51
  85.6 4.5 %collective-permute-start.9 = (bf16[24,704]{1,0:T(8,128)(2,1)}, bf16[24,704]{1,0:T(8,128)(2,1)S(1)}, u32[]{:S(2)}, u32[]{:S(2)}) collective-permute-start(bf16[24,704]{1,0:T(8,128)(2,1)} %multiply_convert_fusion.2), channel_id=1, source_target_pairs={{0,1},{1,2},{2,3},{3,0},{4,5},{5,6},{6,7},{7,4},{8,9},{9,10},{10,1... | collective-permute-start | bytes 101384 | tf_op jit(solution)/shard_map/ppermute | solution.py:51
  85.7 4.4 %collective-permute-start.11 = (bf16[24,704]{1,0:T(8,128)(2,1)}, bf16[24,704]{1,0:T(8,128)(2,1)}, u32[]{:S(2)}, u32[]{:S(2)}) collective-permute-start(bf16[24,704]{1,0:T(8,128)(2,1)} %multiply_convert_fusion.2), channel_id=1, source_target_pairs={{0,3},{1,0},{2,1},{3,2},{4,7},{5,4},{6,5},{7,6},{8,11},{9,8},{10,9... | collective-permute-start | bytes 101384 | tf_op jit(solution)/shard_map/ppermute | solution.py:51
  88.1 4.8 %collective-permute-start.8 = (f32[24576]{0:T(1024)S(1)}, f32[24576]{0:T(1024)S(1)}, u32[]{:S(2)}, u32[]{:S(2)}) collective-permute-start(f32[24576]{0:T(1024)S(1)} %bitcast.194), channel_id=1, source_target_pairs={{0,3},{1,0},{2,1},{3,2},{4,7},{5,4},{6,5},{7,6},{8,11},{9,8},{10,9... | collective-permute-start | bytes 294920 | tf_op jit(solution)/shard_map/ppermute | solution.py:51
  88.2 5.1 %collective-permute-start.6 = (f32[24576]{0:T(1024)S(1)}, f32[24576]{0:T(1024)S(1)}, u32[]{:S(2)}, u32[]{:S(2)}) collective-permute-start(f32[24576]{0:T(1024)S(1)} %bitcast.193), channel_id=1, source_target_pairs={{0,1},{1,2},{2,3},{3,0},{4,5},{5,6},{6,7},{7,4},{8,9},{9,10},{10,1... | collective-permute-start | bytes 294920 | tf_op jit(solution)/shard_map/ppermute | solution.py:51
  89.4 5.7 %collective-permute-start.7 = (f32[24576]{0:T(1024)S(1)}, f32[24576]{0:T(1024)S(1)}, u32[]{:S(2)}, u32[]{:S(2)}) collective-permute-start(f32[24576]{0:T(1024)S(1)} %bitcast.192), channel_id=1, source_target_pairs={{0,2},{1,3},{2,0},{3,1},{4,6},{5,7},{6,4},{7,5},{8,10},{9,11},{10,... | collective-permute-start | bytes 294920 | tf_op jit(solution)/shard_map/ppermute | solution.py:51
  95.9 13.5 %all-to-all-start.3 = ((f32[8,72,128]{2,1,0:T(8,128)}), f32[8,72,128]{2,1,0:T(8,128)S(1)}, u32[]{:S(2)}, u32[]{:S(2)}) async-start(f32[8,72,128]{2,1,0:T(8,128)} %pad_maximum_fusion.4), calls=%async_computation.3 | async-start | bytes 589824 | tf_op jit(solution)/shard_map/all_to_all | solution.py:289
  (6 other events, 57.3 us)

commit v12 on v11

--- a/solution.py
+++ b/solution.py
@@ -105,17 +105,17 @@
     positions = own_lengths[:, None] + jnp.arange(step_count, dtype=jnp.int32)[None, :]
     head_shape = (req_rows, step_count, local_heads, HD)
 
-    def project(part, rows):
-        return jnp.einsum(
-            "rsd,df->rsf", rows, qkv_weight[:, part], preferred_element_type=jnp.float32
-        ) + qkv_bias[part].astype(jnp.float32)
-
-    query_new = rotate(project(0, normed).reshape(head_shape), positions).astype(jnp.bfloat16)
-    query_spread = jnp.broadcast_to(query_new[None], (req_count,) + query_new.shape)
-    normed_late, query_spread = lax.optimization_barrier((normed, query_spread))
-    query_all = lax.all_to_all(query_spread, "req", 0, 0, tiled=True).reshape(
-        (req_count * req_rows,) + query_new.shape[1:]
-    )
+    tokens_all = bcast_a2a(tokens_in, "req", req_count)
+    normed_all = rms_norm(tokens_all, attn_norm)
+    query_proj = jnp.einsum(
+        "rsd,df->rsf", normed_all, qkv_weight[:, 0], preferred_element_type=jnp.float32
+    ) + qkv_bias[0].astype(jnp.float32)
+    all_positions = cache_lengths[:, None] + jnp.arange(step_count, dtype=jnp.int32)[None, :]
+    query_all = rotate(
+        query_proj.reshape(all_requests, step_count, local_heads, HD), all_positions
+    ).astype(jnp.bfloat16)
+    query_new = lax.dynamic_slice_in_dim(query_all, req_index * req_rows, req_rows)
+    normed_late = normed
     key_value = jnp.einsum(
         "rsd,dcf->rscf", normed_late, qkv_weight[:, 1:], preferred_element_type=jnp.float32
     ) + qkv_bias[1:].astype(jnp.float32)

time: 112 us -> 124 us (1.11)
  local copies, waits for them, and re-layouts: 8.81 us -> 14.9 us
  other arithmetic: 11.4 us -> 17 us
  waiting for transfers between devices: 40 us -> 36.7 us
  starting transfers between devices: 25.5 us -> 27.4 us
  matrix products: 24.6 us -> 26.1 us
    unnamed x33 -> x49, local copies, waits for them, and re-layouts: 0.18 us -> 2.15 us
    all_to_all x1, waiting for transfers between devices: 1.95 us -> 0.01 us  [bcast_a2a(): lax.all_to_all(spread, axis, 0, 0, tiled=True)]
    all_to_all x1, starting transfers between devices: 4.05 us -> 6 us  [per_device(): lax.all_to_all(packed, 'req', 0, 0, tiled=True)]
  transfers between devices with their start and end apart: 16 -> 16, of which waited for: 11 -> 10; matrix products, arithmetic and copies ran while one was open for 13% -> 22% of each run, Pallas kernels for 0% -> 0%
where the time goes in v12:
time: 124 us; the launch traced here: 123 us
  waiting for transfers between devices  36.7 us (30%)
  starting transfers between devices  27.4 us (22%)
  matrix products  26.1 us (21%)
  other arithmetic  17 us (14%)
  local copies, waits for them, and re-layouts  14.9 us (12%)
    ppermute x12, waiting for transfers between devices, shift_exchange(): pieces.append(lax.ppermute(send, axis, pairs))  11.6 us
    all_to_all x1, waiting for transfers between devices, per_device(): back = lax.all_to_all(back_in, 'req', 0, 0, tiled=True)  9.33 us
    all_to_all x1, waiting for transfers between devices, per_device(): received = lax.all_to_all(dispatch, 'req', 0, 0, tiled=True)  8.28 us
    all_to_all x1, waiting for transfers between devices, per_device(): lax.all_to_all(packed, 'req', 0, 0, tiled=True)  7.49 us
    all_to_all x1, starting transfers between devices, bcast_a2a(): lax.all_to_all(spread, axis, 0, 0, tiled=True)  7.28 us
    ppermute x12, starting transfers between devices, shift_exchange(): pieces.append(lax.ppermute(send, axis, pairs))  6.84 us
    all_to_all x1, starting transfers between devices, per_device(): lax.all_to_all(packed, 'req', 0, 0, tiled=True)  6 us
    dot_general x1, matrix products, per_device(): jnp.einsum('pxd,pkd->pxk', block_queries, cache_keys, preferred_element_t...  4.03 us
  transfers between devices with their start and end apart: 16, of which 10 were waited for; matrix products, arithmetic and copies ran while one was open for 22% of the time, Pallas kernels for 0%

profile of v12, /device:TPU:0, one launch (start us, length us, event | category | flops | bytes accessed | tf_op | source)
XLA Modules:
  0.0 122.8 jit_solution(15467094467298233356)
XLA Ops:
  0.0 1.9 %broadcast_in_dim.201 = bf16[8,3,4,2048]{3,2,1,0:T(4,128)(2,1)} broadcast(bf16[3,4,2048]{2,1,0:T(4,128)(2,1)} %param.19), dimensions={1,2,3} | broadcast | bytes 442368 | tf_op jit(solution)/shard_map/broadcast_in_dim | solution.py:63
  1.9 7.3 %all-to-all-start = ((bf16[8,3,4,2048]{3,2,1,0:T(4,128)(2,1)}), bf16[8,3,4,2048]{3,2,1,0:T(4,128)(2,1)S(1)}, u32[]{:S(2)}, u32[]{:S(2)}) async-start(bf16[8,3,4,2048]{3,2,1,0:T(4,128)(2,1)} %broadcast_in_dim.201), calls=%async_computation | async-start | bytes 786432 | tf_op jit(solution)/shard_map/all_to_all | solution.py:64
  16.8 1.4 %gather_fusion = s32[40]{0:T(128)S(1)} fusion(s32[24]{0:T(128)} %param.27, s32[1024]{0:T(1024)S(1)} %pad_clamp_fusion.1), kind=kCustom, calls=%fused_computation | custom fusion | bytes 480 | tf_op jit(solution)/shard_map/gather | solution.py:132
  20.2 2.9 %fusion.27 = f32[3,4,2,512]{3,1,2,0:T(4,128)S(1)} fusion(bf16[2048,3,512]{2,0,1:T(8,128)(2,1)} %param.21, bf16[3,4,2048]{2,1,0:T(4,128)(2,1)S(1)} %copy-done.3, f32[2048]{0:T(1024)S(1)} %convert_element_type.115, f32[3,4]{1,0:T(4,128)S(1)} %add_rsqrt_fusion.2, f32[2,512]{1,0:T(2,128)S(1)} %slice_convert_fusion.1), kind=kOutput, calls=%fused_computation.25 | convolution fusion | flops 50442240 | bytes 4304944 | tf_op jit(solution)/shard_map/rsd,dcf->rscf/dot_general | solution.py:119
  26.1 2.1 %fusion.18 = f32[24,4,512]{2,0,1:T(8,128)S(1)} fusion(bf16[2048,3,512]{2,0,1:T(8,128)(2,1)} %param.21, bf16[24,4,2048]{2,1,0:T(4,128)(2,1)S(1)} %bitcast.175, f32[512]{0:T(512)S(1)} %bitcast.202), kind=kOutput, calls=%fused_computation.22 | convolution fusion | flops 201375744 | bytes 2689024 | tf_op jit(solution)/shard_map/rsd,df->rsf/dot_general | solution.py:110
  31.0 4.0 %select_reduce_fusion.2 = (f32[40,16]{1,0:T(8,128)S(1)}, f32[40,16,128]{2,1,0:T(8,128)S(1)}) fusion(pred[40,128]{1,0:T(8,128)(4,1)} %fusion.88, bf16[40,128,512]{2,1,0:T(8,128)(2,1)} %param.24, bf16[40,16,512]{2,1,0:T(8,128)(2,1)S(1)} %broadcast_in_dim.203, pred[16,512]{1,0:T(8,128)(4,1)} %bitcast.197), kind=kOutput, calls=%fused_computation.69 | convolution fusion | flops 84458880 | bytes 6241792 | tf_op jit(solution)/shard_map/pxd,pkd->pxk/dot_general | solution.py:140
  36.4 4.0 %fusion.15 = f32[40,4,4,128]{3,1,2,0:T(4,128)S(1)} fusion(f32[40,4,4,128]{3,2,1,0:T(4,128)S(1)} %bitcast.168, f32[40,4,4]{1,2,0:T(4,128)S(1)} %copy.86, pred[40,128]{1,0:T(8,128)(4,1)} %fusion.88, bf16[40,128,512]{2,1,0:T(8,128)(2,1)} %param.25), kind=kOutput, calls=%fused_computation.21 | convolution fusion | flops 21299200 | bytes 5905920 | tf_op jit(solution)/shard_map/pshk,pkhd->pshd/dot_general | solution.py:148
  41.9 6.0 %all-to-all-start.1 = ((f32[24,17,128]{2,1,0:T(8,128)}), f32[24,17,128]{2,1,0:T(8,128)S(1)}, u32[]{:S(2)}, u32[]{:S(2)}) async-start(f32[24,17,128]{2,1,0:T(8,128)} %pad_maximum_fusion.2), calls=%async_computation.1 | async-start | bytes 589824 | tf_op jit(solution)/shard_map/all_to_all | solution.py:172
  49.5 7.5 %all-to-all-done.1 = f32[24,17,128]{2,1,0:T(8,128)S(1)} async-done(((f32[24,17,128]{2,1,0:T(8,128)}), f32[24,17,128]{2,1,0:T(8,128)S(1)}, u32[]{:S(2)}, u32[]{:S(2)}) %all-to-all-start.1) | async-done | bytes 208928 | tf_op jit(solution)/shard_map/all_to_all | solution.py:172
  58.5 1.5 %collective-permute-start.1 = (f32[12,2048]{1,0:T(8,128)S(1)}, f32[12,2048]{1,0:T(8,128)S(1)}, u32[]{:S(2)}, u32[]{:S(2)}) collective-permute-start(f32[12,2048]{1,0:T(8,128)S(1)} %fusion.134), channel_id=1, source_target_pairs={{0,2},{1,3},{2,0},{3,1},{4,6},{5,7},{6,4},{7,5},{8,10},{9,11},{10,... | collective-permute-start | bytes 294920 | tf_op jit(solution)/shard_map/ppermute | solution.py:51
  61.4 5.7 %collective-permute-done.1 = f32[12,2048]{1,0:T(8,128)S(1)} collective-permute-done((f32[12,2048]{1,0:T(8,128)S(1)}, f32[12,2048]{1,0:T(8,128)S(1)}, u32[]{:S(2)}, u32[]{:S(2)}) %collective-permute-start.1) | collective-permute-done | bytes 98336 | tf_op jit(solution)/shard_map/ppermute | solution.py:51
  68.3 1.6 %multiply_convert_fusion = (bf16[12,2048]{1,0:T(8,128)(2,1)S(1)}, f32[12,2048]{1,0:T(8,128)}) fusion(f32[2048]{0:T(1024)} %convert_element_type.131, f32[12]{0:T(128)S(1)} %rsqrt.30, f32[12,2048]{1,0:T(8,128)} %reshape.488, f32[12,2048]{1,0:T(8,128)S(1)} %select_reduce_fusion), kind=kLoop, calls=%fused_computation.88 | loop fusion | flops 98304 | bytes 352304 | tf_op jit(solution)/shard_map/convert_element_type | solution.py:22
  71.7 3.6 %all-to-all-start.2 = ((bf16[8,144,128]{2,1,0:T(8,128)(2,1)}), bf16[8,144,128]{2,1,0:T(8,128)(2,1)S(1)}, u32[]{:S(2)}, u32[]{:S(2)}) async-start(bf16[8,144,128]{2,1,0:T(8,128)(2,1)} %pad_maximum_fusion.3), calls=%async_computation.2 | async-start | bytes 589824 | tf_op jit(solution)/shard_map/all_to_all | solution.py:248
  75.5 8.3 %all-to-all-done.2 = bf16[8,144,128]{2,1,0:T(8,128)(2,1)S(1)} async-done(((bf16[8,144,128]{2,1,0:T(8,128)(2,1)}), bf16[8,144,128]{2,1,0:T(8,128)(2,1)S(1)}, u32[]{:S(2)}, u32[]{:S(2)}) %all-to-all-start.2) | async-done | bytes 294944 | tf_op jit(solution)/shard_map/all_to_all | solution.py:248
  84.4 1.5 %fusion.135 = f32[96,704]{1,0:T(8,128)S(1)} fusion(bf16[96,512]{1,0:T(8,128)(2,1)S(1)} %reshape.480, bf16[512,704]{0,1:T(8,128)(2,1)} %param.34), kind=kOutput, calls=%fused_computation.222 | convolution fusion | flops 69206016 | bytes 1089536 | tf_op jit(solution)/shard_map/dot_general | solution.py:252
  87.3 1.1 collective-permute-start.4
  88.4 1.9 %fusion.13 = f32[48,352]{1,0:T(8,128)S(1)} fusion(bf16[48,2048]{1,0:T(8,128)(2,1)S(1)} %reshape.479, bf16[1,2048,352]{1,2,0:T(8,128)(2,1)} %param.31), kind=kOutput, calls=%fused_computation.18 | convolution fusion | flops 69206016 | bytes 1705984 | tf_op jit(solution)/shard_map/dot_general | solution.py:261
  90.3 2.9 %fusion.9 = f32[48,2048]{1,0:T(8,128)S(1)} fusion(bf16[1,352,2048]{2,1,0:T(8,128)(2,1)} %param.33, bf16[48,2048]{1,0:T(8,128)(2,1)S(1)} %reshape.479, bf16[1,2048,352]{1,2,0:T(8,128)(2,1)} %param.32, f32[48,352]{1,0:T(8,128)S(1)} %fusion.13), kind=kOutput, calls=%fused_computation.14 | convolution fusion | flops 138513408 | bytes 3540992 | tf_op jit(solution)/shard_map/dot_general | solution.py:267
  93.3 1.6 %collective-permute-done.4 = f32[33792]{0:T(1024)} collective-permute-done((f32[33792]{0:T(1024)S(1)}, f32[33792]{0:T(1024)}, u32[]{:S(2)}, u32[]{:S(2)}) %collective-permute-start.4) | collective-permute-done | bytes 135200 | tf_op jit(solution)/shard_map/ppermute | solution.py:51
  97.6 1.4 %collective-permute-start.11 = (bf16[24,704]{1,0:T(8,128)(2,1)}, bf16[24,704]{1,0:T(8,128)(2,1)}, u32[]{:S(2)}, u32[]{:S(2)}) collective-permute-start(bf16[24,704]{1,0:T(8,128)(2,1)} %multiply_convert_fusion.2), channel_id=1, source_target_pairs={{0,3},{1,0},{2,1},{3,2},{4,7},{5,4},{6,5},{7,6},{8,11},{9,8},{10,9... | collective-permute-start | bytes 101384 | tf_op jit(solution)/shard_map/ppermute | solution.py:51
  103.3 1.4 %fusion.137 = f32[96,512]{1,0:T(8,128)S(1)} fusion(bf16[96,704]{1,0:T(8,128)(2,1)S(1)} %bitcast_select_fusion, bf16[704,512]{1,0:T(8,128)(2,1)} %param.36), kind=kOutput, calls=%fused_computation.224 | convolution fusion | flops 69206016 | bytes 1052672 | tf_op jit(solution)/shard_map/dot_general | solution.py:279
  104.9 2.0 %collective-permute-done.7 = f32[24576]{0:T(1024)S(1)} collective-permute-done((f32[24576]{0:T(1024)S(1)}, f32[24576]{0:T(1024)S(1)}, u32[]{:S(2)}, u32[]{:S(2)}) %collective-permute-start.7) | collective-permute-done | bytes 98336 | tf_op jit(solution)/shard_map/ppermute | solution.py:51
  107.7 3.6 %all-to-all-start.3 = ((f32[8,72,128]{2,1,0:T(8,128)}), f32[8,72,128]{2,1,0:T(8,128)S(1)}, u32[]{:S(2)}, u32[]{:S(2)}) async-start(f32[8,72,128]{2,1,0:T(8,128)} %pad_maximum_fusion.4), calls=%async_computation.3 | async-start | bytes 589824 | tf_op jit(solution)/shard_map/all_to_all | solution.py:289
  111.8 9.3 %all-to-all-done.3 = f32[8,72,128]{2,1,0:T(8,128)S(1)} async-done(((f32[8,72,128]{2,1,0:T(8,128)}), f32[8,72,128]{2,1,0:T(8,128)S(1)}, u32[]{:S(2)}, u32[]{:S(2)}) %all-to-all-start.3) | async-done | bytes 294944 | tf_op jit(solution)/shard_map/all_to_all | solution.py:289
  (188 shorter events, 37.5 us)
Async XLA Ops:
  0.0 58.1 %copy-start = (bf16[512,2048]{1,0:T(8,128)(2,1)S(1)}, bf16[512,2048]{1,0:T(8,128)(2,1)}, u32[]{:S(2)}) copy-start(bf16[512,2048]{1,0:T(8,128)(2,1)} %param.23) | copy-start | bytes 6291460
  0.0 20.2 %copy-start.3 = (bf16[3,4,2048]{2,1,0:T(4,128)(2,1)S(1)}, bf16[3,4,2048]{2,1,0:T(4,128)(2,1)}, u32[]{:S(2)}) copy-start(bf16[3,4,2048]{2,1,0:T(4,128)(2,1)} %param.19) | copy-start | bytes 147460
  1.9 23.6 %all-to-all-start = ((bf16[8,3,4,2048]{3,2,1,0:T(4,128)(2,1)}), bf16[8,3,4,2048]{3,2,1,0:T(4,128)(2,1)S(1)}, u32[]{:S(2)}, u32[]{:S(2)}) async-start(bf16[8,3,4,2048]{3,2,1,0:T(4,128)(2,1)} %broadcast_in_dim.201), calls=%async_computation | async-start | bytes 786432 | tf_op jit(solution)/shard_map/all_to_all | solution.py:64
  40.5 17.4 %copy-start.11 = (f32[3,4,2,512]{3,1,2,0:T(4,128)S(1)}, f32[3,4,2,512]{3,1,2,0:T(4,128)}, u32[]{:S(2)}) copy-start(f32[3,4,2,512]{3,1,2,0:T(4,128)} %copy-done.10) | copy-start | bytes 147460
  41.9 15.0 %all-to-all-start.1 = ((f32[24,17,128]{2,1,0:T(8,128)}), f32[24,17,128]{2,1,0:T(8,128)S(1)}, u32[]{:S(2)}, u32[]{:S(2)}) async-start(f32[24,17,128]{2,1,0:T(8,128)} %pad_maximum_fusion.2), calls=%async_computation.1 | async-start | bytes 589824 | tf_op jit(solution)/shard_map/all_to_all | solution.py:172
  58.5 2.9 %collective-permute-start.2 = (f32[12,2048]{1,0:T(8,128)S(1)}, f32[12,2048]{1,0:T(8,128)S(1)}, u32[]{:S(2)}, u32[]{:S(2)}) collective-permute-start(f32[12,2048]{1,0:T(8,128)S(1)} %fusion.134), channel_id=1, source_target_pairs={{0,3},{1,0},{2,1},{3,2},{4,7},{5,4},{6,5},{7,6},{8,11},{9,8},{10,9... | collective-permute-start | bytes 294920 | tf_op jit(solution)/shard_map/ppermute | solution.py:51
  58.5 8.6 %collective-permute-start.1 = (f32[12,2048]{1,0:T(8,128)S(1)}, f32[12,2048]{1,0:T(8,128)S(1)}, u32[]{:S(2)}, u32[]{:S(2)}) collective-permute-start(f32[12,2048]{1,0:T(8,128)S(1)} %fusion.134), channel_id=1, source_target_pairs={{0,2},{1,3},{2,0},{3,1},{4,6},{5,7},{6,4},{7,5},{8,10},{9,11},{10,... | collective-permute-start | bytes 294920 | tf_op jit(solution)/shard_map/ppermute | solution.py:51
  60.0 7.1 %collective-permute-start = (f32[12,2048]{1,0:T(8,128)S(1)}, f32[12,2048]{1,0:T(8,128)S(1)}, u32[]{:S(2)}, u32[]{:S(2)}) collective-permute-start(f32[12,2048]{1,0:T(8,128)S(1)} %fusion.134), channel_id=1, source_target_pairs={{0,1},{1,2},{2,3},{3,0},{4,5},{5,6},{6,7},{7,4},{8,9},{9,10},{10,1... | collective-permute-start | bytes 294920 | tf_op jit(solution)/shard_map/ppermute | solution.py:51
  68.1 15.9 %copy-start.4 = (bf16[512,704]{0,1:T(8,128)(2,1)S(1)}, bf16[512,704]{0,1:T(8,128)(2,1)}, u32[]{:S(2)}) copy-start(bf16[512,704]{0,1:T(8,128)(2,1)} %param.35) | copy-start | bytes 2162692
  71.7 12.1 %all-to-all-start.2 = ((bf16[8,144,128]{2,1,0:T(8,128)(2,1)}), bf16[8,144,128]{2,1,0:T(8,128)(2,1)S(1)}, u32[]{:S(2)}, u32[]{:S(2)}) async-start(bf16[8,144,128]{2,1,0:T(8,128)(2,1)} %pad_maximum_fusion.3), calls=%async_computation.2 | async-start | bytes 589824 | tf_op jit(solution)/shard_map/all_to_all | solution.py:248
  86.7 6.6 %collective-permute-start.5 = (f32[33792]{0:T(1024)S(1)}, f32[33792]{0:T(1024)}, u32[]{:S(2)}, u32[]{:S(2)}) collective-permute-start(f32[33792]{0:T(1024)S(1)} %bitcast.179), channel_id=1, source_target_pairs={{0,3},{1,0},{2,1},{3,2},{4,7},{5,4},{6,5},{7,6},{8,11},{9,8},{10,9... | collective-permute-start | bytes 405512 | tf_op jit(solution)/shard_map/ppermute | solution.py:51
  86.8 6.5 %collective-permute-start.3 = (f32[33792]{0:T(1024)S(1)}, f32[33792]{0:T(1024)}, u32[]{:S(2)}, u32[]{:S(2)}) collective-permute-start(f32[33792]{0:T(1024)S(1)} %bitcast.178), channel_id=1, source_target_pairs={{0,1},{1,2},{2,3},{3,0},{4,5},{5,6},{6,7},{7,4},{8,9},{9,10},{10,1... | collective-permute-start | bytes 405512 | tf_op jit(solution)/shard_map/ppermute | solution.py:51
  87.3 7.6 %collective-permute-start.4 = (f32[33792]{0:T(1024)S(1)}, f32[33792]{0:T(1024)}, u32[]{:S(2)}, u32[]{:S(2)}) collective-permute-start(f32[33792]{0:T(1024)S(1)} %bitcast.177), channel_id=1, source_target_pairs={{0,2},{1,3},{2,0},{3,1},{4,6},{5,7},{6,4},{7,5},{8,10},{9,11},{10,... | collective-permute-start | bytes 405512 | tf_op jit(solution)/shard_map/ppermute | solution.py:51
  96.7 4.6 %collective-permute-start.10 = (bf16[24,704]{1,0:T(8,128)(2,1)}, bf16[24,704]{1,0:T(8,128)(2,1)S(1)}, u32[]{:S(2)}, u32[]{:S(2)}) collective-permute-start(bf16[24,704]{1,0:T(8,128)(2,1)} %multiply_convert_fusion.2), channel_id=1, source_target_pairs={{0,2},{1,3},{2,0},{3,1},{4,6},{5,7},{6,4},{7,5},{8,10},{9,11},{10,... | collective-permute-start | bytes 101384 | tf_op jit(solution)/shard_map/ppermute | solution.py:51
  97.2 4.5 %collective-permute-start.9 = (bf16[24,704]{1,0:T(8,128)(2,1)}, bf16[24,704]{1,0:T(8,128)(2,1)S(1)}, u32[]{:S(2)}, u32[]{:S(2)}) collective-permute-start(bf16[24,704]{1,0:T(8,128)(2,1)} %multiply_convert_fusion.2), channel_id=1, source_target_pairs={{0,1},{1,2},{2,3},{3,0},{4,5},{5,6},{6,7},{7,4},{8,9},{9,10},{10,1... | collective-permute-start | bytes 101384 | tf_op jit(solution)/shard_map/ppermute | solution.py:51
  97.6 4.2 %collective-permute-start.11 = (bf16[24,704]{1,0:T(8,128)(2,1)}, bf16[24,704]{1,0:T(8,128)(2,1)}, u32[]{:S(2)}, u32[]{:S(2)}) collective-permute-start(bf16[24,704]{1,0:T(8,128)(2,1)} %multiply_convert_fusion.2), channel_id=1, source_target_pairs={{0,3},{1,0},{2,1},{3,2},{4,7},{5,4},{6,5},{7,6},{8,11},{9,8},{10,9... | collective-permute-start | bytes 101384 | tf_op jit(solution)/shard_map/ppermute | solution.py:51
  99.7 11.6 %copy-start.12 = (f32[3,4,4]{2,1,0:T(4,128)S(1)}, f32[3,4,4]{2,1,0:T(4,128)}, u32[]{:S(2)}) copy-start(f32[3,4,4]{2,1,0:T(4,128)} %param.30) | copy-start | bytes 580
  99.7 11.7 %copy-start.14 = (bf16[2048]{0:T(1024)(128)(2,1)S(1)}, bf16[2048]{0:T(1024)(128)(2,1)}, u32[]{:S(2)}) copy-start(bf16[2048]{0:T(1024)(128)(2,1)} %param.37) | copy-start | bytes 12292
  99.7 11.7 %copy-start.17 = (s32[48]{0:T(128)S(1)}, s32[48]{0:T(128)}, u32[]{:S(2)}) copy-start(s32[48]{0:T(128)} %copy-done.16) | copy-start | bytes 580
  99.7 11.7 %copy-start.19 = (s32[48]{0:T(128)S(1)}, s32[48]{0:T(128)}, u32[]{:S(2)}) copy-start(s32[48]{0:T(128)} %copy-done.18) | copy-start | bytes 580
  99.7 5.0 %collective-permute-start.8 = (f32[24576]{0:T(1024)S(1)}, f32[24576]{0:T(1024)S(1)}, u32[]{:S(2)}, u32[]{:S(2)}) collective-permute-start(f32[24576]{0:T(1024)S(1)} %bitcast.189), channel_id=1, source_target_pairs={{0,3},{1,0},{2,1},{3,2},{4,7},{5,4},{6,5},{7,6},{8,11},{9,8},{10,9... | collective-permute-start | bytes 294920 | tf_op jit(solution)/shard_map/ppermute | solution.py:51
  99.8 5.1 %collective-permute-start.6 = (f32[24576]{0:T(1024)S(1)}, f32[24576]{0:T(1024)S(1)}, u32[]{:S(2)}, u32[]{:S(2)}) collective-permute-start(f32[24576]{0:T(1024)S(1)} %bitcast.188), channel_id=1, source_target_pairs={{0,1},{1,2},{2,3},{3,0},{4,5},{5,6},{6,7},{7,4},{8,9},{9,10},{10,1... | collective-permute-start | bytes 294920 | tf_op jit(solution)/shard_map/ppermute | solution.py:51
  101.2 5.7 %collective-permute-start.7 = (f32[24576]{0:T(1024)S(1)}, f32[24576]{0:T(1024)S(1)}, u32[]{:S(2)}, u32[]{:S(2)}) collective-permute-start(f32[24576]{0:T(1024)S(1)} %bitcast.187), channel_id=1, source_target_pairs={{0,2},{1,3},{2,0},{3,1},{4,6},{5,7},{6,4},{7,5},{8,10},{9,11},{10,... | collective-permute-start | bytes 294920 | tf_op jit(solution)/shard_map/ppermute | solution.py:51
  107.7 13.5 %all-to-all-start.3 = ((f32[8,72,128]{2,1,0:T(8,128)}), f32[8,72,128]{2,1,0:T(8,128)S(1)}, u32[]{:S(2)}, u32[]{:S(2)}) async-start(f32[8,72,128]{2,1,0:T(8,128)} %pad_maximum_fusion.4), calls=%async_computation.3 | async-start | bytes 589824 | tf_op jit(solution)/shard_map/all_to_all | solution.py:289
  (14 other events, 76.4 us)

commit v13 on v11

--- a/solution.py
+++ b/solution.py
@@ -206,9 +206,7 @@
     )[..., None]
     attended = attended.astype(jnp.bfloat16).reshape(row_count, head_width)
     attn_part = jnp.dot(attended, out_weight, preferred_element_type=jnp.float32)
-    attn_full = jnp.sum(
-        by_source(shift_exchange(attn_part, "tp", tp_count, spread=True), "tp", tp_count), axis=0
-    )
+    attn_full = sum(shift_exchange(attn_part, "tp", tp_count, spread=True))
     resid = tokens_in.reshape(row_count, model_width).astype(jnp.float32) + attn_full
     mixed = rms_norm(resid, mlp_norm)
     expert_count = req_count * expert_w_gate.shape[0]

time: 112 us -> 111 us (level)
  waiting for transfers between devices: 40 us -> 37.9 us
  starting transfers between devices: 25.5 us -> 26.9 us
    ppermute x12, waiting for transfers between devices: 11.7 us -> 9.19 us  [shift_exchange(): pieces.append(lax.ppermute(send, axis, pairs))]
    ppermute x12, starting transfers between devices: 6.95 us -> 8.72 us  [shift_exchange(): pieces.append(lax.ppermute(send, axis, pairs))]
    unnamed x33 -> x31, local copies, waits for them, and re-layouts: 0.18 us -> 1.37 us
  transfers between devices with their start and end apart: 16 -> 16, of which waited for: 11 -> 9; matrix products, arithmetic and copies ran while one was open for 13% -> 13% of each run, Pallas kernels for 0% -> 0%
where the time goes in v13:
time: 111 us; the launch traced here: 110 us
  waiting for transfers between devices  37.9 us (34%)
  starting transfers between devices  26.9 us (24%)
  matrix products  23.9 us (22%)
  other arithmetic  11.7 us (11%)
  local copies, waits for them, and re-layouts  9.31 us (8%)
    all_to_all x1, waiting for transfers between devices, per_device(): back = lax.all_to_all(back_in, 'req', 0, 0, tiled=True)  9.52 us
    ppermute x12, waiting for transfers between devices, shift_exchange(): pieces.append(lax.ppermute(send, axis, pairs))  9.19 us
    all_to_all x1, waiting for transfers between devices, per_device(): lax.all_to_all(packed, 'req', 0, 0, tiled=True)  8.77 us
    ppermute x12, starting transfers between devices, shift_exchange(): pieces.append(lax.ppermute(send, axis, pairs))  8.72 us
    all_to_all x1, waiting for transfers between devices, per_device(): received = lax.all_to_all(dispatch, 'req', 0, 0, tiled=True)  8.23 us
    all_to_all x1, starting transfers between devices, per_device(): lax.all_to_all(query_spread, 'req', 0, 0, tiled=True)  7.29 us
    dot_general x1, matrix products, per_device(): jnp.einsum('pxd,pkd->pxk', block_queries, cache_keys, preferred_element_t...  4.03 us
    dot_general x1, matrix products, per_device(): jnp.einsum('pshk,pkhd->pshd', weights.astype(jnp.bfloat16), page_values,...  4.01 us
  transfers between devices with their start and end apart: 16, of which 9 were waited for; matrix products, arithmetic and copies ran while one was open for 13% of the time, Pallas kernels for 0%

profile of v13, /device:TPU:0, one launch (start us, length us, event | category | flops | bytes accessed | tf_op | source)
XLA Modules:
  0.0 110.4 jit_solution(16378381411520395731)
XLA Ops:
  4.3 2.0 %fusion.32 = f32[3,4,4,128]{3,1,2,0:T(4,128)S(1)} fusion(bf16[3,4,2048]{2,1,0:T(4,128)(2,1)S(1)} %multiply_convert_fusion.1, bf16[2048,3,512]{2,0,1:T(8,128)(2,1)} %param.21, f32[512]{0:T(512)S(1)} %bitcast.195), kind=kOutput, calls=%fused_computation.25 | convolution fusion | flops 25171968 | bytes 2172928 | tf_op jit(solution)/shard_map/rsd,df->rsf/dot_general | solution.py:109
  7.2 7.3 %all-to-all-start = ((bf16[8,3,4,4,128]{4,3,2,1,0:T(4,128)(2,1)}), bf16[8,3,4,4,128]{4,3,2,1,0:T(4,128)(2,1)S(1)}, u32[]{:S(2)}, u32[]{:S(2)}) async-start(bf16[8,3,4,4,128]{4,3,2,1,0:T(4,128)(2,1)} %broadcast_in_dim.186), calls=%async_computation | async-start | bytes 196608 | tf_op jit(solution)/shard_map/all_to_all | solution.py:116
  16.0 2.9 %fusion.24 = f32[3,4,2,512]{3,1,2,0:T(4,128)S(1)} fusion(bf16[2048,3,512]{2,0,1:T(8,128)(2,1)} %param.21, bf16[3,4,2048]{2,1,0:T(4,128)(2,1)S(1)} %multiply_convert_fusion.1, f32[2,512]{1,0:T(2,128)S(1)} %slice_convert_fusion.1), kind=kOutput, calls=%fused_computation.23 | convolution fusion | flops 50343936 | bytes 4296704 | tf_op jit(solution)/shard_map/rsd,dcf->rscf/dot_general | solution.py:119
  19.4 2.2 %all-to-all-done = bf16[8,3,4,4,128]{4,3,2,1,0:T(4,128)(2,1)S(1)} async-done(((bf16[8,3,4,4,128]{4,3,2,1,0:T(4,128)(2,1)}), bf16[8,3,4,4,128]{4,3,2,1,0:T(4,128)(2,1)S(1)}, u32[]{:S(2)}, u32[]{:S(2)}) %all-to-all-start) | async-done | bytes 98336 | tf_op jit(solution)/shard_map/all_to_all | solution.py:116
  22.9 4.0 %select_reduce_fusion.1 = (f32[40,16]{1,0:T(8,128)S(1)}, f32[40,16,128]{2,1,0:T(8,128)S(1)}) fusion(pred[40,128]{1,0:T(8,128)(4,1)S(1)} %fusion.82, bf16[40,128,512]{2,1,0:T(8,128)(2,1)} %param.24, bf16[40,16,512]{2,1,0:T(8,128)(2,1)S(1)} %broadcast_in_dim.188, pred[16,512]{1,0:T(8,128)(4,1)S(1)} %bitcast.192), kind=kOutput, calls=%fused_computation.58 | convolution fusion | flops 84458880 | bytes 6241792 | tf_op jit(solution)/shard_map/pxd,pkd->pxk/dot_general | solution.py:140
  28.3 4.0 %fusion.15 = f32[40,4,4,128]{3,1,2,0:T(4,128)S(1)} fusion(f32[40,4,4,128]{3,2,1,0:T(4,128)S(1)} %bitcast.169, f32[40,4,4]{1,2,0:T(4,128)S(1)} %copy.82, pred[40,128]{1,0:T(8,128)(4,1)S(1)} %fusion.82, bf16[40,128,512]{2,1,0:T(8,128)(2,1)} %param.25), kind=kOutput, calls=%fused_computation.20 | convolution fusion | flops 21299200 | bytes 5905920 | tf_op jit(solution)/shard_map/pshk,pkhd->pshd/dot_general | solution.py:148
  33.7 3.8 %all-to-all-start.1 = ((f32[24,17,128]{2,1,0:T(8,128)}), f32[24,17,128]{2,1,0:T(8,128)S(1)}, u32[]{:S(2)}, u32[]{:S(2)}) async-start(f32[24,17,128]{2,1,0:T(8,128)} %pad_maximum_fusion.1), calls=%async_computation.1 | async-start | bytes 589824 | tf_op jit(solution)/shard_map/all_to_all | solution.py:172
  37.8 8.8 %all-to-all-done.1 = f32[24,17,128]{2,1,0:T(8,128)S(1)} async-done(((f32[24,17,128]{2,1,0:T(8,128)}), f32[24,17,128]{2,1,0:T(8,128)S(1)}, u32[]{:S(2)}, u32[]{:S(2)}) %all-to-all-start.1) | async-done | bytes 208928 | tf_op jit(solution)/shard_map/all_to_all | solution.py:172
  48.1 1.5 %collective-permute-start.1 = (f32[12,2048]{1,0:T(8,128)S(1)}, f32[12,2048]{1,0:T(8,128)S(1)}, u32[]{:S(2)}, u32[]{:S(2)}) collective-permute-start(f32[12,2048]{1,0:T(8,128)S(1)} %fusion.124), channel_id=1, source_target_pairs={{0,2},{1,3},{2,0},{3,1},{4,6},{5,7},{6,4},{7,5},{8,10},{9,11},{10,... | collective-permute-start | bytes 294920 | tf_op jit(solution)/shard_map/ppermute | solution.py:51
  51.0 5.7 %collective-permute-done.1 = f32[12,2048]{1,0:T(8,128)S(1)} collective-permute-done((f32[12,2048]{1,0:T(8,128)S(1)}, f32[12,2048]{1,0:T(8,128)S(1)}, u32[]{:S(2)}, u32[]{:S(2)}) %collective-permute-start.1) | collective-permute-done | bytes 98336 | tf_op jit(solution)/shard_map/ppermute | solution.py:51
  57.3 1.1 %multiply_reduce_fusion = (f32[12]{0:T(128)S(1)}, f32[12,2048]{1,0:T(8,128)S(1)}) fusion(f32[12,2048]{1,0:T(8,128)S(1)} %reshape.449, f32[12,2048]{1,0:T(8,128)S(1)} %collective-permute-done.2, f32[12,2048]{1,0:T(8,128)} %copy-done.6, f32[12,2048]{1,0:T(8,128)S(1)} %fusion.124, f32[12,2048]{1,0:T(8,128)} %collective-permute-done), kind=kLoop, calls=%fused_computation.76 | loop fusion | flops 147444 | bytes 589872 | tf_op jit(solution)/shard_map/reduce_sum | solution.py:21
  60.3 3.6 %all-to-all-start.2 = ((bf16[8,144,128]{2,1,0:T(8,128)(2,1)}), bf16[8,144,128]{2,1,0:T(8,128)(2,1)S(1)}, u32[]{:S(2)}, u32[]{:S(2)}) async-start(bf16[8,144,128]{2,1,0:T(8,128)(2,1)} %pad_maximum_fusion.2), calls=%async_computation.2 | async-start | bytes 589824 | tf_op jit(solution)/shard_map/all_to_all | solution.py:246
  64.1 8.2 %all-to-all-done.2 = bf16[8,144,128]{2,1,0:T(8,128)(2,1)S(1)} async-done(((bf16[8,144,128]{2,1,0:T(8,128)(2,1)}), bf16[8,144,128]{2,1,0:T(8,128)(2,1)S(1)}, u32[]{:S(2)}, u32[]{:S(2)}) %all-to-all-start.2) | async-done | bytes 294944 | tf_op jit(solution)/shard_map/all_to_all | solution.py:246
  72.9 1.5 %fusion.125 = f32[96,704]{1,0:T(8,128)S(1)} fusion(bf16[96,512]{1,0:T(8,128)(2,1)S(1)} %reshape.441, bf16[512,704]{0,1:T(8,128)(2,1)} %param.34), kind=kOutput, calls=%fused_computation.202 | convolution fusion | flops 69206016 | bytes 1089536 | tf_op jit(solution)/shard_map/dot_general | solution.py:250
  76.4 1.9 %fusion.13 = f32[48,352]{1,0:T(8,128)S(1)} fusion(bf16[48,2048]{1,0:T(8,128)(2,1)S(1)} %reshape.440, bf16[1,2048,352]{1,2,0:T(8,128)(2,1)} %param.31), kind=kOutput, calls=%fused_computation.17 | convolution fusion | flops 69206016 | bytes 1705984 | tf_op jit(solution)/shard_map/dot_general | solution.py:259
  78.3 2.9 %fusion.9 = f32[48,2048]{1,0:T(8,128)S(1)} fusion(bf16[1,352,2048]{2,1,0:T(8,128)(2,1)} %param.33, bf16[48,2048]{1,0:T(8,128)(2,1)S(1)} %reshape.440, bf16[1,2048,352]{1,2,0:T(8,128)(2,1)} %param.32, f32[48,352]{1,0:T(8,128)S(1)} %fusion.13), kind=kOutput, calls=%fused_computation.13 | convolution fusion | flops 138513408 | bytes 3540992 | tf_op jit(solution)/shard_map/dot_general | solution.py:265
  82.4 1.1 add_add_fusion
  84.2 2.3 %collective-permute-start.10 = (bf16[24,704]{1,0:T(8,128)(2,1)}, bf16[24,704]{1,0:T(8,128)(2,1)}, u32[]{:S(2)}, u32[]{:S(2)}) collective-permute-start(bf16[24,704]{1,0:T(8,128)(2,1)} %multiply_convert_fusion.2), channel_id=1, source_target_pairs={{0,2},{1,3},{2,0},{3,1},{4,6},{5,7},{6,4},{7,5},{8,10},{9,11},{10,... | collective-permute-start | bytes 101384 | tf_op jit(solution)/shard_map/ppermute | solution.py:51
  86.5 1.7 %collective-permute-start.11 = (bf16[24,704]{1,0:T(8,128)(2,1)}, bf16[24,704]{1,0:T(8,128)(2,1)}, u32[]{:S(2)}, u32[]{:S(2)}) collective-permute-start(bf16[24,704]{1,0:T(8,128)(2,1)} %multiply_convert_fusion.2), channel_id=1, source_target_pairs={{0,3},{1,0},{2,1},{3,2},{4,7},{5,4},{6,5},{7,6},{8,11},{9,8},{10,9... | collective-permute-start | bytes 101384 | tf_op jit(solution)/shard_map/ppermute | solution.py:51
  89.6 1.2 %collective-permute-start.7 = (f32[24576]{0:T(1024)S(1)}, f32[24576]{0:T(1024)S(1)}, u32[]{:S(2)}, u32[]{:S(2)}) collective-permute-start(f32[24576]{0:T(1024)S(1)} %bitcast.184), channel_id=1, source_target_pairs={{0,2},{1,3},{2,0},{3,1},{4,6},{5,7},{6,4},{7,5},{8,10},{9,11},{10,... | collective-permute-start | bytes 294920 | tf_op jit(solution)/shard_map/ppermute | solution.py:51
  92.3 1.4 %fusion.127 = f32[96,512]{1,0:T(8,128)S(1)} fusion(bf16[96,704]{1,0:T(8,128)(2,1)S(1)} %bitcast_select_fusion, bf16[704,512]{1,0:T(8,128)(2,1)} %param.36), kind=kOutput, calls=%fused_computation.204 | convolution fusion | flops 69206016 | bytes 1052672 | tf_op jit(solution)/shard_map/dot_general | solution.py:277
  93.8 1.5 %collective-permute-done.7 = f32[24576]{0:T(1024)S(1)} collective-permute-done((f32[24576]{0:T(1024)S(1)}, f32[24576]{0:T(1024)S(1)}, u32[]{:S(2)}, u32[]{:S(2)}) %collective-permute-start.7) | collective-permute-done | bytes 98336 | tf_op jit(solution)/shard_map/ppermute | solution.py:51
  96.0 3.4 %all-to-all-start.3 = ((f32[8,72,128]{2,1,0:T(8,128)}), f32[8,72,128]{2,1,0:T(8,128)S(1)}, u32[]{:S(2)}, u32[]{:S(2)}) async-start(f32[8,72,128]{2,1,0:T(8,128)} %pad_maximum_fusion.3), calls=%async_computation.3 | async-start | bytes 589824 | tf_op jit(solution)/shard_map/all_to_all | solution.py:287
  100.0 9.5 %all-to-all-done.3 = f32[8,72,128]{2,1,0:T(8,128)S(1)} async-done(((f32[8,72,128]{2,1,0:T(8,128)}), f32[8,72,128]{2,1,0:T(8,128)S(1)}, u32[]{:S(2)}, u32[]{:S(2)}) %all-to-all-start.3) | async-done | bytes 294944 | tf_op jit(solution)/shard_map/all_to_all | solution.py:287
  (159 shorter events, 26.0 us)
Async XLA Ops:
  0.0 47.7 %copy-start = (bf16[512,2048]{1,0:T(8,128)(2,1)S(1)}, bf16[512,2048]{1,0:T(8,128)(2,1)}, u32[]{:S(2)}) copy-start(bf16[512,2048]{1,0:T(8,128)(2,1)} %param.23) | copy-start | bytes 6291460
  0.0 15.1 %copy-start.1 = (s32[24]{0:T(128)S(1)}, s32[24]{0:T(128)}, u32[]{:S(2)}) copy-start(s32[24]{0:T(128)} %param.27) | copy-start | bytes 292
  0.0 14.5 %copy-start.12 = (bf16[3,512]{1,0:T(4,128)(2,1)S(1)}, bf16[3,512]{1,0:T(4,128)(2,1)}, u32[]{:S(2)}) copy-start(bf16[3,512]{1,0:T(4,128)(2,1)} %param.22) | copy-start | bytes 9220
  0.0 14.5 %copy-start.8 = (s32[3,4,4]{2,1,0:T(4,128)S(1)}, s32[3,4,4]{2,1,0:T(4,128)}, u32[]{:S(2)}) copy-start(s32[3,4,4]{2,1,0:T(4,128)} %param.29) | copy-start | bytes 580
  0.0 14.7 %copy-start.7 = (s32[24,37]{1,0:T(8,128)S(1)}, s32[24,37]{1,0:T(8,128)}, u32[]{:S(2)}) copy-start(s32[24,37]{1,0:T(8,128)} %param.26) | copy-start | bytes 10660
  7.2 14.4 %all-to-all-start = ((bf16[8,3,4,4,128]{4,3,2,1,0:T(4,128)(2,1)}), bf16[8,3,4,4,128]{4,3,2,1,0:T(4,128)(2,1)S(1)}, u32[]{:S(2)}, u32[]{:S(2)}) async-start(bf16[8,3,4,4,128]{4,3,2,1,0:T(4,128)(2,1)} %broadcast_in_dim.186), calls=%async_computation | async-start | bytes 196608 | tf_op jit(solution)/shard_map/all_to_all | solution.py:116
  33.7 12.8 %all-to-all-start.1 = ((f32[24,17,128]{2,1,0:T(8,128)}), f32[24,17,128]{2,1,0:T(8,128)S(1)}, u32[]{:S(2)}, u32[]{:S(2)}) async-start(f32[24,17,128]{2,1,0:T(8,128)} %pad_maximum_fusion.1), calls=%async_computation.1 | async-start | bytes 589824 | tf_op jit(solution)/shard_map/all_to_all | solution.py:172
  37.5 12.6 %copy-start.3 = (bf16[3,4,2048]{2,1,0:T(4,128)(2,1)S(1)}, bf16[3,4,2048]{2,1,0:T(4,128)(2,1)}, u32[]{:S(2)}) copy-start(bf16[3,4,2048]{2,1,0:T(4,128)(2,1)} %param.19) | copy-start | bytes 147460
  48.1 2.9 %collective-permute-start.2 = (f32[12,2048]{1,0:T(8,128)S(1)}, f32[12,2048]{1,0:T(8,128)S(1)}, u32[]{:S(2)}, u32[]{:S(2)}) collective-permute-start(f32[12,2048]{1,0:T(8,128)S(1)} %fusion.124), channel_id=1, source_target_pairs={{0,3},{1,0},{2,1},{3,2},{4,7},{5,4},{6,5},{7,6},{8,11},{9,8},{10,9... | collective-permute-start | bytes 294920 | tf_op jit(solution)/shard_map/ppermute | solution.py:51
  48.1 8.6 %collective-permute-start.1 = (f32[12,2048]{1,0:T(8,128)S(1)}, f32[12,2048]{1,0:T(8,128)S(1)}, u32[]{:S(2)}, u32[]{:S(2)}) collective-permute-start(f32[12,2048]{1,0:T(8,128)S(1)} %fusion.124), channel_id=1, source_target_pairs={{0,2},{1,3},{2,0},{3,1},{4,6},{5,7},{6,4},{7,5},{8,10},{9,11},{10,... | collective-permute-start | bytes 294920 | tf_op jit(solution)/shard_map/ppermute | solution.py:51
  49.6 7.7 %collective-permute-start = (f32[12,2048]{1,0:T(8,128)S(1)}, f32[12,2048]{1,0:T(8,128)}, u32[]{:S(2)}, u32[]{:S(2)}) collective-permute-start(f32[12,2048]{1,0:T(8,128)S(1)} %fusion.124), channel_id=1, source_target_pairs={{0,1},{1,2},{2,3},{3,0},{4,5},{5,6},{6,7},{7,4},{8,9},{9,10},{10,1... | collective-permute-start | bytes 294920 | tf_op jit(solution)/shard_map/ppermute | solution.py:51
  50.1 22.4 %copy-start.2 = (bf16[512,704]{0,1:T(8,128)(2,1)S(1)}, bf16[512,704]{0,1:T(8,128)(2,1)}, u32[]{:S(2)}) copy-start(bf16[512,704]{0,1:T(8,128)(2,1)} %param.35) | copy-start | bytes 2162692
  60.3 12.1 %all-to-all-start.2 = ((bf16[8,144,128]{2,1,0:T(8,128)(2,1)}), bf16[8,144,128]{2,1,0:T(8,128)(2,1)S(1)}, u32[]{:S(2)}, u32[]{:S(2)}) async-start(bf16[8,144,128]{2,1,0:T(8,128)(2,1)} %pad_maximum_fusion.2), calls=%async_computation.2 | async-start | bytes 589824 | tf_op jit(solution)/shard_map/all_to_all | solution.py:246
  75.3 6.0 %collective-permute-start.5 = (f32[33792]{0:T(1024)S(1)}, f32[33792]{0:T(1024)}, u32[]{:S(2)}, u32[]{:S(2)}) collective-permute-start(f32[33792]{0:T(1024)S(1)} %bitcast.179), channel_id=1, source_target_pairs={{0,3},{1,0},{2,1},{3,2},{4,7},{5,4},{6,5},{7,6},{8,11},{9,8},{10,9... | collective-permute-start | bytes 405512 | tf_op jit(solution)/shard_map/ppermute | solution.py:51
  75.3 6.0 %collective-permute-start.3 = (f32[33792]{0:T(1024)S(1)}, f32[33792]{0:T(1024)}, u32[]{:S(2)}, u32[]{:S(2)}) collective-permute-start(f32[33792]{0:T(1024)S(1)} %bitcast.178), channel_id=1, source_target_pairs={{0,1},{1,2},{2,3},{3,0},{4,5},{5,6},{6,7},{7,4},{8,9},{9,10},{10,1... | collective-permute-start | bytes 405512 | tf_op jit(solution)/shard_map/ppermute | solution.py:51
  75.8 6.6 %collective-permute-start.4 = (f32[33792]{0:T(1024)S(1)}, f32[33792]{0:T(1024)}, u32[]{:S(2)}, u32[]{:S(2)}) collective-permute-start(f32[33792]{0:T(1024)S(1)} %bitcast.177), channel_id=1, source_target_pairs={{0,2},{1,3},{2,0},{3,1},{4,6},{5,7},{6,4},{7,5},{8,10},{9,11},{10,... | collective-permute-start | bytes 405512 | tf_op jit(solution)/shard_map/ppermute | solution.py:51
  84.2 5.4 %collective-permute-start.10 = (bf16[24,704]{1,0:T(8,128)(2,1)}, bf16[24,704]{1,0:T(8,128)(2,1)}, u32[]{:S(2)}, u32[]{:S(2)}) collective-permute-start(bf16[24,704]{1,0:T(8,128)(2,1)} %multiply_convert_fusion.2), channel_id=1, source_target_pairs={{0,2},{1,3},{2,0},{3,1},{4,6},{5,7},{6,4},{7,5},{8,10},{9,11},{10,... | collective-permute-start | bytes 101384 | tf_op jit(solution)/shard_map/ppermute | solution.py:51
  86.5 4.3 %collective-permute-start.9 = (bf16[24,704]{1,0:T(8,128)(2,1)}, bf16[24,704]{1,0:T(8,128)(2,1)}, u32[]{:S(2)}, u32[]{:S(2)}) collective-permute-start(bf16[24,704]{1,0:T(8,128)(2,1)} %multiply_convert_fusion.2), channel_id=1, source_target_pairs={{0,1},{1,2},{2,3},{3,0},{4,5},{5,6},{6,7},{7,4},{8,9},{9,10},{10,1... | collective-permute-start | bytes 101384 | tf_op jit(solution)/shard_map/ppermute | solution.py:51
  86.5 4.3 %collective-permute-start.11 = (bf16[24,704]{1,0:T(8,128)(2,1)}, bf16[24,704]{1,0:T(8,128)(2,1)}, u32[]{:S(2)}, u32[]{:S(2)}) collective-permute-start(bf16[24,704]{1,0:T(8,128)(2,1)} %multiply_convert_fusion.2), channel_id=1, source_target_pairs={{0,3},{1,0},{2,1},{3,2},{4,7},{5,4},{6,5},{7,6},{8,11},{9,8},{10,9... | collective-permute-start | bytes 101384 | tf_op jit(solution)/shard_map/ppermute | solution.py:51
  89.0 10.5 %copy-start.11 = (bf16[2048]{0:T(1024)(128)(2,1)S(1)}, bf16[2048]{0:T(1024)(128)(2,1)}, u32[]{:S(2)}) copy-start(bf16[2048]{0:T(1024)(128)(2,1)} %param.37) | copy-start | bytes 12292
  89.0 4.7 %collective-permute-start.8 = (f32[24576]{0:T(1024)S(1)}, f32[24576]{0:T(1024)S(1)}, u32[]{:S(2)}, u32[]{:S(2)}) collective-permute-start(f32[24576]{0:T(1024)S(1)} %bitcast.186), channel_id=1, source_target_pairs={{0,3},{1,0},{2,1},{3,2},{4,7},{5,4},{6,5},{7,6},{8,11},{9,8},{10,9... | collective-permute-start | bytes 294920 | tf_op jit(solution)/shard_map/ppermute | solution.py:51
  89.1 4.7 %collective-permute-start.6 = (f32[24576]{0:T(1024)S(1)}, f32[24576]{0:T(1024)S(1)}, u32[]{:S(2)}, u32[]{:S(2)}) collective-permute-start(f32[24576]{0:T(1024)S(1)} %bitcast.185), channel_id=1, source_target_pairs={{0,1},{1,2},{2,3},{3,0},{4,5},{5,6},{6,7},{7,4},{8,9},{9,10},{10,1... | collective-permute-start | bytes 294920 | tf_op jit(solution)/shard_map/ppermute | solution.py:51
  89.6 5.7 %collective-permute-start.7 = (f32[24576]{0:T(1024)S(1)}, f32[24576]{0:T(1024)S(1)}, u32[]{:S(2)}, u32[]{:S(2)}) collective-permute-start(f32[24576]{0:T(1024)S(1)} %bitcast.184), channel_id=1, source_target_pairs={{0,2},{1,3},{2,0},{3,1},{4,6},{5,7},{6,4},{7,5},{8,10},{9,11},{10,... | collective-permute-start | bytes 294920 | tf_op jit(solution)/shard_map/ppermute | solution.py:51
  96.0 13.5 %all-to-all-start.3 = ((f32[8,72,128]{2,1,0:T(8,128)}), f32[8,72,128]{2,1,0:T(8,128)S(1)}, u32[]{:S(2)}, u32[]{:S(2)}) async-start(f32[8,72,128]{2,1,0:T(8,128)} %pad_maximum_fusion.3), calls=%async_computation.3 | async-start | bytes 589824 | tf_op jit(solution)/shard_map/all_to_all | solution.py:287
  (5 other events, 24.2 us)

commit v14 on v13

--- a/solution.py
+++ b/solution.py
@@ -54,9 +54,14 @@
 
 def by_source(pieces, axis, count):
     me = lax.axis_index(axis)
-    stacked = jnp.stack(pieces)
-    order = (me - jnp.arange(count, dtype=jnp.int32)) % count
-    return jnp.take(stacked, order, axis=0)
+    blocks = []
+    for source in range(count):
+        shift = (me - source) % count
+        block = pieces[count - 1]
+        for candidate in range(count - 2, -1, -1):
+            block = jnp.where(shift == candidate, pieces[candidate], block)
+        blocks.append(block)
+    return jnp.stack(blocks)
 
 
 def bcast_a2a(values, axis, count):

time: 111 us -> 113 us (1.018)
  waiting for transfers between devices: 37.9 us -> 39.3 us
    ppermute x12, waiting for transfers between devices: 9.19 us -> 10.7 us  [shift_exchange(): pieces.append(lax.ppermute(send, axis, pairs))]
  transfers between devices with their start and end apart: 16 -> 16, of which waited for: 9 -> 10; matrix products, arithmetic and copies ran while one was open for 13% -> 13% of each run, Pallas kernels for 0% -> 0%
where the time goes in v14:
time: 113 us; the launch traced here: 112 us
  waiting for transfers between devices  39.3 us (35%)
  starting transfers between devices  26.9 us (24%)
  matrix products  23.9 us (21%)
  other arithmetic  11.6 us (10%)
  local copies, waits for them, and re-layouts  9.25 us (8%)
    ppermute x12, waiting for transfers between devices, shift_exchange(): pieces.append(lax.ppermute(send, axis, pairs))  10.7 us
    all_to_all x1, waiting for transfers between devices, per_device(): back = lax.all_to_all(back_in, 'req', 0, 0, tiled=True)  9.12 us
    all_to_all x1, waiting for transfers between devices, per_device(): lax.all_to_all(packed, 'req', 0, 0, tiled=True)  8.77 us
    ppermute x12, starting transfers between devices, shift_exchange(): pieces.append(lax.ppermute(send, axis, pairs))  8.77 us
    all_to_all x1, waiting for transfers between devices, per_device(): received = lax.all_to_all(dispatch, 'req', 0, 0, tiled=True)  8.44 us
    all_to_all x1, starting transfers between devices, per_device(): lax.all_to_all(query_spread, 'req', 0, 0, tiled=True)  7.29 us
    dot_general x1, matrix products, per_device(): jnp.einsum('pxd,pkd->pxk', block_queries, cache_keys, preferred_element_t...  4.03 us
    dot_general x1, matrix products, per_device(): jnp.einsum('pshk,pkhd->pshd', weights.astype(jnp.bfloat16), page_values,...  4.01 us
  transfers between devices with their start and end apart: 16, of which 10 were waited for; matrix products, arithmetic and copies ran while one was open for 13% of the time, Pallas kernels for 0%

profile of v14, /device:TPU:0, one launch (start us, length us, event | category | flops | bytes accessed | tf_op | source)
XLA Modules:
  0.0 111.5 jit_solution(12536896167930573975)
XLA Ops:
  4.3 2.0 %fusion.32 = f32[3,4,4,128]{3,1,2,0:T(4,128)S(1)} fusion(bf16[3,4,2048]{2,1,0:T(4,128)(2,1)S(1)} %multiply_convert_fusion.1, bf16[2048,3,512]{2,0,1:T(8,128)(2,1)} %param.21, f32[512]{0:T(512)S(1)} %bitcast.195), kind=kOutput, calls=%fused_computation.24 | convolution fusion | flops 25171968 | bytes 2172928 | tf_op jit(solution)/shard_map/rsd,df->rsf/dot_general | solution.py:114
  7.2 7.3 %all-to-all-start = ((bf16[8,3,4,4,128]{4,3,2,1,0:T(4,128)(2,1)}), bf16[8,3,4,4,128]{4,3,2,1,0:T(4,128)(2,1)S(1)}, u32[]{:S(2)}, u32[]{:S(2)}) async-start(bf16[8,3,4,4,128]{4,3,2,1,0:T(4,128)(2,1)} %broadcast_in_dim.172), calls=%async_computation | async-start | bytes 196608 | tf_op jit(solution)/shard_map/all_to_all | solution.py:121
  16.0 2.9 %fusion.24 = f32[3,4,2,512]{3,1,2,0:T(4,128)S(1)} fusion(bf16[2048,3,512]{2,0,1:T(8,128)(2,1)} %param.21, bf16[3,4,2048]{2,1,0:T(4,128)(2,1)S(1)} %multiply_convert_fusion.1, f32[2,512]{1,0:T(2,128)S(1)} %slice_convert_fusion.1), kind=kOutput, calls=%fused_computation.22 | convolution fusion | flops 50343936 | bytes 4296704 | tf_op jit(solution)/shard_map/rsd,dcf->rscf/dot_general | solution.py:124
  19.4 2.2 %all-to-all-done = bf16[8,3,4,4,128]{4,3,2,1,0:T(4,128)(2,1)S(1)} async-done(((bf16[8,3,4,4,128]{4,3,2,1,0:T(4,128)(2,1)}), bf16[8,3,4,4,128]{4,3,2,1,0:T(4,128)(2,1)S(1)}, u32[]{:S(2)}, u32[]{:S(2)}) %all-to-all-start) | async-done | bytes 98336 | tf_op jit(solution)/shard_map/all_to_all | solution.py:121
  22.9 4.0 %select_reduce_fusion.1 = (f32[40,16]{1,0:T(8,128)S(1)}, f32[40,16,128]{2,1,0:T(8,128)S(1)}) fusion(pred[40,128]{1,0:T(8,128)(4,1)S(1)} %fusion.82, bf16[40,128,512]{2,1,0:T(8,128)(2,1)} %param.24, bf16[40,16,512]{2,1,0:T(8,128)(2,1)S(1)} %broadcast_in_dim.174, pred[16,512]{1,0:T(8,128)(4,1)S(1)} %bitcast.192), kind=kOutput, calls=%fused_computation.57 | convolution fusion | flops 84458880 | bytes 6241792 | tf_op jit(solution)/shard_map/pxd,pkd->pxk/dot_general | solution.py:145
  28.3 4.0 %fusion.15 = f32[40,4,4,128]{3,1,2,0:T(4,128)S(1)} fusion(f32[40,4,4,128]{3,2,1,0:T(4,128)S(1)} %bitcast.169, f32[40,4,4]{1,2,0:T(4,128)S(1)} %copy.82, pred[40,128]{1,0:T(8,128)(4,1)S(1)} %fusion.82, bf16[40,128,512]{2,1,0:T(8,128)(2,1)} %param.25), kind=kOutput, calls=%fused_computation.19 | convolution fusion | flops 21299200 | bytes 5905920 | tf_op jit(solution)/shard_map/pshk,pkhd->pshd/dot_general | solution.py:153
  33.7 3.8 %all-to-all-start.1 = ((f32[24,17,128]{2,1,0:T(8,128)}), f32[24,17,128]{2,1,0:T(8,128)S(1)}, u32[]{:S(2)}, u32[]{:S(2)}) async-start(f32[24,17,128]{2,1,0:T(8,128)} %pad_maximum_fusion.1), calls=%async_computation.1 | async-start | bytes 589824 | tf_op jit(solution)/shard_map/all_to_all | solution.py:177
  37.8 8.8 %all-to-all-done.1 = f32[24,17,128]{2,1,0:T(8,128)S(1)} async-done(((f32[24,17,128]{2,1,0:T(8,128)}), f32[24,17,128]{2,1,0:T(8,128)S(1)}, u32[]{:S(2)}, u32[]{:S(2)}) %all-to-all-start.1) | async-done | bytes 208928 | tf_op jit(solution)/shard_map/all_to_all | solution.py:177
  48.1 1.5 %collective-permute-start.1 = (f32[12,2048]{1,0:T(8,128)S(1)}, f32[12,2048]{1,0:T(8,128)S(1)}, u32[]{:S(2)}, u32[]{:S(2)}) collective-permute-start(f32[12,2048]{1,0:T(8,128)S(1)} %fusion.121), channel_id=1, source_target_pairs={{0,2},{1,3},{2,0},{3,1},{4,6},{5,7},{6,4},{7,5},{8,10},{9,11},{10,... | collective-permute-start | bytes 294920 | tf_op jit(solution)/shard_map/ppermute | solution.py:51
  51.0 5.7 %collective-permute-done.1 = f32[12,2048]{1,0:T(8,128)S(1)} collective-permute-done((f32[12,2048]{1,0:T(8,128)S(1)}, f32[12,2048]{1,0:T(8,128)S(1)}, u32[]{:S(2)}, u32[]{:S(2)}) %collective-permute-start.1) | collective-permute-done | bytes 98336 | tf_op jit(solution)/shard_map/ppermute | solution.py:51
  57.4 1.1 multiply_reduce_fusion
  60.3 3.6 %all-to-all-start.2 = ((bf16[8,144,128]{2,1,0:T(8,128)(2,1)}), bf16[8,144,128]{2,1,0:T(8,128)(2,1)S(1)}, u32[]{:S(2)}, u32[]{:S(2)}) async-start(bf16[8,144,128]{2,1,0:T(8,128)(2,1)} %pad_maximum_fusion.2), calls=%async_computation.2 | async-start | bytes 589824 | tf_op jit(solution)/shard_map/all_to_all | solution.py:251
  63.9 8.4 %all-to-all-done.2 = bf16[8,144,128]{2,1,0:T(8,128)(2,1)S(1)} async-done(((bf16[8,144,128]{2,1,0:T(8,128)(2,1)}), bf16[8,144,128]{2,1,0:T(8,128)(2,1)S(1)}, u32[]{:S(2)}, u32[]{:S(2)}) %all-to-all-start.2) | async-done | bytes 294944 | tf_op jit(solution)/shard_map/all_to_all | solution.py:251
  72.9 1.5 %fusion.122 = f32[96,704]{1,0:T(8,128)S(1)} fusion(bf16[96,512]{1,0:T(8,128)(2,1)S(1)} %reshape.387, bf16[512,704]{0,1:T(8,128)(2,1)} %param.34), kind=kOutput, calls=%fused_computation.191 | convolution fusion | flops 69206016 | bytes 1089536 | tf_op jit(solution)/shard_map/dot_general | solution.py:255
  76.4 1.9 %fusion.13 = f32[48,352]{1,0:T(8,128)S(1)} fusion(bf16[48,2048]{1,0:T(8,128)(2,1)S(1)} %reshape.386, bf16[1,2048,352]{1,2,0:T(8,128)(2,1)} %param.31), kind=kOutput, calls=%fused_computation.16 | convolution fusion | flops 69206016 | bytes 1705984 | tf_op jit(solution)/shard_map/dot_general | solution.py:264
  78.3 2.9 %fusion.9 = f32[48,2048]{1,0:T(8,128)S(1)} fusion(bf16[1,352,2048]{2,1,0:T(8,128)(2,1)} %param.33, bf16[48,2048]{1,0:T(8,128)(2,1)S(1)} %reshape.386, bf16[1,2048,352]{1,2,0:T(8,128)(2,1)} %param.32, f32[48,352]{1,0:T(8,128)S(1)} %fusion.13), kind=kOutput, calls=%fused_computation.12 | convolution fusion | flops 138513408 | bytes 3540992 | tf_op jit(solution)/shard_map/dot_general | solution.py:270
  82.4 1.1 add_add_fusion
  84.2 2.1 %collective-permute-start.11 = (bf16[24,704]{1,0:T(8,128)(2,1)}, bf16[24,704]{1,0:T(8,128)(2,1)S(1)}, u32[]{:S(2)}, u32[]{:S(2)}) collective-permute-start(bf16[24,704]{1,0:T(8,128)(2,1)} %multiply_convert_fusion.2), channel_id=1, source_target_pairs={{0,3},{1,0},{2,1},{3,2},{4,7},{5,4},{6,5},{7,6},{8,11},{9,8},{10,9... | collective-permute-start | bytes 101384 | tf_op jit(solution)/shard_map/ppermute | solution.py:51
  88.1 1.6 %collective-permute-start.8 = (f32[24576]{0:T(1024)}, f32[24576]{0:T(1024)S(1)}, u32[]{:S(2)}, u32[]{:S(2)}) collective-permute-start(f32[24576]{0:T(1024)} %bitcast.47), channel_id=1, source_target_pairs={{0,3},{1,0},{2,1},{3,2},{4,7},{5,4},{6,5},{7,6},{8,11},{9,8},{10,9... | collective-permute-start | bytes 294920 | tf_op jit(solution)/shard_map/ppermute | solution.py:51
  89.7 1.7 %collective-permute-start.7 = (f32[24576]{0:T(1024)S(1)}, f32[24576]{0:T(1024)S(1)}, u32[]{:S(2)}, u32[]{:S(2)}) collective-permute-start(f32[24576]{0:T(1024)S(1)} %bitcast.185), channel_id=1, source_target_pairs={{0,2},{1,3},{2,0},{3,1},{4,6},{5,7},{6,4},{7,5},{8,10},{9,11},{10,... | collective-permute-start | bytes 294920 | tf_op jit(solution)/shard_map/ppermute | solution.py:51
  92.4 1.4 %fusion.124 = f32[96,512]{1,0:T(8,128)S(1)} fusion(bf16[96,704]{1,0:T(8,128)(2,1)S(1)} %bitcast.174, bf16[704,512]{1,0:T(8,128)(2,1)} %param.36), kind=kOutput, calls=%fused_computation.193 | convolution fusion | flops 69206016 | bytes 1052672 | tf_op jit(solution)/shard_map/dot_general | solution.py:282
  94.3 2.5 %collective-permute-done.7 = f32[24576]{0:T(1024)S(1)} collective-permute-done((f32[24576]{0:T(1024)S(1)}, f32[24576]{0:T(1024)S(1)}, u32[]{:S(2)}, u32[]{:S(2)}) %collective-permute-start.7) | collective-permute-done | bytes 98336 | tf_op jit(solution)/shard_map/ppermute | solution.py:51
  97.6 3.4 %all-to-all-start.3 = ((f32[8,72,128]{2,1,0:T(8,128)}), f32[8,72,128]{2,1,0:T(8,128)S(1)}, u32[]{:S(2)}, u32[]{:S(2)}) async-start(f32[8,72,128]{2,1,0:T(8,128)} %pad_maximum_fusion.3), calls=%async_computation.3 | async-start | bytes 589824 | tf_op jit(solution)/shard_map/all_to_all | solution.py:292
  101.5 9.1 %all-to-all-done.3 = f32[8,72,128]{2,1,0:T(8,128)S(1)} async-done(((f32[8,72,128]{2,1,0:T(8,128)}), f32[8,72,128]{2,1,0:T(8,128)S(1)}, u32[]{:S(2)}, u32[]{:S(2)}) %all-to-all-start.3) | async-done | bytes 294944 | tf_op jit(solution)/shard_map/all_to_all | solution.py:292
  (154 shorter events, 26.5 us)
Async XLA Ops:
  0.0 47.7 %copy-start = (bf16[512,2048]{1,0:T(8,128)(2,1)S(1)}, bf16[512,2048]{1,0:T(8,128)(2,1)}, u32[]{:S(2)}) copy-start(bf16[512,2048]{1,0:T(8,128)(2,1)} %param.23) | copy-start | bytes 6291460
  0.0 15.1 %copy-start.1 = (s32[24]{0:T(128)S(1)}, s32[24]{0:T(128)}, u32[]{:S(2)}) copy-start(s32[24]{0:T(128)} %param.27) | copy-start | bytes 292
  0.0 14.5 %copy-start.13 = (bf16[3,512]{1,0:T(4,128)(2,1)S(1)}, bf16[3,512]{1,0:T(4,128)(2,1)}, u32[]{:S(2)}) copy-start(bf16[3,512]{1,0:T(4,128)(2,1)} %param.22) | copy-start | bytes 9220
  0.0 14.5 %copy-start.9 = (s32[3,4,4]{2,1,0:T(4,128)S(1)}, s32[3,4,4]{2,1,0:T(4,128)}, u32[]{:S(2)}) copy-start(s32[3,4,4]{2,1,0:T(4,128)} %param.29) | copy-start | bytes 580
  0.0 14.7 %copy-start.8 = (s32[24,37]{1,0:T(8,128)S(1)}, s32[24,37]{1,0:T(8,128)}, u32[]{:S(2)}) copy-start(s32[24,37]{1,0:T(8,128)} %param.26) | copy-start | bytes 10660
  7.2 14.4 %all-to-all-start = ((bf16[8,3,4,4,128]{4,3,2,1,0:T(4,128)(2,1)}), bf16[8,3,4,4,128]{4,3,2,1,0:T(4,128)(2,1)S(1)}, u32[]{:S(2)}, u32[]{:S(2)}) async-start(bf16[8,3,4,4,128]{4,3,2,1,0:T(4,128)(2,1)} %broadcast_in_dim.172), calls=%async_computation | async-start | bytes 196608 | tf_op jit(solution)/shard_map/all_to_all | solution.py:121
  33.7 12.8 %all-to-all-start.1 = ((f32[24,17,128]{2,1,0:T(8,128)}), f32[24,17,128]{2,1,0:T(8,128)S(1)}, u32[]{:S(2)}, u32[]{:S(2)}) async-start(f32[24,17,128]{2,1,0:T(8,128)} %pad_maximum_fusion.1), calls=%async_computation.1 | async-start | bytes 589824 | tf_op jit(solution)/shard_map/all_to_all | solution.py:177
  48.1 2.9 %collective-permute-start.2 = (f32[12,2048]{1,0:T(8,128)S(1)}, f32[12,2048]{1,0:T(8,128)S(1)}, u32[]{:S(2)}, u32[]{:S(2)}) collective-permute-start(f32[12,2048]{1,0:T(8,128)S(1)} %fusion.121), channel_id=1, source_target_pairs={{0,3},{1,0},{2,1},{3,2},{4,7},{5,4},{6,5},{7,6},{8,11},{9,8},{10,9... | collective-permute-start | bytes 294920 | tf_op jit(solution)/shard_map/ppermute | solution.py:51
  48.1 8.6 %collective-permute-start.1 = (f32[12,2048]{1,0:T(8,128)S(1)}, f32[12,2048]{1,0:T(8,128)S(1)}, u32[]{:S(2)}, u32[]{:S(2)}) collective-permute-start(f32[12,2048]{1,0:T(8,128)S(1)} %fusion.121), channel_id=1, source_target_pairs={{0,2},{1,3},{2,0},{3,1},{4,6},{5,7},{6,4},{7,5},{8,10},{9,11},{10,... | collective-permute-start | bytes 294920 | tf_op jit(solution)/shard_map/ppermute | solution.py:51
  49.7 7.7 %collective-permute-start = (f32[12,2048]{1,0:T(8,128)S(1)}, f32[12,2048]{1,0:T(8,128)}, u32[]{:S(2)}, u32[]{:S(2)}) collective-permute-start(f32[12,2048]{1,0:T(8,128)S(1)} %fusion.121), channel_id=1, source_target_pairs={{0,1},{1,2},{2,3},{3,0},{4,5},{5,6},{6,7},{7,4},{8,9},{9,10},{10,1... | collective-permute-start | bytes 294920 | tf_op jit(solution)/shard_map/ppermute | solution.py:51
  50.2 22.4 %copy-start.2 = (bf16[512,704]{0,1:T(8,128)(2,1)S(1)}, bf16[512,704]{0,1:T(8,128)(2,1)}, u32[]{:S(2)}) copy-start(bf16[512,704]{0,1:T(8,128)(2,1)} %param.35) | copy-start | bytes 2162692
  60.3 12.1 %all-to-all-start.2 = ((bf16[8,144,128]{2,1,0:T(8,128)(2,1)}), bf16[8,144,128]{2,1,0:T(8,128)(2,1)S(1)}, u32[]{:S(2)}, u32[]{:S(2)}) async-start(bf16[8,144,128]{2,1,0:T(8,128)(2,1)} %pad_maximum_fusion.2), calls=%async_computation.2 | async-start | bytes 589824 | tf_op jit(solution)/shard_map/all_to_all | solution.py:251
  75.3 6.0 %collective-permute-start.5 = (f32[33792]{0:T(1024)S(1)}, f32[33792]{0:T(1024)}, u32[]{:S(2)}, u32[]{:S(2)}) collective-permute-start(f32[33792]{0:T(1024)S(1)} %bitcast.180), channel_id=1, source_target_pairs={{0,3},{1,0},{2,1},{3,2},{4,7},{5,4},{6,5},{7,6},{8,11},{9,8},{10,9... | collective-permute-start | bytes 405512 | tf_op jit(solution)/shard_map/ppermute | solution.py:51
  75.4 6.0 %collective-permute-start.3 = (f32[33792]{0:T(1024)S(1)}, f32[33792]{0:T(1024)}, u32[]{:S(2)}, u32[]{:S(2)}) collective-permute-start(f32[33792]{0:T(1024)S(1)} %bitcast.179), channel_id=1, source_target_pairs={{0,1},{1,2},{2,3},{3,0},{4,5},{5,6},{6,7},{7,4},{8,9},{9,10},{10,1... | collective-permute-start | bytes 405512 | tf_op jit(solution)/shard_map/ppermute | solution.py:51
  75.9 6.6 %collective-permute-start.4 = (f32[33792]{0:T(1024)S(1)}, f32[33792]{0:T(1024)}, u32[]{:S(2)}, u32[]{:S(2)}) collective-permute-start(f32[33792]{0:T(1024)S(1)} %bitcast.178), channel_id=1, source_target_pairs={{0,2},{1,3},{2,0},{3,1},{4,6},{5,7},{6,4},{7,5},{8,10},{9,11},{10,... | collective-permute-start | bytes 405512 | tf_op jit(solution)/shard_map/ppermute | solution.py:51
  84.2 5.5 %collective-permute-start.11 = (bf16[24,704]{1,0:T(8,128)(2,1)}, bf16[24,704]{1,0:T(8,128)(2,1)S(1)}, u32[]{:S(2)}, u32[]{:S(2)}) collective-permute-start(bf16[24,704]{1,0:T(8,128)(2,1)} %multiply_convert_fusion.2), channel_id=1, source_target_pairs={{0,3},{1,0},{2,1},{3,2},{4,7},{5,4},{6,5},{7,6},{8,11},{9,8},{10,9... | collective-permute-start | bytes 101384 | tf_op jit(solution)/shard_map/ppermute | solution.py:51
  86.3 5.1 %collective-permute-start.10 = (bf16[24,704]{1,0:T(8,128)(2,1)}, bf16[24,704]{1,0:T(8,128)(2,1)}, u32[]{:S(2)}, u32[]{:S(2)}) collective-permute-start(bf16[24,704]{1,0:T(8,128)(2,1)} %multiply_convert_fusion.2), channel_id=1, source_target_pairs={{0,2},{1,3},{2,0},{3,1},{4,6},{5,7},{6,4},{7,5},{8,10},{9,11},{10,... | collective-permute-start | bytes 101384 | tf_op jit(solution)/shard_map/ppermute | solution.py:51
  86.6 4.8 %collective-permute-start.9 = (bf16[24,704]{1,0:T(8,128)(2,1)}, bf16[24,704]{1,0:T(8,128)(2,1)}, u32[]{:S(2)}, u32[]{:S(2)}) collective-permute-start(bf16[24,704]{1,0:T(8,128)(2,1)} %multiply_convert_fusion.2), channel_id=1, source_target_pairs={{0,1},{1,2},{2,3},{3,0},{4,5},{5,6},{6,7},{7,4},{8,9},{9,10},{10,1... | collective-permute-start | bytes 101384 | tf_op jit(solution)/shard_map/ppermute | solution.py:51
  88.0 13.1 %copy-start.12 = (bf16[2048]{0:T(1024)(128)(2,1)S(1)}, bf16[2048]{0:T(1024)(128)(2,1)}, u32[]{:S(2)}) copy-start(bf16[2048]{0:T(1024)(128)(2,1)} %param.37) | copy-start | bytes 12292
  88.1 13.4 %copy-start.5 = (bf16[12,2048]{1,0:T(8,128)(2,1)S(1)}, bf16[12,2048]{1,0:T(8,128)(2,1)}, u32[]{:S(2)}) copy-start(bf16[12,2048]{1,0:T(8,128)(2,1)} %copy-done.4) | copy-start | bytes 147460
  88.1 5.7 %collective-permute-start.8 = (f32[24576]{0:T(1024)}, f32[24576]{0:T(1024)S(1)}, u32[]{:S(2)}, u32[]{:S(2)}) collective-permute-start(f32[24576]{0:T(1024)} %bitcast.47), channel_id=1, source_target_pairs={{0,3},{1,0},{2,1},{3,2},{4,7},{5,4},{6,5},{7,6},{8,11},{9,8},{10,9... | collective-permute-start | bytes 294920 | tf_op jit(solution)/shard_map/ppermute | solution.py:51
  89.6 4.7 %collective-permute-start.6 = (f32[24576]{0:T(1024)S(1)}, f32[24576]{0:T(1024)S(1)}, u32[]{:S(2)}, u32[]{:S(2)}) collective-permute-start(f32[24576]{0:T(1024)S(1)} %bitcast.186), channel_id=1, source_target_pairs={{0,1},{1,2},{2,3},{3,0},{4,5},{5,6},{6,7},{7,4},{8,9},{9,10},{10,1... | collective-permute-start | bytes 294920 | tf_op jit(solution)/shard_map/ppermute | solution.py:51
  89.7 7.1 %collective-permute-start.7 = (f32[24576]{0:T(1024)S(1)}, f32[24576]{0:T(1024)S(1)}, u32[]{:S(2)}, u32[]{:S(2)}) collective-permute-start(f32[24576]{0:T(1024)S(1)} %bitcast.185), channel_id=1, source_target_pairs={{0,2},{1,3},{2,0},{3,1},{4,6},{5,7},{6,4},{7,5},{8,10},{9,11},{10,... | collective-permute-start | bytes 294920 | tf_op jit(solution)/shard_map/ppermute | solution.py:51
  97.6 13.1 %all-to-all-start.3 = ((f32[8,72,128]{2,1,0:T(8,128)}), f32[8,72,128]{2,1,0:T(8,128)S(1)}, u32[]{:S(2)}, u32[]{:S(2)}) async-start(f32[8,72,128]{2,1,0:T(8,128)} %pad_maximum_fusion.3), calls=%async_computation.3 | async-start | bytes 589824 | tf_op jit(solution)/shard_map/all_to_all | solution.py:292
  (6 other events, 31.9 us)

commit v15 on v13

--- a/solution.py
+++ b/solution.py
@@ -111,11 +111,10 @@
         ) + qkv_bias[part].astype(jnp.float32)
 
     query_new = rotate(project(0, normed).reshape(head_shape), positions).astype(jnp.bfloat16)
-    query_spread = jnp.broadcast_to(query_new[None], (req_count,) + query_new.shape)
-    normed_late, query_spread = lax.optimization_barrier((normed, query_spread))
-    query_all = lax.all_to_all(query_spread, "req", 0, 0, tiled=True).reshape(
-        (req_count * req_rows,) + query_new.shape[1:]
-    )
+    normed_late, query_new = lax.optimization_barrier((normed, query_new))
+    query_all = by_source(
+        shift_exchange(query_new, "req", req_count, spread=True), "req", req_count
+    ).reshape((req_count * req_rows,) + query_new.shape[1:])
     key_value = jnp.einsum(
         "rsd,dcf->rscf", normed_late, qkv_weight[:, 1:], preferred_element_type=jnp.float32
     ) + qkv_bias[1:].astype(jnp.float32)

time: 111 us -> 123 us (1.11)
  waiting for transfers between devices: 37.9 us -> 45.6 us
  starting transfers between devices: 26.9 us -> 30.3 us
    ppermute x12 -> x19, waiting for transfers between devices: 9.19 us -> 20.1 us  [shift_exchange(): pieces.append(lax.ppermute(send, axis, pairs))]
    ppermute x12 -> x19, starting transfers between devices: 8.72 us -> 19.5 us  [shift_exchange(): pieces.append(lax.ppermute(send, axis, pairs))]
    all_to_all x1 -> x0, starting transfers between devices: 7.29 us -> none  [per_device(): lax.all_to_all(query_spread, 'req', 0, 0, tiled=True)]
    all_to_all x1 -> x0, waiting for transfers between devices: 2.19 us -> none  [per_device(): lax.all_to_all(query_spread, 'req', 0, 0, tiled=True)]
  transfers between devices with their start and end apart: 16 -> 22, of which waited for: 9 -> 10; matrix products, arithmetic and copies ran while one was open for 13% -> 12% of each run, Pallas kernels for 0% -> 0%
where the time goes in v15:
time: 123 us; the launch traced here: 122 us
  waiting for transfers between devices  45.6 us (37%)
  starting transfers between devices  30.3 us (25%)
  matrix products  23.9 us (19%)
  other arithmetic  11.9 us (10%)
  local copies, waits for them, and re-layouts  9.61 us (8%)
    ppermute x19, waiting for transfers between devices, shift_exchange(): pieces.append(lax.ppermute(send, axis, pairs))  20.1 us
    ppermute x19, starting transfers between devices, shift_exchange(): pieces.append(lax.ppermute(send, axis, pairs))  19.5 us
    all_to_all x1, waiting for transfers between devices, per_device(): back = lax.all_to_all(back_in, 'req', 0, 0, tiled=True)  9.23 us
    all_to_all x1, waiting for transfers between devices, per_device(): lax.all_to_all(packed, 'req', 0, 0, tiled=True)  8.13 us
    all_to_all x1, waiting for transfers between devices, per_device(): received = lax.all_to_all(dispatch, 'req', 0, 0, tiled=True)  8.13 us
    dot_general x1, matrix products, per_device(): jnp.einsum('pxd,pkd->pxk', block_queries, cache_keys, preferred_element_t...  4.03 us
    dot_general x1, matrix products, per_device(): jnp.einsum('pshk,pkhd->pshd', weights.astype(jnp.bfloat16), page_values,...  4.01 us
    all_to_all x1, starting transfers between devices, per_device(): back = lax.all_to_all(back_in, 'req', 0, 0, tiled=True)  3.91 us
  transfers between devices with their start and end apart: 22, of which 10 were waited for; matrix products, arithmetic and copies ran while one was open for 12% of the time, Pallas kernels for 0%

profile of v15, /device:TPU:0, one launch (start us, length us, event | category | flops | bytes accessed | tf_op | source)
XLA Modules:
  0.0 122.1 jit_solution(5417634974768690417)
XLA Ops:
  4.3 2.0 %fusion.32 = f32[3,4,4,128]{3,1,2,0:T(4,128)S(1)} fusion(bf16[3,4,2048]{2,1,0:T(4,128)(2,1)S(1)} %multiply_convert_fusion.1, bf16[2048,3,512]{2,0,1:T(8,128)(2,1)} %param.21, f32[512]{0:T(512)S(1)} %bitcast.213), kind=kOutput, calls=%fused_computation.26 | convolution fusion | flops 25171968 | bytes 2172928 | tf_op jit(solution)/shard_map/rsd,df->rsf/dot_general | solution.py:109
  6.5 6.0 %collective-permute-start.6 = (bf16[3,4,4,128]{3,1,2,0:T(4,128)(2,1)S(1)}, bf16[3,4,4,128]{3,1,2,0:T(4,128)(2,1)S(1)}, u32[]{:S(2)}, u32[]{:S(2)}) collective-permute-start(bf16[3,4,4,128]{3,1,2,0:T(4,128)(2,1)S(1)} %pad_maximum_fusion.5), channel_id=1, source_target_pairs={{0,28},{4,0},{8,4},{12,8},{16,12},{20,16},{24,20},{28,24},{1,29},{... | collective-permute-start | bytes 36872 | tf_op jit(solution)/shard_map/ppermute | solution.py:51
  13.0 3.0 %collective-permute-start.3 = (bf16[3,4,4,128]{3,1,2,0:T(4,128)(2,1)S(1)}, bf16[3,4,4,128]{3,1,2,0:T(4,128)(2,1)S(1)}, u32[]{:S(2)}, u32[]{:S(2)}) collective-permute-start(bf16[3,4,4,128]{3,1,2,0:T(4,128)(2,1)S(1)} %pad_maximum_fusion.5), channel_id=1, source_target_pairs={{0,16},{4,20},{8,24},{12,28},{16,0},{20,4},{24,8},{28,12},{1,17},{... | collective-permute-start | bytes 36872 | tf_op jit(solution)/shard_map/ppermute | solution.py:51
  16.0 1.5 %collective-permute-start = (bf16[3,4,4,128]{3,1,2,0:T(4,128)(2,1)S(1)}, bf16[3,4,4,128]{3,1,2,0:T(4,128)(2,1)S(1)}, u32[]{:S(2)}, u32[]{:S(2)}) collective-permute-start(bf16[3,4,4,128]{3,1,2,0:T(4,128)(2,1)S(1)} %pad_maximum_fusion.5), channel_id=1, source_target_pairs={{0,4},{4,8},{8,12},{12,16},{16,20},{20,24},{24,28},{28,0},{1,5},{5... | collective-permute-start | bytes 36872 | tf_op jit(solution)/shard_map/ppermute | solution.py:51
  18.9 2.9 %fusion.24 = f32[3,4,2,512]{3,1,2,0:T(4,128)S(1)} fusion(bf16[2048,3,512]{2,0,1:T(8,128)(2,1)} %param.21, bf16[3,4,2048]{2,1,0:T(4,128)(2,1)S(1)} %multiply_convert_fusion.1, f32[2,512]{1,0:T(2,128)S(1)} %slice_convert_fusion.1), kind=kOutput, calls=%fused_computation.24 | convolution fusion | flops 50343936 | bytes 4296704 | tf_op jit(solution)/shard_map/rsd,dcf->rscf/dot_general | solution.py:118
  22.7 5.5 %collective-permute-done.1 = bf16[3,4,4,128]{3,1,2,0:T(4,128)(2,1)S(1)} collective-permute-done((bf16[3,4,4,128]{3,1,2,0:T(4,128)(2,1)S(1)}, bf16[3,4,4,128]{3,1,2,0:T(4,128)(2,1)S(1)}, u32[]{:S(2)}, u32[]{:S(2)}) %collective-permute-start.1) | collective-permute-done | bytes 12320 | tf_op jit(solution)/shard_map/ppermute | solution.py:51
  28.2 5.5 %collective-permute-done.2 = bf16[3,4,4,128]{3,1,2,0:T(4,128)(2,1)S(1)} collective-permute-done((bf16[3,4,4,128]{3,1,2,0:T(4,128)(2,1)S(1)}, bf16[3,4,4,128]{3,1,2,0:T(4,128)(2,1)S(1)}, u32[]{:S(2)}, u32[]{:S(2)}) %collective-permute-start.2) | collective-permute-done | bytes 12320 | tf_op jit(solution)/shard_map/ppermute | solution.py:51
  35.9 4.0 %select_reduce_fusion.1 = (f32[40,16]{1,0:T(8,128)S(1)}, f32[40,16,128]{2,1,0:T(8,128)S(1)}) fusion(pred[40,128]{1,0:T(8,128)(4,1)S(1)} %fusion.82, bf16[40,128,512]{2,1,0:T(8,128)(2,1)} %param.24, bf16[40,16,512]{2,1,0:T(8,128)(2,1)S(1)} %broadcast_in_dim.199, pred[16,512]{1,0:T(8,128)(4,1)S(1)} %bitcast.210), kind=kOutput, calls=%fused_computation.59 | convolution fusion | flops 84458880 | bytes 6241792 | tf_op jit(solution)/shard_map/pxd,pkd->pxk/dot_general | solution.py:139
  41.3 4.0 %fusion.15 = f32[40,4,4,128]{3,1,2,0:T(4,128)S(1)} fusion(f32[40,4,4,128]{3,2,1,0:T(4,128)S(1)} %bitcast.188, f32[40,4,4]{1,2,0:T(4,128)S(1)} %copy.82, pred[40,128]{1,0:T(8,128)(4,1)S(1)} %fusion.82, bf16[40,128,512]{2,1,0:T(8,128)(2,1)} %param.25), kind=kOutput, calls=%fused_computation.21 | convolution fusion | flops 21299200 | bytes 5905920 | tf_op jit(solution)/shard_map/pshk,pkhd->pshd/dot_general | solution.py:147
  46.8 3.4 %all-to-all-start = ((f32[24,17,128]{2,1,0:T(8,128)}), f32[24,17,128]{2,1,0:T(8,128)S(1)}, u32[]{:S(2)}, u32[]{:S(2)}) async-start(f32[24,17,128]{2,1,0:T(8,128)} %pad_maximum_fusion.1), calls=%async_computation | async-start | bytes 589824 | tf_op jit(solution)/shard_map/all_to_all | solution.py:171
  50.4 8.1 %all-to-all-done = f32[24,17,128]{2,1,0:T(8,128)S(1)} async-done(((f32[24,17,128]{2,1,0:T(8,128)}), f32[24,17,128]{2,1,0:T(8,128)S(1)}, u32[]{:S(2)}, u32[]{:S(2)}) %all-to-all-start) | async-done | bytes 208928 | tf_op jit(solution)/shard_map/all_to_all | solution.py:171
  60.1 1.5 %collective-permute-start.8 = (f32[12,2048]{1,0:T(8,128)S(1)}, f32[12,2048]{1,0:T(8,128)S(1)}, u32[]{:S(2)}, u32[]{:S(2)}) collective-permute-start(f32[12,2048]{1,0:T(8,128)S(1)} %fusion.127), channel_id=1, source_target_pairs={{0,2},{1,3},{2,0},{3,1},{4,6},{5,7},{6,4},{7,5},{8,10},{9,11},{10,... | collective-permute-start | bytes 294920 | tf_op jit(solution)/shard_map/ppermute | solution.py:51
  63.0 5.7 %collective-permute-done.8 = f32[12,2048]{1,0:T(8,128)S(1)} collective-permute-done((f32[12,2048]{1,0:T(8,128)S(1)}, f32[12,2048]{1,0:T(8,128)S(1)}, u32[]{:S(2)}, u32[]{:S(2)}) %collective-permute-start.8) | collective-permute-done | bytes 98336 | tf_op jit(solution)/shard_map/ppermute | solution.py:51
  72.3 3.4 %all-to-all-start.1 = ((bf16[8,144,128]{2,1,0:T(8,128)(2,1)}), bf16[8,144,128]{2,1,0:T(8,128)(2,1)S(1)}, u32[]{:S(2)}, u32[]{:S(2)}) async-start(bf16[8,144,128]{2,1,0:T(8,128)(2,1)} %pad_maximum_fusion.2), calls=%async_computation.1 | async-start | bytes 589824 | tf_op jit(solution)/shard_map/all_to_all | solution.py:245
  76.0 8.1 %all-to-all-done.1 = bf16[8,144,128]{2,1,0:T(8,128)(2,1)S(1)} async-done(((bf16[8,144,128]{2,1,0:T(8,128)(2,1)}), bf16[8,144,128]{2,1,0:T(8,128)(2,1)S(1)}, u32[]{:S(2)}, u32[]{:S(2)}) %all-to-all-start.1) | async-done | bytes 294944 | tf_op jit(solution)/shard_map/all_to_all | solution.py:245
  84.7 1.5 %fusion.128 = f32[96,704]{1,0:T(8,128)S(1)} fusion(bf16[96,512]{1,0:T(8,128)(2,1)S(1)} %reshape.479, bf16[512,704]{0,1:T(8,128)(2,1)} %param.34), kind=kOutput, calls=%fused_computation.225 | convolution fusion | flops 69206016 | bytes 1089536 | tf_op jit(solution)/shard_map/dot_general | solution.py:249
  88.3 1.9 %fusion.13 = f32[48,352]{1,0:T(8,128)S(1)} fusion(bf16[48,2048]{1,0:T(8,128)(2,1)S(1)} %reshape.478, bf16[1,2048,352]{1,2,0:T(8,128)(2,1)} %param.31), kind=kOutput, calls=%fused_computation.18 | convolution fusion | flops 69206016 | bytes 1705984 | tf_op jit(solution)/shard_map/dot_general | solution.py:258
  90.2 2.9 %fusion.9 = f32[48,2048]{1,0:T(8,128)S(1)} fusion(bf16[1,352,2048]{2,1,0:T(8,128)(2,1)} %param.33, bf16[48,2048]{1,0:T(8,128)(2,1)S(1)} %reshape.478, bf16[1,2048,352]{1,2,0:T(8,128)(2,1)} %param.32, f32[48,352]{1,0:T(8,128)S(1)} %fusion.13), kind=kOutput, calls=%fused_computation.14 | convolution fusion | flops 138513408 | bytes 3540992 | tf_op jit(solution)/shard_map/dot_general | solution.py:264
  96.0 2.0 %collective-permute-start.17 = (bf16[24,704]{1,0:T(8,128)(2,1)}, bf16[24,704]{1,0:T(8,128)(2,1)}, u32[]{:S(2)}, u32[]{:S(2)}) collective-permute-start(bf16[24,704]{1,0:T(8,128)(2,1)} %multiply_convert_fusion.2), channel_id=1, source_target_pairs={{0,2},{1,3},{2,0},{3,1},{4,6},{5,7},{6,4},{7,5},{8,10},{9,11},{10,... | collective-permute-start | bytes 101384 | tf_op jit(solution)/shard_map/ppermute | solution.py:51
  98.0 1.7 %collective-permute-start.18 = (bf16[24,704]{1,0:T(8,128)(2,1)}, bf16[24,704]{1,0:T(8,128)(2,1)}, u32[]{:S(2)}, u32[]{:S(2)}) collective-permute-start(bf16[24,704]{1,0:T(8,128)(2,1)} %multiply_convert_fusion.2), channel_id=1, source_target_pairs={{0,3},{1,0},{2,1},{3,2},{4,7},{5,4},{6,5},{7,6},{8,11},{9,8},{10,9... | collective-permute-start | bytes 101384 | tf_op jit(solution)/shard_map/ppermute | solution.py:51
  103.8 1.4 %fusion.130 = f32[96,512]{1,0:T(8,128)S(1)} fusion(bf16[96,704]{1,0:T(8,128)(2,1)S(1)} %bitcast_select_fusion, bf16[704,512]{1,0:T(8,128)(2,1)} %param.36), kind=kOutput, calls=%fused_computation.227 | convolution fusion | flops 69206016 | bytes 1052672 | tf_op jit(solution)/shard_map/dot_general | solution.py:276
  105.2 1.5 %collective-permute-done.14 = f32[24576]{0:T(1024)S(1)} collective-permute-done((f32[24576]{0:T(1024)S(1)}, f32[24576]{0:T(1024)S(1)}, u32[]{:S(2)}, u32[]{:S(2)}) %collective-permute-start.14) | collective-permute-done | bytes 98336 | tf_op jit(solution)/shard_map/ppermute | solution.py:51
  107.5 3.9 %all-to-all-start.2 = ((f32[8,72,128]{2,1,0:T(8,128)}), f32[8,72,128]{2,1,0:T(8,128)S(1)}, u32[]{:S(2)}, u32[]{:S(2)}) async-start(f32[8,72,128]{2,1,0:T(8,128)} %pad_maximum_fusion.3), calls=%async_computation.2 | async-start | bytes 589824 | tf_op jit(solution)/shard_map/all_to_all | solution.py:286
  111.9 9.2 %all-to-all-done.2 = f32[8,72,128]{2,1,0:T(8,128)S(1)} async-done(((f32[8,72,128]{2,1,0:T(8,128)}), f32[8,72,128]{2,1,0:T(8,128)S(1)}, u32[]{:S(2)}, u32[]{:S(2)}) %all-to-all-start.2) | async-done | bytes 294944 | tf_op jit(solution)/shard_map/all_to_all | solution.py:286
  (185 shorter events, 30.5 us)
Async XLA Ops:
  0.0 59.7 %copy-start = (bf16[512,2048]{1,0:T(8,128)(2,1)S(1)}, bf16[512,2048]{1,0:T(8,128)(2,1)}, u32[]{:S(2)}) copy-start(bf16[512,2048]{1,0:T(8,128)(2,1)} %param.23) | copy-start | bytes 6291460
  6.5 27.2 %collective-permute-start.6 = (bf16[3,4,4,128]{3,1,2,0:T(4,128)(2,1)S(1)}, bf16[3,4,4,128]{3,1,2,0:T(4,128)(2,1)S(1)}, u32[]{:S(2)}, u32[]{:S(2)}) collective-permute-start(bf16[3,4,4,128]{3,1,2,0:T(4,128)(2,1)S(1)} %pad_maximum_fusion.5), channel_id=1, source_target_pairs={{0,28},{4,0},{8,4},{12,8},{16,12},{20,16},{24,20},{28,24},{1,29},{... | collective-permute-start | bytes 36872 | tf_op jit(solution)/shard_map/ppermute | solution.py:51
  12.5 21.2 %collective-permute-start.5 = (bf16[3,4,4,128]{3,1,2,0:T(4,128)(2,1)S(1)}, bf16[3,4,4,128]{3,1,2,0:T(4,128)(2,1)S(1)}, u32[]{:S(2)}, u32[]{:S(2)}) collective-permute-start(bf16[3,4,4,128]{3,1,2,0:T(4,128)(2,1)S(1)} %pad_maximum_fusion.5), channel_id=1, source_target_pairs={{0,24},{4,28},{8,0},{12,4},{16,8},{20,12},{24,16},{28,20},{1,25},{... | collective-permute-start | bytes 36872 | tf_op jit(solution)/shard_map/ppermute | solution.py:51
  13.0 20.7 %collective-permute-start.4 = (bf16[3,4,4,128]{3,1,2,0:T(4,128)(2,1)S(1)}, bf16[3,4,4,128]{3,1,2,0:T(4,128)(2,1)S(1)}, u32[]{:S(2)}, u32[]{:S(2)}) collective-permute-start(bf16[3,4,4,128]{3,1,2,0:T(4,128)(2,1)S(1)} %pad_maximum_fusion.5), channel_id=1, source_target_pairs={{0,20},{4,24},{8,28},{12,0},{16,4},{20,8},{24,12},{28,16},{1,21},{... | collective-permute-start | bytes 36872 | tf_op jit(solution)/shard_map/ppermute | solution.py:51
  13.0 20.7 %collective-permute-start.3 = (bf16[3,4,4,128]{3,1,2,0:T(4,128)(2,1)S(1)}, bf16[3,4,4,128]{3,1,2,0:T(4,128)(2,1)S(1)}, u32[]{:S(2)}, u32[]{:S(2)}) collective-permute-start(bf16[3,4,4,128]{3,1,2,0:T(4,128)(2,1)S(1)} %pad_maximum_fusion.5), channel_id=1, source_target_pairs={{0,16},{4,20},{8,24},{12,28},{16,0},{20,4},{24,8},{28,12},{1,17},{... | collective-permute-start | bytes 36872 | tf_op jit(solution)/shard_map/ppermute | solution.py:51
  16.0 6.7 %collective-permute-start = (bf16[3,4,4,128]{3,1,2,0:T(4,128)(2,1)S(1)}, bf16[3,4,4,128]{3,1,2,0:T(4,128)(2,1)S(1)}, u32[]{:S(2)}, u32[]{:S(2)}) collective-permute-start(bf16[3,4,4,128]{3,1,2,0:T(4,128)(2,1)S(1)} %pad_maximum_fusion.5), channel_id=1, source_target_pairs={{0,4},{4,8},{8,12},{12,16},{16,20},{20,24},{24,28},{28,0},{1,5},{5... | collective-permute-start | bytes 36872 | tf_op jit(solution)/shard_map/ppermute | solution.py:51
  22.6 5.5 %collective-permute-start.1 = (bf16[3,4,4,128]{3,1,2,0:T(4,128)(2,1)S(1)}, bf16[3,4,4,128]{3,1,2,0:T(4,128)(2,1)S(1)}, u32[]{:S(2)}, u32[]{:S(2)}) collective-permute-start(bf16[3,4,4,128]{3,1,2,0:T(4,128)(2,1)S(1)} %pad_maximum_fusion.5), channel_id=1, source_target_pairs={{0,8},{4,12},{8,16},{12,20},{16,24},{20,28},{24,0},{28,4},{1,9},{5... | collective-permute-start | bytes 36872 | tf_op jit(solution)/shard_map/ppermute | solution.py:51
  28.1 5.5 %collective-permute-start.2 = (bf16[3,4,4,128]{3,1,2,0:T(4,128)(2,1)S(1)}, bf16[3,4,4,128]{3,1,2,0:T(4,128)(2,1)S(1)}, u32[]{:S(2)}, u32[]{:S(2)}) collective-permute-start(bf16[3,4,4,128]{3,1,2,0:T(4,128)(2,1)S(1)} %pad_maximum_fusion.5), channel_id=1, source_target_pairs={{0,12},{4,16},{8,20},{12,24},{16,28},{20,0},{24,4},{28,8},{1,13},{... | collective-permute-start | bytes 36872 | tf_op jit(solution)/shard_map/ppermute | solution.py:51
  46.8 11.8 %all-to-all-start = ((f32[24,17,128]{2,1,0:T(8,128)}), f32[24,17,128]{2,1,0:T(8,128)S(1)}, u32[]{:S(2)}, u32[]{:S(2)}) async-start(f32[24,17,128]{2,1,0:T(8,128)} %pad_maximum_fusion.1), calls=%async_computation | async-start | bytes 589824 | tf_op jit(solution)/shard_map/all_to_all | solution.py:171
  60.1 2.9 %collective-permute-start.9 = (f32[12,2048]{1,0:T(8,128)S(1)}, f32[12,2048]{1,0:T(8,128)S(1)}, u32[]{:S(2)}, u32[]{:S(2)}) collective-permute-start(f32[12,2048]{1,0:T(8,128)S(1)} %fusion.127), channel_id=1, source_target_pairs={{0,3},{1,0},{2,1},{3,2},{4,7},{5,4},{6,5},{7,6},{8,11},{9,8},{10,9... | collective-permute-start | bytes 294920 | tf_op jit(solution)/shard_map/ppermute | solution.py:51
  60.1 8.6 %collective-permute-start.8 = (f32[12,2048]{1,0:T(8,128)S(1)}, f32[12,2048]{1,0:T(8,128)S(1)}, u32[]{:S(2)}, u32[]{:S(2)}) collective-permute-start(f32[12,2048]{1,0:T(8,128)S(1)} %fusion.127), channel_id=1, source_target_pairs={{0,2},{1,3},{2,0},{3,1},{4,6},{5,7},{6,4},{7,5},{8,10},{9,11},{10,... | collective-permute-start | bytes 294920 | tf_op jit(solution)/shard_map/ppermute | solution.py:51
  61.7 7.7 %collective-permute-start.7 = (f32[12,2048]{1,0:T(8,128)S(1)}, f32[12,2048]{1,0:T(8,128)}, u32[]{:S(2)}, u32[]{:S(2)}) collective-permute-start(f32[12,2048]{1,0:T(8,128)S(1)} %fusion.127), channel_id=1, source_target_pairs={{0,1},{1,2},{2,3},{3,0},{4,5},{5,6},{6,7},{7,4},{8,9},{9,10},{10,1... | collective-permute-start | bytes 294920 | tf_op jit(solution)/shard_map/ppermute | solution.py:51
  62.2 22.1 %copy-start.2 = (bf16[512,704]{0,1:T(8,128)(2,1)S(1)}, bf16[512,704]{0,1:T(8,128)(2,1)}, u32[]{:S(2)}) copy-start(bf16[512,704]{0,1:T(8,128)(2,1)} %param.35) | copy-start | bytes 2162692
  72.3 11.8 %all-to-all-start.1 = ((bf16[8,144,128]{2,1,0:T(8,128)(2,1)}), bf16[8,144,128]{2,1,0:T(8,128)(2,1)S(1)}, u32[]{:S(2)}, u32[]{:S(2)}) async-start(bf16[8,144,128]{2,1,0:T(8,128)(2,1)} %pad_maximum_fusion.2), calls=%async_computation.1 | async-start | bytes 589824 | tf_op jit(solution)/shard_map/all_to_all | solution.py:245
  87.0 6.1 %collective-permute-start.12 = (f32[33792]{0:T(1024)S(1)}, f32[33792]{0:T(1024)}, u32[]{:S(2)}, u32[]{:S(2)}) collective-permute-start(f32[33792]{0:T(1024)S(1)} %bitcast.197), channel_id=1, source_target_pairs={{0,3},{1,0},{2,1},{3,2},{4,7},{5,4},{6,5},{7,6},{8,11},{9,8},{10,9... | collective-permute-start | bytes 405512 | tf_op jit(solution)/shard_map/ppermute | solution.py:51
  87.1 6.2 %collective-permute-start.10 = (f32[33792]{0:T(1024)S(1)}, f32[33792]{0:T(1024)}, u32[]{:S(2)}, u32[]{:S(2)}) collective-permute-start(f32[33792]{0:T(1024)S(1)} %bitcast.196), channel_id=1, source_target_pairs={{0,1},{1,2},{2,3},{3,0},{4,5},{5,6},{6,7},{7,4},{8,9},{9,10},{10,1... | collective-permute-start | bytes 405512 | tf_op jit(solution)/shard_map/ppermute | solution.py:51
  87.6 6.7 %collective-permute-start.11 = (f32[33792]{0:T(1024)S(1)}, f32[33792]{0:T(1024)}, u32[]{:S(2)}, u32[]{:S(2)}) collective-permute-start(f32[33792]{0:T(1024)S(1)} %bitcast.195), channel_id=1, source_target_pairs={{0,2},{1,3},{2,0},{3,1},{4,6},{5,7},{6,4},{7,5},{8,10},{9,11},{10,... | collective-permute-start | bytes 405512 | tf_op jit(solution)/shard_map/ppermute | solution.py:51
  96.0 5.0 %collective-permute-start.17 = (bf16[24,704]{1,0:T(8,128)(2,1)}, bf16[24,704]{1,0:T(8,128)(2,1)}, u32[]{:S(2)}, u32[]{:S(2)}) collective-permute-start(bf16[24,704]{1,0:T(8,128)(2,1)} %multiply_convert_fusion.2), channel_id=1, source_target_pairs={{0,2},{1,3},{2,0},{3,1},{4,6},{5,7},{6,4},{7,5},{8,10},{9,11},{10,... | collective-permute-start | bytes 101384 | tf_op jit(solution)/shard_map/ppermute | solution.py:51
  98.0 4.3 %collective-permute-start.16 = (bf16[24,704]{1,0:T(8,128)(2,1)}, bf16[24,704]{1,0:T(8,128)(2,1)}, u32[]{:S(2)}, u32[]{:S(2)}) collective-permute-start(bf16[24,704]{1,0:T(8,128)(2,1)} %multiply_convert_fusion.2), channel_id=1, source_target_pairs={{0,1},{1,2},{2,3},{3,0},{4,5},{5,6},{6,7},{7,4},{8,9},{9,10},{10,1... | collective-permute-start | bytes 101384 | tf_op jit(solution)/shard_map/ppermute | solution.py:51
  98.0 4.3 %collective-permute-start.18 = (bf16[24,704]{1,0:T(8,128)(2,1)}, bf16[24,704]{1,0:T(8,128)(2,1)}, u32[]{:S(2)}, u32[]{:S(2)}) collective-permute-start(bf16[24,704]{1,0:T(8,128)(2,1)} %multiply_convert_fusion.2), channel_id=1, source_target_pairs={{0,3},{1,0},{2,1},{3,2},{4,7},{5,4},{6,5},{7,6},{8,11},{9,8},{10,9... | collective-permute-start | bytes 101384 | tf_op jit(solution)/shard_map/ppermute | solution.py:51
  100.5 4.7 %collective-permute-start.15 = (f32[24576]{0:T(1024)S(1)}, f32[24576]{0:T(1024)S(1)}, u32[]{:S(2)}, u32[]{:S(2)}) collective-permute-start(f32[24576]{0:T(1024)S(1)} %bitcast.204), channel_id=1, source_target_pairs={{0,3},{1,0},{2,1},{3,2},{4,7},{5,4},{6,5},{7,6},{8,11},{9,8},{10,9... | collective-permute-start | bytes 294920 | tf_op jit(solution)/shard_map/ppermute | solution.py:51
  100.6 4.7 %collective-permute-start.13 = (f32[24576]{0:T(1024)S(1)}, f32[24576]{0:T(1024)S(1)}, u32[]{:S(2)}, u32[]{:S(2)}) collective-permute-start(f32[24576]{0:T(1024)S(1)} %bitcast.203), channel_id=1, source_target_pairs={{0,1},{1,2},{2,3},{3,0},{4,5},{5,6},{6,7},{7,4},{8,9},{9,10},{10,1... | collective-permute-start | bytes 294920 | tf_op jit(solution)/shard_map/ppermute | solution.py:51
  101.1 5.7 %collective-permute-start.14 = (f32[24576]{0:T(1024)S(1)}, f32[24576]{0:T(1024)S(1)}, u32[]{:S(2)}, u32[]{:S(2)}) collective-permute-start(f32[24576]{0:T(1024)S(1)} %bitcast.202), channel_id=1, source_target_pairs={{0,2},{1,3},{2,0},{3,1},{4,6},{5,7},{6,4},{7,5},{8,10},{9,11},{10,... | collective-permute-start | bytes 294920 | tf_op jit(solution)/shard_map/ppermute | solution.py:51
  107.5 13.7 %all-to-all-start.2 = ((f32[8,72,128]{2,1,0:T(8,128)}), f32[8,72,128]{2,1,0:T(8,128)S(1)}, u32[]{:S(2)}, u32[]{:S(2)}) async-start(f32[8,72,128]{2,1,0:T(8,128)} %pad_maximum_fusion.3), calls=%async_computation.2 | async-start | bytes 589824 | tf_op jit(solution)/shard_map/all_to_all | solution.py:286
  (11 other events, 119.0 us)
